TPU v7x, 512 devices: a whole 4x4x16 slice. The times are simulated.
512 devices in a mesh: leaf: 128 (over z, y, core), grp: 4 (over x).
Axes of the slice: x: 4, y: 4, z: 16, core: 2. Of those that a mesh axis runs over, the one named last changes fastest.
Arguments:
- sources: bfloat16 [16, 2097152], P(None, ('leaf', 'grp')), may hold values from -6 to 6
- points: float32 [3, 2097152], P(None, ('leaf', 'grp')), may hold values from -3 to 83
- near_offsets: int32 [32768, 6], P(('leaf', 'grp')), may hold values from -16 to 16, as said below
- far_offsets: int32 [32768, 8], P(('leaf', 'grp')), may hold values from -32 to 32, as said below
- source_basis: bfloat16 [32768, 2048], P(('leaf', 'grp')), may hold values from -0.75 to 0.75
- target_basis: bfloat16 [32768, 2048], P(('leaf', 'grp')), may hold values from -1 to 1
- leaf_coupling: bfloat16 [32768, 8, 1024], P(('leaf', 'grp')), may hold values from -0.375 to 0.375
- leaf_up: bfloat16 [32768, 1024], P(('leaf', 'grp')), may hold values from -0.125 to 0.125
- leaf_down: bfloat16 [32768, 1024], P(('leaf', 'grp')), may hold values from -1 to 1
- tree_up: bfloat16 [512, 3, 1024], P(('leaf', 'grp')), may hold values from -1 to 1, as said below
- tree_down: bfloat16 [512, 3, 1024], P(('leaf', 'grp')), may hold values from -1 to 1, as said below
- tree_coupling: bfloat16 [512, 4, 4, 1024], P(('leaf', 'grp')), may hold values from -1 to 1, as said below
Outputs:
- product: float32 [16, 2097152], P(None, ('leaf', 'grp'))
Inputs may be any that keep to these rules, and one draw needn't show every extreme that they name: `near_offsets`: each row holds 6 distinct offsets, one of them 0 and one of them 16 or -16; the first leaf of each device subtree (i % 64 = 0) holds -16, the last holds 16. `far_offsets`: each row holds 8 distinct offsets of magnitude 16 + 1 to 32, one of them of magnitude 32; the first leaf of each device subtree holds -32, the last holds 32. tree_up[d, s] is the same for all d with equal d // 2**s. tree_down[d, s] is the same for all d with equal d // 2**s. tree_coupling[d, s] is the same for all d with equal d // 2**s.
All inputs are finite; a program needn't handle non-finite values.
Results may differ from a plain program's by a relative error of at most 0.0012.
Values sent between devices are 32-bit elements; how exact they have to be, the bound alone decides.
No kernel may reach another device: no remote copies, remote signals or barrier semaphores. Data moves between devices by JAX's collectives and lax.ppermute only.
A program may use at most 128 MiB of HBM per device.

v0:
```python
import jax
import jax.numpy as jnp
from jax import lax
from jax.sharding import PartitionSpec as P

CLUSTER = 64
RANK = 32
RHS = 16
NEAR_REACH = 16
NEAR_BLOCKS = 6
FAR_REACH = 32
FAR_BLOCKS = 8
TOP_LEVELS = 3


amplitude = 0.15
length_scale = 1.0
nugget = 0.5
partner_steps = (-3, -2, 2, 3)
highest = lax.Precision.HIGHEST


def passed_along(block, axis, distance):
    devices = range(lax.axis_size(axis))
    route = [(i - distance, i) for i in devices if i - distance in devices]
    return lax.ppermute(block, axis, route)


def extended_2(block, sides, width):
    for axis, dim in sides:
        count = lax.axis_size(axis)
        forward = [(i, i + 1) for i in range(count - 1)]
        backward = [(target, source) for source, target in forward]
        low = lax.ppermute(
            lax.slice_in_dim(block, block.shape[dim] - width, None, axis=dim), axis, forward
        )
        high = lax.ppermute(lax.slice_in_dim(block, 0, width, axis=dim), axis, backward)
        block = jnp.concatenate([low, block, high], axis=dim)
    return block


def from_partner(value, axis, bit):
    return lax.ppermute(value, axis, [(i, i ^ 1 << bit) for i in range(lax.axis_size(axis))])


def matern_term(extended, target_points, slot_offsets):
    leaf_count = target_points.shape[1]
    column_count = extended.shape[0] - 3
    source_leaf = jnp.arange(leaf_count, dtype=jnp.int32) + NEAR_REACH + slot_offsets
    chosen = jnp.take(extended, source_leaf, axis=1)
    squared = jnp.zeros((leaf_count, CLUSTER, CLUSTER), jnp.float32)
    for component in range(3):
        separation = (
            chosen[column_count + component][:, :, None] - target_points[component][:, None, :]
        )
        squared = squared + separation * separation
    kernel = (amplitude * jnp.exp(-jnp.sqrt(squared) / length_scale)).astype(jnp.bfloat16)
    values = chosen[:column_count].astype(jnp.bfloat16)
    return jnp.einsum("rla,lab->rlb", values, kernel, preferred_element_type=jnp.float32)


def apply_matrix(coefficients, matrix):
    return jnp.dot(
        coefficients,
        matrix.reshape(RANK, RANK),
        precision=highest,
        preferred_element_type=jnp.float32,
    )


def partner_coefficients(coefficients, distance):
    return passed_along(coefficients, ("leaf", "grp"), distance)


def local(
    sources,
    points,
    near_offsets,
    far_offsets,
    source_basis,
    target_basis,
    leaf_coupling,
    leaf_up,
    leaf_down,
    tree_up,
    tree_down,
    tree_coupling,
):
    leaf_count = near_offsets.shape[0]
    packed = jnp.concatenate([sources.astype(jnp.float32), points], axis=0)
    padded = extended_2(packed, ((("leaf", "grp"), 1),), NEAR_REACH * CLUSTER)
    extended = padded.reshape(RHS + 3, leaf_count + 2 * NEAR_REACH, CLUSTER)
    target_points = points.reshape(3, leaf_count, CLUSTER)
    leaf_values = sources.reshape(RHS, leaf_count, CLUSTER)
    near_sum = nugget * leaf_values.astype(jnp.float32)
    for near_slot in range(NEAR_BLOCKS):
        near_sum = near_sum + matern_term(extended, target_points, near_offsets[:, near_slot])
    leaf_coefficients = jnp.einsum(
        "rla,lak->lrk",
        leaf_values,
        source_basis.reshape(leaf_count, CLUSTER, RANK),
        preferred_element_type=jnp.float32,
    )
    rimmed = extended_2(
        leaf_coefficients.reshape(leaf_count, RHS * RANK), ((("leaf", "grp"), 0),), FAR_REACH
    )
    far_index = jnp.arange(leaf_count, dtype=jnp.int32)[:, None] + FAR_REACH + far_offsets
    partner_blocks = jnp.take(rimmed, far_index, axis=0).reshape(leaf_count, FAR_BLOCKS, RHS, RANK)
    leaf_far = jnp.einsum(
        "lfrk,lfkq->lrq",
        partner_blocks,
        leaf_coupling.reshape(leaf_count, FAR_BLOCKS, RANK, RANK),
        precision=highest,
        preferred_element_type=jnp.float32,
    )
    root_coefficients = jnp.einsum(
        "lrk,lkq->rq",
        leaf_coefficients,
        leaf_up.reshape(leaf_count, RANK, RANK),
        precision=highest,
        preferred_element_type=jnp.float32,
    )
    up_matrices = tree_up[0]
    down_matrices = tree_down[0]
    cross_matrices = tree_coupling[0]
    level_terms = []
    level_coefficients = [root_coefficients]
    current = root_coefficients
    for tree_level in range(TOP_LEVELS):
        lifted = apply_matrix(current, up_matrices[tree_level])
        current = lifted + from_partner(lifted, ("leaf", "grp"), tree_level)
        level_coefficients.append(current)
    for tree_level in range(TOP_LEVELS + 1):
        summed = jnp.zeros((RHS, RANK), jnp.float32)
        for partner_slot, partner_step in enumerate(partner_steps):
            arrived = partner_coefficients(
                level_coefficients[tree_level], -partner_step * 2**tree_level
            )
            summed = summed + apply_matrix(arrived, cross_matrices[tree_level, partner_slot])
        level_terms.append(summed)
    downward = level_terms[TOP_LEVELS]
    for tree_level in reversed(range(TOP_LEVELS)):
        downward = level_terms[tree_level] + apply_matrix(downward, down_matrices[tree_level])
    from_root = jnp.einsum(
        "rk,lkq->lrq",
        downward,
        leaf_down.reshape(leaf_count, RANK, RANK),
        precision=highest,
        preferred_element_type=jnp.float32,
    )
    leaf_field = leaf_far + from_root
    far_out = jnp.einsum(
        "lrk,lka->rla",
        leaf_field,
        target_basis.reshape(leaf_count, RANK, CLUSTER),
        precision=highest,
        preferred_element_type=jnp.float32,
    )
    return (near_sum + far_out).reshape(RHS, leaf_count * CLUSTER)


def solution(mesh):
    placed = (
        P(None, ("leaf", "grp")),
        P(None, ("leaf", "grp")),
        P(("leaf", "grp"), None),
        P(("leaf", "grp"), None),
        P(("leaf", "grp"), None),
        P(("leaf", "grp"), None),
        P(("leaf", "grp"), None, None),
        P(("leaf", "grp"), None),
        P(("leaf", "grp"), None),
        P(("leaf", "grp"), None, None),
        P(("leaf", "grp"), None, None),
        P(("leaf", "grp"), None, None, None),
    )
    return jax.shard_map(
        local, mesh=mesh, in_specs=placed, out_specs=P(None, ("leaf", "grp")), check_vma=False
    )
```

profile of v0, /device:TPU:383, one launch (start us, length us, event | category | flops | bytes accessed | tf_op | source)
XLA Modules:
  0.0 216.9 jit_solution(1646866990124350100)
XLA Ops:
  0.0 1.3 copy.25
  1.3 1.1 copy.27
  2.4 1.2 reshape.86
  3.7 0.8 copy.39
  5.0 0.8 convolution_bitcast_fusion.8
  5.7 2.1 collective-permute-start.7
  7.9 4.6 %collective-permute-start.6 = (f32[16,32]{1,0:T(8,128)S(1)}, f32[16,32]{1,0:T(8,128)}, u32[]{:S(2)}, u32[]{:S(2)}) collective-permute-start(f32[16,32]{1,0:T(8,128)S(1)} %convolution_bitcast_fusion.8), channel_id=1, source_target_pairs={{2,0},{3,1},{4,2},{5,3},{6,4},{7,5},{8,6},{9,7},{10,8},{11,9},{12,... | collective-permute-start | bytes 6152 | tf_op jit(solution)/shard_map/ppermute | solution.py:26
  12.5 6.7 %collective-permute-start.5 = (f32[16,32]{1,0:T(8,128)S(1)}, f32[16,32]{1,0:T(8,128)}, u32[]{:S(2)}, u32[]{:S(2)}) collective-permute-start(f32[16,32]{1,0:T(8,128)S(1)} %convolution_bitcast_fusion.8), channel_id=1, source_target_pairs={{0,2},{1,3},{2,4},{3,5},{4,6},{5,7},{6,8},{7,9},{8,10},{9,11},{10,... | collective-permute-start | bytes 6152 | tf_op jit(solution)/shard_map/ppermute | solution.py:26
  19.2 3.5 %collective-permute-start.4 = (f32[16,32]{1,0:T(8,128)S(1)}, f32[16,32]{1,0:T(8,128)}, u32[]{:S(2)}, u32[]{:S(2)}) collective-permute-start(f32[16,32]{1,0:T(8,128)S(1)} %convolution_bitcast_fusion.8), channel_id=1, source_target_pairs={{0,3},{1,4},{2,5},{3,6},{4,7},{5,8},{6,9},{7,10},{8,11},{9,12},{10... | collective-permute-start | bytes 6152 | tf_op jit(solution)/shard_map/ppermute | solution.py:26
  23.5 2.7 %collective-permute-start.8 = (f32[16,32]{1,0:T(8,128)}, f32[16,32]{1,0:T(8,128)}, u32[]{:S(2)}, u32[]{:S(2)}) collective-permute-start(f32[16,32]{1,0:T(8,128)} %fusion.90), channel_id=1, source_target_pairs={{0,1},{1,0},{2,3},{3,2},{4,5},{5,4},{6,7},{7,6},{8,9},{9,8},{10,11... | collective-permute-start | bytes 6152 | tf_op jit(solution)/shard_map/ppermute | solution.py:43
  26.2 0.8 fusion.86
  45.8 0.8 copy.40
  46.6 2.4 %copy.31 = bf16[64,8,1024]{0,2,1:T(8,128)(2,1)S(1)} copy(bf16[64,8,1024]{2,1,0:T(8,128)(2,1)} %param.20) | data formatting | bytes 2097152 | tf_op args[6]
  49.0 6.8 %copy.36 = bf16[64,8,32,32]{3,2,1,0:T(8,128)(2,1)} copy(bf16[64,8,32,32]{0,3,2,1:T(8,128)(2,1)S(1)} %bitcast.157) | data formatting | bytes 2097152 | tf_op jit(solution)/shard_map/reshape | solution.py:112
  56.0 1.2 slice.251
  57.3 1.1 slice.249
  58.4 1.3 copy.24
  59.7 1.5 reshape.93
  63.2 2.5 %collective-permute-start.3 = (f32[32,512]{1,0:T(8,128)S(1)}, f32[32,512]{1,0:T(8,128)S(1)}, u32[]{:S(2)}, u32[]{:S(2)}) collective-permute-start(f32[32,512]{1,0:T(8,128)S(1)} %slice.251), channel_id=1, source_target_pairs={{1,0},{2,1},{3,2},{4,3},{5,4},{6,5},{7,6},{8,7},{9,8},{10,9},{11,1... | collective-permute-start | bytes 196616 | tf_op jit(solution)/shard_map/ppermute | solution.py:37
  66.5 0.8 fusion.94
  67.3 8.4 %collective-permute-start.2 = (f32[32,512]{1,0:T(8,128)S(1)}, f32[32,512]{1,0:T(8,128)S(1)}, u32[]{:S(2)}, u32[]{:S(2)}) collective-permute-start(f32[32,512]{1,0:T(8,128)S(1)} %slice.249), channel_id=1, source_target_pairs={{0,1},{1,2},{2,3},{3,4},{4,5},{5,6},{6,7},{7,8},{8,9},{9,10},{10,1... | collective-permute-start | bytes 196616 | tf_op jit(solution)/shard_map/ppermute | solution.py:34
  75.7 0.8 fusion.89
  76.6 1.9 collective-permute-start.12
  78.5 0.8 fusion.88
  79.3 1.9 collective-permute-start.13
  81.3 0.8 fusion.87
  82.1 3.1 %collective-permute-done.13 = f32[16,32]{1,0:T(8,128)S(1)} collective-permute-done((f32[16,32]{1,0:T(8,128)S(1)}, f32[16,32]{1,0:T(8,128)S(1)}, u32[]{:S(2)}, u32[]{:S(2)}) %collective-permute-start.13) | collective-permute-done | bytes 2080 | tf_op jit(solution)/shard_map/ppermute | solution.py:43
  85.2 1.9 collective-permute-start.11
  87.3 7.0 %collective-permute-start.10 = (f32[16,32]{1,0:T(8,128)S(1)}, f32[16,32]{1,0:T(8,128)S(1)}, u32[]{:S(2)}, u32[]{:S(2)}) collective-permute-start(f32[16,32]{1,0:T(8,128)S(1)} %add.217), channel_id=1, source_target_pairs={{0,4},{1,5},{2,6},{3,7},{4,8},{5,9},{6,10},{7,11},{8,12},{9,13},{1... | collective-permute-start | bytes 6152 | tf_op jit(solution)/shard_map/ppermute | solution.py:26
  94.4 1.9 collective-permute-start.17
  96.5 1.9 collective-permute-start.16
  98.5 4.5 %collective-permute-done.17 = f32[16,32]{1,0:T(8,128)S(1)} collective-permute-done((f32[16,32]{1,0:T(8,128)S(1)}, f32[16,32]{1,0:T(8,128)S(1)}, u32[]{:S(2)}, u32[]{:S(2)}) %collective-permute-start.17) | collective-permute-done | bytes 2080 | tf_op jit(solution)/shard_map/ppermute | solution.py:26
  103.0 2.2 %collective-permute-start.15 = (f32[16,32]{1,0:T(8,128)S(1)}, f32[16,32]{1,0:T(8,128)S(1)}, u32[]{:S(2)}, u32[]{:S(2)}) collective-permute-start(f32[16,32]{1,0:T(8,128)S(1)} %add.221), channel_id=1, source_target_pairs={{0,8},{1,9},{2,10},{3,11},{4,12},{5,13},{6,14},{7,15},{8,16},{9,17... | collective-permute-start | bytes 6152 | tf_op jit(solution)/shard_map/ppermute | solution.py:26
  105.3 1.9 collective-permute-start.18
  107.4 1.0 collective-permute-done.18
  108.4 1.9 collective-permute-start.1
  110.4 1.9 collective-permute-start.22
  112.4 4.4 %collective-permute-done.22 = f32[16,32]{1,0:T(8,128)S(1)} collective-permute-done((f32[16,32]{1,0:T(8,128)S(1)}, f32[16,32]{1,0:T(8,128)S(1)}, u32[]{:S(2)}, u32[]{:S(2)}) %collective-permute-start.22) | collective-permute-done | bytes 2080 | tf_op jit(solution)/shard_map/ppermute | solution.py:26
  116.9 1.9 collective-permute-start.21
  118.9 6.0 %collective-permute-done.21 = f32[16,32]{1,0:T(8,128)S(1)} collective-permute-done((f32[16,32]{1,0:T(8,128)S(1)}, f32[16,32]{1,0:T(8,128)S(1)}, u32[]{:S(2)}, u32[]{:S(2)}) %collective-permute-start.21) | collective-permute-done | bytes 2080 | tf_op jit(solution)/shard_map/ppermute | solution.py:26
  124.9 1.9 collective-permute-start.20
  126.9 3.8 %collective-permute-done.20 = f32[16,32]{1,0:T(8,128)S(1)} collective-permute-done((f32[16,32]{1,0:T(8,128)S(1)}, f32[16,32]{1,0:T(8,128)S(1)}, u32[]{:S(2)}, u32[]{:S(2)}) %collective-permute-start.20) | collective-permute-done | bytes 2080 | tf_op jit(solution)/shard_map/ppermute | solution.py:26
  130.8 1.9 collective-permute-start.19
  132.8 3.5 %collective-permute-done.19 = f32[16,32]{1,0:T(8,128)S(1)} collective-permute-done((f32[16,32]{1,0:T(8,128)S(1)}, f32[16,32]{1,0:T(8,128)S(1)}, u32[]{:S(2)}, u32[]{:S(2)}) %collective-permute-start.19) | collective-permute-done | bytes 2080 | tf_op jit(solution)/shard_map/ppermute | solution.py:26
  136.3 9.3 %collective-permute-start.14 = (f32[16,32]{1,0:T(8,128)S(1)}, f32[16,32]{1,0:T(8,128)S(1)}, u32[]{:S(2)}, u32[]{:S(2)}) collective-permute-start(f32[16,32]{1,0:T(8,128)S(1)} %add.221), channel_id=1, source_target_pairs={{0,12},{1,13},{2,14},{3,15},{4,16},{5,17},{6,18},{7,19},{8,20},{9,... | collective-permute-start | bytes 6152 | tf_op jit(solution)/shard_map/ppermute | solution.py:26
  146.4 5.9 %collective-permute-start.9 = (f32[16,32]{1,0:T(8,128)S(1)}, f32[16,32]{1,0:T(8,128)S(1)}, u32[]{:S(2)}, u32[]{:S(2)}) collective-permute-start(f32[16,32]{1,0:T(8,128)S(1)} %add.217), channel_id=1, source_target_pairs={{0,6},{1,7},{2,8},{3,9},{4,10},{5,11},{6,12},{7,13},{8,14},{9,15},... | collective-permute-start | bytes 6152 | tf_op jit(solution)/shard_map/ppermute | solution.py:26
  153.1 16.9 %collective-permute-start = (f32[19,1024]{1,0:T(8,128)S(1)}, f32[19,1024]{1,0:T(8,128)}, u32[]{:S(2)}, u32[]{:S(2)}) collective-permute-start(f32[19,1024]{1,0:T(8,128)S(1)} %copy-done.14), channel_id=1, source_target_pairs={{0,1},{1,2},{2,3},{3,4},{4,5},{5,6},{6,7},{7,8},{8,9},{9,10},{10,1... | collective-permute-start | bytes 233480 | tf_op jit(solution)/shard_map/ppermute | solution.py:34
  170.3 0.8 fusion.28
  171.6 1.6 gather_fusion
  173.2 2.5 %gather.10 = f32[64,8,16,32]{3,2,1,0:T(8,128)} reshape(f32[512,512]{1,0:T(8,128)S(1)} %gather_fusion) | data formatting | bytes 2097152 | tf_op jit(solution)/shard_map/jit(_take)/gather | solution.py:108
  175.7 8.4 %fusion.14 = f32[64,16,32]{2,1,0:T(8,128)S(1)} fusion(f32[64,16,32]{2,1,0:T(8,128)S(1)} %convolution_bitcast_fusion.6, bf16[64,8,32,32]{3,2,1,0:T(8,128)(2,1)} %copy.36, f32[64,8,16,32]{3,2,1,0:T(8,128)} %gather.10, pred[64,8]{1,0:T(8,128)(4,1)S(1)} %copy-done.35), kind=kOutput, calls=%fused_computation.33 | convolution fusion | flops 100958208 | bytes 2359808 | tf_op jit(solution)/shard_map/lfrk,lfkq->lrq/dot_general | solution.py:109
  184.1 1.4 convolution_bitcast_fusion.7
  185.5 1.0 pad_maximum_fusion
  187.4 0.8 gather_fusion.2
  188.2 0.8 gather_fusion.1
  189.3 0.8 copy-done
  194.1 0.9 gather_fusion.5
  196.1 3.3 %fusion.13 = f32[16,64,64]{2,0,1:T(8,128)S(1)} fusion(f32[64,64]{1,0:T(8,128)S(1)} %copy-done.31, f32[64,64]{1,0:T(8,128)S(1)} %bitcast.167, f32[64,64]{1,0:T(8,128)S(1)} %copy-done.32, f32[64,64]{1,0:T(8,128)S(1)} %bitcast.168, f32[64,64]{1,0:T(8,128)S(1)} %copy-done.33, f32[64,64]{1,0:T(8,128)S(1)} %bitcast.166, f32[19,64,64]{2,0,1:T(8,128)S(1)} %copy-done.3, ...), kind=kOutput, calls=%fused_computation.30 | convolution fusion | flops 11468800 | bytes 983040 | tf_op jit(solution)/shard_map/rla,lab->rlb/dot_general | solution.py:59
  199.4 3.3 %fusion.12 = f32[16,64,64]{2,0,1:T(8,128)S(1)} fusion(f32[16,64,64]{2,0,1:T(8,128)S(1)} %fusion.13, f32[64,64]{1,0:T(8,128)S(1)} %bitcast.164, f32[64,64]{1,0:T(8,128)S(1)} %bitcast.165, f32[64,64]{1,0:T(8,128)S(1)} %bitcast.163, f32[64,64]{1,0:T(8,128)S(1)} %copy-done.31, f32[64,64]{1,0:T(8,128)S(1)} %copy-done.32, f32[64,64]{1,0:T(8,128)S(1)} %copy-done.33, ...), kind=kOutput, calls=%fused_computation.28 | convolution fusion | flops 11337728 | bytes 1245184 | tf_op jit(solution)/shard_map/rla,lab->rlb/dot_general | solution.py:59
  202.7 3.3 %fusion.11 = f32[16,64,64]{2,0,1:T(8,128)S(1)} fusion(f32[16,64,64]{2,0,1:T(8,128)S(1)} %fusion.12, f32[64,64]{1,0:T(8,128)S(1)} %bitcast.173, f32[64,64]{1,0:T(8,128)S(1)} %bitcast.174, f32[64,64]{1,0:T(8,128)S(1)} %bitcast.172, f32[64,64]{1,0:T(8,128)S(1)} %copy-done.31, f32[64,64]{1,0:T(8,128)S(1)} %copy-done.32, f32[64,64]{1,0:T(8,128)S(1)} %copy-done.33, ...), kind=kOutput, calls=%fused_computation.26 | convolution fusion | flops 11337728 | bytes 1245184 | tf_op jit(solution)/shard_map/rla,lab->rlb/dot_general | solution.py:59
  205.9 3.3 %fusion.10 = f32[16,64,64]{2,0,1:T(8,128)S(1)} fusion(f32[16,64,64]{2,0,1:T(8,128)S(1)} %fusion.11, f32[64,64]{1,0:T(8,128)S(1)} %bitcast.170, f32[64,64]{1,0:T(8,128)S(1)} %bitcast.171, f32[64,64]{1,0:T(8,128)S(1)} %bitcast.169, f32[64,64]{1,0:T(8,128)S(1)} %copy-done.31, f32[64,64]{1,0:T(8,128)S(1)} %copy-done.32, f32[64,64]{1,0:T(8,128)S(1)} %copy-done.33, ...), kind=kOutput, calls=%fused_computation.24 | convolution fusion | flops 11337728 | bytes 1245184 | tf_op jit(solution)/shard_map/rla,lab->rlb/dot_general | solution.py:59
  209.2 3.3 %fusion.9 = f32[16,64,64]{2,0,1:T(8,128)S(1)} fusion(f32[16,64,64]{2,0,1:T(8,128)S(1)} %fusion.10, f32[64,64]{1,0:T(8,128)S(1)} %bitcast.179, f32[64,64]{1,0:T(8,128)S(1)} %bitcast.180, f32[64,64]{1,0:T(8,128)S(1)} %bitcast.178, f32[64,64]{1,0:T(8,128)S(1)} %copy-done.31, f32[64,64]{1,0:T(8,128)S(1)} %copy-done.32, f32[64,64]{1,0:T(8,128)S(1)} %copy-done.33, ...), kind=kOutput, calls=%fused_computation.22 | convolution fusion | flops 11337728 | bytes 1245184 | tf_op jit(solution)/shard_map/rla,lab->rlb/dot_general | solution.py:59
  212.5 3.3 %fusion.8 = f32[16,64,64]{2,0,1:T(8,128)S(1)} fusion(f32[16,64,64]{2,0,1:T(8,128)S(1)} %copy-done.8, f32[16,64,64]{2,0,1:T(8,128)S(1)} %fusion.9, f32[64,64]{1,0:T(8,128)S(1)} %bitcast.176, f32[64,64]{1,0:T(8,128)S(1)} %bitcast.177, f32[64,64]{1,0:T(8,128)S(1)} %bitcast.175, f32[64,64]{1,0:T(8,128)S(1)} %copy-done.31, f32[64,64]{1,0:T(8,128)S(1)} %copy-done.32, ...), kind=kOutput, calls=%fused_computation.20 | convolution fusion | flops 11403264 | bytes 1769472 | tf_op jit(solution)/shard_map/rla,lab->rlb/dot_general | solution.py:59
  216.0 0.9 reshape.94
  (192 shorter events, 32.8 us)
Async XLA Ops:
  0.0 3.6 %copy-start.11 = (bf16[64,1024]{1,0:T(8,128)(2,1)S(1)}, bf16[64,1024]{1,0:T(8,128)(2,1)}, u32[]{:S(2)}) copy-start(bf16[64,1024]{1,0:T(8,128)(2,1)} %param.21) | copy-start | bytes 393220
  2.4 20.3 %copy-start.36 = (bf16[1,3,1024]{2,1,0:T(4,128)(2,1)S(1)}, bf16[1,3,1024]{2,1,0:T(4,128)(2,1)}, u32[]{:S(2)}) copy-start(bf16[1,3,1024]{2,1,0:T(4,128)(2,1)} %param.23) | copy-start | bytes 18436
  4.5 22.8 %copy-start.9 = (bf16[16,4096]{1,0:T(8,128)(2,1)S(1)}, bf16[16,4096]{1,0:T(8,128)(2,1)}, u32[]{:S(2)}) copy-start(bf16[16,4096]{1,0:T(8,128)(2,1)} %param.14) | copy-start | bytes 393220
  4.5 24.1 %copy-start.13 = (bf16[1,4,4,1024]{3,2,1,0:T(4,128)(2,1)S(1)}, bf16[1,4,4,1024]{3,2,1,0:T(4,128)(2,1)}, u32[]{:S(2)}) copy-start(bf16[1,4,4,1024]{3,2,1,0:T(4,128)(2,1)} %param.25) | copy-start | bytes 98308
  4.6 27.0 %copy-start.37 = (bf16[1,3,1024]{2,1,0:T(4,128)(2,1)S(1)}, bf16[1,3,1024]{2,1,0:T(4,128)(2,1)}, u32[]{:S(2)}) copy-start(bf16[1,3,1024]{2,1,0:T(4,128)(2,1)} %param.24) | copy-start | bytes 18436
  4.9 29.5 %copy-start.38 = (s32[64,8]{0,1:T(8,128)S(1)}, s32[64,8]{0,1:T(8,128)}, u32[]{:S(2)}) copy-start(s32[64,8]{0,1:T(8,128)} %param.17) | copy-start | bytes 6148
  4.9 30.2 %copy-start.10 = (f32[3,4096]{1,0:T(4,128)S(1)}, f32[3,4096]{1,0:T(4,128)}, u32[]{:S(2)}) copy-start(f32[3,4096]{1,0:T(4,128)} %param.15) | copy-start | bytes 147460
  4.9 31.1 %copy-start.39 = (s32[64,6]{0,1:T(8,128)S(1)}, s32[64,6]{0,1:T(8,128)}, u32[]{:S(2)}) copy-start(s32[64,6]{0,1:T(8,128)} %param.16) | copy-start | bytes 4612
  5.0 40.7 %copy-start.12 = (bf16[64,1024]{1,0:T(8,128)(2,1)S(1)}, bf16[64,1024]{1,0:T(8,128)(2,1)}, u32[]{:S(2)}) copy-start(bf16[64,1024]{1,0:T(8,128)(2,1)} %param.22) | copy-start | bytes 393220
  5.7 61.5 %collective-permute-start.7 = (f32[16,32]{1,0:T(8,128)S(1)}, f32[16,32]{1,0:T(8,128)}, u32[]{:S(2)}, u32[]{:S(2)}) collective-permute-start(f32[16,32]{1,0:T(8,128)S(1)} %convolution_bitcast_fusion.8), channel_id=1, source_target_pairs={{3,0},{4,1},{5,2},{6,3},{7,4},{8,5},{9,6},{10,7},{11,8},{12,9},{13... | collective-permute-start | bytes 6152 | tf_op jit(solution)/shard_map/ppermute | solution.py:26
  7.9 68.7 %collective-permute-start.6 = (f32[16,32]{1,0:T(8,128)S(1)}, f32[16,32]{1,0:T(8,128)}, u32[]{:S(2)}, u32[]{:S(2)}) collective-permute-start(f32[16,32]{1,0:T(8,128)S(1)} %convolution_bitcast_fusion.8), channel_id=1, source_target_pairs={{2,0},{3,1},{4,2},{5,3},{6,4},{7,5},{8,6},{9,7},{10,8},{11,9},{12,... | collective-permute-start | bytes 6152 | tf_op jit(solution)/shard_map/ppermute | solution.py:26
  12.5 66.9 %collective-permute-start.5 = (f32[16,32]{1,0:T(8,128)S(1)}, f32[16,32]{1,0:T(8,128)}, u32[]{:S(2)}, u32[]{:S(2)}) collective-permute-start(f32[16,32]{1,0:T(8,128)S(1)} %convolution_bitcast_fusion.8), channel_id=1, source_target_pairs={{0,2},{1,3},{2,4},{3,5},{4,6},{5,7},{6,8},{7,9},{8,10},{9,11},{10,... | collective-permute-start | bytes 6152 | tf_op jit(solution)/shard_map/ppermute | solution.py:26
  19.2 151.1 %collective-permute-start.4 = (f32[16,32]{1,0:T(8,128)S(1)}, f32[16,32]{1,0:T(8,128)}, u32[]{:S(2)}, u32[]{:S(2)}) collective-permute-start(f32[16,32]{1,0:T(8,128)S(1)} %convolution_bitcast_fusion.8), channel_id=1, source_target_pairs={{0,3},{1,4},{2,5},{3,6},{4,7},{5,8},{6,9},{7,10},{8,11},{9,12},{10... | collective-permute-start | bytes 6152 | tf_op jit(solution)/shard_map/ppermute | solution.py:26
  23.5 39.7 %collective-permute-start.8 = (f32[16,32]{1,0:T(8,128)}, f32[16,32]{1,0:T(8,128)}, u32[]{:S(2)}, u32[]{:S(2)}) collective-permute-start(f32[16,32]{1,0:T(8,128)} %fusion.90), channel_id=1, source_target_pairs={{0,1},{1,0},{2,3},{3,2},{4,5},{5,4},{6,7},{7,6},{8,9},{9,8},{10,11... | collective-permute-start | bytes 6152 | tf_op jit(solution)/shard_map/ppermute | solution.py:43
  55.8 25.5 %copy-start.30 = (bf16[32,32]{1,0:T(8,128)(2,1)S(1)}, bf16[32,32]{1,0:T(8,128)(2,1)}, u32[]{:S(2)}) copy-start(bf16[32,32]{1,0:T(8,128)(2,1)} %reshape_squeeze.67) | copy-start | bytes 6148
  55.8 31.4 %copy-start.26 = (bf16[32,32]{1,0:T(8,128)(2,1)S(1)}, bf16[32,32]{1,0:T(8,128)(2,1)}, u32[]{:S(2)}) copy-start(bf16[32,32]{1,0:T(8,128)(2,1)} %reshape_squeeze.80) | copy-start | bytes 6148
  55.8 38.5 %copy-start.29 = (bf16[32,32]{1,0:T(8,128)(2,1)S(1)}, bf16[32,32]{1,0:T(8,128)(2,1)}, u32[]{:S(2)}) copy-start(bf16[32,32]{1,0:T(8,128)(2,1)} %reshape_squeeze.74) | copy-start | bytes 6148
  55.8 40.5 %copy-start.28 = (bf16[32,32]{1,0:T(8,128)(2,1)S(1)}, bf16[32,32]{1,0:T(8,128)(2,1)}, u32[]{:S(2)}) copy-start(bf16[32,32]{1,0:T(8,128)(2,1)} %reshape_squeeze.73) | copy-start | bytes 6148
  55.8 42.6 %copy-start.27 = (bf16[32,32]{1,0:T(8,128)(2,1)S(1)}, bf16[32,32]{1,0:T(8,128)(2,1)}, u32[]{:S(2)}) copy-start(bf16[32,32]{1,0:T(8,128)(2,1)} %reshape_squeeze.72) | copy-start | bytes 6148
  55.8 49.4 %copy-start.25 = (bf16[32,32]{1,0:T(8,128)(2,1)S(1)}, bf16[32,32]{1,0:T(8,128)(2,1)}, u32[]{:S(2)}) copy-start(bf16[32,32]{1,0:T(8,128)(2,1)} %reshape_squeeze.79) | copy-start | bytes 6148
  55.8 51.4 %copy-start.24 = (bf16[32,32]{1,0:T(8,128)(2,1)S(1)}, bf16[32,32]{1,0:T(8,128)(2,1)}, u32[]{:S(2)}) copy-start(bf16[32,32]{1,0:T(8,128)(2,1)} %reshape_squeeze.78) | copy-start | bytes 6148
  55.9 52.6 %copy-start.15 = (f32[19,1024]{1,0:T(8,128)S(1)}, f32[19,1024]{1,0:T(8,128)}, u32[]{:S(2)}) copy-start(f32[19,1024]{1,0:T(8,128)} %get-tuple-element.66) | copy-start | bytes 233476
  55.9 56.4 %copy-start.23 = (bf16[32,32]{1,0:T(8,128)(2,1)S(1)}, bf16[32,32]{1,0:T(8,128)(2,1)}, u32[]{:S(2)}) copy-start(bf16[32,32]{1,0:T(8,128)(2,1)} %reshape_squeeze.77) | copy-start | bytes 6148
  55.9 62.9 %copy-start.19 = (bf16[32,32]{1,0:T(8,128)(2,1)S(1)}, bf16[32,32]{1,0:T(8,128)(2,1)}, u32[]{:S(2)}) copy-start(bf16[32,32]{1,0:T(8,128)(2,1)} %reshape_squeeze.84) | copy-start | bytes 6148
  55.9 70.9 %copy-start.18 = (bf16[32,32]{1,0:T(8,128)(2,1)S(1)}, bf16[32,32]{1,0:T(8,128)(2,1)}, u32[]{:S(2)}) copy-start(bf16[32,32]{1,0:T(8,128)(2,1)} %reshape_squeeze.83) | copy-start | bytes 6148
  55.9 76.8 %copy-start.17 = (bf16[32,32]{1,0:T(8,128)(2,1)S(1)}, bf16[32,32]{1,0:T(8,128)(2,1)}, u32[]{:S(2)}) copy-start(bf16[32,32]{1,0:T(8,128)(2,1)} %reshape_squeeze.82) | copy-start | bytes 6148
  55.9 89.7 %copy-start.34 = (bf16[32,32]{1,0:T(8,128)(2,1)S(1)}, bf16[32,32]{1,0:T(8,128)(2,1)}, u32[]{:S(2)}) copy-start(bf16[32,32]{1,0:T(8,128)(2,1)} %reshape_squeeze.81) | copy-start | bytes 6148
  55.9 89.9 %copy-start.16 = (bf16[32,32]{1,0:T(8,128)(2,1)S(1)}, bf16[32,32]{1,0:T(8,128)(2,1)}, u32[]{:S(2)}) copy-start(bf16[32,32]{1,0:T(8,128)(2,1)} %reshape_squeeze.85) | copy-start | bytes 6148
  55.9 97.2 %copy-start.14 = (f32[19,1024]{1,0:T(8,128)S(1)}, f32[19,1024]{1,0:T(8,128)}, u32[]{:S(2)}) copy-start(f32[19,1024]{1,0:T(8,128)} %get-tuple-element.65) | copy-start | bytes 233476
  55.9 114.1 %copy-start.22 = (bf16[32,32]{1,0:T(8,128)(2,1)S(1)}, bf16[32,32]{1,0:T(8,128)(2,1)}, u32[]{:S(2)}) copy-start(bf16[32,32]{1,0:T(8,128)(2,1)} %reshape_squeeze.71) | copy-start | bytes 6148
  55.9 114.2 %copy-start.20 = (bf16[32,32]{1,0:T(8,128)(2,1)S(1)}, bf16[32,32]{1,0:T(8,128)(2,1)}, u32[]{:S(2)}) copy-start(bf16[32,32]{1,0:T(8,128)(2,1)} %reshape_squeeze.87) | copy-start | bytes 6148
  56.0 114.4 %copy-start.21 = (bf16[32,32]{1,0:T(8,128)(2,1)S(1)}, bf16[32,32]{1,0:T(8,128)(2,1)}, u32[]{:S(2)}) copy-start(bf16[32,32]{1,0:T(8,128)(2,1)} %reshape_squeeze.66) | copy-start | bytes 6148
  63.2 108.3 %collective-permute-start.3 = (f32[32,512]{1,0:T(8,128)S(1)}, f32[32,512]{1,0:T(8,128)S(1)}, u32[]{:S(2)}, u32[]{:S(2)}) collective-permute-start(f32[32,512]{1,0:T(8,128)S(1)} %slice.251), channel_id=1, source_target_pairs={{1,0},{2,1},{3,2},{4,3},{5,4},{6,5},{7,6},{8,7},{9,8},{10,9},{11,1... | collective-permute-start | bytes 196616 | tf_op jit(solution)/shard_map/ppermute | solution.py:37
  67.3 104.2 %collective-permute-start.2 = (f32[32,512]{1,0:T(8,128)S(1)}, f32[32,512]{1,0:T(8,128)S(1)}, u32[]{:S(2)}, u32[]{:S(2)}) collective-permute-start(f32[32,512]{1,0:T(8,128)S(1)} %slice.249), channel_id=1, source_target_pairs={{0,1},{1,2},{2,3},{3,4},{4,5},{5,6},{6,7},{7,8},{8,9},{9,10},{10,1... | collective-permute-start | bytes 196616 | tf_op jit(solution)/shard_map/ppermute | solution.py:34
  76.6 10.7 %collective-permute-start.12 = (f32[16,32]{1,0:T(8,128)S(1)}, f32[16,32]{1,0:T(8,128)S(1)}, u32[]{:S(2)}, u32[]{:S(2)}) collective-permute-start(f32[16,32]{1,0:T(8,128)S(1)} %add.217), channel_id=1, source_target_pairs={{6,0},{7,1},{8,2},{9,3},{10,4},{11,5},{12,6},{13,7},{14,8},{15,9},... | collective-permute-start | bytes 6152 | tf_op jit(solution)/shard_map/ppermute | solution.py:26
  79.3 5.9 %collective-permute-start.13 = (f32[16,32]{1,0:T(8,128)S(1)}, f32[16,32]{1,0:T(8,128)S(1)}, u32[]{:S(2)}, u32[]{:S(2)}) collective-permute-start(f32[16,32]{1,0:T(8,128)S(1)} %fusion.94), channel_id=1, source_target_pairs={{0,2},{1,3},{2,0},{3,1},{4,6},{5,7},{6,4},{7,5},{8,10},{9,11},{10,... | collective-permute-start | bytes 6152 | tf_op jit(solution)/shard_map/ppermute | solution.py:43
  85.2 9.2 %collective-permute-start.11 = (f32[16,32]{1,0:T(8,128)S(1)}, f32[16,32]{1,0:T(8,128)S(1)}, u32[]{:S(2)}, u32[]{:S(2)}) collective-permute-start(f32[16,32]{1,0:T(8,128)S(1)} %add.217), channel_id=1, source_target_pairs={{4,0},{5,1},{6,2},{7,3},{8,4},{9,5},{10,6},{11,7},{12,8},{13,9},{1... | collective-permute-start | bytes 6152 | tf_op jit(solution)/shard_map/ppermute | solution.py:26
  87.3 9.2 %collective-permute-start.10 = (f32[16,32]{1,0:T(8,128)S(1)}, f32[16,32]{1,0:T(8,128)S(1)}, u32[]{:S(2)}, u32[]{:S(2)}) collective-permute-start(f32[16,32]{1,0:T(8,128)S(1)} %add.217), channel_id=1, source_target_pairs={{0,4},{1,5},{2,6},{3,7},{4,8},{5,9},{6,10},{7,11},{8,12},{9,13},{1... | collective-permute-start | bytes 6152 | tf_op jit(solution)/shard_map/ppermute | solution.py:26
  94.4 8.6 %collective-permute-start.17 = (f32[16,32]{1,0:T(8,128)S(1)}, f32[16,32]{1,0:T(8,128)S(1)}, u32[]{:S(2)}, u32[]{:S(2)}) collective-permute-start(f32[16,32]{1,0:T(8,128)S(1)} %add.221), channel_id=1, source_target_pairs={{12,0},{13,1},{14,2},{15,3},{16,4},{17,5},{18,6},{19,7},{20,8},{21... | collective-permute-start | bytes 6152 | tf_op jit(solution)/shard_map/ppermute | solution.py:26
  96.5 8.9 %collective-permute-start.16 = (f32[16,32]{1,0:T(8,128)S(1)}, f32[16,32]{1,0:T(8,128)S(1)}, u32[]{:S(2)}, u32[]{:S(2)}) collective-permute-start(f32[16,32]{1,0:T(8,128)S(1)} %add.221), channel_id=1, source_target_pairs={{8,0},{9,1},{10,2},{11,3},{12,4},{13,5},{14,6},{15,7},{16,8},{17,9... | collective-permute-start | bytes 6152 | tf_op jit(solution)/shard_map/ppermute | solution.py:26
  103.0 7.4 %collective-permute-start.15 = (f32[16,32]{1,0:T(8,128)S(1)}, f32[16,32]{1,0:T(8,128)S(1)}, u32[]{:S(2)}, u32[]{:S(2)}) collective-permute-start(f32[16,32]{1,0:T(8,128)S(1)} %add.221), channel_id=1, source_target_pairs={{0,8},{1,9},{2,10},{3,11},{4,12},{5,13},{6,14},{7,15},{8,16},{9,17... | collective-permute-start | bytes 6152 | tf_op jit(solution)/shard_map/ppermute | solution.py:26
  105.3 3.1 %collective-permute-start.18 = (f32[16,32]{1,0:T(8,128)S(1)}, f32[16,32]{1,0:T(8,128)S(1)}, u32[]{:S(2)}, u32[]{:S(2)}) collective-permute-start(f32[16,32]{1,0:T(8,128)S(1)} %fusion.98), channel_id=1, source_target_pairs={{0,4},{1,5},{2,6},{3,7},{4,0},{5,1},{6,2},{7,3},{8,12},{9,13},{10,... | collective-permute-start | bytes 6152 | tf_op jit(solution)/shard_map/ppermute | solution.py:43
  108.4 77.1 %collective-permute-start.1 = (f32[19,1024]{1,0:T(8,128)S(1)}, f32[19,1024]{1,0:T(8,128)}, u32[]{:S(2)}, u32[]{:S(2)}) collective-permute-start(f32[19,1024]{1,0:T(8,128)S(1)} %copy-done.15), channel_id=1, source_target_pairs={{1,0},{2,1},{3,2},{4,3},{5,4},{6,5},{7,6},{8,7},{9,8},{10,9},{11,1... | collective-permute-start | bytes 233480 | tf_op jit(solution)/shard_map/ppermute | solution.py:37
  110.4 6.5 %collective-permute-start.22 = (f32[16,32]{1,0:T(8,128)S(1)}, f32[16,32]{1,0:T(8,128)S(1)}, u32[]{:S(2)}, u32[]{:S(2)}) collective-permute-start(f32[16,32]{1,0:T(8,128)S(1)} %add.225), channel_id=1, source_target_pairs={{24,0},{25,1},{26,2},{27,3},{28,4},{29,5},{30,6},{31,7},{32,8},{33... | collective-permute-start | bytes 6152 | tf_op jit(solution)/shard_map/ppermute | solution.py:26
  116.9 8.0 %collective-permute-start.21 = (f32[16,32]{1,0:T(8,128)S(1)}, f32[16,32]{1,0:T(8,128)S(1)}, u32[]{:S(2)}, u32[]{:S(2)}) collective-permute-start(f32[16,32]{1,0:T(8,128)S(1)} %add.225), channel_id=1, source_target_pairs={{16,0},{17,1},{18,2},{19,3},{20,4},{21,5},{22,6},{23,7},{24,8},{25... | collective-permute-start | bytes 6152 | tf_op jit(solution)/shard_map/ppermute | solution.py:26
  124.9 5.9 %collective-permute-start.20 = (f32[16,32]{1,0:T(8,128)S(1)}, f32[16,32]{1,0:T(8,128)S(1)}, u32[]{:S(2)}, u32[]{:S(2)}) collective-permute-start(f32[16,32]{1,0:T(8,128)S(1)} %add.225), channel_id=1, source_target_pairs={{0,16},{1,17},{2,18},{3,19},{4,20},{5,21},{6,22},{7,23},{8,24},{9,... | collective-permute-start | bytes 6152 | tf_op jit(solution)/shard_map/ppermute | solution.py:26
  130.8 5.6 %collective-permute-start.19 = (f32[16,32]{1,0:T(8,128)S(1)}, f32[16,32]{1,0:T(8,128)S(1)}, u32[]{:S(2)}, u32[]{:S(2)}) collective-permute-start(f32[16,32]{1,0:T(8,128)S(1)} %add.225), channel_id=1, source_target_pairs={{0,24},{1,25},{2,26},{3,27},{4,28},{5,29},{6,30},{7,31},{8,32},{9,... | collective-permute-start | bytes 6152 | tf_op jit(solution)/shard_map/ppermute | solution.py:26
  136.3 10.1 %collective-permute-start.14 = (f32[16,32]{1,0:T(8,128)S(1)}, f32[16,32]{1,0:T(8,128)S(1)}, u32[]{:S(2)}, u32[]{:S(2)}) collective-permute-start(f32[16,32]{1,0:T(8,128)S(1)} %add.221), channel_id=1, source_target_pairs={{0,12},{1,13},{2,14},{3,15},{4,16},{5,17},{6,18},{7,19},{8,20},{9,... | collective-permute-start | bytes 6152 | tf_op jit(solution)/shard_map/ppermute | solution.py:26
  146.4 6.7 %collective-permute-start.9 = (f32[16,32]{1,0:T(8,128)S(1)}, f32[16,32]{1,0:T(8,128)S(1)}, u32[]{:S(2)}, u32[]{:S(2)}) collective-permute-start(f32[16,32]{1,0:T(8,128)S(1)} %add.217), channel_id=1, source_target_pairs={{0,6},{1,7},{2,8},{3,9},{4,10},{5,11},{6,12},{7,13},{8,14},{9,15},... | collective-permute-start | bytes 6152 | tf_op jit(solution)/shard_map/ppermute | solution.py:26
  153.1 32.4 %collective-permute-start = (f32[19,1024]{1,0:T(8,128)S(1)}, f32[19,1024]{1,0:T(8,128)}, u32[]{:S(2)}, u32[]{:S(2)}) collective-permute-start(f32[19,1024]{1,0:T(8,128)S(1)} %copy-done.14), channel_id=1, source_target_pairs={{0,1},{1,2},{2,3},{3,4},{4,5},{5,6},{6,7},{7,8},{8,9},{9,10},{10,1... | collective-permute-start | bytes 233480 | tf_op jit(solution)/shard_map/ppermute | solution.py:34
  173.2 2.5 %copy-start.35 = (pred[64,8]{1,0:T(8,128)(4,1)S(1)}, pred[64,8]{1,0:T(8,128)(4,1)}, u32[]{:S(2)}) copy-start(pred[64,8]{1,0:T(8,128)(4,1)} %copy.24) | copy-start | bytes 1540
  186.9 2.1 copy-start.44
  186.9 2.1 copy-start.45
  189.2 2.7 %copy-start.42 = (pred[64]{0:T(512)(128)(4,1)S(1)}, pred[64]{0:T(512)(128)(4,1)}, u32[]{:S(2)}) copy-start(pred[64]{0:T(512)(128)(4,1)} %get-tuple-element.67) | copy-start | bytes 196
  189.2 2.7 %copy-start.43 = (pred[64]{0:T(512)(128)(4,1)S(1)}, pred[64]{0:T(512)(128)(4,1)}, u32[]{:S(2)}) copy-start(pred[64]{0:T(512)(128)(4,1)} %get-tuple-element.69) | copy-start | bytes 196
  192.2 2.8 %copy-start.40 = (pred[64]{0:T(512)(128)(4,1)S(1)}, pred[64]{0:T(512)(128)(4,1)}, u32[]{:S(2)}) copy-start(pred[64]{0:T(512)(128)(4,1)} %get-tuple-element.31) | copy-start | bytes 196
  192.2 2.8 %copy-start.41 = (pred[64]{0:T(512)(128)(4,1)S(1)}, pred[64]{0:T(512)(128)(4,1)}, u32[]{:S(2)}) copy-start(pred[64]{0:T(512)(128)(4,1)} %get-tuple-element.75) | copy-start | bytes 196
  194.0 1.3 copy-start.31
  194.1 1.3 copy-start.32
  194.1 1.3 copy-start.33
  196.1 3.3 %copy-start.1 = (f32[19,64,64]{2,0,1:T(8,128)S(1)}, f32[19,64,64]{2,0,1:T(8,128)}, u32[]{:S(2)}) copy-start(f32[19,64,64]{2,0,1:T(8,128)} %copy-done) | copy-start | bytes 933892
  199.4 3.3 %copy-start.7 = (f32[19,64,64]{2,0,1:T(8,128)S(1)}, f32[19,64,64]{2,0,1:T(8,128)}, u32[]{:S(2)}) copy-start(f32[19,64,64]{2,0,1:T(8,128)} %copy-done.6) | copy-start | bytes 933892
  202.7 3.3 %copy-start.5 = (f32[19,64,64]{2,0,1:T(8,128)S(1)}, f32[19,64,64]{2,0,1:T(8,128)}, u32[]{:S(2)}) copy-start(f32[19,64,64]{2,0,1:T(8,128)} %copy-done.4) | copy-start | bytes 933892
  209.2 3.3 %copy-start.8 = (f32[16,64,64]{2,0,1:T(8,128)S(1)}, f32[16,64,64]{2,0,1:T(8,128)}, u32[]{:S(2)}) copy-start(f32[16,64,64]{2,0,1:T(8,128)} %convolution_bitcast_fusion.7) | copy-start | bytes 786436
  (5 other events, 5.2 us)
where the time goes:
time: 218 us; the launch traced here: 217 us
  starting transfers between devices  92.9 us (43%)
  local copies, waits for them, and re-layouts  50.6 us (23%)
  matrix products  37.7 us (17%)
  waiting for transfers between devices  27.5 us (13%)
  other arithmetic  7.17 us (3%)
    ppermute x16, starting transfers between devices, passed_along(): return lax.ppermute(block, axis, route)  56.6 us
    ppermute x2, starting transfers between devices, extended_2(): lax.ppermute(lax.slice_in_dim(block, block.shape[dim] - width, None, axis...  25.4 us
    ppermute x16, waiting for transfers between devices, passed_along(): return lax.ppermute(block, axis, route)  23.3 us
    dot_general x6, matrix products, matern_term(): jnp.einsum('rla,lab->rlb', values, kernel, preferred_element_type=jnp.flo...  19.7 us
    another operation x22, local copies, waits for them, and re-layouts, apply_matrix(): matrix.reshape(RANK, RANK)  13 us
    dot_general x1, matrix products, local(): jnp.einsum('lfrk,lfkq->lrq', partner_blocks, leaf_coupling.reshape(leaf_c...  8.4 us
    unnamed x96, local copies, waits for them, and re-layouts  6.95 us
    reshape x1, local copies, waits for them, and re-layouts, local(): leaf_coupling.reshape(leaf_count, FAR_BLOCKS, RANK, RANK)  6.8 us
  transfers between devices with their start and end apart: 23, of which 9 were waited for; matrix products, arithmetic and copies ran while one was open for 27% of the time, Pallas kernels for 0%

commit v1 on v0

v1 whole, which is shorter than its diff:
```python
import jax
import jax.numpy as jnp
from jax import lax
from jax.sharding import PartitionSpec as P

CLUSTER = 64
RANK = 32
RHS = 16
NEAR_REACH = 16
NEAR_BLOCKS = 6
FAR_REACH = 32
FAR_BLOCKS = 8
TOP_LEVELS = 3


amplitude = 0.15
length_scale = 1.0
nugget = 0.5
partner_steps = (-3, -2, 2, 3)
highest = lax.Precision.HIGHEST
AXES = ("leaf", "grp")


def device_count():
    return lax.axis_size("leaf") * lax.axis_size("grp")


def swap_with(value, mask):
    n = device_count()
    return lax.ppermute(value, AXES, [(i, i ^ mask) for i in range(n)])


def receive_from(value, step):
    n = device_count()
    return lax.ppermute(value, AXES, [(s, s - step) for s in range(n) if 0 <= s - step < n])


def matern_term(extended, target_points, slot_offsets):
    leaf_count = target_points.shape[1]
    column_count = extended.shape[0] - 3
    source_leaf = jnp.arange(leaf_count, dtype=jnp.int32) + NEAR_REACH + slot_offsets
    chosen = jnp.take(extended, source_leaf, axis=1)
    squared = jnp.zeros((leaf_count, CLUSTER, CLUSTER), jnp.float32)
    for component in range(3):
        separation = (
            chosen[column_count + component][:, :, None] - target_points[component][:, None, :]
        )
        squared = squared + separation * separation
    kernel = (amplitude * jnp.exp(-jnp.sqrt(squared) / length_scale)).astype(jnp.bfloat16)
    values = chosen[:column_count].astype(jnp.bfloat16)
    return jnp.einsum("rla,lab->rlb", values, kernel, preferred_element_type=jnp.float32)


def mm(a, b):
    return jnp.matmul(a, b, precision=highest, preferred_element_type=jnp.float32)


def ordered(bit, own, other):
    return jnp.where(bit == 0, jnp.concatenate([own, other]), jnp.concatenate([other, own]))


def tree_field(root_coefficients, tree_up, tree_down, tree_coupling, me):
    up = tree_up[0].astype(jnp.float32).reshape(TOP_LEVELS, RANK, RANK)
    down = tree_down[0].astype(jnp.float32).reshape(TOP_LEVELS, RANK, RANK)
    cross = tree_coupling[0].astype(jnp.float32).reshape(TOP_LEVELS + 1, 4, RANK, RANK)
    eye = jnp.eye(RANK, dtype=jnp.float32)
    lift1 = up[0]
    lift2 = mm(lift1, up[1])
    lift3 = mm(lift2, up[2])
    lifts = jnp.stack([eye, lift1, lift2, lift3])
    push1 = down[0]
    push2 = mm(down[1], push1)
    push3 = mm(down[2], push2)
    pushes = jnp.stack([eye, push1, push2, push3])
    weights = jnp.einsum("sqkp,spm->sqkm", cross, pushes, precision=highest)

    p = jnp.einsum("rk,skq->srq", root_coefficients, lifts, precision=highest)

    bit0 = me & 1
    bit1 = (me >> 1) & 1
    bit2 = (me >> 2) & 1
    got1 = swap_with(p, 1)
    pairs0 = ordered(bit0, p[0:1], got1[0:1])
    coef1 = p[1] + got1[1]
    part2 = p[2] + got1[2]
    part3 = p[3] + got1[3]
    got2 = swap_with(jnp.concatenate([pairs0, coef1[None], part2[None], part3[None]]), 2)
    quads0 = ordered(bit1, pairs0, got2[0:2])
    pairs1 = ordered(bit1, coef1[None], got2[2:3])
    coef2 = part2 + got2[3]
    part3 = part3 + got2[4]
    got3 = swap_with(jnp.concatenate([quads0, pairs1, coef2[None], part3[None]]), 4)
    octs0 = ordered(bit2, quads0, got3[0:4])
    quads1 = ordered(bit2, pairs1, got3[4:6])
    pairs2 = ordered(bit2, coef2[None], got3[6:7])
    coef3 = (part3 + got3[7])[None]

    node = 8
    ahead1 = receive_from(jnp.concatenate([octs0[0:3], quads1[0:3], pairs2]), node)
    behind1 = receive_from(jnp.concatenate([octs0[5:8], quads1[1:4], pairs2]), -node)
    ahead2 = receive_from(jnp.concatenate([pairs2[0:1], coef3]), 2 * node)
    behind2 = receive_from(jnp.concatenate([pairs2[1:2], coef3]), -2 * node)
    ahead3 = receive_from(coef3, 3 * node)
    behind3 = receive_from(coef3, -3 * node)

    window0 = jnp.concatenate([behind1[0:3], octs0, ahead1[0:3]])
    window1 = jnp.concatenate([behind1[3:6], quads1, ahead1[3:6]])
    window2 = jnp.concatenate([behind2[0:1], behind1[6:8], pairs2, ahead1[6:8], ahead2[0:1]])
    steps = jnp.array(partner_steps, dtype=jnp.int32) + 3
    chosen0 = jnp.take(window0, (me & 7) + steps, axis=0, mode="clip")
    chosen1 = jnp.take(window1, ((me >> 1) & 3) + steps, axis=0, mode="clip")
    chosen2 = jnp.take(window2, bit2 + steps, axis=0, mode="clip")
    chosen3 = jnp.concatenate([behind3, behind2[1:2], ahead2[1:2], ahead3])
    chosen = jnp.stack([chosen0, chosen1, chosen2, chosen3])
    return jnp.einsum("sqrk,sqkm->rm", chosen, weights, precision=highest)


def local(
    sources,
    points,
    near_offsets,
    far_offsets,
    source_basis,
    target_basis,
    leaf_coupling,
    leaf_up,
    leaf_down,
    tree_up,
    tree_down,
    tree_coupling,
):
    leaf_count = near_offsets.shape[0]
    n = device_count()
    me = lax.axis_index("leaf") * lax.axis_size("grp") + lax.axis_index("grp")
    leaf_values = sources.reshape(RHS, leaf_count, CLUSTER)
    leaf_coefficients = jnp.einsum(
        "rla,lak->lrk",
        leaf_values,
        source_basis.reshape(leaf_count, CLUSTER, RANK),
        preferred_element_type=jnp.float32,
    )
    coef_rows = leaf_coefficients.reshape(leaf_count, RHS * RANK)

    packed = jnp.concatenate([sources.astype(jnp.float32), points], axis=0)
    width = NEAR_REACH * CLUSTER
    to_right = jnp.concatenate(
        [packed[:, -width:].reshape(-1), coef_rows[-FAR_REACH:].reshape(-1)]
    )
    to_left = jnp.concatenate([packed[:, :width].reshape(-1), coef_rows[:FAR_REACH].reshape(-1)])
    from_left = lax.ppermute(to_right, AXES, [(i, i + 1) for i in range(n - 1)])
    from_right = lax.ppermute(to_left, AXES, [(i + 1, i) for i in range(n - 1)])
    split = (RHS + 3) * width
    extended = jnp.concatenate(
        [
            from_left[:split].reshape(RHS + 3, width),
            packed,
            from_right[:split].reshape(RHS + 3, width),
        ],
        axis=1,
    ).reshape(RHS + 3, leaf_count + 2 * NEAR_REACH, CLUSTER)
    rimmed = jnp.concatenate(
        [
            from_left[split:].reshape(FAR_REACH, RHS * RANK),
            coef_rows,
            from_right[split:].reshape(FAR_REACH, RHS * RANK),
        ]
    )

    target_points = points.reshape(3, leaf_count, CLUSTER)
    near_sum = nugget * leaf_values.astype(jnp.float32)
    for near_slot in range(NEAR_BLOCKS):
        near_sum = near_sum + matern_term(extended, target_points, near_offsets[:, near_slot])

    far_index = jnp.arange(leaf_count, dtype=jnp.int32)[:, None] + FAR_REACH + far_offsets
    partner_blocks = jnp.take(rimmed, far_index, axis=0).reshape(leaf_count, FAR_BLOCKS, RHS, RANK)
    leaf_far = jnp.einsum(
        "lfrk,lfkq->lrq",
        partner_blocks,
        leaf_coupling.reshape(leaf_count, FAR_BLOCKS, RANK, RANK),
        precision=highest,
        preferred_element_type=jnp.float32,
    )
    root_coefficients = jnp.einsum(
        "lrk,lkq->rq",
        leaf_coefficients,
        leaf_up.reshape(leaf_count, RANK, RANK),
        precision=highest,
        preferred_element_type=jnp.float32,
    )
    downward = tree_field(root_coefficients, tree_up, tree_down, tree_coupling, me)
    from_root = jnp.einsum(
        "rk,lkq->lrq",
        downward,
        leaf_down.reshape(leaf_count, RANK, RANK),
        precision=highest,
        preferred_element_type=jnp.float32,
    )
    leaf_field = leaf_far + from_root
    far_out = jnp.einsum(
        "lrk,lka->rla",
        leaf_field,
        target_basis.reshape(leaf_count, RANK, CLUSTER),
        precision=highest,
        preferred_element_type=jnp.float32,
    )
    return (near_sum + far_out).reshape(RHS, leaf_count * CLUSTER)


def solution(mesh):
    placed = (
        P(None, AXES),
        P(None, AXES),
        P(AXES, None),
        P(AXES, None),
        P(AXES, None),
        P(AXES, None),
        P(AXES, None, None),
        P(AXES, None),
        P(AXES, None),
        P(AXES, None, None),
        P(AXES, None, None),
        P(AXES, None, None, None),
    )
    return jax.shard_map(
        local, mesh=mesh, in_specs=placed, out_specs=P(None, AXES), check_vma=False
    )
```

time: 218 us -> 146 us (0.67)
  the two profiles are of different devices: /device:TPU:383 before, /device:TPU:124 now
where the time goes in v1:
time: 146 us; the launch traced here: 145 us
  local copies, waits for them, and re-layouts  42.7 us (29%)
  starting transfers between devices  34.6 us (24%)
  matrix products  32.4 us (22%)
  waiting for transfers between devices  25.4 us (17%)
  other arithmetic  8.94 us (6%)
    ppermute x6, waiting for transfers between devices, receive_from(): lax.ppermute(value, AXES, [(s, s - step) for s in range(n) if 0 <= s - st...  20.5 us
    dot_general x6, matrix products, matern_term(): jnp.einsum('rla,lab->rlb', values, kernel, preferred_element_type=jnp.flo...  19.7 us
    ppermute x6, starting transfers between devices, receive_from(): lax.ppermute(value, AXES, [(s, s - step) for s in range(n) if 0 <= s - st...  18.3 us
    ppermute x3, starting transfers between devices, swap_with(): return lax.ppermute(value, AXES, [(i, i ^ mask) for i in range(n)])  10.5 us
    dot_general x1, matrix products, local(): jnp.einsum('lfrk,lfkq->lrq', partner_blocks, leaf_coupling.reshape(leaf_c...  8.27 us
    reshape x1, local copies, waits for them, and re-layouts, local(): leaf_coupling.reshape(leaf_count, FAR_BLOCKS, RANK, RANK)  6.87 us
    unnamed x87, local copies, waits for them, and re-layouts  6.78 us
    gather x6, local copies, waits for them, and re-layouts, matern_term(): chosen = jnp.take(extended, source_leaf, axis=1)  4.93 us
  transfers between devices with their start and end apart: 11, of which 5 were waited for; matrix products, arithmetic and copies ran while one was open for 21% of the time, Pallas kernels for 0%

profile of v1, /device:TPU:124, one launch (start us, length us, event | category | flops | bytes accessed | tf_op | source)
XLA Modules:
  0.0 145.2 jit_solution(3452998271635259294)
XLA Ops:
  0.0 1.2 reshape.168
  1.2 1.0 convert_element_type.48
  2.2 1.3 copy.18
  3.5 1.1 copy.20
  5.3 0.7 pad_maximum_fusion.3
  6.0 2.4 %collective-permute-start.1 = (f32[35840]{0:T(1024)}, f32[35840]{0:T(1024)}, u32[]{:S(2)}, u32[]{:S(2)}) collective-permute-start(f32[35840]{0:T(1024)} %pad_maximum_fusion.3), channel_id=1, source_target_pairs={{1,0},{2,1},{3,2},{4,3},{5,4},{6,5},{7,6},{8,7},{9,8},{10,9},{11,1... | collective-permute-start | bytes 430088 | tf_op jit(solution)/shard_map/ppermute | solution.py:151
  8.5 0.7 pad_maximum_fusion.2
  9.2 3.4 %collective-permute-start = (f32[35840]{0:T(1024)}, f32[35840]{0:T(1024)}, u32[]{:S(2)}, u32[]{:S(2)}) collective-permute-start(f32[35840]{0:T(1024)} %pad_maximum_fusion.2), channel_id=1, source_target_pairs={{0,1},{1,2},{2,3},{3,4},{4,5},{5,6},{6,7},{7,8},{8,9},{9,10},{10,1... | collective-permute-start | bytes 430088 | tf_op jit(solution)/shard_map/ppermute | solution.py:150
  12.9 0.8 copy.38
  13.7 0.8 fusion.103
  15.2 4.0 %collective-permute-start.2 = (f32[4,16,32]{2,1,0:T(8,128)S(1)}, f32[4,16,32]{2,1,0:T(8,128)S(1)}, u32[]{:S(2)}, u32[]{:S(2)}) collective-permute-start(f32[4,16,32]{2,1,0:T(8,128)S(1)} %convolution_bitcast_fusion.8), channel_id=1, source_target_pairs={{0,1},{1,0},{2,3},{3,2},{4,5},{5,4},{6,7},{7,6},{8,9},{9,8},{10,11... | collective-permute-start | bytes 24584 | tf_op jit(solution)/shard_map/ppermute | solution.py:30
  19.3 0.7 slice_reduce_fusion.2
  24.0 1.4 fusion.70
  26.0 1.9 %collective-permute-start.3 = (f32[5,16,32]{2,1,0:T(8,128)S(1)}, f32[5,16,32]{2,1,0:T(8,128)S(1)}, u32[]{:S(2)}, u32[]{:S(2)}) collective-permute-start(f32[5,16,32]{2,1,0:T(8,128)S(1)} %pad_maximum_fusion.15), channel_id=1, source_target_pairs={{0,2},{1,3},{2,0},{3,1},{4,6},{5,7},{6,4},{7,5},{8,10},{9,11},{10,... | collective-permute-start | bytes 30728 | tf_op jit(solution)/shard_map/ppermute | solution.py:30
  28.6 4.9 %collective-permute-done.3 = f32[5,16,32]{2,1,0:T(8,128)S(1)} collective-permute-done((f32[5,16,32]{2,1,0:T(8,128)S(1)}, f32[5,16,32]{2,1,0:T(8,128)S(1)}, u32[]{:S(2)}, u32[]{:S(2)}) %collective-permute-start.3) | collective-permute-done | bytes 10272 | tf_op jit(solution)/shard_map/ppermute | solution.py:30
  34.1 4.5 %collective-permute-start.4 = (f32[8,16,32]{2,1,0:T(8,128)}, f32[8,16,32]{2,1,0:T(8,128)}, u32[]{:S(2)}, u32[]{:S(2)}) collective-permute-start(f32[8,16,32]{2,1,0:T(8,128)} %fusion.63), channel_id=1, source_target_pairs={{0,4},{1,5},{2,6},{3,7},{4,0},{5,1},{6,2},{7,3},{8,12},{9,13},{10,... | collective-permute-start | bytes 49160 | tf_op jit(solution)/shard_map/ppermute | solution.py:30
  38.7 0.9 copy.28
  39.6 1.4 copy.31
  41.1 6.9 %copy.36 = bf16[64,8,32,32]{3,2,1,0:T(8,128)(2,1)} copy(bf16[64,8,32,32]{0,3,2,1:T(8,128)(2,1)S(1)} %bitcast.148) | data formatting | bytes 2097152 | tf_op jit(solution)/shard_map/reshape | solution.py:179
  48.6 0.8 copy.45
  49.9 0.7 sub.258
  50.6 0.7 sub.253
  51.2 0.7 sub.122
  51.9 0.7 fusion.98
  52.6 1.9 %collective-permute-start.10 = (f32[1,16,32]{2,1,0:T(8,128)S(1)}, f32[1,16,32]{2,1,0:T(8,128)S(1)}, u32[]{:S(2)}, u32[]{:S(2)}) collective-permute-start(f32[1,16,32]{2,1,0:T(8,128)S(1)} %get-tuple-element.58), channel_id=1, source_target_pairs={{24,0},{25,1},{26,2},{27,3},{28,4},{29,5},{30,6},{31,7},{32,8},{33... | collective-permute-start | bytes 6152 | tf_op jit(solution)/shard_map/ppermute | solution.py:35
  54.5 6.0 %collective-permute-start.9 = (f32[1,16,32]{2,1,0:T(8,128)S(1)}, f32[1,16,32]{2,1,0:T(8,128)S(1)}, u32[]{:S(2)}, u32[]{:S(2)}) collective-permute-start(f32[1,16,32]{2,1,0:T(8,128)S(1)} %get-tuple-element.58), channel_id=1, source_target_pairs={{0,24},{1,25},{2,26},{3,27},{4,28},{5,29},{6,30},{7,31},{8,32},{9,... | collective-permute-start | bytes 6152 | tf_op jit(solution)/shard_map/ppermute | solution.py:35
  60.6 1.9 %collective-permute-start.7 = (f32[2,16,32]{2,1,0:T(8,128)S(1)}, f32[2,16,32]{2,1,0:T(8,128)S(1)}, u32[]{:S(2)}, u32[]{:S(2)}) collective-permute-start(f32[2,16,32]{2,1,0:T(8,128)S(1)} %get-tuple-element.77), channel_id=1, source_target_pairs={{0,16},{1,17},{2,18},{3,19},{4,20},{5,21},{6,22},{7,23},{8,24},{9,... | collective-permute-start | bytes 12296 | tf_op jit(solution)/shard_map/ppermute | solution.py:35
  62.6 0.7 slice.476
  63.3 0.8 slice.474
  64.1 3.7 %collective-permute-done.7 = f32[2,16,32]{2,1,0:T(8,128)S(1)} collective-permute-done((f32[2,16,32]{2,1,0:T(8,128)S(1)}, f32[2,16,32]{2,1,0:T(8,128)S(1)}, u32[]{:S(2)}, u32[]{:S(2)}) %collective-permute-start.7) | collective-permute-done | bytes 4128 | tf_op jit(solution)/shard_map/ppermute | solution.py:35
  67.8 4.5 %collective-permute-start.5 = (f32[8,16,32]{2,1,0:T(8,128)S(1)}, f32[8,16,32]{2,1,0:T(8,128)S(1)}, u32[]{:S(2)}, u32[]{:S(2)}) collective-permute-start(f32[8,16,32]{2,1,0:T(8,128)S(1)} %get-tuple-element.72), channel_id=1, source_target_pairs={{0,8},{1,9},{2,10},{3,11},{4,12},{5,13},{6,14},{7,15},{8,16},{9,17... | collective-permute-start | bytes 49160 | tf_op jit(solution)/shard_map/ppermute | solution.py:35
  72.3 1.9 %collective-permute-done.5 = f32[8,16,32]{2,1,0:T(8,128)S(1)} collective-permute-done((f32[8,16,32]{2,1,0:T(8,128)S(1)}, f32[8,16,32]{2,1,0:T(8,128)S(1)}, u32[]{:S(2)}, u32[]{:S(2)}) %collective-permute-start.5) | collective-permute-done | bytes 16416 | tf_op jit(solution)/shard_map/ppermute | solution.py:35
  74.1 1.9 %collective-permute-start.6 = (f32[8,16,32]{2,1,0:T(8,128)S(1)}, f32[8,16,32]{2,1,0:T(8,128)S(1)}, u32[]{:S(2)}, u32[]{:S(2)}) collective-permute-start(f32[8,16,32]{2,1,0:T(8,128)S(1)} %get-tuple-element.71), channel_id=1, source_target_pairs={{8,0},{9,1},{10,2},{11,3},{12,4},{13,5},{14,6},{15,7},{16,8},{17,9... | collective-permute-start | bytes 49160 | tf_op jit(solution)/shard_map/ppermute | solution.py:35
  76.1 7.9 %collective-permute-done.6 = f32[8,16,32]{2,1,0:T(8,128)S(1)} collective-permute-done((f32[8,16,32]{2,1,0:T(8,128)S(1)}, f32[8,16,32]{2,1,0:T(8,128)S(1)}, u32[]{:S(2)}, u32[]{:S(2)}) %collective-permute-start.6) | collective-permute-done | bytes 16416 | tf_op jit(solution)/shard_map/ppermute | solution.py:35
  83.9 2.1 %collective-permute-start.8 = (f32[2,16,32]{2,1,0:T(8,128)S(1)}, f32[2,16,32]{2,1,0:T(8,128)S(1)}, u32[]{:S(2)}, u32[]{:S(2)}) collective-permute-start(f32[2,16,32]{2,1,0:T(8,128)S(1)} %get-tuple-element.78), channel_id=1, source_target_pairs={{16,0},{17,1},{18,2},{19,3},{20,4},{21,5},{22,6},{23,7},{24,8},{25... | collective-permute-start | bytes 12296 | tf_op jit(solution)/shard_map/ppermute | solution.py:35
  86.1 7.1 %collective-permute-done.8 = f32[2,16,32]{2,1,0:T(8,128)S(1)} collective-permute-done((f32[2,16,32]{2,1,0:T(8,128)S(1)}, f32[2,16,32]{2,1,0:T(8,128)S(1)}, u32[]{:S(2)}, u32[]{:S(2)}) %collective-permute-start.8) | collective-permute-done | bytes 4128 | tf_op jit(solution)/shard_map/ppermute | solution.py:35
  93.2 0.7 gather_fusion.3
  93.9 0.7 gather_fusion.2
  94.6 0.7 gather_fusion.1
  95.6 0.9 slice.461
  96.5 0.8 slice.460
  97.4 1.6 %gather_fusion = f32[512,512]{1,0:T(8,128)S(1)} fusion(f32[128,512]{1,0:T(8,128)S(1)} %pad_maximum_fusion.1, s32[1024]{0:T(1024)S(1)} %get-tuple-element.94), kind=kCustom, calls=%fused_computation.6 | custom fusion | bytes 2099200 | tf_op jit(solution)/shard_map/jit(_take)/gather | solution.py:175
  99.0 2.6 %gather.22 = f32[64,8,16,32]{3,2,1,0:T(8,128)} reshape(f32[512,512]{1,0:T(8,128)S(1)} %gather_fusion) | data formatting | bytes 2097152 | tf_op jit(solution)/shard_map/jit(_take)/gather | solution.py:175
  101.6 0.9 slice.435
  102.5 0.9 slice.433
  104.4 0.6 gather_fusion.4
  105.3 0.8 copy-done.5
  106.1 0.9 gather_fusion.5
  107.2 0.8 copy-done.7
  108.1 0.9 gather_fusion.6
  109.2 0.8 copy-done.9
  110.0 0.9 gather_fusion.7
  111.1 0.8 copy-done.11
  111.9 0.9 gather_fusion.8
  113.0 0.8 fusion.89
  113.9 0.8 gather_fusion.9
  114.9 8.3 %fusion.4 = f32[64,16,32]{2,1,0:T(8,128)S(1)} fusion(bf16[64,8,32,32]{3,2,1,0:T(8,128)(2,1)} %copy.36, f32[64,8,16,32]{3,2,1,0:T(8,128)} %gather.22, pred[64,8]{1,0:T(8,128)(4,1)S(1)} %copy.27), kind=kOutput, calls=%fused_computation.20 | convolution fusion | flops 100925440 | bytes 2228736 | tf_op jit(solution)/shard_map/lfrk,lfkq->lrq/dot_general | solution.py:176
  124.4 3.3 %fusion.13 = f32[16,64,64]{2,0,1:T(8,128)S(1)} fusion(f32[64,64]{1,0:T(8,128)S(1)} %copy-done.23, f32[64,64]{1,0:T(8,128)S(1)} %bitcast.160, f32[64,64]{1,0:T(8,128)S(1)} %copy-done.24, f32[64,64]{1,0:T(8,128)S(1)} %bitcast.161, f32[64,64]{1,0:T(8,128)S(1)} %copy-done.25, f32[64,64]{1,0:T(8,128)S(1)} %bitcast.159, f32[19,64,64]{2,0,1:T(8,128)S(1)} %copy-done.6, ...), kind=kOutput, calls=%fused_computation.33 | convolution fusion | flops 11468800 | bytes 983040 | tf_op jit(solution)/shard_map/rla,lab->rlb/dot_general | solution.py:51
  127.7 3.3 %fusion.12 = f32[16,64,64]{2,0,1:T(8,128)S(1)} fusion(f32[16,64,64]{2,0,1:T(8,128)S(1)} %fusion.13, f32[64,64]{1,0:T(8,128)S(1)} %bitcast.163, f32[64,64]{1,0:T(8,128)S(1)} %bitcast.164, f32[64,64]{1,0:T(8,128)S(1)} %bitcast.162, f32[64,64]{1,0:T(8,128)S(1)} %copy-done.23, f32[64,64]{1,0:T(8,128)S(1)} %copy-done.24, f32[64,64]{1,0:T(8,128)S(1)} %copy-done.25, ...), kind=kOutput, calls=%fused_computation.31 | convolution fusion | flops 11337728 | bytes 1245184 | tf_op jit(solution)/shard_map/rla,lab->rlb/dot_general | solution.py:51
  131.0 3.3 %fusion.11 = f32[16,64,64]{2,0,1:T(8,128)S(1)} fusion(f32[16,64,64]{2,0,1:T(8,128)S(1)} %fusion.12, f32[64,64]{1,0:T(8,128)S(1)} %bitcast.166, f32[64,64]{1,0:T(8,128)S(1)} %bitcast.167, f32[64,64]{1,0:T(8,128)S(1)} %bitcast.165, f32[64,64]{1,0:T(8,128)S(1)} %copy-done.23, f32[64,64]{1,0:T(8,128)S(1)} %copy-done.24, f32[64,64]{1,0:T(8,128)S(1)} %copy-done.25, ...), kind=kOutput, calls=%fused_computation.29 | convolution fusion | flops 11337728 | bytes 1245184 | tf_op jit(solution)/shard_map/rla,lab->rlb/dot_general | solution.py:51
  134.3 3.3 %fusion.10 = f32[16,64,64]{2,0,1:T(8,128)S(1)} fusion(f32[16,64,64]{2,0,1:T(8,128)S(1)} %fusion.11, f32[64,64]{1,0:T(8,128)S(1)} %bitcast.169, f32[64,64]{1,0:T(8,128)S(1)} %bitcast.170, f32[64,64]{1,0:T(8,128)S(1)} %bitcast.168, f32[64,64]{1,0:T(8,128)S(1)} %copy-done.23, f32[64,64]{1,0:T(8,128)S(1)} %copy-done.24, f32[64,64]{1,0:T(8,128)S(1)} %copy-done.25, ...), kind=kOutput, calls=%fused_computation.27 | convolution fusion | flops 11337728 | bytes 1245184 | tf_op jit(solution)/shard_map/rla,lab->rlb/dot_general | solution.py:51
  137.6 3.3 %fusion.9 = f32[16,64,64]{2,0,1:T(8,128)S(1)} fusion(f32[16,64,64]{2,0,1:T(8,128)S(1)} %fusion.10, f32[64,64]{1,0:T(8,128)S(1)} %bitcast.172, f32[64,64]{1,0:T(8,128)S(1)} %bitcast.173, f32[64,64]{1,0:T(8,128)S(1)} %bitcast.171, f32[64,64]{1,0:T(8,128)S(1)} %copy-done.23, f32[64,64]{1,0:T(8,128)S(1)} %copy-done.24, f32[64,64]{1,0:T(8,128)S(1)} %copy-done.25, ...), kind=kOutput, calls=%fused_computation.25 | convolution fusion | flops 11337728 | bytes 1245184 | tf_op jit(solution)/shard_map/rla,lab->rlb/dot_general | solution.py:51
  140.9 3.3 %fusion.8 = f32[16,64,64]{2,0,1:T(8,128)S(1)} fusion(f32[16,64,64]{2,0,1:T(8,128)S(1)} %convolution_bitcast_fusion.7, f32[16,64,64]{2,0,1:T(8,128)S(1)} %fusion.9, f32[64,64]{1,0:T(8,128)S(1)} %bitcast.175, f32[64,64]{1,0:T(8,128)S(1)} %bitcast.176, f32[64,64]{1,0:T(8,128)S(1)} %bitcast.174, f32[64,64]{1,0:T(8,128)S(1)} %copy-done.23, ...), kind=kOutput, calls=%fused_computation.23 | convolution fusion | flops 11403264 | bytes 1769472 | tf_op jit(solution)/shard_map/rla,lab->rlb/dot_general | solution.py:51
  144.3 0.9 reshape.181
  (174 shorter events, 12.8 us)
Async XLA Ops:
  1.2 3.9 %copy-start.1 = (bf16[16,64,64]{2,1,0:T(8,128)(2,1)}, bf16[16,64,64]{2,1,0:T(8,128)(2,1)S(1)}, u32[]{:S(2)}) copy-start(bf16[16,64,64]{2,1,0:T(8,128)(2,1)S(1)} %reshape.168) | copy-start | bytes 393220
  2.2 3.0 %copy-start.15 = (f32[3,4096]{1,0:T(4,128)S(1)}, f32[3,4096]{1,0:T(4,128)}, u32[]{:S(2)}) copy-start(f32[3,4096]{1,0:T(4,128)} %param.16) | copy-start | bytes 147460
  4.6 8.1 %copy-start.26 = (bf16[1,3,1024]{2,1,0:T(4,128)(2,1)S(1)}, bf16[1,3,1024]{2,1,0:T(4,128)(2,1)}, u32[]{:S(2)}) copy-start(bf16[1,3,1024]{2,1,0:T(4,128)(2,1)} %param.24) | copy-start | bytes 18436
  4.6 8.1 %copy-start.27 = (bf16[1,3,1024]{2,1,0:T(4,128)(2,1)S(1)}, bf16[1,3,1024]{2,1,0:T(4,128)(2,1)}, u32[]{:S(2)}) copy-start(bf16[1,3,1024]{2,1,0:T(4,128)(2,1)} %param.25) | copy-start | bytes 18436
  4.6 8.1 %copy-start.17 = (bf16[64,1024]{1,0:T(8,128)(2,1)S(1)}, bf16[64,1024]{1,0:T(8,128)(2,1)}, u32[]{:S(2)}) copy-start(bf16[64,1024]{1,0:T(8,128)(2,1)} %param.22) | copy-start | bytes 393220
  5.2 14.9 %copy-start.31 = (s32[64,8]{0,1:T(8,128)S(1)}, s32[64,8]{0,1:T(8,128)}, u32[]{:S(2)}) copy-start(s32[64,8]{0,1:T(8,128)} %param.18) | copy-start | bytes 6148
  5.2 15.6 %copy-start.32 = (s32[64,6]{0,1:T(8,128)S(1)}, s32[64,6]{0,1:T(8,128)}, u32[]{:S(2)}) copy-start(s32[64,6]{0,1:T(8,128)} %param.17) | copy-start | bytes 4612
  5.2 16.2 %copy-start.22 = (bf16[1,4,4,1024]{3,2,1,0:T(4,128)(2,1)S(1)}, bf16[1,4,4,1024]{3,2,1,0:T(4,128)(2,1)}, u32[]{:S(2)}) copy-start(bf16[1,4,4,1024]{3,2,1,0:T(4,128)(2,1)} %param.26) | copy-start | bytes 98308
  5.3 17.5 %copy-start.39 = (s32[4]{0:T(128)S(1)}, s32[4]{0:T(128)}, u32[]{:S(2)}) copy-start(s32[4]{0:T(128)} %constant.69) | copy-start | bytes 52
  6.0 89.6 %collective-permute-start.1 = (f32[35840]{0:T(1024)}, f32[35840]{0:T(1024)}, u32[]{:S(2)}, u32[]{:S(2)}) collective-permute-start(f32[35840]{0:T(1024)} %pad_maximum_fusion.3), channel_id=1, source_target_pairs={{1,0},{2,1},{3,2},{4,3},{5,4},{6,5},{7,6},{8,7},{9,8},{10,9},{11,1... | collective-permute-start | bytes 430088 | tf_op jit(solution)/shard_map/ppermute | solution.py:151
  9.2 87.3 %collective-permute-start = (f32[35840]{0:T(1024)}, f32[35840]{0:T(1024)}, u32[]{:S(2)}, u32[]{:S(2)}) collective-permute-start(f32[35840]{0:T(1024)} %pad_maximum_fusion.2), channel_id=1, source_target_pairs={{0,1},{1,2},{2,3},{3,4},{4,5},{5,6},{6,7},{7,8},{8,9},{9,10},{10,1... | collective-permute-start | bytes 430088 | tf_op jit(solution)/shard_map/ppermute | solution.py:150
  12.9 26.7 %copy-start = (bf16[64,8,1024]{2,1,0:T(8,128)(2,1)S(1)}, bf16[64,8,1024]{2,1,0:T(8,128)(2,1)}, u32[]{:S(2)}) copy-start(bf16[64,8,1024]{2,1,0:T(8,128)(2,1)} %param.21) | copy-start | bytes 3145732
  15.2 10.8 %collective-permute-start.2 = (f32[4,16,32]{2,1,0:T(8,128)S(1)}, f32[4,16,32]{2,1,0:T(8,128)S(1)}, u32[]{:S(2)}, u32[]{:S(2)}) collective-permute-start(f32[4,16,32]{2,1,0:T(8,128)S(1)} %convolution_bitcast_fusion.8), channel_id=1, source_target_pairs={{0,1},{1,0},{2,3},{3,2},{4,5},{5,4},{6,7},{7,6},{8,9},{9,8},{10,11... | collective-permute-start | bytes 24584 | tf_op jit(solution)/shard_map/ppermute | solution.py:30
  26.0 7.4 %collective-permute-start.3 = (f32[5,16,32]{2,1,0:T(8,128)S(1)}, f32[5,16,32]{2,1,0:T(8,128)S(1)}, u32[]{:S(2)}, u32[]{:S(2)}) collective-permute-start(f32[5,16,32]{2,1,0:T(8,128)S(1)} %pad_maximum_fusion.15), channel_id=1, source_target_pairs={{0,2},{1,3},{2,0},{3,1},{4,6},{5,7},{6,4},{7,5},{8,10},{9,11},{10,... | collective-permute-start | bytes 30728 | tf_op jit(solution)/shard_map/ppermute | solution.py:30
  34.1 17.8 %collective-permute-start.4 = (f32[8,16,32]{2,1,0:T(8,128)}, f32[8,16,32]{2,1,0:T(8,128)}, u32[]{:S(2)}, u32[]{:S(2)}) collective-permute-start(f32[8,16,32]{2,1,0:T(8,128)} %fusion.63), channel_id=1, source_target_pairs={{0,4},{1,5},{2,6},{3,7},{4,0},{5,1},{6,2},{7,3},{8,12},{9,13},{10,... | collective-permute-start | bytes 49160 | tf_op jit(solution)/shard_map/ppermute | solution.py:30
  41.0 6.9 %copy-start.3 = (f32[64,16,32]{0,2,1:T(8,128)S(1)}, f32[64,16,32]{0,2,1:T(8,128)}, u32[]{:S(2)}) copy-start(f32[64,16,32]{0,2,1:T(8,128)} %copy.28) | copy-start | bytes 393220
  41.0 7.0 %copy-start.30 = (pred[64,8]{0,1:T(8,128)(4,1)S(1)}, pred[64,8]{0,1:T(8,128)(4,1)}, u32[]{:S(2)}) copy-start(pred[64,8]{0,1:T(8,128)(4,1)} %get-tuple-element.27) | copy-start | bytes 1540
  41.0 7.2 %copy-start.4 = (f32[4,32,4,32]{3,1,2,0:T(8,128)S(1)}, f32[4,32,4,32]{3,1,2,0:T(8,128)}, u32[]{:S(2)}) copy-start(f32[4,32,4,32]{3,1,2,0:T(8,128)} %fusion.70) | copy-start | bytes 196612
  41.0 7.3 %copy-start.18 = (bf16[64,1024]{1,0:T(8,128)(2,1)S(1)}, bf16[64,1024]{1,0:T(8,128)(2,1)}, u32[]{:S(2)}) copy-start(bf16[64,1024]{1,0:T(8,128)(2,1)} %param.23) | copy-start | bytes 393220
  47.9 1.4 copy-start.16
  47.9 1.9 %copy-start.21 = (f32[4096]{0:T(1024)S(1)}, f32[4096]{0:T(1024)}, u32[]{:S(2)}) copy-start(f32[4096]{0:T(1024)} %get-tuple-element.7) | copy-start | bytes 49156
  47.9 2.6 %copy-start.20 = (f32[4096]{0:T(1024)S(1)}, f32[4096]{0:T(1024)}, u32[]{:S(2)}) copy-start(f32[4096]{0:T(1024)} %get-tuple-element.8) | copy-start | bytes 49156
  47.9 3.3 %copy-start.19 = (f32[4096]{0:T(1024)S(1)}, f32[4096]{0:T(1024)}, u32[]{:S(2)}) copy-start(f32[4096]{0:T(1024)} %get-tuple-element.6) | copy-start | bytes 49156
  52.6 40.6 %collective-permute-start.10 = (f32[1,16,32]{2,1,0:T(8,128)S(1)}, f32[1,16,32]{2,1,0:T(8,128)S(1)}, u32[]{:S(2)}, u32[]{:S(2)}) collective-permute-start(f32[1,16,32]{2,1,0:T(8,128)S(1)} %get-tuple-element.58), channel_id=1, source_target_pairs={{24,0},{25,1},{26,2},{27,3},{28,4},{29,5},{30,6},{31,7},{32,8},{33... | collective-permute-start | bytes 6152 | tf_op jit(solution)/shard_map/ppermute | solution.py:35
  54.5 38.7 %collective-permute-start.9 = (f32[1,16,32]{2,1,0:T(8,128)S(1)}, f32[1,16,32]{2,1,0:T(8,128)S(1)}, u32[]{:S(2)}, u32[]{:S(2)}) collective-permute-start(f32[1,16,32]{2,1,0:T(8,128)S(1)} %get-tuple-element.58), channel_id=1, source_target_pairs={{0,24},{1,25},{2,26},{3,27},{4,28},{5,29},{6,30},{7,31},{8,32},{9,... | collective-permute-start | bytes 6152 | tf_op jit(solution)/shard_map/ppermute | solution.py:35
  60.6 7.1 %collective-permute-start.7 = (f32[2,16,32]{2,1,0:T(8,128)S(1)}, f32[2,16,32]{2,1,0:T(8,128)S(1)}, u32[]{:S(2)}, u32[]{:S(2)}) collective-permute-start(f32[2,16,32]{2,1,0:T(8,128)S(1)} %get-tuple-element.77), channel_id=1, source_target_pairs={{0,16},{1,17},{2,18},{3,19},{4,20},{5,21},{6,22},{7,23},{8,24},{9,... | collective-permute-start | bytes 12296 | tf_op jit(solution)/shard_map/ppermute | solution.py:35
  67.8 6.4 %collective-permute-start.5 = (f32[8,16,32]{2,1,0:T(8,128)S(1)}, f32[8,16,32]{2,1,0:T(8,128)S(1)}, u32[]{:S(2)}, u32[]{:S(2)}) collective-permute-start(f32[8,16,32]{2,1,0:T(8,128)S(1)} %get-tuple-element.72), channel_id=1, source_target_pairs={{0,8},{1,9},{2,10},{3,11},{4,12},{5,13},{6,14},{7,15},{8,16},{9,17... | collective-permute-start | bytes 49160 | tf_op jit(solution)/shard_map/ppermute | solution.py:35
  74.1 9.8 %collective-permute-start.6 = (f32[8,16,32]{2,1,0:T(8,128)S(1)}, f32[8,16,32]{2,1,0:T(8,128)S(1)}, u32[]{:S(2)}, u32[]{:S(2)}) collective-permute-start(f32[8,16,32]{2,1,0:T(8,128)S(1)} %get-tuple-element.71), channel_id=1, source_target_pairs={{8,0},{9,1},{10,2},{11,3},{12,4},{13,5},{14,6},{15,7},{16,8},{17,9... | collective-permute-start | bytes 49160 | tf_op jit(solution)/shard_map/ppermute | solution.py:35
  83.9 9.2 %collective-permute-start.8 = (f32[2,16,32]{2,1,0:T(8,128)S(1)}, f32[2,16,32]{2,1,0:T(8,128)S(1)}, u32[]{:S(2)}, u32[]{:S(2)}) collective-permute-start(f32[2,16,32]{2,1,0:T(8,128)S(1)} %get-tuple-element.78), channel_id=1, source_target_pairs={{16,0},{17,1},{18,2},{19,3},{20,4},{21,5},{22,6},{23,7},{24,8},{25... | collective-permute-start | bytes 12296 | tf_op jit(solution)/shard_map/ppermute | solution.py:35
  103.5 1.6 %copy-start.38 = (pred[64]{0:T(512)(128)(4,1)S(1)}, pred[64]{0:T(512)(128)(4,1)}, u32[]{:S(2)}) copy-start(pred[64]{0:T(512)(128)(4,1)} %get-tuple-element.85) | copy-start | bytes 196
  104.4 2.6 %copy-start.37 = (pred[64]{0:T(512)(128)(4,1)S(1)}, pred[64]{0:T(512)(128)(4,1)}, u32[]{:S(2)}) copy-start(pred[64]{0:T(512)(128)(4,1)} %get-tuple-element.83) | copy-start | bytes 196
  105.2 0.9 copy-start.5
  106.1 2.8 %copy-start.36 = (pred[64]{0:T(512)(128)(4,1)S(1)}, pred[64]{0:T(512)(128)(4,1)}, u32[]{:S(2)}) copy-start(pred[64]{0:T(512)(128)(4,1)} %get-tuple-element.81) | copy-start | bytes 196
  107.2 0.9 copy-start.7
  108.1 2.8 %copy-start.35 = (pred[64]{0:T(512)(128)(4,1)S(1)}, pred[64]{0:T(512)(128)(4,1)}, u32[]{:S(2)}) copy-start(pred[64]{0:T(512)(128)(4,1)} %get-tuple-element.79) | copy-start | bytes 196
  109.1 0.9 copy-start.9
  110.0 2.8 %copy-start.34 = (pred[64]{0:T(512)(128)(4,1)S(1)}, pred[64]{0:T(512)(128)(4,1)}, u32[]{:S(2)}) copy-start(pred[64]{0:T(512)(128)(4,1)} %get-tuple-element.87) | copy-start | bytes 196
  111.0 0.9 copy-start.11
  111.9 2.7 %copy-start.33 = (pred[64]{0:T(512)(128)(4,1)S(1)}, pred[64]{0:T(512)(128)(4,1)}, u32[]{:S(2)}) copy-start(pred[64]{0:T(512)(128)(4,1)} %get-tuple-element.15) | copy-start | bytes 196
  113.0 0.9 copy-start.13
  123.2 1.0 copy-start.2
  123.2 1.2 copy-start.6
  123.2 1.2 copy-start.23
  123.2 1.2 copy-start.24
  123.2 1.2 copy-start.25
  124.4 3.3 %copy-start.8 = (f32[19,64,64]{2,0,1:T(8,128)S(1)}, f32[19,64,64]{2,0,1:T(8,128)}, u32[]{:S(2)}) copy-start(f32[19,64,64]{2,0,1:T(8,128)} %copy-done.7) | copy-start | bytes 933892
  127.7 3.3 %copy-start.10 = (f32[19,64,64]{2,0,1:T(8,128)S(1)}, f32[19,64,64]{2,0,1:T(8,128)}, u32[]{:S(2)}) copy-start(f32[19,64,64]{2,0,1:T(8,128)} %copy-done.9) | copy-start | bytes 933892
  131.0 3.3 %copy-start.12 = (f32[19,64,64]{2,0,1:T(8,128)S(1)}, f32[19,64,64]{2,0,1:T(8,128)}, u32[]{:S(2)}) copy-start(f32[19,64,64]{2,0,1:T(8,128)} %copy-done.11) | copy-start | bytes 933892
  134.3 3.3 %copy-start.14 = (f32[19,64,64]{2,0,1:T(8,128)S(1)}, f32[19,64,64]{2,0,1:T(8,128)}, u32[]{:S(2)}) copy-start(f32[19,64,64]{2,0,1:T(8,128)} %copy-done.13) | copy-start | bytes 933892
  134.3 3.3 %copy-start.28 = (f32[1,64,64]{2,0,1:T(1,128)S(1)}, f32[1,64,64]{2,0,1:T(1,128)}, u32[]{:S(2)}) copy-start(f32[1,64,64]{2,0,1:T(1,128)} %get-tuple-element.33) | copy-start | bytes 49156
  134.3 3.3 %copy-start.29 = (f32[1,64,64]{2,0,1:T(1,128)S(1)}, f32[1,64,64]{2,0,1:T(1,128)}, u32[]{:S(2)}) copy-start(f32[1,64,64]{2,0,1:T(1,128)} %get-tuple-element.34) | copy-start | bytes 49156

commit v2 on v1

--- a/solution.py
+++ b/solution.py
@@ -53,6 +53,14 @@
 
 def mm(a, b):
     return jnp.matmul(a, b, precision=highest, preferred_element_type=jnp.float32)
+
+
+def split3(x):
+    hi = lax.reduce_precision(x, exponent_bits=8, mantissa_bits=7)
+    rest = x - hi
+    mid = lax.reduce_precision(rest, exponent_bits=8, mantissa_bits=7)
+    lo = rest - mid
+    return jnp.stack([hi, mid, lo]).astype(jnp.bfloat16)
 
 
 def ordered(bit, own, other):
@@ -96,12 +104,12 @@
     coef3 = (part3 + got3[7])[None]
 
     node = 8
-    ahead1 = receive_from(jnp.concatenate([octs0[0:3], quads1[0:3], pairs2]), node)
-    behind1 = receive_from(jnp.concatenate([octs0[5:8], quads1[1:4], pairs2]), -node)
-    ahead2 = receive_from(jnp.concatenate([pairs2[0:1], coef3]), 2 * node)
-    behind2 = receive_from(jnp.concatenate([pairs2[1:2], coef3]), -2 * node)
-    ahead3 = receive_from(coef3, 3 * node)
-    behind3 = receive_from(coef3, -3 * node)
+    ahead1 = receive_from(jnp.concatenate([octs0[0:3], quads1[0:3], pairs2, coef3]), node)
+    behind1 = receive_from(jnp.concatenate([octs0[5:8], quads1[1:4], pairs2, coef3]), -node)
+    ahead2 = receive_from(jnp.concatenate([pairs2[0:1], coef3, ahead1[8:9]]), 2 * node)
+    behind2 = receive_from(jnp.concatenate([pairs2[1:2], coef3, behind1[8:9]]), -2 * node)
+    ahead3 = ahead2[2:3]
+    behind3 = behind2[2:3]
 
     window0 = jnp.concatenate([behind1[0:3], octs0, ahead1[0:3]])
     window1 = jnp.concatenate([behind1[3:6], quads1, ahead1[3:6]])
@@ -174,10 +182,9 @@
     far_index = jnp.arange(leaf_count, dtype=jnp.int32)[:, None] + FAR_REACH + far_offsets
     partner_blocks = jnp.take(rimmed, far_index, axis=0).reshape(leaf_count, FAR_BLOCKS, RHS, RANK)
     leaf_far = jnp.einsum(
-        "lfrk,lfkq->lrq",
-        partner_blocks,
+        "slfrk,lfkq->lrq",
+        split3(partner_blocks),
         leaf_coupling.reshape(leaf_count, FAR_BLOCKS, RANK, RANK),
-        precision=highest,
         preferred_element_type=jnp.float32,
     )
     root_coefficients = jnp.einsum(

time: 146 us -> 156 us (1.068)
  the two profiles are of different devices: /device:TPU:124 before, /device:TPU:392 now
where the time goes in v2:
time: 156 us; the launch traced here: 155 us
  local copies, waits for them, and re-layouts  61.5 us (39%)
  starting transfers between devices  36.9 us (24%)
  matrix products  28.7 us (18%)
  other arithmetic  15.9 us (10%)
  waiting for transfers between devices  10.9 us (7%)
    ppermute x4, starting transfers between devices, receive_from(): lax.ppermute(value, AXES, [(s, s - step) for s in range(n) if 0 <= s - st...  21.1 us
    dot_general x6, matrix products, matern_term(): jnp.einsum('rla,lab->rlb', values, kernel, preferred_element_type=jnp.flo...  19.7 us
    unnamed x96, local copies, waits for them, and re-layouts  11.9 us
    gather x6, local copies, waits for them, and re-layouts, matern_term(): chosen = jnp.take(extended, source_leaf, axis=1)  10 us
    ppermute x3, starting transfers between devices, swap_with(): return lax.ppermute(value, AXES, [(i, i ^ mask) for i in range(n)])  9.95 us
    ppermute x4, waiting for transfers between devices, receive_from(): lax.ppermute(value, AXES, [(s, s - step) for s in range(n) if 0 <= s - st...  8.14 us
    gather x3, local copies, waits for them, and re-layouts, local(): jnp.take(rimmed, far_index, axis=0)  8.05 us
    select_n x6, other arithmetic, matern_term(): chosen = jnp.take(extended, source_leaf, axis=1)  7.65 us
  transfers between devices with their start and end apart: 9, of which 4 were waited for; matrix products, arithmetic and copies ran while one was open for 19% of the time, Pallas kernels for 0%

profile of v2, /device:TPU:392, one launch (start us, length us, event | category | flops | bytes accessed | tf_op | source)
XLA Modules:
  0.0 154.9 jit_solution(16532871435253008132)
XLA Ops:
  0.0 0.9 slice_reduce_fusion.5
  0.9 0.7 convert_reduce_fusion.1
  1.6 1.2 copy.88
  2.8 1.1 copy.90
  3.9 1.2 reshape.198
  5.3 0.8 copy.105
  6.8 0.8 fusion.97
  8.0 3.4 %collective-permute-start.2 = (f32[4,16,32]{2,1,0:T(8,128)S(1)}, f32[4,16,32]{2,1,0:T(8,128)S(1)}, u32[]{:S(2)}, u32[]{:S(2)}) collective-permute-start(f32[4,16,32]{2,1,0:T(8,128)S(1)} %convolution_bitcast_fusion.10), channel_id=1, source_target_pairs={{0,1},{1,0},{2,3},{3,2},{4,5},{5,4},{6,7},{7,6},{8,9},{9,8},{10,11... | collective-permute-start | bytes 24584 | tf_op jit(solution)/shard_map/ppermute | solution.py:30
  12.4 3.0 %collective-permute-start.1 = (f32[35840]{0:T(1024)}, f32[35840]{0:T(1024)}, u32[]{:S(2)}, u32[]{:S(2)}) collective-permute-start(f32[35840]{0:T(1024)} %pad_maximum_fusion.3), channel_id=1, source_target_pairs={{1,0},{2,1},{3,2},{4,3},{5,4},{6,5},{7,6},{8,7},{9,8},{10,9},{11,1... | collective-permute-start | bytes 430088 | tf_op jit(solution)/shard_map/ppermute | solution.py:159
  16.3 2.8 %collective-permute-start = (f32[35840]{0:T(1024)}, f32[35840]{0:T(1024)}, u32[]{:S(2)}, u32[]{:S(2)}) collective-permute-start(f32[35840]{0:T(1024)} %pad_maximum_fusion.2), channel_id=1, source_target_pairs={{0,1},{1,2},{2,3},{3,4},{4,5},{5,6},{6,7},{7,8},{8,9},{9,10},{10,1... | collective-permute-start | bytes 430088 | tf_op jit(solution)/shard_map/ppermute | solution.py:158
  23.1 1.4 convolution_bitcast_fusion.9
  25.2 4.6 %collective-permute-start.3 = (f32[5,16,32]{2,1,0:T(8,128)S(1)}, f32[5,16,32]{2,1,0:T(8,128)S(1)}, u32[]{:S(2)}, u32[]{:S(2)}) collective-permute-start(f32[5,16,32]{2,1,0:T(8,128)S(1)} %pad_maximum_fusion.17), channel_id=1, source_target_pairs={{0,2},{1,3},{2,0},{3,1},{4,6},{5,7},{6,4},{7,5},{8,10},{9,11},{10,... | collective-permute-start | bytes 30728 | tf_op jit(solution)/shard_map/ppermute | solution.py:30
  29.9 2.7 %collective-permute-done.3 = f32[5,16,32]{2,1,0:T(8,128)S(1)} collective-permute-done((f32[5,16,32]{2,1,0:T(8,128)S(1)}, f32[5,16,32]{2,1,0:T(8,128)S(1)}, u32[]{:S(2)}, u32[]{:S(2)}) %collective-permute-start.3) | collective-permute-done | bytes 10272 | tf_op jit(solution)/shard_map/ppermute | solution.py:30
  33.3 1.9 %collective-permute-start.4 = (f32[8,16,32]{2,1,0:T(8,128)}, f32[8,16,32]{2,1,0:T(8,128)}, u32[]{:S(2)}, u32[]{:S(2)}) collective-permute-start(f32[8,16,32]{2,1,0:T(8,128)} %fusion.57), channel_id=1, source_target_pairs={{0,4},{1,5},{2,6},{3,7},{4,0},{5,1},{6,2},{7,3},{8,12},{9,13},{10,... | collective-permute-start | bytes 49160 | tf_op jit(solution)/shard_map/ppermute | solution.py:30
  35.6 0.8 copy.111
  36.5 2.4 %copy.102 = bf16[64,8,1024]{0,2,1:T(8,128)(2,1)S(1)} copy(bf16[64,8,1024]{2,1,0:T(8,128)(2,1)} %param.21) | data formatting | bytes 2097152 | tf_op args[6]
  39.0 6.8 %copy.103 = bf16[64,8,32,32]{3,2,1,0:T(8,128)(2,1)} copy(bf16[64,8,32,32]{0,3,2,1:T(8,128)(2,1)S(1)} %bitcast.148) | data formatting | bytes 2097152 | tf_op jit(solution)/shard_map/reshape | solution.py:187
  45.8 2.3 %reshape.210 = bf16[64,32,64]{2,1,0:T(8,128)(2,1)} reshape(bf16[64,2048]{1,0:T(8,128)(2,1)} %param.20) | data formatting | bytes 524288 | tf_op jit(solution)/shard_map/reshape | solution.py:209
  51.6 0.8 slice.488
  52.4 3.5 %collective-permute-start.5 = (f32[9,16,32]{2,1,0:T(8,128)S(1)}, f32[9,16,32]{2,1,0:T(8,128)S(1)}, u32[]{:S(2)}, u32[]{:S(2)}) collective-permute-start(f32[9,16,32]{2,1,0:T(8,128)S(1)} %get-tuple-element.75), channel_id=1, source_target_pairs={{0,8},{1,9},{2,10},{3,11},{4,12},{5,13},{6,14},{7,15},{8,16},{9,17... | collective-permute-start | bytes 55304 | tf_op jit(solution)/shard_map/ppermute | solution.py:35
  55.9 4.1 %collective-permute-start.6 = (f32[9,16,32]{2,1,0:T(8,128)S(1)}, f32[9,16,32]{2,1,0:T(8,128)S(1)}, u32[]{:S(2)}, u32[]{:S(2)}) collective-permute-start(f32[9,16,32]{2,1,0:T(8,128)S(1)} %get-tuple-element.76), channel_id=1, source_target_pairs={{8,0},{9,1},{10,2},{11,3},{12,4},{13,5},{14,6},{15,7},{16,8},{17,9... | collective-permute-start | bytes 55304 | tf_op jit(solution)/shard_map/ppermute | solution.py:35
  60.1 1.0 collective-permute-done.5
  61.1 1.2 collective-permute-done.6
  62.3 11.6 %collective-permute-start.8 = (f32[3,16,32]{2,1,0:T(8,128)S(1)}, f32[3,16,32]{2,1,0:T(8,128)S(1)}, u32[]{:S(2)}, u32[]{:S(2)}) collective-permute-start(f32[3,16,32]{2,1,0:T(8,128)S(1)} %get-tuple-element.80), channel_id=1, source_target_pairs={{16,0},{17,1},{18,2},{19,3},{20,4},{21,5},{22,6},{23,7},{24,8},{25... | collective-permute-start | bytes 18440 | tf_op jit(solution)/shard_map/ppermute | solution.py:35
  73.9 1.9 %collective-permute-start.7 = (f32[3,16,32]{2,1,0:T(8,128)S(1)}, f32[3,16,32]{2,1,0:T(8,128)S(1)}, u32[]{:S(2)}, u32[]{:S(2)}) collective-permute-start(f32[3,16,32]{2,1,0:T(8,128)S(1)} %get-tuple-element.79), channel_id=1, source_target_pairs={{0,16},{1,17},{2,18},{3,19},{4,20},{5,21},{6,22},{7,23},{8,24},{9,... | collective-permute-start | bytes 18440 | tf_op jit(solution)/shard_map/ppermute | solution.py:35
  77.2 6.0 %collective-permute-done.7 = f32[3,16,32]{2,1,0:T(8,128)S(1)} collective-permute-done((f32[3,16,32]{2,1,0:T(8,128)S(1)}, f32[3,16,32]{2,1,0:T(8,128)S(1)}, u32[]{:S(2)}, u32[]{:S(2)}) %collective-permute-start.7) | collective-permute-done | bytes 6176 | tf_op jit(solution)/shard_map/ppermute | solution.py:35
  84.1 1.2 convolution_bitcast_fusion.6
  85.4 0.8 slice.475
  86.2 0.8 slice.474
  87.1 1.8 %gather_fusion = f32[512,512]{1,0:T(8,128)S(1)} fusion(f32[128,512]{1,0:T(8,128)S(1)} %pad_maximum_fusion.1, s32[1024]{0:T(1024)S(1)} %get-tuple-element.98), kind=kCustom, calls=%fused_computation.6 | custom fusion | bytes 2099200 | tf_op jit(solution)/shard_map/jit(_take)/gather | solution.py:183
  88.9 2.6 %gather.22 = f32[1,64,8,16,32]{4,3,2,1,0:T(8,128)} reshape(f32[512,512]{1,0:T(8,128)S(1)} %gather_fusion) | data formatting | bytes 2097152 | tf_op jit(solution)/shard_map/jit(_take)/gather | solution.py:183
  91.5 3.6 %copy.100 = f32[1,64,8,16,32]{1,4,3,2,0:T(8,128)S(1)} copy(f32[1,64,8,16,32]{4,3,2,1,0:T(8,128)} %gather.22) | data formatting | bytes 2097152 | tf_op jit(solution)/shard_map/jit(_take)/gather | solution.py:183
  95.2 0.8 reduce-precision_convert_fusion.1
  96.0 0.9 convert_reduce_fusion
  96.8 3.2 %copy.121 = bf16[64,8,16,32]{3,2,1,0:T(8,128)(2,1)S(1)} copy(bf16[64,8,16,32]{0,3,2,1:T(8,128)(2,1)S(1)} %convert_reduce_fusion) | data formatting | bytes 1048576
  100.1 0.9 slice.449
  101.0 0.9 slice.447
  102.0 1.3 reshape.204
  103.3 1.7 %copy.91 = f32[19,96,64]{2,0,1:T(8,128)S(1)} copy(f32[19,96,64]{2,1,0:T(8,128)} %reshape.204) | data formatting | bytes 933888 | tf_op jit(solution)/shard_map/reshape | solution.py:168
  105.1 1.5 gather_fusion.4
  106.6 1.3 select_bitcast_fusion.5
  107.9 0.9 copy-done.5
  108.9 1.7 %gather_fusion.5 = f32[64,19,64]{2,1,0:T(8,128)} fusion(f32[19,96,64]{2,0,1:T(8,128)S(1)} %copy.91, s32[1024]{0:T(1024)} %get-tuple-element.103), kind=kCustom, calls=%fused_computation.1.clone | custom fusion | bytes 622848 | tf_op jit(solution)/shard_map/jit(_take)/gather | solution.py:42
  110.5 1.3 select_bitcast_fusion.4
  111.8 0.9 copy-done.7
  112.8 1.7 %gather_fusion.6 = f32[64,19,64]{2,1,0:T(8,128)} fusion(f32[19,96,64]{2,0,1:T(8,128)S(1)} %copy.91, s32[1024]{0:T(1024)} %get-tuple-element.102), kind=kCustom, calls=%fused_computation.2.clone | custom fusion | bytes 622848 | tf_op jit(solution)/shard_map/jit(_take)/gather | solution.py:42
  114.4 1.3 select_bitcast_fusion.3
  115.7 0.9 copy-done.9
  117.3 1.8 %gather_fusion.7 = f32[64,19,64]{2,1,0:T(8,128)} fusion(f32[19,96,64]{2,0,1:T(8,128)S(1)} %copy.91, s32[1024]{0:T(1024)} %get-tuple-element.101), kind=kCustom, calls=%fused_computation.3.clone | custom fusion | bytes 622848 | tf_op jit(solution)/shard_map/jit(_take)/gather | solution.py:42
  119.1 1.3 select_bitcast_fusion.2
  120.3 0.9 copy-done.11
  121.9 1.8 %gather_fusion.8 = f32[64,19,64]{2,1,0:T(8,128)} fusion(f32[19,96,64]{2,0,1:T(8,128)S(1)} %copy.91, s32[1024]{0:T(1024)} %get-tuple-element.100), kind=kCustom, calls=%fused_computation.4.clone | custom fusion | bytes 622848 | tf_op jit(solution)/shard_map/jit(_take)/gather | solution.py:42
  123.7 1.3 select_bitcast_fusion.1
  125.0 0.9 copy-done.13
  126.6 1.6 %gather_fusion.9 = f32[64,19,64]{2,1,0:T(8,128)} fusion(f32[19,96,64]{2,0,1:T(8,128)S(1)} %copy.91, s32[1024]{0:T(1024)S(1)} %get-tuple-element.99), kind=kCustom, calls=%fused_computation.5.clone | custom fusion | bytes 622848 | tf_op jit(solution)/shard_map/jit(_take)/gather | solution.py:42
  128.2 1.3 select_bitcast_fusion
  129.7 3.7 %fusion.8 = f32[64,16,32]{2,1,0:T(8,128)S(1)} fusion(f32[64,16,32]{2,1,0:T(8,128)S(1)} %copy-done, bf16[64,8,16,32]{3,2,1,0:T(8,128)(2,1)S(1)} %copy.121, bf16[64,8,32,32]{3,2,1,0:T(8,128)(2,1)} %copy.103), kind=kOutput, calls=%fused_computation.37 | convolution fusion | flops 16809984 | bytes 1835008 | tf_op jit(solution)/shard_map/slfrk,lfkq->lrq/dot_general | solution.py:184
  134.0 3.3 %fusion.7 = f32[16,64,64]{2,0,1:T(8,128)S(1)} fusion(f32[64,64]{1,0:T(8,128)S(1)} %copy-done.23, f32[64,64]{1,0:T(8,128)S(1)} %bitcast.159, f32[64,64]{1,0:T(8,128)S(1)} %copy-done.24, f32[64,64]{1,0:T(8,128)S(1)} %bitcast.160, f32[64,64]{1,0:T(8,128)S(1)} %copy-done.25, f32[64,64]{1,0:T(8,128)S(1)} %bitcast.158, f32[19,64,64]{2,0,1:T(8,128)S(1)} %copy-done.6, ...), kind=kOutput, calls=%fused_computation.34 | convolution fusion | flops 11468800 | bytes 983040 | tf_op jit(solution)/shard_map/rla,lab->rlb/dot_general | solution.py:51
  137.3 3.3 %fusion.6 = f32[16,64,64]{2,0,1:T(8,128)S(1)} fusion(f32[16,64,64]{2,0,1:T(8,128)S(1)} %fusion.7, f32[64,64]{1,0:T(8,128)S(1)} %bitcast.162, f32[64,64]{1,0:T(8,128)S(1)} %bitcast.163, f32[64,64]{1,0:T(8,128)S(1)} %bitcast.161, f32[64,64]{1,0:T(8,128)S(1)} %copy-done.23, f32[64,64]{1,0:T(8,128)S(1)} %copy-done.24, f32[64,64]{1,0:T(8,128)S(1)} %copy-done.25, ...), kind=kOutput, calls=%fused_computation.32 | convolution fusion | flops 11337728 | bytes 1245184 | tf_op jit(solution)/shard_map/rla,lab->rlb/dot_general | solution.py:51
  140.7 3.3 %fusion.5 = f32[16,64,64]{2,0,1:T(8,128)S(1)} fusion(f32[16,64,64]{2,0,1:T(8,128)S(1)} %fusion.6, f32[64,64]{1,0:T(8,128)S(1)} %bitcast.165, f32[64,64]{1,0:T(8,128)S(1)} %bitcast.166, f32[64,64]{1,0:T(8,128)S(1)} %bitcast.164, f32[64,64]{1,0:T(8,128)S(1)} %copy-done.23, f32[64,64]{1,0:T(8,128)S(1)} %copy-done.24, f32[64,64]{1,0:T(8,128)S(1)} %copy-done.25, ...), kind=kOutput, calls=%fused_computation.30 | convolution fusion | flops 11337728 | bytes 1245184 | tf_op jit(solution)/shard_map/rla,lab->rlb/dot_general | solution.py:51
  144.0 3.3 %fusion.4 = f32[16,64,64]{2,0,1:T(8,128)S(1)} fusion(f32[16,64,64]{2,0,1:T(8,128)S(1)} %fusion.5, f32[64,64]{1,0:T(8,128)S(1)} %bitcast.168, f32[64,64]{1,0:T(8,128)S(1)} %bitcast.169, f32[64,64]{1,0:T(8,128)S(1)} %bitcast.167, f32[64,64]{1,0:T(8,128)S(1)} %copy-done.23, f32[64,64]{1,0:T(8,128)S(1)} %copy-done.24, f32[64,64]{1,0:T(8,128)S(1)} %copy-done.25, ...), kind=kOutput, calls=%fused_computation.28 | convolution fusion | flops 11337728 | bytes 1245184 | tf_op jit(solution)/shard_map/rla,lab->rlb/dot_general | solution.py:51
  147.3 3.3 %fusion.3 = f32[16,64,64]{2,0,1:T(8,128)S(1)} fusion(f32[16,64,64]{2,0,1:T(8,128)S(1)} %fusion.4, f32[64,64]{1,0:T(8,128)S(1)} %bitcast.171, f32[64,64]{1,0:T(8,128)S(1)} %bitcast.172, f32[64,64]{1,0:T(8,128)S(1)} %bitcast.170, f32[64,64]{1,0:T(8,128)S(1)} %copy-done.23, f32[64,64]{1,0:T(8,128)S(1)} %copy-done.24, f32[64,64]{1,0:T(8,128)S(1)} %copy-done.25, ...), kind=kOutput, calls=%fused_computation.26 | convolution fusion | flops 11337728 | bytes 1245184 | tf_op jit(solution)/shard_map/rla,lab->rlb/dot_general | solution.py:51
  150.6 3.3 %fusion.2 = f32[16,64,64]{2,0,1:T(8,128)S(1)} fusion(f32[16,64,64]{2,0,1:T(8,128)S(1)} %convolution_bitcast_fusion.8, f32[16,64,64]{2,0,1:T(8,128)S(1)} %fusion.3, f32[64,64]{1,0:T(8,128)S(1)} %bitcast.174, f32[64,64]{1,0:T(8,128)S(1)} %bitcast.175, f32[64,64]{1,0:T(8,128)S(1)} %bitcast.173, f32[64,64]{1,0:T(8,128)S(1)} %copy-done.23, ...), kind=kOutput, calls=%fused_computation.24 | convolution fusion | flops 11403264 | bytes 1769472 | tf_op jit(solution)/shard_map/rla,lab->rlb/dot_general | solution.py:51
  154.1 0.9 reshape.211
  (183 shorter events, 17.8 us)
Async XLA Ops:
  0.0 5.1 %copy-start.17 = (bf16[64,1024]{1,0:T(8,128)(2,1)S(1)}, bf16[64,1024]{1,0:T(8,128)(2,1)}, u32[]{:S(2)}) copy-start(bf16[64,1024]{1,0:T(8,128)(2,1)} %param.22) | copy-start | bytes 393220
  5.1 6.4 %copy-start.2 = (bf16[16,64,64]{2,1,0:T(8,128)(2,1)}, bf16[16,64,64]{2,1,0:T(8,128)(2,1)S(1)}, u32[]{:S(2)}) copy-start(bf16[16,64,64]{2,1,0:T(8,128)(2,1)S(1)} %reshape.198) | copy-start | bytes 393220
  5.3 6.2 %copy-start.15 = (bf16[16,4096]{1,0:T(8,128)(2,1)S(1)}, bf16[16,4096]{1,0:T(8,128)(2,1)}, u32[]{:S(2)}) copy-start(bf16[16,4096]{1,0:T(8,128)(2,1)} %param.15) | copy-start | bytes 393220
  6.4 5.3 %copy-start.16 = (f32[3,4096]{1,0:T(4,128)S(1)}, f32[3,4096]{1,0:T(4,128)}, u32[]{:S(2)}) copy-start(f32[3,4096]{1,0:T(4,128)} %param.16) | copy-start | bytes 147460
  7.6 11.5 %copy-start.26 = (bf16[1,3,1024]{2,1,0:T(4,128)(2,1)S(1)}, bf16[1,3,1024]{2,1,0:T(4,128)(2,1)}, u32[]{:S(2)}) copy-start(bf16[1,3,1024]{2,1,0:T(4,128)(2,1)} %param.25) | copy-start | bytes 18436
  7.6 12.3 %copy-start.22 = (bf16[1,4,4,1024]{3,2,1,0:T(4,128)(2,1)S(1)}, bf16[1,4,4,1024]{3,2,1,0:T(4,128)(2,1)}, u32[]{:S(2)}) copy-start(bf16[1,4,4,1024]{3,2,1,0:T(4,128)(2,1)} %param.26) | copy-start | bytes 98308
  7.6 12.7 %copy-start.34 = (s32[64,8]{0,1:T(8,128)S(1)}, s32[64,8]{0,1:T(8,128)}, u32[]{:S(2)}) copy-start(s32[64,8]{0,1:T(8,128)} %param.18) | copy-start | bytes 6148
  7.6 13.5 %copy-start.36 = (s32[64,6]{0,1:T(8,128)S(1)}, s32[64,6]{0,1:T(8,128)}, u32[]{:S(2)}) copy-start(s32[64,6]{0,1:T(8,128)} %param.17) | copy-start | bytes 4612
  7.8 14.1 %copy-start.43 = (s32[4]{0:T(128)S(1)}, s32[4]{0:T(128)}, u32[]{:S(2)}) copy-start(s32[4]{0:T(128)} %constant.71) | copy-start | bytes 52
  8.0 17.1 %collective-permute-start.2 = (f32[4,16,32]{2,1,0:T(8,128)S(1)}, f32[4,16,32]{2,1,0:T(8,128)S(1)}, u32[]{:S(2)}, u32[]{:S(2)}) collective-permute-start(f32[4,16,32]{2,1,0:T(8,128)S(1)} %convolution_bitcast_fusion.10), channel_id=1, source_target_pairs={{0,1},{1,0},{2,3},{3,2},{4,5},{5,4},{6,7},{7,6},{8,9},{9,8},{10,11... | collective-permute-start | bytes 24584 | tf_op jit(solution)/shard_map/ppermute | solution.py:30
  11.7 23.8 %copy-start.18 = (bf16[64,1024]{1,0:T(8,128)(2,1)S(1)}, bf16[64,1024]{1,0:T(8,128)(2,1)}, u32[]{:S(2)}) copy-start(bf16[64,1024]{1,0:T(8,128)(2,1)} %param.23) | copy-start | bytes 393220
  12.4 73.0 %collective-permute-start.1 = (f32[35840]{0:T(1024)}, f32[35840]{0:T(1024)}, u32[]{:S(2)}, u32[]{:S(2)}) collective-permute-start(f32[35840]{0:T(1024)} %pad_maximum_fusion.3), channel_id=1, source_target_pairs={{1,0},{2,1},{3,2},{4,3},{5,4},{6,5},{7,6},{8,7},{9,8},{10,9},{11,1... | collective-permute-start | bytes 430088 | tf_op jit(solution)/shard_map/ppermute | solution.py:159
  16.3 70.0 %collective-permute-start = (f32[35840]{0:T(1024)}, f32[35840]{0:T(1024)}, u32[]{:S(2)}, u32[]{:S(2)}) collective-permute-start(f32[35840]{0:T(1024)} %pad_maximum_fusion.2), channel_id=1, source_target_pairs={{0,1},{1,2},{2,3},{3,4},{4,5},{5,6},{6,7},{7,8},{8,9},{9,10},{10,1... | collective-permute-start | bytes 430088 | tf_op jit(solution)/shard_map/ppermute | solution.py:158
  25.2 7.4 %collective-permute-start.3 = (f32[5,16,32]{2,1,0:T(8,128)S(1)}, f32[5,16,32]{2,1,0:T(8,128)S(1)}, u32[]{:S(2)}, u32[]{:S(2)}) collective-permute-start(f32[5,16,32]{2,1,0:T(8,128)S(1)} %pad_maximum_fusion.17), channel_id=1, source_target_pairs={{0,2},{1,3},{2,0},{3,1},{4,6},{5,7},{6,4},{7,5},{8,10},{9,11},{10,... | collective-permute-start | bytes 30728 | tf_op jit(solution)/shard_map/ppermute | solution.py:30
  33.3 16.9 %collective-permute-start.4 = (f32[8,16,32]{2,1,0:T(8,128)}, f32[8,16,32]{2,1,0:T(8,128)}, u32[]{:S(2)}, u32[]{:S(2)}) collective-permute-start(f32[8,16,32]{2,1,0:T(8,128)} %fusion.57), channel_id=1, source_target_pairs={{0,4},{1,5},{2,6},{3,7},{4,0},{5,1},{6,2},{7,3},{8,12},{9,13},{10,... | collective-permute-start | bytes 49160 | tf_op jit(solution)/shard_map/ppermute | solution.py:30
  38.9 9.2 %copy-start.21 = (f32[4096]{0:T(1024)S(1)}, f32[4096]{0:T(1024)}, u32[]{:S(2)}) copy-start(f32[4096]{0:T(1024)} %get-tuple-element.7) | copy-start | bytes 49156
  38.9 9.9 %copy-start.20 = (f32[4096]{0:T(1024)S(1)}, f32[4096]{0:T(1024)}, u32[]{:S(2)}) copy-start(f32[4096]{0:T(1024)} %get-tuple-element.8) | copy-start | bytes 49156
  38.9 10.5 %copy-start.19 = (f32[4096]{0:T(1024)S(1)}, f32[4096]{0:T(1024)}, u32[]{:S(2)}) copy-start(f32[4096]{0:T(1024)} %get-tuple-element.6) | copy-start | bytes 49156
  45.8 38.1 %copy-start.4 = (f32[4,4,32,32]{2,3,1,0:T(8,128)S(1)}, f32[4,4,32,32]{2,3,1,0:T(8,128)}, u32[]{:S(2)}) copy-start(f32[4,4,32,32]{2,3,1,0:T(8,128)} %convolution_bitcast_fusion.9) | copy-start | bytes 196612
  52.4 8.6 %collective-permute-start.5 = (f32[9,16,32]{2,1,0:T(8,128)S(1)}, f32[9,16,32]{2,1,0:T(8,128)S(1)}, u32[]{:S(2)}, u32[]{:S(2)}) collective-permute-start(f32[9,16,32]{2,1,0:T(8,128)S(1)} %get-tuple-element.75), channel_id=1, source_target_pairs={{0,8},{1,9},{2,10},{3,11},{4,12},{5,13},{6,14},{7,15},{8,16},{9,17... | collective-permute-start | bytes 55304 | tf_op jit(solution)/shard_map/ppermute | solution.py:35
  55.9 6.3 %collective-permute-start.6 = (f32[9,16,32]{2,1,0:T(8,128)S(1)}, f32[9,16,32]{2,1,0:T(8,128)S(1)}, u32[]{:S(2)}, u32[]{:S(2)}) collective-permute-start(f32[9,16,32]{2,1,0:T(8,128)S(1)} %get-tuple-element.76), channel_id=1, source_target_pairs={{8,0},{9,1},{10,2},{11,3},{12,4},{13,5},{14,6},{15,7},{16,8},{17,9... | collective-permute-start | bytes 55304 | tf_op jit(solution)/shard_map/ppermute | solution.py:35
  62.3 21.0 %collective-permute-start.8 = (f32[3,16,32]{2,1,0:T(8,128)S(1)}, f32[3,16,32]{2,1,0:T(8,128)S(1)}, u32[]{:S(2)}, u32[]{:S(2)}) collective-permute-start(f32[3,16,32]{2,1,0:T(8,128)S(1)} %get-tuple-element.80), channel_id=1, source_target_pairs={{16,0},{17,1},{18,2},{19,3},{20,4},{21,5},{22,6},{23,7},{24,8},{25... | collective-permute-start | bytes 18440 | tf_op jit(solution)/shard_map/ppermute | solution.py:35
  73.9 9.3 %collective-permute-start.7 = (f32[3,16,32]{2,1,0:T(8,128)S(1)}, f32[3,16,32]{2,1,0:T(8,128)S(1)}, u32[]{:S(2)}, u32[]{:S(2)}) collective-permute-start(f32[3,16,32]{2,1,0:T(8,128)S(1)} %get-tuple-element.79), channel_id=1, source_target_pairs={{0,16},{1,17},{2,18},{3,19},{4,20},{5,21},{6,22},{7,23},{8,24},{9,... | collective-permute-start | bytes 18440 | tf_op jit(solution)/shard_map/ppermute | solution.py:35
  91.5 3.7 %copy-start.35 = (pred[64,8]{0,1:T(8,128)(4,1)S(1)}, pred[64,8]{0,1:T(8,128)(4,1)}, u32[]{:S(2)}) copy-start(pred[64,8]{0,1:T(8,128)(4,1)} %get-tuple-element.27) | copy-start | bytes 1540
  102.0 4.6 %copy-start.42 = (pred[64]{0:T(512)(128)(4,1)S(1)}, pred[64]{0:T(512)(128)(4,1)}, u32[]{:S(2)}) copy-start(pred[64]{0:T(512)(128)(4,1)} %get-tuple-element.87) | copy-start | bytes 196
  105.1 5.5 %copy-start.41 = (pred[64]{0:T(512)(128)(4,1)S(1)}, pred[64]{0:T(512)(128)(4,1)}, u32[]{:S(2)}) copy-start(pred[64]{0:T(512)(128)(4,1)} %get-tuple-element.85) | copy-start | bytes 196
  107.9 0.9 copy-start.5
  108.8 5.6 %copy-start.40 = (pred[64]{0:T(512)(128)(4,1)S(1)}, pred[64]{0:T(512)(128)(4,1)}, u32[]{:S(2)}) copy-start(pred[64]{0:T(512)(128)(4,1)} %get-tuple-element.83) | copy-start | bytes 196
  111.8 0.9 copy-start.7
  112.8 6.3 %copy-start.39 = (pred[64]{0:T(512)(128)(4,1)S(1)}, pred[64]{0:T(512)(128)(4,1)}, u32[]{:S(2)}) copy-start(pred[64]{0:T(512)(128)(4,1)} %get-tuple-element.81) | copy-start | bytes 196
  115.7 0.9 copy-start.9
  117.3 6.5 %copy-start.38 = (pred[64]{0:T(512)(128)(4,1)S(1)}, pred[64]{0:T(512)(128)(4,1)}, u32[]{:S(2)}) copy-start(pred[64]{0:T(512)(128)(4,1)} %get-tuple-element.89) | copy-start | bytes 196
  120.3 0.9 copy-start.11
  121.9 6.3 %copy-start.37 = (pred[64]{0:T(512)(128)(4,1)S(1)}, pred[64]{0:T(512)(128)(4,1)}, u32[]{:S(2)}) copy-start(pred[64]{0:T(512)(128)(4,1)} %get-tuple-element.15) | copy-start | bytes 196
  125.0 0.9 copy-start.13
  128.2 1.4 copy-start
  129.7 3.8 %copy-start.1 = (bf16[64,32,64]{2,1,0:T(8,128)(2,1)S(1)}, bf16[64,32,64]{2,1,0:T(8,128)(2,1)}, u32[]{:S(2)}) copy-start(bf16[64,32,64]{2,1,0:T(8,128)(2,1)} %reshape.210) | copy-start | bytes 786436
  129.7 4.3 %copy-start.3 = (bf16[16,64,64]{2,1,0:T(8,128)(2,1)S(1)}, bf16[16,64,64]{2,1,0:T(8,128)(2,1)}, u32[]{:S(2)}) copy-start(bf16[16,64,64]{2,1,0:T(8,128)(2,1)} %copy-done.2) | copy-start | bytes 393220
  129.7 4.3 %copy-start.6 = (f32[19,64,64]{2,0,1:T(8,128)S(1)}, f32[19,64,64]{2,0,1:T(8,128)}, u32[]{:S(2)}) copy-start(f32[19,64,64]{2,0,1:T(8,128)} %copy-done.5) | copy-start | bytes 933892
  129.7 4.3 %copy-start.23 = (f32[64,64]{1,0:T(8,128)S(1)}, f32[64,64]{1,0:T(8,128)}, u32[]{:S(2)}) copy-start(f32[64,64]{1,0:T(8,128)} %sub.282) | copy-start | bytes 49156
  129.7 4.3 %copy-start.24 = (f32[64,64]{1,0:T(8,128)S(1)}, f32[64,64]{1,0:T(8,128)}, u32[]{:S(2)}) copy-start(f32[64,64]{1,0:T(8,128)} %sub.277) | copy-start | bytes 49156
  129.7 4.3 %copy-start.25 = (f32[64,64]{1,0:T(8,128)S(1)}, f32[64,64]{1,0:T(8,128)}, u32[]{:S(2)}) copy-start(f32[64,64]{1,0:T(8,128)} %sub.272) | copy-start | bytes 49156
  134.0 3.3 %copy-start.8 = (f32[19,64,64]{2,0,1:T(8,128)S(1)}, f32[19,64,64]{2,0,1:T(8,128)}, u32[]{:S(2)}) copy-start(f32[19,64,64]{2,0,1:T(8,128)} %copy-done.7) | copy-start | bytes 933892
  137.3 3.3 %copy-start.10 = (f32[19,64,64]{2,0,1:T(8,128)S(1)}, f32[19,64,64]{2,0,1:T(8,128)}, u32[]{:S(2)}) copy-start(f32[19,64,64]{2,0,1:T(8,128)} %copy-done.9) | copy-start | bytes 933892
  137.3 3.3 %copy-start.27 = (f32[1,64,64]{2,0,1:T(1,128)S(1)}, f32[1,64,64]{2,0,1:T(1,128)}, u32[]{:S(2)}) copy-start(f32[1,64,64]{2,0,1:T(1,128)} %get-tuple-element.43) | copy-start | bytes 49156
  140.6 3.3 %copy-start.12 = (f32[19,64,64]{2,0,1:T(8,128)S(1)}, f32[19,64,64]{2,0,1:T(8,128)}, u32[]{:S(2)}) copy-start(f32[19,64,64]{2,0,1:T(8,128)} %copy-done.11) | copy-start | bytes 933892
  140.6 3.3 %copy-start.28 = (f32[1,64,64]{2,0,1:T(1,128)S(1)}, f32[1,64,64]{2,0,1:T(1,128)}, u32[]{:S(2)}) copy-start(f32[1,64,64]{2,0,1:T(1,128)} %get-tuple-element.38) | copy-start | bytes 49156
  140.6 3.3 %copy-start.29 = (f32[1,64,64]{2,0,1:T(1,128)S(1)}, f32[1,64,64]{2,0,1:T(1,128)}, u32[]{:S(2)}) copy-start(f32[1,64,64]{2,0,1:T(1,128)} %get-tuple-element.39) | copy-start | bytes 49156
  140.6 3.3 %copy-start.30 = (f32[1,64,64]{2,0,1:T(1,128)S(1)}, f32[1,64,64]{2,0,1:T(1,128)}, u32[]{:S(2)}) copy-start(f32[1,64,64]{2,0,1:T(1,128)} %get-tuple-element.40) | copy-start | bytes 49156
  144.0 3.3 %copy-start.14 = (f32[19,64,64]{2,0,1:T(8,128)S(1)}, f32[19,64,64]{2,0,1:T(8,128)}, u32[]{:S(2)}) copy-start(f32[19,64,64]{2,0,1:T(8,128)} %copy-done.13) | copy-start | bytes 933892
  144.0 3.3 %copy-start.31 = (f32[1,64,64]{2,0,1:T(1,128)S(1)}, f32[1,64,64]{2,0,1:T(1,128)}, u32[]{:S(2)}) copy-start(f32[1,64,64]{2,0,1:T(1,128)} %get-tuple-element.35) | copy-start | bytes 49156
  144.0 3.3 %copy-start.32 = (f32[1,64,64]{2,0,1:T(1,128)S(1)}, f32[1,64,64]{2,0,1:T(1,128)}, u32[]{:S(2)}) copy-start(f32[1,64,64]{2,0,1:T(1,128)} %get-tuple-element.36) | copy-start | bytes 49156
  144.0 3.3 %copy-start.33 = (f32[1,64,64]{2,0,1:T(1,128)S(1)}, f32[1,64,64]{2,0,1:T(1,128)}, u32[]{:S(2)}) copy-start(f32[1,64,64]{2,0,1:T(1,128)} %get-tuple-element.37) | copy-start | bytes 49156

commit v3 on v2

--- a/solution.py
+++ b/solution.py
@@ -35,32 +35,27 @@
     return lax.ppermute(value, AXES, [(s, s - step) for s in range(n) if 0 <= s - step < n])
 
 
-def matern_term(extended, target_points, slot_offsets):
+def near_field(extended, target_points, near_offsets, leaf_values):
     leaf_count = target_points.shape[1]
     column_count = extended.shape[0] - 3
-    source_leaf = jnp.arange(leaf_count, dtype=jnp.int32) + NEAR_REACH + slot_offsets
-    chosen = jnp.take(extended, source_leaf, axis=1)
-    squared = jnp.zeros((leaf_count, CLUSTER, CLUSTER), jnp.float32)
+    by_leaf = jnp.transpose(extended, (1, 0, 2))
+    source_leaf = jnp.arange(leaf_count, dtype=jnp.int32)[:, None] + NEAR_REACH + near_offsets
+    chosen = jnp.take(by_leaf, source_leaf, axis=0, mode="clip")
+    squared = jnp.zeros((leaf_count, NEAR_BLOCKS, CLUSTER, CLUSTER), jnp.float32)
     for component in range(3):
         separation = (
-            chosen[column_count + component][:, :, None] - target_points[component][:, None, :]
+            chosen[:, :, column_count + component, :, None]
+            - target_points[component][:, None, None, :]
         )
         squared = squared + separation * separation
     kernel = (amplitude * jnp.exp(-jnp.sqrt(squared) / length_scale)).astype(jnp.bfloat16)
-    values = chosen[:column_count].astype(jnp.bfloat16)
-    return jnp.einsum("rla,lab->rlb", values, kernel, preferred_element_type=jnp.float32)
+    values = chosen[:, :, :column_count].astype(jnp.bfloat16)
+    near = jnp.einsum("lnra,lnab->rlb", values, kernel, preferred_element_type=jnp.float32)
+    return nugget * leaf_values.astype(jnp.float32) + near
 
 
 def mm(a, b):
     return jnp.matmul(a, b, precision=highest, preferred_element_type=jnp.float32)
-
-
-def split3(x):
-    hi = lax.reduce_precision(x, exponent_bits=8, mantissa_bits=7)
-    rest = x - hi
-    mid = lax.reduce_precision(rest, exponent_bits=8, mantissa_bits=7)
-    lo = rest - mid
-    return jnp.stack([hi, mid, lo]).astype(jnp.bfloat16)
 
 
 def ordered(bit, own, other):
@@ -175,16 +170,15 @@
     )
 
     target_points = points.reshape(3, leaf_count, CLUSTER)
-    near_sum = nugget * leaf_values.astype(jnp.float32)
-    for near_slot in range(NEAR_BLOCKS):
-        near_sum = near_sum + matern_term(extended, target_points, near_offsets[:, near_slot])
+    near_sum = near_field(extended, target_points, near_offsets, leaf_values)
 
     far_index = jnp.arange(leaf_count, dtype=jnp.int32)[:, None] + FAR_REACH + far_offsets
     partner_blocks = jnp.take(rimmed, far_index, axis=0).reshape(leaf_count, FAR_BLOCKS, RHS, RANK)
     leaf_far = jnp.einsum(
-        "slfrk,lfkq->lrq",
-        split3(partner_blocks),
+        "lfrk,lfkq->lrq",
+        partner_blocks,
         leaf_coupling.reshape(leaf_count, FAR_BLOCKS, RANK, RANK),
+        precision=highest,
         preferred_element_type=jnp.float32,
     )
     root_coefficients = jnp.einsum(

time: 156 us -> 134 us (0.86)
  the two profiles are of different devices: /device:TPU:392 before, /device:TPU:394 now
where the time goes in v3:
time: 134 us
  local copies, waits for them, and re-layouts  42.1 us (31%)
  starting transfers between devices  37.3 us (28%)
  matrix products  35.8 us (27%)
  waiting for transfers between devices  9.87 us (7%)
  other arithmetic  7.4 us (6%)
    dot_general x1, matrix products, near_field(): jnp.einsum('lnra,lnab->rlb', values, kernel, preferred_element_type=jnp.f...  22.9 us
    ppermute x4, starting transfers between devices, receive_from(): lax.ppermute(value, AXES, [(s, s - step) for s in range(n) if 0 <= s - st...  22.2 us
    ppermute x3, starting transfers between devices, swap_with(): return lax.ppermute(value, AXES, [(i, i ^ mask) for i in range(n)])  9.31 us
    dot_general x1, matrix products, local(): jnp.einsum('lfrk,lfkq->lrq', partner_blocks, leaf_coupling.reshape(leaf_c...  8.41 us
    ppermute x4, waiting for transfers between devices, receive_from(): lax.ppermute(value, AXES, [(s, s - step) for s in range(n) if 0 <= s - st...  7.96 us
    reshape x1, local copies, waits for them, and re-layouts, local(): leaf_coupling.reshape(leaf_count, FAR_BLOCKS, RANK, RANK)  6.9 us
    gather x2, local copies, waits for them, and re-layouts, local(): jnp.take(rimmed, far_index, axis=0)  4.25 us
    sub x6, local copies, waits for them, and re-layouts, near_field(): chosen[:, :, column_count + component, :, None]  3.46 us
  transfers between devices with their start and end apart: 9, of which 4 were waited for; matrix products, arithmetic and copies ran while one was open for 23% of the time, Pallas kernels for 0%

profile of v3, /device:TPU:394, one launch (start us, length us, event | category | flops | bytes accessed | tf_op | source)
XLA Modules:
  0.0 133.5 jit_solution(2741534470881586526)
XLA Ops:
  0.0 1.2 reshape.153
  1.3 1.0 convert_element_type.28
  2.3 1.2 copy.18
  3.6 1.1 copy.20
  4.7 0.4 fusion.13
  5.3 0.7 pad_maximum_fusion.3
  6.0 2.4 %collective-permute-start.1 = (f32[35840]{0:T(1024)}, f32[35840]{0:T(1024)}, u32[]{:S(2)}, u32[]{:S(2)}) collective-permute-start(f32[35840]{0:T(1024)} %pad_maximum_fusion.3), channel_id=1, source_target_pairs={{1,0},{2,1},{3,2},{4,3},{5,4},{6,5},{7,6},{8,7},{9,8},{10,9},{11,1... | collective-permute-start | bytes 430088 | tf_op jit(solution)/shard_map/ppermute | solution.py:154
  8.5 0.7 pad_maximum_fusion.2
  9.2 3.4 %collective-permute-start = (f32[35840]{0:T(1024)}, f32[35840]{0:T(1024)}, u32[]{:S(2)}, u32[]{:S(2)}) collective-permute-start(f32[35840]{0:T(1024)} %pad_maximum_fusion.2), channel_id=1, source_target_pairs={{0,1},{1,2},{2,3},{3,4},{4,5},{5,6},{6,7},{7,8},{8,9},{9,10},{10,1... | collective-permute-start | bytes 430088 | tf_op jit(solution)/shard_map/ppermute | solution.py:153
  12.9 0.8 copy.41
  13.7 0.8 fusion.50
  15.0 0.2 convolution_bitcast_fusion.2
  15.2 2.5 %collective-permute-start.2 = (f32[4,16,32]{2,1,0:T(8,128)S(1)}, f32[4,16,32]{2,1,0:T(8,128)S(1)}, u32[]{:S(2)}, u32[]{:S(2)}) collective-permute-start(f32[4,16,32]{2,1,0:T(8,128)S(1)} %convolution_bitcast_fusion.2), channel_id=1, source_target_pairs={{0,1},{1,0},{2,3},{3,2},{4,5},{5,4},{6,7},{7,6},{8,9},{9,8},{10,11... | collective-permute-start | bytes 24584 | tf_op jit(solution)/shard_map/ppermute | solution.py:30
  17.9 0.6 compare_and_fusion
  19.7 1.5 %fusion.25 = f32[4,32,4,32]{3,1,2,0:T(8,128)} fusion(bf16[4,4,32,32]{3,2,1,0:T(8,128)(2,1)S(1)} %reshape.163, f32[1,32,32]{2,1,0:T(8,128)S(1)} %fusion.35, f32[1,32,32]{2,1,0:T(8,128)S(1)} %convolution_bitcast_fusion.3, f32[1,32,32]{2,1,0:T(8,128)S(1)} %bitcast.101, f32[1,32,32]{2,1,0:T(8,128)S(1)} %reshape.168), kind=kOutput, calls=%fused_computation.57 | convolution fusion | flops 6303744 | bytes 114688 | tf_op jit(solution)/shard_map/sqkp,spm->sqkm/dot_general | solution.py:78
  21.2 4.9 %collective-permute-start.3 = (f32[5,16,32]{2,1,0:T(8,128)S(1)}, f32[5,16,32]{2,1,0:T(8,128)S(1)}, u32[]{:S(2)}, u32[]{:S(2)}) collective-permute-start(f32[5,16,32]{2,1,0:T(8,128)S(1)} %pad_maximum_fusion.17), channel_id=1, source_target_pairs={{0,2},{1,3},{2,0},{3,1},{4,6},{5,7},{6,4},{7,5},{8,10},{9,11},{10,... | collective-permute-start | bytes 30728 | tf_op jit(solution)/shard_map/ppermute | solution.py:30
  26.1 0.6 pad_clamp_fusion.1
  26.7 1.9 %collective-permute-done.3 = f32[5,16,32]{2,1,0:T(8,128)S(1)} collective-permute-done((f32[5,16,32]{2,1,0:T(8,128)S(1)}, f32[5,16,32]{2,1,0:T(8,128)S(1)}, u32[]{:S(2)}, u32[]{:S(2)}) %collective-permute-start.3) | collective-permute-done | bytes 10272 | tf_op jit(solution)/shard_map/ppermute | solution.py:30
  28.7 0.6 fusion.18
  29.3 1.9 %collective-permute-start.4 = (f32[8,16,32]{2,1,0:T(8,128)}, f32[8,16,32]{2,1,0:T(8,128)}, u32[]{:S(2)}, u32[]{:S(2)}) collective-permute-start(f32[8,16,32]{2,1,0:T(8,128)} %fusion.18), channel_id=1, source_target_pairs={{0,4},{1,5},{2,6},{3,7},{4,0},{5,1},{6,2},{7,3},{8,12},{9,13},{10,... | collective-permute-start | bytes 49160 | tf_op jit(solution)/shard_map/ppermute | solution.py:30
  31.3 0.6 pad_clamp_fusion
  31.9 0.9 copy.30
  32.8 0.7 sub.63
  33.5 0.7 sub.58
  34.1 0.7 sub.53
  34.8 1.4 %copy.33 = bf16[64,8,1024]{0,2,1:T(8,128)(2,1)S(1)} copy(bf16[64,8,1024]{2,1,0:T(8,128)(2,1)S(1)} %copy-done) | data formatting | bytes 2097152 | tf_op args[6]
  36.3 6.9 %copy.39 = bf16[64,8,32,32]{3,2,1,0:T(8,128)(2,1)} copy(bf16[64,8,32,32]{0,3,2,1:T(8,128)(2,1)S(1)} %bitcast.88) | data formatting | bytes 2097152 | tf_op jit(solution)/shard_map/reshape | solution.py:180
  43.3 0.7 copy.29
  44.0 0.2 copy.68
  44.4 0.8 copy.48
  45.2 1.5 %reshape.165 = bf16[64,32,64]{2,1,0:T(8,128)(2,1)S(1)} reshape(bf16[64,2048]{1,0:T(8,128)(2,1)} %param.18) | data formatting | bytes 524288 | tf_op jit(solution)/shard_map/reshape | solution.py:203
  46.7 0.7 fusion.45
  47.4 0.7 slice.336
  48.1 0.8 maximum_select_fusion.1
  48.9 0.8 slice.334
  49.7 0.8 fusion.16
  50.6 3.5 %collective-permute-start.5 = (f32[9,16,32]{2,1,0:T(8,128)S(1)}, f32[9,16,32]{2,1,0:T(8,128)S(1)}, u32[]{:S(2)}, u32[]{:S(2)}) collective-permute-start(f32[9,16,32]{2,1,0:T(8,128)S(1)} %get-tuple-element.44), channel_id=1, source_target_pairs={{0,8},{1,9},{2,10},{3,11},{4,12},{5,13},{6,14},{7,15},{8,16},{9,17... | collective-permute-start | bytes 55304 | tf_op jit(solution)/shard_map/ppermute | solution.py:35
  54.1 5.0 %collective-permute-start.6 = (f32[9,16,32]{2,1,0:T(8,128)S(1)}, f32[9,16,32]{2,1,0:T(8,128)S(1)}, u32[]{:S(2)}, u32[]{:S(2)}) collective-permute-start(f32[9,16,32]{2,1,0:T(8,128)S(1)} %get-tuple-element.45), channel_id=1, source_target_pairs={{8,0},{9,1},{10,2},{11,3},{12,4},{13,5},{14,6},{15,7},{16,8},{17,9... | collective-permute-start | bytes 55304 | tf_op jit(solution)/shard_map/ppermute | solution.py:35
  59.1 1.0 collective-permute-done.5
  60.1 1.2 collective-permute-done.6
  61.3 11.6 %collective-permute-start.8 = (f32[3,16,32]{2,1,0:T(8,128)S(1)}, f32[3,16,32]{2,1,0:T(8,128)S(1)}, u32[]{:S(2)}, u32[]{:S(2)}) collective-permute-start(f32[3,16,32]{2,1,0:T(8,128)S(1)} %get-tuple-element.49), channel_id=1, source_target_pairs={{16,0},{17,1},{18,2},{19,3},{20,4},{21,5},{22,6},{23,7},{24,8},{25... | collective-permute-start | bytes 18440 | tf_op jit(solution)/shard_map/ppermute | solution.py:35
  72.9 2.1 %collective-permute-start.7 = (f32[3,16,32]{2,1,0:T(8,128)S(1)}, f32[3,16,32]{2,1,0:T(8,128)S(1)}, u32[]{:S(2)}, u32[]{:S(2)}) collective-permute-start(f32[3,16,32]{2,1,0:T(8,128)S(1)} %get-tuple-element.48), channel_id=1, source_target_pairs={{0,16},{1,17},{2,18},{3,19},{4,20},{5,21},{6,22},{7,23},{8,24},{9,... | collective-permute-start | bytes 18440 | tf_op jit(solution)/shard_map/ppermute | solution.py:35
  75.0 0.7 gather_fusion.3
  75.7 0.7 gather_fusion.2
  76.4 5.8 %collective-permute-done.7 = f32[3,16,32]{2,1,0:T(8,128)S(1)} collective-permute-done((f32[3,16,32]{2,1,0:T(8,128)S(1)}, f32[3,16,32]{2,1,0:T(8,128)S(1)}, u32[]{:S(2)}, u32[]{:S(2)}) %collective-permute-start.7) | collective-permute-done | bytes 6176 | tf_op jit(solution)/shard_map/ppermute | solution.py:35
  82.3 0.7 gather_fusion.4
  83.0 0.3 convolution_bitcast_fusion.5
  83.3 0.9 slice.315
  84.2 0.9 slice.313
  85.2 0.4 reshape.159
  85.6 0.6 copy.64
  86.1 3.3 %gather_fusion = f32[384,19,64]{2,1,0:T(8,128)} fusion(f32[96,19,64]{2,1,0:T(8,128)S(1)} %bitcast.87, s32[1024]{0:T(1024)S(1)} %get-tuple-element.58), kind=kCustom, calls=%fused_computation | custom fusion | bytes 3737088 | tf_op jit(solution)/shard_map/jit(_take)/gather | solution.py:43
  89.4 3.2 %fusion.40 = (f32[64,6,1,64]{3,2,1,0:T(1,128)S(1)}, f32[64,6,1,64]{3,2,1,0:T(1,128)S(1)}, f32[64,6,1,64]{3,2,1,0:T(1,128)S(1)}) fusion(f32[64,6,19,64]{3,2,1,0:T(8,128)} %bitcast.89), kind=kLoop, calls=%fused_computation.116 | loop fusion | bytes 589824 | tf_op jit(solution)/shard_map/slice | solution.py:47
  92.6 0.7 copy.66
  93.3 0.7 copy.67
  94.0 0.8 slice.321
  94.9 0.8 slice.320
  95.8 1.6 %gather_fusion.1 = f32[512,512]{1,0:T(8,128)S(1)} fusion(f32[128,512]{1,0:T(8,128)S(1)} %pad_maximum_fusion.1, s32[1024]{0:T(1024)S(1)} %get-tuple-element.57), kind=kCustom, calls=%fused_computation.1 | custom fusion | bytes 2099200 | tf_op jit(solution)/shard_map/jit(_take)/gather | solution.py:176
  97.4 2.6 %gather.24 = f32[64,8,16,32]{3,2,1,0:T(8,128)} reshape(f32[512,512]{1,0:T(8,128)S(1)} %gather_fusion.1) | data formatting | bytes 2097152 | tf_op jit(solution)/shard_map/jit(_take)/gather | solution.py:176
  100.1 8.4 %fusion.5 = f32[64,16,32]{2,1,0:T(8,128)S(1)} fusion(bf16[64,8,32,32]{3,2,1,0:T(8,128)(2,1)} %copy.39, f32[64,8,16,32]{3,2,1,0:T(8,128)} %gather.24, pred[64,8]{1,0:T(8,128)(4,1)S(1)} %copy-done.14), kind=kOutput, calls=%fused_computation.12 | convolution fusion | flops 100925440 | bytes 2228736 | tf_op jit(solution)/shard_map/lfrk,lfkq->lrq/dot_general | solution.py:177
  108.5 0.4 fusion.8
  109.0 22.9 %fusion.11 = f32[16,64,64]{2,0,1:T(8,128)S(1)} fusion(f32[64,64]{1,0:T(8,128)S(1)} %copy-done.16, f32[64,6,64]{2,1,0:T(8,128)S(1)} %bitcast.98, f32[64,64]{1,0:T(8,128)S(1)} %copy-done.17, f32[64,6,64]{2,1,0:T(8,128)S(1)} %bitcast.99, f32[64,64]{1,0:T(8,128)S(1)} %copy-done.18, f32[64,6,64]{2,1,0:T(8,128)S(1)} %bitcast.100, ...), kind=kOutput, calls=%fused_computation.18 | convolution fusion | flops 67829760 | bytes 2981888 | tf_op jit(solution)/shard_map/lnra,lnab->rlb/dot_general | solution.py:53
  131.9 0.5 fusion.9
  132.6 0.9 reshape.166
  (130 shorter events, 3.3 us)
Async XLA Ops:
  0.0 5.2 %copy-start.5 = (f32[3,4096]{1,0:T(4,128)S(1)}, f32[3,4096]{1,0:T(4,128)}, u32[]{:S(2)}) copy-start(f32[3,4096]{1,0:T(4,128)} %param.14) | copy-start | bytes 147460
  0.0 12.6 %copy-start.19 = (bf16[1,3,1024]{2,1,0:T(4,128)(2,1)S(1)}, bf16[1,3,1024]{2,1,0:T(4,128)(2,1)}, u32[]{:S(2)}) copy-start(bf16[1,3,1024]{2,1,0:T(4,128)(2,1)} %param.22) | copy-start | bytes 18436
  0.0 12.7 %copy-start.20 = (bf16[1,3,1024]{2,1,0:T(4,128)(2,1)S(1)}, bf16[1,3,1024]{2,1,0:T(4,128)(2,1)}, u32[]{:S(2)}) copy-start(bf16[1,3,1024]{2,1,0:T(4,128)(2,1)} %param.23) | copy-start | bytes 18436
  0.0 12.7 %copy-start.11 = (bf16[64,1024]{1,0:T(8,128)(2,1)S(1)}, bf16[64,1024]{1,0:T(8,128)(2,1)}, u32[]{:S(2)}) copy-start(bf16[64,1024]{1,0:T(8,128)(2,1)} %param.20) | copy-start | bytes 393220
  1.3 17.5 %copy-start.1 = (bf16[16,64,64]{2,1,0:T(8,128)(2,1)}, bf16[16,64,64]{2,1,0:T(8,128)(2,1)S(1)}, u32[]{:S(2)}) copy-start(bf16[16,64,64]{2,1,0:T(8,128)(2,1)S(1)} %reshape.153) | copy-start | bytes 393220
  1.3 16.7 %copy-start.22 = (s32[64,8]{0,1:T(8,128)S(1)}, s32[64,8]{0,1:T(8,128)}, u32[]{:S(2)}) copy-start(s32[64,8]{0,1:T(8,128)} %param.16) | copy-start | bytes 6148
  1.3 17.4 %copy-start.23 = (s32[64,6]{0,1:T(8,128)S(1)}, s32[64,6]{0,1:T(8,128)}, u32[]{:S(2)}) copy-start(s32[64,6]{0,1:T(8,128)} %param.15) | copy-start | bytes 4612
  1.3 17.7 %copy-start.15 = (bf16[1,4,4,1024]{3,2,1,0:T(4,128)(2,1)S(1)}, bf16[1,4,4,1024]{3,2,1,0:T(4,128)(2,1)}, u32[]{:S(2)}) copy-start(bf16[1,4,4,1024]{3,2,1,0:T(4,128)(2,1)} %param.24) | copy-start | bytes 98308
  3.6 17.6 %copy-start.24 = (s32[4]{0:T(128)S(1)}, s32[4]{0:T(128)}, u32[]{:S(2)}) copy-start(s32[4]{0:T(128)} %constant.59) | copy-start | bytes 52
  4.7 30.2 %copy-start = (bf16[64,8,1024]{2,1,0:T(8,128)(2,1)S(1)}, bf16[64,8,1024]{2,1,0:T(8,128)(2,1)}, u32[]{:S(2)}) copy-start(bf16[64,8,1024]{2,1,0:T(8,128)(2,1)} %param.19) | copy-start | bytes 3145732
  6.0 77.3 %collective-permute-start.1 = (f32[35840]{0:T(1024)}, f32[35840]{0:T(1024)}, u32[]{:S(2)}, u32[]{:S(2)}) collective-permute-start(f32[35840]{0:T(1024)} %pad_maximum_fusion.3), channel_id=1, source_target_pairs={{1,0},{2,1},{3,2},{4,3},{5,4},{6,5},{7,6},{8,7},{9,8},{10,9},{11,1... | collective-permute-start | bytes 430088 | tf_op jit(solution)/shard_map/ppermute | solution.py:154
  9.2 75.0 %collective-permute-start = (f32[35840]{0:T(1024)}, f32[35840]{0:T(1024)}, u32[]{:S(2)}, u32[]{:S(2)}) collective-permute-start(f32[35840]{0:T(1024)} %pad_maximum_fusion.2), channel_id=1, source_target_pairs={{0,1},{1,2},{2,3},{3,4},{4,5},{5,6},{6,7},{7,8},{8,9},{9,10},{10,1... | collective-permute-start | bytes 430088 | tf_op jit(solution)/shard_map/ppermute | solution.py:153
  15.2 6.0 %collective-permute-start.2 = (f32[4,16,32]{2,1,0:T(8,128)S(1)}, f32[4,16,32]{2,1,0:T(8,128)S(1)}, u32[]{:S(2)}, u32[]{:S(2)}) collective-permute-start(f32[4,16,32]{2,1,0:T(8,128)S(1)} %convolution_bitcast_fusion.2), channel_id=1, source_target_pairs={{0,1},{1,0},{2,3},{3,2},{4,5},{5,4},{6,7},{7,6},{8,9},{9,8},{10,11... | collective-permute-start | bytes 24584 | tf_op jit(solution)/shard_map/ppermute | solution.py:30
  21.2 7.4 %collective-permute-start.3 = (f32[5,16,32]{2,1,0:T(8,128)S(1)}, f32[5,16,32]{2,1,0:T(8,128)S(1)}, u32[]{:S(2)}, u32[]{:S(2)}) collective-permute-start(f32[5,16,32]{2,1,0:T(8,128)S(1)} %pad_maximum_fusion.17), channel_id=1, source_target_pairs={{0,2},{1,3},{2,0},{3,1},{4,6},{5,7},{6,4},{7,5},{8,10},{9,11},{10,... | collective-permute-start | bytes 30728 | tf_op jit(solution)/shard_map/ppermute | solution.py:30
  28.7 14.5 %copy-start.7 = (f32[4,16,32]{2,1,0:T(8,128)}, f32[4,16,32]{2,1,0:T(8,128)S(1)}, u32[]{:S(2)}) copy-start(f32[4,16,32]{2,1,0:T(8,128)S(1)} %maximum_select_fusion) | copy-start | bytes 24580
  28.7 14.5 %copy-start.13 = (f32[1,16,32]{2,1,0:T(8,128)}, f32[1,16,32]{2,1,0:T(8,128)S(1)}, u32[]{:S(2)}) copy-start(f32[1,16,32]{2,1,0:T(8,128)S(1)} %get-tuple-element.35) | copy-start | bytes 6148
  28.7 14.5 %copy-start.10 = (f32[2,16,32]{2,1,0:T(8,128)}, f32[2,16,32]{2,1,0:T(8,128)S(1)}, u32[]{:S(2)}) copy-start(f32[2,16,32]{2,1,0:T(8,128)S(1)} %maximum_select_fusion.3) | copy-start | bytes 12292
  29.3 17.3 %collective-permute-start.4 = (f32[8,16,32]{2,1,0:T(8,128)}, f32[8,16,32]{2,1,0:T(8,128)}, u32[]{:S(2)}, u32[]{:S(2)}) collective-permute-start(f32[8,16,32]{2,1,0:T(8,128)} %fusion.18), channel_id=1, source_target_pairs={{0,4},{1,5},{2,6},{3,7},{4,0},{5,1},{6,2},{7,3},{8,12},{9,13},{10,... | collective-permute-start | bytes 49160 | tf_op jit(solution)/shard_map/ppermute | solution.py:30
  36.2 7.0 %copy-start.3 = (f32[64,16,32]{0,2,1:T(8,128)S(1)}, f32[64,16,32]{0,2,1:T(8,128)}, u32[]{:S(2)}) copy-start(f32[64,16,32]{0,2,1:T(8,128)} %copy.30) | copy-start | bytes 393220
  36.2 7.1 %copy-start.21 = (pred[64,8]{0,1:T(8,128)(4,1)S(1)}, pred[64,8]{0,1:T(8,128)(4,1)}, u32[]{:S(2)}) copy-start(pred[64,8]{0,1:T(8,128)(4,1)} %get-tuple-element.14) | copy-start | bytes 1540
  36.2 7.8 %copy-start.4 = (f32[4,32,4,32]{3,1,2,0:T(8,128)S(1)}, f32[4,32,4,32]{3,1,2,0:T(8,128)}, u32[]{:S(2)}) copy-start(f32[4,32,4,32]{3,1,2,0:T(8,128)} %fusion.25) | copy-start | bytes 196612
  36.3 8.0 %copy-start.12 = (bf16[64,1024]{1,0:T(8,128)(2,1)S(1)}, bf16[64,1024]{1,0:T(8,128)(2,1)}, u32[]{:S(2)}) copy-start(bf16[64,1024]{1,0:T(8,128)(2,1)} %param.21) | copy-start | bytes 393220
  43.2 42.0 %copy-start.6 = (f32[3,4096]{1,0:T(4,128)S(1)}, f32[3,4096]{1,0:T(4,128)}, u32[]{:S(2)}) copy-start(f32[3,4096]{1,0:T(4,128)} %param.14) | copy-start | bytes 147460
  50.6 9.5 %collective-permute-start.5 = (f32[9,16,32]{2,1,0:T(8,128)S(1)}, f32[9,16,32]{2,1,0:T(8,128)S(1)}, u32[]{:S(2)}, u32[]{:S(2)}) collective-permute-start(f32[9,16,32]{2,1,0:T(8,128)S(1)} %get-tuple-element.44), channel_id=1, source_target_pairs={{0,8},{1,9},{2,10},{3,11},{4,12},{5,13},{6,14},{7,15},{8,16},{9,17... | collective-permute-start | bytes 55304 | tf_op jit(solution)/shard_map/ppermute | solution.py:35
  54.1 7.2 %collective-permute-start.6 = (f32[9,16,32]{2,1,0:T(8,128)S(1)}, f32[9,16,32]{2,1,0:T(8,128)S(1)}, u32[]{:S(2)}, u32[]{:S(2)}) collective-permute-start(f32[9,16,32]{2,1,0:T(8,128)S(1)} %get-tuple-element.45), channel_id=1, source_target_pairs={{8,0},{9,1},{10,2},{11,3},{12,4},{13,5},{14,6},{15,7},{16,8},{17,9... | collective-permute-start | bytes 55304 | tf_op jit(solution)/shard_map/ppermute | solution.py:35
  61.3 21.0 %collective-permute-start.8 = (f32[3,16,32]{2,1,0:T(8,128)S(1)}, f32[3,16,32]{2,1,0:T(8,128)S(1)}, u32[]{:S(2)}, u32[]{:S(2)}) collective-permute-start(f32[3,16,32]{2,1,0:T(8,128)S(1)} %get-tuple-element.49), channel_id=1, source_target_pairs={{16,0},{17,1},{18,2},{19,3},{20,4},{21,5},{22,6},{23,7},{24,8},{25... | collective-permute-start | bytes 18440 | tf_op jit(solution)/shard_map/ppermute | solution.py:35
  72.9 9.3 %collective-permute-start.7 = (f32[3,16,32]{2,1,0:T(8,128)S(1)}, f32[3,16,32]{2,1,0:T(8,128)S(1)}, u32[]{:S(2)}, u32[]{:S(2)}) collective-permute-start(f32[3,16,32]{2,1,0:T(8,128)S(1)} %get-tuple-element.48), channel_id=1, source_target_pairs={{0,16},{1,17},{2,18},{3,19},{4,20},{5,21},{6,22},{7,23},{8,24},{9,... | collective-permute-start | bytes 18440 | tf_op jit(solution)/shard_map/ppermute | solution.py:35
  97.4 2.6 %copy-start.14 = (pred[64,8]{1,0:T(8,128)(4,1)S(1)}, pred[64,8]{1,0:T(8,128)(4,1)}, u32[]{:S(2)}) copy-start(pred[64,8]{1,0:T(8,128)(4,1)} %copy.29) | copy-start | bytes 1540
  97.4 11.5 %slice-start = ((s8[4718592]{0:T(1024)(128)(4,1)}), s8[524288]{0:T(1024)(128)(4,1)S(1)}, s32[]{:S(2)}) async-start(s8[4718592]{0:T(1024)(128)(4,1)} %bitcast.90), calls=%async_computation | async-start | bytes 1048576
  100.1 8.9 %slice-start.1 = ((s8[4718592]{0:T(1024)(128)(4,1)}), s8[4194304]{0:T(1024)(128)(4,1)S(1)}, s32[]{:S(2)}) async-start(s8[4718592]{0:T(1024)(128)(4,1)} %bitcast.90), calls=%async_computation.1 | async-start | bytes 8388608
  100.1 8.9 %copy-start.2 = (bf16[16,64,64]{2,1,0:T(8,128)(2,1)S(1)}, bf16[16,64,64]{2,1,0:T(8,128)(2,1)}, u32[]{:S(2)}) copy-start(bf16[16,64,64]{2,1,0:T(8,128)(2,1)} %copy-done.1) | copy-start | bytes 393220
  100.1 8.9 %copy-start.8 = (f32[64,6,1,64]{3,1,0,2:T(8,128)S(1)}, f32[64,6,1,64]{3,1,0,2:T(8,128)}, u32[]{:S(2)}) copy-start(f32[64,6,1,64]{3,1,0,2:T(8,128)} %copy.66) | copy-start | bytes 294916
  100.1 8.9 %copy-start.9 = (f32[64,6,1,64]{3,1,0,2:T(8,128)S(1)}, f32[64,6,1,64]{3,1,0,2:T(8,128)}, u32[]{:S(2)}) copy-start(f32[64,6,1,64]{3,1,0,2:T(8,128)} %copy.67) | copy-start | bytes 294916
  100.1 8.9 %copy-start.16 = (f32[64,64]{1,0:T(8,128)S(1)}, f32[64,64]{1,0:T(8,128)}, u32[]{:S(2)}) copy-start(f32[64,64]{1,0:T(8,128)} %sub.63) | copy-start | bytes 49156
  100.1 8.9 %copy-start.17 = (f32[64,64]{1,0:T(8,128)S(1)}, f32[64,64]{1,0:T(8,128)}, u32[]{:S(2)}) copy-start(f32[64,64]{1,0:T(8,128)} %sub.58) | copy-start | bytes 49156
  100.1 8.9 %copy-start.18 = (f32[64,64]{1,0:T(8,128)S(1)}, f32[64,64]{1,0:T(8,128)}, u32[]{:S(2)}) copy-start(f32[64,64]{1,0:T(8,128)} %sub.53) | copy-start | bytes 49156

commit v4 on v3

--- a/solution.py
+++ b/solution.py
@@ -41,16 +41,19 @@
     by_leaf = jnp.transpose(extended, (1, 0, 2))
     source_leaf = jnp.arange(leaf_count, dtype=jnp.int32)[:, None] + NEAR_REACH + near_offsets
     chosen = jnp.take(by_leaf, source_leaf, axis=0, mode="clip")
-    squared = jnp.zeros((leaf_count, NEAR_BLOCKS, CLUSTER, CLUSTER), jnp.float32)
+    chosen = jnp.transpose(chosen, (0, 2, 1, 3)).reshape(
+        leaf_count, column_count + 3, NEAR_BLOCKS * CLUSTER
+    )
+    squared = jnp.zeros((leaf_count, CLUSTER, NEAR_BLOCKS * CLUSTER), jnp.float32)
     for component in range(3):
         separation = (
-            chosen[:, :, column_count + component, :, None]
-            - target_points[component][:, None, None, :]
+            chosen[:, column_count + component][:, None, :]
+            - target_points[component][:, :, None]
         )
         squared = squared + separation * separation
     kernel = (amplitude * jnp.exp(-jnp.sqrt(squared) / length_scale)).astype(jnp.bfloat16)
-    values = chosen[:, :, :column_count].astype(jnp.bfloat16)
-    near = jnp.einsum("lnra,lnab->rlb", values, kernel, preferred_element_type=jnp.float32)
+    values = chosen[:, :column_count].astype(jnp.bfloat16)
+    near = jnp.einsum("lrm,lbm->rlb", values, kernel, preferred_element_type=jnp.float32)
     return nugget * leaf_values.astype(jnp.float32) + near
 
 

time: 134 us -> 124 us (0.925)
  matrix products: 35.8 us -> 19.6 us
  local copies, waits for them, and re-layouts: 42.1 us -> 47.4 us
    dot_general x1, matrix products: 22.9 us -> 5.86 us  [near_field(): jnp.einsum('lrm,lbm->rlb', values, kernel, preferred_element_type=jnp.flo...]
    gather x1 -> x2, local copies, waits for them, and re-layouts: 3.3 us -> 8.85 us  [near_field(): chosen = jnp.take(by_leaf, source_leaf, axis=0, mode='clip')]
    reshape x0 -> x1, local copies, waits for them, and re-layouts: none -> 3.67 us  [near_field(): jnp.transpose(chosen, (0, 2, 1, 3))]
    slice x2, local copies, waits for them, and re-layouts: 3.28 us -> 1.13 us  [the longest x1 1.01 us: near_field(): values = chosen[:, :column_count].astype(jnp.bfloat16)]
    sub x6 -> x4, local copies, waits for them, and re-layouts: 3.46 us -> 2.03 us  [near_field(): chosen[:, column_count + component][:, None, :]]
    unnamed x61 -> x53, local copies, waits for them, and re-layouts: 3.09 us -> 3.07 us
  transfers between devices with their start and end apart: 9 -> 9, of which waited for: 4 -> 4; matrix products, arithmetic and copies ran while one was open for 23% -> 25% of each run, Pallas kernels for 0% -> 0%
where the time goes in v4:
time: 124 us; the launch traced here: 123 us
  local copies, waits for them, and re-layouts  47.4 us (38%)
  starting transfers between devices  37.3 us (30%)
  matrix products  19.6 us (16%)
  waiting for transfers between devices  9.89 us (8%)
  other arithmetic  7.39 us (6%)
    ppermute x4, starting transfers between devices, receive_from(): lax.ppermute(value, AXES, [(s, s - step) for s in range(n) if 0 <= s - st...  22.2 us
    ppermute x3, starting transfers between devices, swap_with(): return lax.ppermute(value, AXES, [(i, i ^ mask) for i in range(n)])  9.33 us
    gather x2, local copies, waits for them, and re-layouts, near_field(): chosen = jnp.take(by_leaf, source_leaf, axis=0, mode='clip')  8.85 us
    dot_general x1, matrix products, local(): jnp.einsum('lfrk,lfkq->lrq', partner_blocks, leaf_coupling.reshape(leaf_c...  8.35 us
    ppermute x4, waiting for transfers between devices, receive_from(): lax.ppermute(value, AXES, [(s, s - step) for s in range(n) if 0 <= s - st...  7.96 us
    reshape x1, local copies, waits for them, and re-layouts, local(): leaf_coupling.reshape(leaf_count, FAR_BLOCKS, RANK, RANK)  6.82 us
    dot_general x1, matrix products, near_field(): jnp.einsum('lrm,lbm->rlb', values, kernel, preferred_element_type=jnp.flo...  5.86 us
    gather x2, local copies, waits for them, and re-layouts, local(): jnp.take(rimmed, far_index, axis=0)  4.14 us
  transfers between devices with their start and end apart: 9, of which 4 were waited for; matrix products, arithmetic and copies ran while one was open for 25% of the time, Pallas kernels for 0%

profile of v4, /device:TPU:394, one launch (start us, length us, event | category | flops | bytes accessed | tf_op | source)
XLA Modules:
  0.0 122.5 jit_solution(14176883176136968618)
XLA Ops:
  0.0 1.2 %reshape.153 = bf16[16,64,64]{2,1,0:T(8,128)(2,1)S(1)} reshape(bf16[16,4096]{1,0:T(8,128)(2,1)} %param.13) | data formatting | bytes 262144 | tf_op jit(solution)/shard_map/reshape | solution.py:141
  1.3 1.0 convert_element_type.28
  2.3 1.2 copy.35
  3.6 1.1 copy.37
  4.7 0.4 fusion.14
  5.3 0.7 pad_maximum_fusion.3
  6.0 2.4 %collective-permute-start.1 = (f32[35840]{0:T(1024)}, f32[35840]{0:T(1024)}, u32[]{:S(2)}, u32[]{:S(2)}) collective-permute-start(f32[35840]{0:T(1024)} %pad_maximum_fusion.3), channel_id=1, source_target_pairs={{1,0},{2,1},{3,2},{4,3},{5,4},{6,5},{7,6},{8,7},{9,8},{10,9},{11,1... | collective-permute-start | bytes 430088 | tf_op jit(solution)/shard_map/ppermute | solution.py:157
  8.5 0.7 pad_maximum_fusion.2
  9.2 3.4 %collective-permute-start = (f32[35840]{0:T(1024)}, f32[35840]{0:T(1024)}, u32[]{:S(2)}, u32[]{:S(2)}) collective-permute-start(f32[35840]{0:T(1024)} %pad_maximum_fusion.2), channel_id=1, source_target_pairs={{0,1},{1,2},{2,3},{3,4},{4,5},{5,6},{6,7},{7,8},{8,9},{9,10},{10,1... | collective-permute-start | bytes 430088 | tf_op jit(solution)/shard_map/ppermute | solution.py:156
  12.9 0.8 copy.49
  13.7 0.8 fusion.49
  15.0 0.2 convolution_bitcast_fusion.3
  15.2 2.5 %collective-permute-start.2 = (f32[4,16,32]{2,1,0:T(8,128)S(1)}, f32[4,16,32]{2,1,0:T(8,128)S(1)}, u32[]{:S(2)}, u32[]{:S(2)}) collective-permute-start(f32[4,16,32]{2,1,0:T(8,128)S(1)} %convolution_bitcast_fusion.3), channel_id=1, source_target_pairs={{0,1},{1,0},{2,3},{3,2},{4,5},{5,4},{6,7},{7,6},{8,9},{9,8},{10,11... | collective-permute-start | bytes 24584 | tf_op jit(solution)/shard_map/ppermute | solution.py:30
  18.0 0.6 compare_and_fusion
  19.7 1.5 %convolution_bitcast_fusion.2 = f32[4,4,32,32]{2,3,1,0:T(8,128)} fusion(bf16[4,4,32,32]{3,2,1,0:T(8,128)(2,1)S(1)} %reshape.164, f32[1,32,32]{2,1,0:T(8,128)S(1)} %fusion.35, f32[1,32,32]{2,1,0:T(8,128)S(1)} %convolution_bitcast_fusion.4, f32[1,32,32]{2,1,0:T(8,128)S(1)} %bitcast.90, f32[1,32,32]{2,1,0:T(8,128)S(1)} %reshape.169), kind=kOutput, calls=%fused_computation.21 | convolution fusion | flops 6303744 | bytes 114688 | tf_op jit(solution)/shard_map/sqkp,spm->sqkm/dot_general | solution.py:81
  21.2 4.9 %collective-permute-start.3 = (f32[5,16,32]{2,1,0:T(8,128)S(1)}, f32[5,16,32]{2,1,0:T(8,128)S(1)}, u32[]{:S(2)}, u32[]{:S(2)}) collective-permute-start(f32[5,16,32]{2,1,0:T(8,128)S(1)} %pad_maximum_fusion.17), channel_id=1, source_target_pairs={{0,2},{1,3},{2,0},{3,1},{4,6},{5,7},{6,4},{7,5},{8,10},{9,11},{10,... | collective-permute-start | bytes 30728 | tf_op jit(solution)/shard_map/ppermute | solution.py:30
  26.1 0.6 pad_clamp_fusion.1
  26.7 1.9 %collective-permute-done.3 = f32[5,16,32]{2,1,0:T(8,128)S(1)} collective-permute-done((f32[5,16,32]{2,1,0:T(8,128)S(1)}, f32[5,16,32]{2,1,0:T(8,128)S(1)}, u32[]{:S(2)}, u32[]{:S(2)}) %collective-permute-start.3) | collective-permute-done | bytes 10272 | tf_op jit(solution)/shard_map/ppermute | solution.py:30
  28.7 0.6 fusion.19
  29.3 1.9 %collective-permute-start.4 = (f32[8,16,32]{2,1,0:T(8,128)}, f32[8,16,32]{2,1,0:T(8,128)}, u32[]{:S(2)}, u32[]{:S(2)}) collective-permute-start(f32[8,16,32]{2,1,0:T(8,128)} %fusion.19), channel_id=1, source_target_pairs={{0,4},{1,5},{2,6},{3,7},{4,0},{5,1},{6,2},{7,3},{8,12},{9,13},{10,... | collective-permute-start | bytes 49160 | tf_op jit(solution)/shard_map/ppermute | solution.py:30
  31.2 0.6 pad_clamp_fusion
  31.8 0.9 copy.43
  32.8 0.7 sub.63
  33.4 0.7 sub.58
  34.1 0.7 sub.53
  34.8 1.4 %copy.46 = bf16[64,8,1024]{0,2,1:T(8,128)(2,1)S(1)} copy(bf16[64,8,1024]{2,1,0:T(8,128)(2,1)S(1)} %copy-done) | data formatting | bytes 2097152 | tf_op args[6]
  36.2 6.8 %copy.47 = bf16[64,8,32,32]{3,2,1,0:T(8,128)(2,1)} copy(bf16[64,8,32,32]{0,3,2,1:T(8,128)(2,1)S(1)} %bitcast.85) | data formatting | bytes 2097152 | tf_op jit(solution)/shard_map/reshape | solution.py:183
  43.2 0.7 copy.42
  44.1 0.8 copy.55
  44.9 1.5 %reshape.166 = bf16[64,32,64]{2,1,0:T(8,128)(2,1)S(1)} reshape(bf16[64,2048]{1,0:T(8,128)(2,1)} %param.18) | data formatting | bytes 524288 | tf_op jit(solution)/shard_map/reshape | solution.py:206
  46.3 0.7 fusion.44
  47.1 0.7 slice.336
  47.8 0.8 maximum_select_fusion.1
  48.6 0.8 slice.334
  49.4 0.8 fusion.17
  50.2 3.5 %collective-permute-start.5 = (f32[9,16,32]{2,1,0:T(8,128)S(1)}, f32[9,16,32]{2,1,0:T(8,128)S(1)}, u32[]{:S(2)}, u32[]{:S(2)}) collective-permute-start(f32[9,16,32]{2,1,0:T(8,128)S(1)} %get-tuple-element.44), channel_id=1, source_target_pairs={{0,8},{1,9},{2,10},{3,11},{4,12},{5,13},{6,14},{7,15},{8,16},{9,17... | collective-permute-start | bytes 55304 | tf_op jit(solution)/shard_map/ppermute | solution.py:35
  53.7 5.0 %collective-permute-start.6 = (f32[9,16,32]{2,1,0:T(8,128)S(1)}, f32[9,16,32]{2,1,0:T(8,128)S(1)}, u32[]{:S(2)}, u32[]{:S(2)}) collective-permute-start(f32[9,16,32]{2,1,0:T(8,128)S(1)} %get-tuple-element.45), channel_id=1, source_target_pairs={{8,0},{9,1},{10,2},{11,3},{12,4},{13,5},{14,6},{15,7},{16,8},{17,9... | collective-permute-start | bytes 55304 | tf_op jit(solution)/shard_map/ppermute | solution.py:35
  58.8 1.0 collective-permute-done.5
  59.8 1.2 collective-permute-done.6
  60.9 11.6 %collective-permute-start.8 = (f32[3,16,32]{2,1,0:T(8,128)S(1)}, f32[3,16,32]{2,1,0:T(8,128)S(1)}, u32[]{:S(2)}, u32[]{:S(2)}) collective-permute-start(f32[3,16,32]{2,1,0:T(8,128)S(1)} %get-tuple-element.49), channel_id=1, source_target_pairs={{16,0},{17,1},{18,2},{19,3},{20,4},{21,5},{22,6},{23,7},{24,8},{25... | collective-permute-start | bytes 18440 | tf_op jit(solution)/shard_map/ppermute | solution.py:35
  72.5 2.1 %collective-permute-start.7 = (f32[3,16,32]{2,1,0:T(8,128)S(1)}, f32[3,16,32]{2,1,0:T(8,128)S(1)}, u32[]{:S(2)}, u32[]{:S(2)}) collective-permute-start(f32[3,16,32]{2,1,0:T(8,128)S(1)} %get-tuple-element.48), channel_id=1, source_target_pairs={{0,16},{1,17},{2,18},{3,19},{4,20},{5,21},{6,22},{7,23},{8,24},{9,... | collective-permute-start | bytes 18440 | tf_op jit(solution)/shard_map/ppermute | solution.py:35
  74.7 0.7 gather_fusion.3
  75.4 0.7 gather_fusion.2
  76.1 5.8 %collective-permute-done.7 = f32[3,16,32]{2,1,0:T(8,128)S(1)} collective-permute-done((f32[3,16,32]{2,1,0:T(8,128)S(1)}, f32[3,16,32]{2,1,0:T(8,128)S(1)}, u32[]{:S(2)}, u32[]{:S(2)}) %collective-permute-start.7) | collective-permute-done | bytes 6176 | tf_op jit(solution)/shard_map/ppermute | solution.py:35
  82.0 0.7 gather_fusion.4
  82.6 1.2 %convolution_bitcast_fusion.6 = f32[16,32,1]{1,0,2:T(8,128)S(1)} fusion(f32[4,4,32,32]{2,3,1,0:T(8,128)} %convolution_bitcast_fusion.2, f32[1,4,16,32]{3,2,1,0:T(8,128)S(1)} %maximum_bitcast_fusion, f32[1,4,16,32]{3,2,1,0:T(8,128)S(1)} %bitcast.93, f32[1,4,16,32]{3,2,1,0:T(8,128)S(1)} %bitcast.91, f32[1,4,16,32]{3,2,1,0:T(8,128)S(1)} %bitcast.92), kind=kOutput, calls=%fused_computation.25 | convolution fusion | flops 3170304 | bytes 100352 | tf_op jit(solution)/shard_map/sqrk,sqkm->rm/dot_general | solution.py:121
  83.9 0.9 slice.315
  84.8 0.9 slice.313
  85.8 0.4 reshape.159
  86.2 0.6 copy.78
  86.8 3.3 %gather_fusion = f32[384,19,64]{2,1,0:T(8,128)} fusion(f32[96,19,64]{2,1,0:T(8,128)S(1)} %bitcast.82, s32[1024]{0:T(1024)S(1)} %get-tuple-element.58), kind=kCustom, calls=%fused_computation | custom fusion | bytes 3737088 | tf_op jit(solution)/shard_map/jit(_take)/gather | solution.py:43
  90.1 5.5 %copy.77 = f32[64,6,19,64]{3,1,0,2:T(8,128)} copy(f32[64,6,19,64]{3,2,1,0:T(8,128)} %bitcast.84) | data formatting | bytes 3735552 | tf_op jit(solution)/shard_map/jit(_take)/gather | solution.py:43
  95.6 3.7 %reshape.160 = f32[64,19,384]{2,0,1:T(8,128)S(1)} reshape(f32[64,19,6,64]{3,2,0,1:T(8,128)} %bitcast.83) | data formatting | bytes 3735552 | tf_op jit(solution)/shard_map/reshape | solution.py:44
  99.3 1.0 slice.387
  100.3 0.8 slice.321
  101.2 0.8 slice.320
  102.1 1.6 %gather_fusion.1 = f32[512,512]{1,0:T(8,128)S(1)} fusion(f32[128,512]{1,0:T(8,128)S(1)} %pad_maximum_fusion.1, s32[1024]{0:T(1024)S(1)} %get-tuple-element.57), kind=kCustom, calls=%fused_computation.1 | custom fusion | bytes 2099200 | tf_op jit(solution)/shard_map/jit(_take)/gather | solution.py:179
  103.7 2.5 %gather.24 = f32[64,8,16,32]{3,2,1,0:T(8,128)} reshape(f32[512,512]{1,0:T(8,128)S(1)} %gather_fusion.1) | data formatting | bytes 2097152 | tf_op jit(solution)/shard_map/jit(_take)/gather | solution.py:179
  106.3 8.3 %fusion.6 = f32[64,16,32]{2,1,0:T(8,128)S(1)} fusion(bf16[64,8,32,32]{3,2,1,0:T(8,128)(2,1)} %copy.47, f32[64,8,16,32]{3,2,1,0:T(8,128)} %gather.24, pred[64,8]{1,0:T(8,128)(4,1)S(1)} %copy-done.12), kind=kOutput, calls=%fused_computation.14 | convolution fusion | flops 100925440 | bytes 2228736 | tf_op jit(solution)/shard_map/lfrk,lfkq->lrq/dot_general | solution.py:180
  114.6 0.4 fusion.9
  115.0 5.9 %fusion.11 = f32[16,64,64]{2,0,1:T(8,128)S(1)} fusion(f32[64,64]{1,0:T(8,128)S(1)} %copy-done.14, f32[64,384]{1,0:T(8,128)S(1)} %get-tuple-element.17, f32[64,64]{1,0:T(8,128)S(1)} %copy-done.15, f32[64,384]{1,0:T(8,128)S(1)} %get-tuple-element.18, f32[64,64]{1,0:T(8,128)S(1)} %copy-done.16, f32[64,384]{1,0:T(8,128)S(1)} %get-tuple-element.16, ...), kind=kOutput, calls=%fused_computation.19 | convolution fusion | flops 67829760 | bytes 1523712 | tf_op jit(solution)/shard_map/lrm,lbm->rlb/dot_general | solution.py:56
  120.9 0.6 fusion.10
  121.5 0.2 copy.56
  121.6 0.9 reshape.167
  (120 shorter events, 3.2 us)
Async XLA Ops:
  0.0 5.2 %copy-start.5 = (f32[3,4096]{1,0:T(4,128)S(1)}, f32[3,4096]{1,0:T(4,128)}, u32[]{:S(2)}) copy-start(f32[3,4096]{1,0:T(4,128)} %param.14) | copy-start | bytes 147460
  0.0 12.6 %copy-start.17 = (bf16[1,3,1024]{2,1,0:T(4,128)(2,1)S(1)}, bf16[1,3,1024]{2,1,0:T(4,128)(2,1)}, u32[]{:S(2)}) copy-start(bf16[1,3,1024]{2,1,0:T(4,128)(2,1)} %param.22) | copy-start | bytes 18436
  0.0 12.7 %copy-start.18 = (bf16[1,3,1024]{2,1,0:T(4,128)(2,1)S(1)}, bf16[1,3,1024]{2,1,0:T(4,128)(2,1)}, u32[]{:S(2)}) copy-start(bf16[1,3,1024]{2,1,0:T(4,128)(2,1)} %param.23) | copy-start | bytes 18436
  0.0 12.7 %copy-start.9 = (bf16[64,1024]{1,0:T(8,128)(2,1)S(1)}, bf16[64,1024]{1,0:T(8,128)(2,1)}, u32[]{:S(2)}) copy-start(bf16[64,1024]{1,0:T(8,128)(2,1)} %param.20) | copy-start | bytes 393220
  1.3 17.5 %copy-start.1 = (bf16[16,64,64]{2,1,0:T(8,128)(2,1)}, bf16[16,64,64]{2,1,0:T(8,128)(2,1)S(1)}, u32[]{:S(2)}) copy-start(bf16[16,64,64]{2,1,0:T(8,128)(2,1)S(1)} %reshape.153) | copy-start | bytes 393220
  1.3 16.7 %copy-start.20 = (s32[64,8]{0,1:T(8,128)S(1)}, s32[64,8]{0,1:T(8,128)}, u32[]{:S(2)}) copy-start(s32[64,8]{0,1:T(8,128)} %param.16) | copy-start | bytes 6148
  1.3 17.4 %copy-start.21 = (s32[64,6]{0,1:T(8,128)S(1)}, s32[64,6]{0,1:T(8,128)}, u32[]{:S(2)}) copy-start(s32[64,6]{0,1:T(8,128)} %param.15) | copy-start | bytes 4612
  1.3 17.7 %copy-start.13 = (bf16[1,4,4,1024]{3,2,1,0:T(4,128)(2,1)S(1)}, bf16[1,4,4,1024]{3,2,1,0:T(4,128)(2,1)}, u32[]{:S(2)}) copy-start(bf16[1,4,4,1024]{3,2,1,0:T(4,128)(2,1)} %param.24) | copy-start | bytes 98308
  3.6 17.6 %copy-start.22 = (s32[4]{0:T(128)S(1)}, s32[4]{0:T(128)}, u32[]{:S(2)}) copy-start(s32[4]{0:T(128)} %constant.59) | copy-start | bytes 52
  4.7 30.1 %copy-start = (bf16[64,8,1024]{2,1,0:T(8,128)(2,1)S(1)}, bf16[64,8,1024]{2,1,0:T(8,128)(2,1)}, u32[]{:S(2)}) copy-start(bf16[64,8,1024]{2,1,0:T(8,128)(2,1)} %param.19) | copy-start | bytes 3145732
  6.0 78.0 %collective-permute-start.1 = (f32[35840]{0:T(1024)}, f32[35840]{0:T(1024)}, u32[]{:S(2)}, u32[]{:S(2)}) collective-permute-start(f32[35840]{0:T(1024)} %pad_maximum_fusion.3), channel_id=1, source_target_pairs={{1,0},{2,1},{3,2},{4,3},{5,4},{6,5},{7,6},{8,7},{9,8},{10,9},{11,1... | collective-permute-start | bytes 430088 | tf_op jit(solution)/shard_map/ppermute | solution.py:157
  9.2 75.6 %collective-permute-start = (f32[35840]{0:T(1024)}, f32[35840]{0:T(1024)}, u32[]{:S(2)}, u32[]{:S(2)}) collective-permute-start(f32[35840]{0:T(1024)} %pad_maximum_fusion.2), channel_id=1, source_target_pairs={{0,1},{1,2},{2,3},{3,4},{4,5},{5,6},{6,7},{7,8},{8,9},{9,10},{10,1... | collective-permute-start | bytes 430088 | tf_op jit(solution)/shard_map/ppermute | solution.py:156
  15.2 6.0 %collective-permute-start.2 = (f32[4,16,32]{2,1,0:T(8,128)S(1)}, f32[4,16,32]{2,1,0:T(8,128)S(1)}, u32[]{:S(2)}, u32[]{:S(2)}) collective-permute-start(f32[4,16,32]{2,1,0:T(8,128)S(1)} %convolution_bitcast_fusion.3), channel_id=1, source_target_pairs={{0,1},{1,0},{2,3},{3,2},{4,5},{5,4},{6,7},{7,6},{8,9},{9,8},{10,11... | collective-permute-start | bytes 24584 | tf_op jit(solution)/shard_map/ppermute | solution.py:30
  21.2 7.4 %collective-permute-start.3 = (f32[5,16,32]{2,1,0:T(8,128)S(1)}, f32[5,16,32]{2,1,0:T(8,128)S(1)}, u32[]{:S(2)}, u32[]{:S(2)}) collective-permute-start(f32[5,16,32]{2,1,0:T(8,128)S(1)} %pad_maximum_fusion.17), channel_id=1, source_target_pairs={{0,2},{1,3},{2,0},{3,1},{4,6},{5,7},{6,4},{7,5},{8,10},{9,11},{10,... | collective-permute-start | bytes 30728 | tf_op jit(solution)/shard_map/ppermute | solution.py:30
  28.6 14.4 %copy-start.7 = (f32[4,16,32]{2,1,0:T(8,128)}, f32[4,16,32]{2,1,0:T(8,128)S(1)}, u32[]{:S(2)}) copy-start(f32[4,16,32]{2,1,0:T(8,128)S(1)} %maximum_select_fusion) | copy-start | bytes 24580
  28.7 14.4 %copy-start.11 = (f32[1,16,32]{2,1,0:T(8,128)}, f32[1,16,32]{2,1,0:T(8,128)S(1)}, u32[]{:S(2)}) copy-start(f32[1,16,32]{2,1,0:T(8,128)S(1)} %get-tuple-element.35) | copy-start | bytes 6148
  28.7 14.4 %copy-start.8 = (f32[2,16,32]{2,1,0:T(8,128)}, f32[2,16,32]{2,1,0:T(8,128)S(1)}, u32[]{:S(2)}) copy-start(f32[2,16,32]{2,1,0:T(8,128)S(1)} %maximum_select_fusion.3) | copy-start | bytes 12292
  29.3 17.0 %collective-permute-start.4 = (f32[8,16,32]{2,1,0:T(8,128)}, f32[8,16,32]{2,1,0:T(8,128)}, u32[]{:S(2)}, u32[]{:S(2)}) collective-permute-start(f32[8,16,32]{2,1,0:T(8,128)} %fusion.19), channel_id=1, source_target_pairs={{0,4},{1,5},{2,6},{3,7},{4,0},{5,1},{6,2},{7,3},{8,12},{9,13},{10,... | collective-permute-start | bytes 49160 | tf_op jit(solution)/shard_map/ppermute | solution.py:30
  36.2 6.9 %copy-start.3 = (f32[64,16,32]{0,2,1:T(8,128)S(1)}, f32[64,16,32]{0,2,1:T(8,128)}, u32[]{:S(2)}) copy-start(f32[64,16,32]{0,2,1:T(8,128)} %copy.43) | copy-start | bytes 393220
  36.2 7.0 %copy-start.19 = (pred[64,8]{0,1:T(8,128)(4,1)S(1)}, pred[64,8]{0,1:T(8,128)(4,1)}, u32[]{:S(2)}) copy-start(pred[64,8]{0,1:T(8,128)(4,1)} %get-tuple-element.14) | copy-start | bytes 1540
  36.2 7.7 %copy-start.10 = (bf16[64,1024]{1,0:T(8,128)(2,1)S(1)}, bf16[64,1024]{1,0:T(8,128)(2,1)}, u32[]{:S(2)}) copy-start(bf16[64,1024]{1,0:T(8,128)(2,1)} %param.21) | copy-start | bytes 393220
  43.1 42.7 %copy-start.6 = (f32[3,4096]{1,0:T(4,128)S(1)}, f32[3,4096]{1,0:T(4,128)}, u32[]{:S(2)}) copy-start(f32[3,4096]{1,0:T(4,128)} %param.14) | copy-start | bytes 147460
  50.2 9.5 %collective-permute-start.5 = (f32[9,16,32]{2,1,0:T(8,128)S(1)}, f32[9,16,32]{2,1,0:T(8,128)S(1)}, u32[]{:S(2)}, u32[]{:S(2)}) collective-permute-start(f32[9,16,32]{2,1,0:T(8,128)S(1)} %get-tuple-element.44), channel_id=1, source_target_pairs={{0,8},{1,9},{2,10},{3,11},{4,12},{5,13},{6,14},{7,15},{8,16},{9,17... | collective-permute-start | bytes 55304 | tf_op jit(solution)/shard_map/ppermute | solution.py:35
  53.7 7.2 %collective-permute-start.6 = (f32[9,16,32]{2,1,0:T(8,128)S(1)}, f32[9,16,32]{2,1,0:T(8,128)S(1)}, u32[]{:S(2)}, u32[]{:S(2)}) collective-permute-start(f32[9,16,32]{2,1,0:T(8,128)S(1)} %get-tuple-element.45), channel_id=1, source_target_pairs={{8,0},{9,1},{10,2},{11,3},{12,4},{13,5},{14,6},{15,7},{16,8},{17,9... | collective-permute-start | bytes 55304 | tf_op jit(solution)/shard_map/ppermute | solution.py:35
  60.9 21.0 %collective-permute-start.8 = (f32[3,16,32]{2,1,0:T(8,128)S(1)}, f32[3,16,32]{2,1,0:T(8,128)S(1)}, u32[]{:S(2)}, u32[]{:S(2)}) collective-permute-start(f32[3,16,32]{2,1,0:T(8,128)S(1)} %get-tuple-element.49), channel_id=1, source_target_pairs={{16,0},{17,1},{18,2},{19,3},{20,4},{21,5},{22,6},{23,7},{24,8},{25... | collective-permute-start | bytes 18440 | tf_op jit(solution)/shard_map/ppermute | solution.py:35
  72.5 9.3 %collective-permute-start.7 = (f32[3,16,32]{2,1,0:T(8,128)S(1)}, f32[3,16,32]{2,1,0:T(8,128)S(1)}, u32[]{:S(2)}, u32[]{:S(2)}) collective-permute-start(f32[3,16,32]{2,1,0:T(8,128)S(1)} %get-tuple-element.48), channel_id=1, source_target_pairs={{0,16},{1,17},{2,18},{3,19},{4,20},{5,21},{6,22},{7,23},{8,24},{9,... | collective-permute-start | bytes 18440 | tf_op jit(solution)/shard_map/ppermute | solution.py:35
  103.7 2.5 %copy-start.12 = (pred[64,8]{1,0:T(8,128)(4,1)S(1)}, pred[64,8]{1,0:T(8,128)(4,1)}, u32[]{:S(2)}) copy-start(pred[64,8]{1,0:T(8,128)(4,1)} %copy.42) | copy-start | bytes 1540
  106.2 8.8 %copy-start.2 = (bf16[16,64,64]{2,1,0:T(8,128)(2,1)S(1)}, bf16[16,64,64]{2,1,0:T(8,128)(2,1)}, u32[]{:S(2)}) copy-start(bf16[16,64,64]{2,1,0:T(8,128)(2,1)} %copy-done.1) | copy-start | bytes 393220
  106.2 8.8 %copy-start.4 = (bf16[64,16,384]{2,0,1:T(8,128)(2,1)S(1)}, bf16[64,16,384]{2,0,1:T(8,128)(2,1)}, u32[]{:S(2)}) copy-start(bf16[64,16,384]{2,0,1:T(8,128)(2,1)} %slice.387) | copy-start | bytes 2359300
  106.2 8.8 %copy-start.14 = (f32[64,64]{1,0:T(8,128)S(1)}, f32[64,64]{1,0:T(8,128)}, u32[]{:S(2)}) copy-start(f32[64,64]{1,0:T(8,128)} %sub.63) | copy-start | bytes 49156
  106.2 8.8 %copy-start.15 = (f32[64,64]{1,0:T(8,128)S(1)}, f32[64,64]{1,0:T(8,128)}, u32[]{:S(2)}) copy-start(f32[64,64]{1,0:T(8,128)} %sub.58) | copy-start | bytes 49156
  106.2 8.8 %copy-start.16 = (f32[64,64]{1,0:T(8,128)S(1)}, f32[64,64]{1,0:T(8,128)}, u32[]{:S(2)}) copy-start(f32[64,64]{1,0:T(8,128)} %sub.53) | copy-start | bytes 49156

commit v5 on v4

--- a/solution.py
+++ b/solution.py
@@ -39,21 +39,24 @@
     leaf_count = target_points.shape[1]
     column_count = extended.shape[0] - 3
     by_leaf = jnp.transpose(extended, (1, 0, 2))
-    source_leaf = jnp.arange(leaf_count, dtype=jnp.int32)[:, None] + NEAR_REACH + near_offsets
-    chosen = jnp.take(by_leaf, source_leaf, axis=0, mode="clip")
-    chosen = jnp.transpose(chosen, (0, 2, 1, 3)).reshape(
-        leaf_count, column_count + 3, NEAR_BLOCKS * CLUSTER
-    )
+    base = jnp.arange(leaf_count, dtype=jnp.int32) + NEAR_REACH
+    chosen = jnp.concatenate(
+        [
+            jnp.take(by_leaf, base + near_offsets[:, near_slot], axis=0, mode="clip")
+            for near_slot in range(NEAR_BLOCKS)
+        ],
+        axis=2,
+    )
+    chosen = jnp.transpose(chosen, (1, 0, 2))
     squared = jnp.zeros((leaf_count, CLUSTER, NEAR_BLOCKS * CLUSTER), jnp.float32)
     for component in range(3):
         separation = (
-            chosen[:, column_count + component][:, None, :]
-            - target_points[component][:, :, None]
+            chosen[column_count + component][:, None, :] - target_points[component][:, :, None]
         )
         squared = squared + separation * separation
     kernel = (amplitude * jnp.exp(-jnp.sqrt(squared) / length_scale)).astype(jnp.bfloat16)
-    values = chosen[:, :column_count].astype(jnp.bfloat16)
-    near = jnp.einsum("lrm,lbm->rlb", values, kernel, preferred_element_type=jnp.float32)
+    values = chosen[:column_count].astype(jnp.bfloat16)
+    near = jnp.einsum("rlm,lbm->rlb", values, kernel, preferred_element_type=jnp.float32)
     return nugget * leaf_values.astype(jnp.float32) + near
 
 

time: 124 us -> 124 us (level)
  local copies, waits for them, and re-layouts: 47.4 us -> 48.9 us
    concatenate x0 -> x1, local copies, waits for them, and re-layouts: none -> 4.43 us  [near_field(): jnp.concatenate([jnp.take(by_leaf, base + near_offsets[:, near_slot], axi...]
    reshape x1 -> x0, local copies, waits for them, and re-layouts: 3.67 us -> none  [near_field(): jnp.transpose(chosen, (0, 2, 1, 3))]
    gather x0 -> x3, other arithmetic: none -> 1.81 us  [near_field(): jnp.take(by_leaf, base + near_offsets[:, near_slot], axis=0, mode='clip')]
    gather x2 -> x6, local copies, waits for them, and re-layouts: 8.85 us -> 7.22 us  [near_field(): jnp.take(by_leaf, base + near_offsets[:, near_slot], axis=0, mode='clip')]
    select_n x6, other arithmetic: 1.67 us -> 0.05 us  [ordered(): jnp.where(bit == 0, jnp.concatenate([own, other]), jnp.concatenate([other...]
    unnamed x53 -> x58, local copies, waits for them, and re-layouts: 3.07 us -> 3.1 us
where the time goes in v5:
time: 124 us; the launch traced here: 123 us
  local copies, waits for them, and re-layouts  48.9 us (39%)
  starting transfers between devices  36.8 us (30%)
  matrix products  18.4 us (15%)
  waiting for transfers between devices  11 us (9%)
  other arithmetic  6.96 us (6%)
    ppermute x4, starting transfers between devices, receive_from(): lax.ppermute(value, AXES, [(s, s - step) for s in range(n) if 0 <= s - st...  22.2 us
    ppermute x3, starting transfers between devices, swap_with(): return lax.ppermute(value, AXES, [(i, i ^ mask) for i in range(n)])  8.79 us
    dot_general x1, matrix products, local(): jnp.einsum('lfrk,lfkq->lrq', partner_blocks, leaf_coupling.reshape(leaf_c...  8.41 us
    ppermute x4, waiting for transfers between devices, receive_from(): lax.ppermute(value, AXES, [(s, s - step) for s in range(n) if 0 <= s - st...  7.96 us
    gather x6, local copies, waits for them, and re-layouts, near_field(): jnp.take(by_leaf, base + near_offsets[:, near_slot], axis=0, mode='clip')  7.22 us
    reshape x1, local copies, waits for them, and re-layouts, local(): leaf_coupling.reshape(leaf_count, FAR_BLOCKS, RANK, RANK)  6.89 us
    dot_general x1, matrix products, near_field(): jnp.einsum('rlm,lbm->rlb', values, kernel, preferred_element_type=jnp.flo...  5.45 us
    concatenate x1, local copies, waits for them, and re-layouts, near_field(): jnp.concatenate([jnp.take(by_leaf, base + near_offsets[:, near_slot], axi...  4.43 us
  transfers between devices with their start and end apart: 9, of which 4 were waited for; matrix products, arithmetic and copies ran while one was open for 25% of the time, Pallas kernels for 0%

profile of v5, /device:TPU:394, one launch (start us, length us, event | category | flops | bytes accessed | tf_op | source)
XLA Modules:
  0.0 122.9 jit_solution(1074795944878982696)
XLA Ops:
  0.0 1.2 %reshape.160 = bf16[16,64,64]{2,1,0:T(8,128)(2,1)S(1)} reshape(bf16[16,4096]{1,0:T(8,128)(2,1)} %param.13) | data formatting | bytes 262144 | tf_op jit(solution)/shard_map/reshape | solution.py:144
  1.3 1.0 convert_element_type.28
  2.3 1.2 copy.18
  3.6 1.1 copy.20
  4.7 0.4 fusion.13
  5.3 0.7 pad_maximum_fusion.3
  5.9 2.4 %collective-permute-start.1 = (f32[35840]{0:T(1024)}, f32[35840]{0:T(1024)}, u32[]{:S(2)}, u32[]{:S(2)}) collective-permute-start(f32[35840]{0:T(1024)} %pad_maximum_fusion.3), channel_id=1, source_target_pairs={{1,0},{2,1},{3,2},{4,3},{5,4},{6,5},{7,6},{8,7},{9,8},{10,9},{11,1... | collective-permute-start | bytes 430088 | tf_op jit(solution)/shard_map/ppermute | solution.py:160
  8.5 0.7 pad_maximum_fusion.2
  9.2 3.4 %collective-permute-start = (f32[35840]{0:T(1024)}, f32[35840]{0:T(1024)}, u32[]{:S(2)}, u32[]{:S(2)}) collective-permute-start(f32[35840]{0:T(1024)} %pad_maximum_fusion.2), channel_id=1, source_target_pairs={{0,1},{1,2},{2,3},{3,4},{4,5},{5,6},{6,7},{7,8},{8,9},{9,10},{10,1... | collective-permute-start | bytes 430088 | tf_op jit(solution)/shard_map/ppermute | solution.py:159
  12.9 0.8 copy.33
  13.6 0.8 fusion.50
  15.2 2.5 %collective-permute-start.2 = (f32[4,16,32]{2,1,0:T(8,128)S(1)}, f32[4,16,32]{2,1,0:T(8,128)S(1)}, u32[]{:S(2)}, u32[]{:S(2)}) collective-permute-start(f32[4,16,32]{2,1,0:T(8,128)S(1)} %convolution_bitcast_fusion.2), channel_id=1, source_target_pairs={{0,1},{1,0},{2,3},{3,2},{4,5},{5,4},{6,7},{7,6},{8,9},{9,8},{10,11... | collective-permute-start | bytes 24584 | tf_op jit(solution)/shard_map/ppermute | solution.py:30
  18.4 0.6 pad_clamp_fusion.8
  19.0 0.6 pad_clamp_fusion.6
  19.6 0.6 pad_clamp_fusion.4
  20.2 0.6 compare_and_fusion
  21.0 1.5 %fusion.25 = f32[4,32,4,32]{3,1,2,0:T(8,128)} fusion(bf16[4,4,32,32]{3,2,1,0:T(8,128)(2,1)S(1)} %reshape.170, f32[1,32,32]{2,1,0:T(8,128)S(1)} %fusion.35, f32[1,32,32]{2,1,0:T(8,128)S(1)} %convolution_bitcast_fusion.3, f32[1,32,32]{2,1,0:T(8,128)S(1)} %bitcast.107, f32[1,32,32]{2,1,0:T(8,128)S(1)} %reshape.175), kind=kOutput, calls=%fused_computation.62 | convolution fusion | flops 6303744 | bytes 114688 | tf_op jit(solution)/shard_map/sqkp,spm->sqkm/dot_general | solution.py:84
  22.5 0.6 pad_clamp_fusion.1
  23.4 4.4 %collective-permute-start.3 = (f32[5,16,32]{2,1,0:T(8,128)S(1)}, f32[5,16,32]{2,1,0:T(8,128)S(1)}, u32[]{:S(2)}, u32[]{:S(2)}) collective-permute-start(f32[5,16,32]{2,1,0:T(8,128)S(1)} %pad_maximum_fusion.17), channel_id=1, source_target_pairs={{0,2},{1,3},{2,0},{3,1},{4,6},{5,7},{6,4},{7,5},{8,10},{9,11},{10,... | collective-permute-start | bytes 30728 | tf_op jit(solution)/shard_map/ppermute | solution.py:30
  27.8 3.0 %collective-permute-done.3 = f32[5,16,32]{2,1,0:T(8,128)S(1)} collective-permute-done((f32[5,16,32]{2,1,0:T(8,128)S(1)}, f32[5,16,32]{2,1,0:T(8,128)S(1)}, u32[]{:S(2)}, u32[]{:S(2)}) %collective-permute-start.3) | collective-permute-done | bytes 10272 | tf_op jit(solution)/shard_map/ppermute | solution.py:30
  30.8 0.6 fusion.18
  31.4 1.9 %collective-permute-start.4 = (f32[8,16,32]{2,1,0:T(8,128)}, f32[8,16,32]{2,1,0:T(8,128)}, u32[]{:S(2)}, u32[]{:S(2)}) collective-permute-start(f32[8,16,32]{2,1,0:T(8,128)} %fusion.18), channel_id=1, source_target_pairs={{0,4},{1,5},{2,6},{3,7},{4,0},{5,1},{6,2},{7,3},{8,12},{9,13},{10,... | collective-permute-start | bytes 49160 | tf_op jit(solution)/shard_map/ppermute | solution.py:30
  33.4 1.0 copy.23
  34.3 0.7 sub.63
  35.0 0.7 sub.58
  35.7 0.7 sub.53
  36.3 1.4 %copy.26 = bf16[64,8,1024]{0,2,1:T(8,128)(2,1)S(1)} copy(bf16[64,8,1024]{2,1,0:T(8,128)(2,1)S(1)} %copy-done.3) | data formatting | bytes 2097152 | tf_op args[6]
  37.8 6.9 %copy.31 = bf16[64,8,32,32]{3,2,1,0:T(8,128)(2,1)} copy(bf16[64,8,32,32]{0,3,2,1:T(8,128)(2,1)S(1)} %bitcast.99) | data formatting | bytes 2097152 | tf_op jit(solution)/shard_map/reshape | solution.py:186
  44.7 0.8 copy.24
  45.5 0.7 copy.22
  46.5 1.5 %copy.40 = bf16[64,32,32]{2,1,0:T(8,128)(2,1)} copy(bf16[64,32,32]{0,2,1:T(8,128)(2,1)S(1)} %bitcast.105) | data formatting | bytes 262144 | tf_op jit(solution)/shard_map/reshape | solution.py:201
  48.0 1.3 %reshape.172 = bf16[64,32,64]{2,1,0:T(8,128)(2,1)} reshape(bf16[64,2048]{1,0:T(8,128)(2,1)S(1)} %copy-done.10) | data formatting | bytes 524288 | tf_op jit(solution)/shard_map/reshape | solution.py:209
  49.3 0.7 fusion.45
  50.1 0.7 slice.370
  50.8 0.8 slice.368
  51.6 3.5 %collective-permute-start.5 = (f32[9,16,32]{2,1,0:T(8,128)S(1)}, f32[9,16,32]{2,1,0:T(8,128)S(1)}, u32[]{:S(2)}, u32[]{:S(2)}) collective-permute-start(f32[9,16,32]{2,1,0:T(8,128)S(1)} %get-tuple-element.44), channel_id=1, source_target_pairs={{0,8},{1,9},{2,10},{3,11},{4,12},{5,13},{6,14},{7,15},{8,16},{9,17... | collective-permute-start | bytes 55304 | tf_op jit(solution)/shard_map/ppermute | solution.py:35
  55.1 5.0 %collective-permute-start.6 = (f32[9,16,32]{2,1,0:T(8,128)S(1)}, f32[9,16,32]{2,1,0:T(8,128)S(1)}, u32[]{:S(2)}, u32[]{:S(2)}) collective-permute-start(f32[9,16,32]{2,1,0:T(8,128)S(1)} %get-tuple-element.45), channel_id=1, source_target_pairs={{8,0},{9,1},{10,2},{11,3},{12,4},{13,5},{14,6},{15,7},{16,8},{17,9... | collective-permute-start | bytes 55304 | tf_op jit(solution)/shard_map/ppermute | solution.py:35
  60.1 1.0 collective-permute-done.5
  61.1 1.2 collective-permute-done.6
  62.3 11.6 %collective-permute-start.8 = (f32[3,16,32]{2,1,0:T(8,128)S(1)}, f32[3,16,32]{2,1,0:T(8,128)S(1)}, u32[]{:S(2)}, u32[]{:S(2)}) collective-permute-start(f32[3,16,32]{2,1,0:T(8,128)S(1)} %get-tuple-element.49), channel_id=1, source_target_pairs={{16,0},{17,1},{18,2},{19,3},{20,4},{21,5},{22,6},{23,7},{24,8},{25... | collective-permute-start | bytes 18440 | tf_op jit(solution)/shard_map/ppermute | solution.py:35
  73.9 2.1 %collective-permute-start.7 = (f32[3,16,32]{2,1,0:T(8,128)S(1)}, f32[3,16,32]{2,1,0:T(8,128)S(1)}, u32[]{:S(2)}, u32[]{:S(2)}) collective-permute-start(f32[3,16,32]{2,1,0:T(8,128)S(1)} %get-tuple-element.48), channel_id=1, source_target_pairs={{0,16},{1,17},{2,18},{3,19},{4,20},{5,21},{6,22},{7,23},{8,24},{9,... | collective-permute-start | bytes 18440 | tf_op jit(solution)/shard_map/ppermute | solution.py:35
  76.1 0.7 gather_fusion.8
  76.8 0.7 gather_fusion.7
  77.4 5.8 %collective-permute-done.7 = f32[3,16,32]{2,1,0:T(8,128)S(1)} collective-permute-done((f32[3,16,32]{2,1,0:T(8,128)S(1)}, f32[3,16,32]{2,1,0:T(8,128)S(1)}, u32[]{:S(2)}, u32[]{:S(2)}) %collective-permute-start.7) | collective-permute-done | bytes 6176 | tf_op jit(solution)/shard_map/ppermute | solution.py:35
  83.3 0.6 gather_fusion.9
  84.2 0.9 slice.349
  85.1 0.9 slice.347
  86.5 0.6 copy.56
  87.0 0.8 gather_fusion
  87.8 0.8 gather_fusion.1
  88.6 0.8 gather_fusion.2
  89.3 1.6 %gather_fusion.3 = f32[64,19,64]{2,1,0:T(8,128)} fusion(f32[96,19,64]{2,1,0:T(8,128)S(1)} %bitcast.96, s32[1024]{0:T(1024)} %get-tuple-element.63), kind=kCustom, calls=%fused_computation.3 | custom fusion | bytes 622848 | tf_op jit(solution)/shard_map/jit(_take)/gather | solution.py:45
  91.0 1.7 %gather_fusion.4 = f32[64,19,64]{2,1,0:T(8,128)} fusion(f32[96,19,64]{2,1,0:T(8,128)S(1)} %bitcast.97, s32[1024]{0:T(1024)} %get-tuple-element.62), kind=kCustom, calls=%fused_computation.4 | custom fusion | bytes 622848 | tf_op jit(solution)/shard_map/jit(_take)/gather | solution.py:45
  92.6 1.7 %gather_fusion.5 = f32[64,19,64]{2,1,0:T(8,128)} fusion(f32[96,19,64]{2,1,0:T(8,128)S(1)} %bitcast.98, s32[1024]{0:T(1024)} %get-tuple-element.61), kind=kCustom, calls=%fused_computation.5 | custom fusion | bytes 622848 | tf_op jit(solution)/shard_map/jit(_take)/gather | solution.py:45
  94.3 4.4 %concatenate.89 = f32[64,19,384]{2,1,0:T(8,128)} concatenate(f32[64,19,64]{2,1,0:T(8,128)S(1)} %gather_fusion, f32[64,19,64]{2,1,0:T(8,128)S(1)} %gather_fusion.1, f32[64,19,64]{2,1,0:T(8,128)S(1)} %gather_fusion.2, f32[64,19,64]{2,1,0:T(8,128)} %gather_fusion.3, f32[64,19,64]{2,1,0:T(8,128)} %gather_fusion.4, f32[64,19,64]{2,1,0:T(8,128)} %gather_fusion.5), dimensions={2} | concatenate | bytes 3735552 | tf_op jit(solution)/shard_map/concatenate | solution.py:43
  98.7 2.2 %fusion.40 = (f32[1,64,384]{2,0,1:T(1,128)S(1)}, f32[1,64,384]{2,0,1:T(1,128)S(1)}, f32[1,64,384]{2,0,1:T(1,128)S(1)}) fusion(f32[19,64,384]{2,0,1:T(8,128)} %bitcast.100), kind=kLoop, calls=%fused_computation.131 | loop fusion | bytes 589824 | tf_op jit(solution)/shard_map/slice | solution.py:54
  101.0 0.8 slice.355
  101.8 0.8 slice.354
  102.7 1.6 %gather_fusion.6 = f32[512,512]{1,0:T(8,128)S(1)} fusion(f32[128,512]{1,0:T(8,128)S(1)} %pad_maximum_fusion.1, s32[1024]{0:T(1024)S(1)} %pad_clamp_fusion.3), kind=kCustom, calls=%fused_computation.6 | custom fusion | bytes 2099200 | tf_op jit(solution)/shard_map/jit(_take)/gather | solution.py:182
  104.4 2.6 %gather.44 = f32[64,8,16,32]{3,2,1,0:T(8,128)} reshape(f32[512,512]{1,0:T(8,128)S(1)} %gather_fusion.6) | data formatting | bytes 2097152 | tf_op jit(solution)/shard_map/jit(_take)/gather | solution.py:182
  107.0 8.4 %fusion.6 = f32[64,16,32]{2,1,0:T(8,128)S(1)} fusion(bf16[64,8,32,32]{3,2,1,0:T(8,128)(2,1)} %copy.31, f32[64,8,16,32]{3,2,1,0:T(8,128)} %gather.44, pred[64,8]{1,0:T(8,128)(4,1)S(1)} %copy-done.13), kind=kOutput, calls=%fused_computation.18 | convolution fusion | flops 100925440 | bytes 2228736 | tf_op jit(solution)/shard_map/lfrk,lfkq->lrq/dot_general | solution.py:183
  115.8 5.5 %fusion.11 = f32[16,64,64]{2,0,1:T(8,128)S(1)} fusion(f32[64,64]{1,0:T(8,128)S(1)} %copy-done.15, f32[64,384]{1,0:T(8,128)S(1)} %bitcast.111, f32[64,64]{1,0:T(8,128)S(1)} %copy-done.16, f32[64,384]{1,0:T(8,128)S(1)} %bitcast.112, f32[64,64]{1,0:T(8,128)S(1)} %copy-done.17, f32[64,384]{1,0:T(8,128)S(1)} %bitcast.113, f32[19,64,384]{2,0,1:T(8,128)S(1)} %bitcast.101, ...), kind=kOutput, calls=%fused_computation.23 | convolution fusion | flops 67829760 | bytes 1703936 | tf_op jit(solution)/shard_map/rlm,lbm->rlb/dot_general | solution.py:59
  121.3 0.5 fusion.10
  122.0 0.9 reshape.173
  (129 shorter events, 4.4 us)
Async XLA Ops:
  0.0 5.2 %copy-start.9 = (f32[3,4096]{1,0:T(4,128)S(1)}, f32[3,4096]{1,0:T(4,128)}, u32[]{:S(2)}) copy-start(f32[3,4096]{1,0:T(4,128)} %param.14) | copy-start | bytes 147460
  0.0 12.6 %copy-start.18 = (bf16[1,3,1024]{2,1,0:T(4,128)(2,1)S(1)}, bf16[1,3,1024]{2,1,0:T(4,128)(2,1)}, u32[]{:S(2)}) copy-start(bf16[1,3,1024]{2,1,0:T(4,128)(2,1)} %param.22) | copy-start | bytes 18436
  0.0 12.6 %copy-start.19 = (bf16[1,3,1024]{2,1,0:T(4,128)(2,1)S(1)}, bf16[1,3,1024]{2,1,0:T(4,128)(2,1)}, u32[]{:S(2)}) copy-start(bf16[1,3,1024]{2,1,0:T(4,128)(2,1)} %param.23) | copy-start | bytes 18436
  0.0 12.7 %copy-start.11 = (bf16[64,1024]{1,0:T(8,128)(2,1)S(1)}, bf16[64,1024]{1,0:T(8,128)(2,1)}, u32[]{:S(2)}) copy-start(bf16[64,1024]{1,0:T(8,128)(2,1)} %param.20) | copy-start | bytes 393220
  1.3 13.2 %copy-start.4 = (bf16[16,64,64]{2,1,0:T(8,128)(2,1)}, bf16[16,64,64]{2,1,0:T(8,128)(2,1)S(1)}, u32[]{:S(2)}) copy-start(bf16[16,64,64]{2,1,0:T(8,128)(2,1)S(1)} %reshape.160) | copy-start | bytes 393220
  3.5 14.4 %copy-start.22 = (s32[64,6]{0,1:T(8,128)S(1)}, s32[64,6]{0,1:T(8,128)}, u32[]{:S(2)}) copy-start(s32[64,6]{0,1:T(8,128)} %param.15) | copy-start | bytes 4612
  3.5 14.4 %copy-start.14 = (bf16[1,4,4,1024]{3,2,1,0:T(4,128)(2,1)S(1)}, bf16[1,4,4,1024]{3,2,1,0:T(4,128)(2,1)}, u32[]{:S(2)}) copy-start(bf16[1,4,4,1024]{3,2,1,0:T(4,128)(2,1)} %param.24) | copy-start | bytes 98308
  3.5 16.7 %copy-start.21 = (s32[64,8]{0,1:T(8,128)S(1)}, s32[64,8]{0,1:T(8,128)}, u32[]{:S(2)}) copy-start(s32[64,8]{0,1:T(8,128)} %param.16) | copy-start | bytes 6148
  4.6 17.9 %copy-start.23 = (s32[4]{0:T(128)S(1)}, s32[4]{0:T(128)}, u32[]{:S(2)}) copy-start(s32[4]{0:T(128)} %constant.59) | copy-start | bytes 52
  5.0 31.3 %copy-start.3 = (bf16[64,8,1024]{2,1,0:T(8,128)(2,1)S(1)}, bf16[64,8,1024]{2,1,0:T(8,128)(2,1)}, u32[]{:S(2)}) copy-start(bf16[64,8,1024]{2,1,0:T(8,128)(2,1)} %param.19) | copy-start | bytes 3145732
  5.9 78.2 %collective-permute-start.1 = (f32[35840]{0:T(1024)}, f32[35840]{0:T(1024)}, u32[]{:S(2)}, u32[]{:S(2)}) collective-permute-start(f32[35840]{0:T(1024)} %pad_maximum_fusion.3), channel_id=1, source_target_pairs={{1,0},{2,1},{3,2},{4,3},{5,4},{6,5},{7,6},{8,7},{9,8},{10,9},{11,1... | collective-permute-start | bytes 430088 | tf_op jit(solution)/shard_map/ppermute | solution.py:160
  9.2 76.0 %collective-permute-start = (f32[35840]{0:T(1024)}, f32[35840]{0:T(1024)}, u32[]{:S(2)}, u32[]{:S(2)}) collective-permute-start(f32[35840]{0:T(1024)} %pad_maximum_fusion.2), channel_id=1, source_target_pairs={{0,1},{1,2},{2,3},{3,4},{4,5},{5,6},{6,7},{7,8},{8,9},{9,10},{10,1... | collective-permute-start | bytes 430088 | tf_op jit(solution)/shard_map/ppermute | solution.py:159
  15.2 8.1 %collective-permute-start.2 = (f32[4,16,32]{2,1,0:T(8,128)S(1)}, f32[4,16,32]{2,1,0:T(8,128)S(1)}, u32[]{:S(2)}, u32[]{:S(2)}) collective-permute-start(f32[4,16,32]{2,1,0:T(8,128)S(1)} %convolution_bitcast_fusion.2), channel_id=1, source_target_pairs={{0,1},{1,0},{2,3},{3,2},{4,5},{5,4},{6,7},{7,6},{8,9},{9,8},{10,11... | collective-permute-start | bytes 24584 | tf_op jit(solution)/shard_map/ppermute | solution.py:30
  23.4 7.4 %collective-permute-start.3 = (f32[5,16,32]{2,1,0:T(8,128)S(1)}, f32[5,16,32]{2,1,0:T(8,128)S(1)}, u32[]{:S(2)}, u32[]{:S(2)}) collective-permute-start(f32[5,16,32]{2,1,0:T(8,128)S(1)} %pad_maximum_fusion.17), channel_id=1, source_target_pairs={{0,2},{1,3},{2,0},{3,1},{4,6},{5,7},{6,4},{7,5},{8,10},{9,11},{10,... | collective-permute-start | bytes 30728 | tf_op jit(solution)/shard_map/ppermute | solution.py:30
  31.4 17.9 %collective-permute-start.4 = (f32[8,16,32]{2,1,0:T(8,128)}, f32[8,16,32]{2,1,0:T(8,128)}, u32[]{:S(2)}, u32[]{:S(2)}) collective-permute-start(f32[8,16,32]{2,1,0:T(8,128)} %fusion.18), channel_id=1, source_target_pairs={{0,4},{1,5},{2,6},{3,7},{4,0},{5,1},{6,2},{7,3},{8,12},{9,13},{10,... | collective-permute-start | bytes 49160 | tf_op jit(solution)/shard_map/ppermute | solution.py:30
  36.3 9.1 %copy-start.20 = (pred[64,8]{0,1:T(8,128)(4,1)S(1)}, pred[64,8]{0,1:T(8,128)(4,1)}, u32[]{:S(2)}) copy-start(pred[64,8]{0,1:T(8,128)(4,1)} %get-tuple-element.14) | copy-start | bytes 1540
  37.7 6.9 %copy-start.6 = (f32[64,16,32]{0,2,1:T(8,128)S(1)}, f32[64,16,32]{0,2,1:T(8,128)}, u32[]{:S(2)}) copy-start(f32[64,16,32]{0,2,1:T(8,128)} %copy.23) | copy-start | bytes 393220
  37.8 8.4 %copy-start.7 = (f32[4,32,4,32]{3,1,2,0:T(8,128)S(1)}, f32[4,32,4,32]{3,1,2,0:T(8,128)}, u32[]{:S(2)}) copy-start(f32[4,32,4,32]{3,1,2,0:T(8,128)} %fusion.25) | copy-start | bytes 196612
  37.8 8.6 %copy-start.12 = (bf16[64,1024]{1,0:T(8,128)(2,1)S(1)}, bf16[64,1024]{1,0:T(8,128)(2,1)}, u32[]{:S(2)}) copy-start(bf16[64,1024]{1,0:T(8,128)(2,1)} %param.21) | copy-start | bytes 393220
  37.8 10.2 %copy-start.10 = (bf16[64,2048]{1,0:T(8,128)(2,1)S(1)}, bf16[64,2048]{1,0:T(8,128)(2,1)}, u32[]{:S(2)}) copy-start(bf16[64,2048]{1,0:T(8,128)(2,1)} %param.18) | copy-start | bytes 786436
  51.6 9.5 %collective-permute-start.5 = (f32[9,16,32]{2,1,0:T(8,128)S(1)}, f32[9,16,32]{2,1,0:T(8,128)S(1)}, u32[]{:S(2)}, u32[]{:S(2)}) collective-permute-start(f32[9,16,32]{2,1,0:T(8,128)S(1)} %get-tuple-element.44), channel_id=1, source_target_pairs={{0,8},{1,9},{2,10},{3,11},{4,12},{5,13},{6,14},{7,15},{8,16},{9,17... | collective-permute-start | bytes 55304 | tf_op jit(solution)/shard_map/ppermute | solution.py:35
  55.1 7.2 %collective-permute-start.6 = (f32[9,16,32]{2,1,0:T(8,128)S(1)}, f32[9,16,32]{2,1,0:T(8,128)S(1)}, u32[]{:S(2)}, u32[]{:S(2)}) collective-permute-start(f32[9,16,32]{2,1,0:T(8,128)S(1)} %get-tuple-element.45), channel_id=1, source_target_pairs={{8,0},{9,1},{10,2},{11,3},{12,4},{13,5},{14,6},{15,7},{16,8},{17,9... | collective-permute-start | bytes 55304 | tf_op jit(solution)/shard_map/ppermute | solution.py:35
  62.3 21.0 %collective-permute-start.8 = (f32[3,16,32]{2,1,0:T(8,128)S(1)}, f32[3,16,32]{2,1,0:T(8,128)S(1)}, u32[]{:S(2)}, u32[]{:S(2)}) collective-permute-start(f32[3,16,32]{2,1,0:T(8,128)S(1)} %get-tuple-element.49), channel_id=1, source_target_pairs={{16,0},{17,1},{18,2},{19,3},{20,4},{21,5},{22,6},{23,7},{24,8},{25... | collective-permute-start | bytes 18440 | tf_op jit(solution)/shard_map/ppermute | solution.py:35
  73.9 9.3 %collective-permute-start.7 = (f32[3,16,32]{2,1,0:T(8,128)S(1)}, f32[3,16,32]{2,1,0:T(8,128)S(1)}, u32[]{:S(2)}, u32[]{:S(2)}) collective-permute-start(f32[3,16,32]{2,1,0:T(8,128)S(1)} %get-tuple-element.48), channel_id=1, source_target_pairs={{0,16},{1,17},{2,18},{3,19},{4,20},{5,21},{6,22},{7,23},{8,24},{9,... | collective-permute-start | bytes 18440 | tf_op jit(solution)/shard_map/ppermute | solution.py:35
  94.3 8.4 %copy-start.8 = (f32[64,512]{1,0:T(8,128)S(1)}, f32[64,512]{1,0:T(8,128)}, u32[]{:S(2)}) copy-start(f32[64,512]{1,0:T(8,128)} %copy.24) | copy-start | bytes 393220
  104.3 2.6 %copy-start.13 = (pred[64,8]{1,0:T(8,128)(4,1)S(1)}, pred[64,8]{1,0:T(8,128)(4,1)}, u32[]{:S(2)}) copy-start(pred[64,8]{1,0:T(8,128)(4,1)} %copy.22) | copy-start | bytes 1540
  106.9 8.5 %copy-start.1 = (bf16[64,32,32]{2,1,0:T(8,128)(2,1)S(1)}, bf16[64,32,32]{2,1,0:T(8,128)(2,1)}, u32[]{:S(2)}) copy-start(bf16[64,32,32]{2,1,0:T(8,128)(2,1)} %copy.40) | copy-start | bytes 393220
  106.9 8.8 %copy-start = (f32[64,19,384]{2,1,0:T(8,128)S(1)}, f32[64,19,384]{2,1,0:T(8,128)}, u32[]{:S(2)}) copy-start(f32[64,19,384]{2,1,0:T(8,128)} %concatenate.89) | copy-start | bytes 5603332
  106.9 8.8 %copy-start.5 = (bf16[16,64,64]{2,1,0:T(8,128)(2,1)S(1)}, bf16[16,64,64]{2,1,0:T(8,128)(2,1)}, u32[]{:S(2)}) copy-start(bf16[16,64,64]{2,1,0:T(8,128)(2,1)} %copy-done.4) | copy-start | bytes 393220
  107.0 8.8 %copy-start.15 = (f32[64,64]{1,0:T(8,128)S(1)}, f32[64,64]{1,0:T(8,128)}, u32[]{:S(2)}) copy-start(f32[64,64]{1,0:T(8,128)} %sub.63) | copy-start | bytes 49156
  107.0 8.8 %copy-start.16 = (f32[64,64]{1,0:T(8,128)S(1)}, f32[64,64]{1,0:T(8,128)}, u32[]{:S(2)}) copy-start(f32[64,64]{1,0:T(8,128)} %sub.58) | copy-start | bytes 49156
  107.0 8.8 %copy-start.17 = (f32[64,64]{1,0:T(8,128)S(1)}, f32[64,64]{1,0:T(8,128)}, u32[]{:S(2)}) copy-start(f32[64,64]{1,0:T(8,128)} %sub.53) | copy-start | bytes 49156
  115.8 5.5 %copy-start.2 = (bf16[64,32,64]{2,1,0:T(8,128)(2,1)S(1)}, bf16[64,32,64]{2,1,0:T(8,128)(2,1)}, u32[]{:S(2)}) copy-start(bf16[64,32,64]{2,1,0:T(8,128)(2,1)} %reshape.172) | copy-start | bytes 786436

commit v6 on v5

--- a/solution.py
+++ b/solution.py
@@ -68,7 +68,7 @@
     return jnp.where(bit == 0, jnp.concatenate([own, other]), jnp.concatenate([other, own]))
 
 
-def tree_field(root_coefficients, tree_up, tree_down, tree_coupling, me):
+def tree_weights(tree_up, tree_down, tree_coupling):
     up = tree_up[0].astype(jnp.float32).reshape(TOP_LEVELS, RANK, RANK)
     down = tree_down[0].astype(jnp.float32).reshape(TOP_LEVELS, RANK, RANK)
     cross = tree_coupling[0].astype(jnp.float32).reshape(TOP_LEVELS + 1, 4, RANK, RANK)
@@ -82,27 +82,22 @@
     push3 = mm(down[2], push2)
     pushes = jnp.stack([eye, push1, push2, push3])
     weights = jnp.einsum("sqkp,spm->sqkm", cross, pushes, precision=highest)
-
-    p = jnp.einsum("rk,skq->srq", root_coefficients, lifts, precision=highest)
-
+    return lifts, weights
+
+
+def tree_field(p, partner_p, weights, me):
     bit0 = me & 1
-    bit1 = (me >> 1) & 1
+    pair = (me >> 1) & 3
     bit2 = (me >> 2) & 1
-    got1 = swap_with(p, 1)
-    pairs0 = ordered(bit0, p[0:1], got1[0:1])
-    coef1 = p[1] + got1[1]
-    part2 = p[2] + got1[2]
-    part3 = p[3] + got1[3]
-    got2 = swap_with(jnp.concatenate([pairs0, coef1[None], part2[None], part3[None]]), 2)
-    quads0 = ordered(bit1, pairs0, got2[0:2])
-    pairs1 = ordered(bit1, coef1[None], got2[2:3])
-    coef2 = part2 + got2[3]
-    part3 = part3 + got2[4]
-    got3 = swap_with(jnp.concatenate([quads0, pairs1, coef2[None], part3[None]]), 4)
-    octs0 = ordered(bit2, quads0, got3[0:4])
-    quads1 = ordered(bit2, pairs1, got3[4:6])
-    pairs2 = ordered(bit2, coef2[None], got3[6:7])
-    coef3 = (part3 + got3[7])[None]
+    pairs0 = ordered(bit0, p[0:1], partner_p[0:1])
+    summed = p[1:4] + partner_p[1:4]
+    mine = jnp.concatenate([pairs0, summed])
+    held = jnp.stack([mine, swap_with(mine, 2), swap_with(mine, 4), swap_with(mine, 6)])
+    node_pairs = jnp.take(held, pair ^ jnp.arange(4, dtype=jnp.int32), axis=0, mode="clip")
+    octs0 = node_pairs[:, 0:2].reshape(8, RHS, RANK)
+    quads1 = node_pairs[:, 2]
+    pairs2 = node_pairs[0::2, 3] + node_pairs[1::2, 3]
+    coef3 = jnp.sum(node_pairs[:, 4], axis=0)[None]
 
     node = 8
     ahead1 = receive_from(jnp.concatenate([octs0[0:3], quads1[0:3], pairs2, coef3]), node)
@@ -117,7 +112,7 @@
     window2 = jnp.concatenate([behind2[0:1], behind1[6:8], pairs2, ahead1[6:8], ahead2[0:1]])
     steps = jnp.array(partner_steps, dtype=jnp.int32) + 3
     chosen0 = jnp.take(window0, (me & 7) + steps, axis=0, mode="clip")
-    chosen1 = jnp.take(window1, ((me >> 1) & 3) + steps, axis=0, mode="clip")
+    chosen1 = jnp.take(window1, pair + steps, axis=0, mode="clip")
     chosen2 = jnp.take(window2, bit2 + steps, axis=0, mode="clip")
     chosen3 = jnp.concatenate([behind3, behind2[1:2], ahead2[1:2], ahead3])
     chosen = jnp.stack([chosen0, chosen1, chosen2, chosen3])
@@ -150,15 +145,31 @@
     )
     coef_rows = leaf_coefficients.reshape(leaf_count, RHS * RANK)
 
+    root_coefficients = jnp.einsum(
+        "lrk,lkq->rq",
+        leaf_coefficients,
+        leaf_up.reshape(leaf_count, RANK, RANK),
+        precision=highest,
+        preferred_element_type=jnp.float32,
+    )
+    lifts, weights = tree_weights(tree_up, tree_down, tree_coupling)
+    p = jnp.einsum("rk,skq->srq", root_coefficients, lifts, precision=highest)
+
     packed = jnp.concatenate([sources.astype(jnp.float32), points], axis=0)
     width = NEAR_REACH * CLUSTER
     to_right = jnp.concatenate(
-        [packed[:, -width:].reshape(-1), coef_rows[-FAR_REACH:].reshape(-1)]
-    )
-    to_left = jnp.concatenate([packed[:, :width].reshape(-1), coef_rows[:FAR_REACH].reshape(-1)])
+        [packed[:, -width:].reshape(-1), coef_rows[-FAR_REACH:].reshape(-1), p.reshape(-1)]
+    )
+    to_left = jnp.concatenate(
+        [packed[:, :width].reshape(-1), coef_rows[:FAR_REACH].reshape(-1), p.reshape(-1)]
+    )
     from_left = lax.ppermute(to_right, AXES, [(i, i + 1) for i in range(n - 1)])
     from_right = lax.ppermute(to_left, AXES, [(i + 1, i) for i in range(n - 1)])
     split = (RHS + 3) * width
+    split2 = split + FAR_REACH * RHS * RANK
+    partner_p = jnp.where(
+        (me & 1) == 0, from_right[split2:], from_left[split2:]
+    ).reshape(TOP_LEVELS + 1, RHS, RANK)
     extended = jnp.concatenate(
         [
             from_left[:split].reshape(RHS + 3, width),
@@ -169,9 +180,9 @@
     ).reshape(RHS + 3, leaf_count + 2 * NEAR_REACH, CLUSTER)
     rimmed = jnp.concatenate(
         [
-            from_left[split:].reshape(FAR_REACH, RHS * RANK),
+            from_left[split:split2].reshape(FAR_REACH, RHS * RANK),
             coef_rows,
-            from_right[split:].reshape(FAR_REACH, RHS * RANK),
+            from_right[split:split2].reshape(FAR_REACH, RHS * RANK),
         ]
     )
 
@@ -187,14 +198,7 @@
         precision=highest,
         preferred_element_type=jnp.float32,
     )
-    root_coefficients = jnp.einsum(
-        "lrk,lkq->rq",
-        leaf_coefficients,
-        leaf_up.reshape(leaf_count, RANK, RANK),
-        precision=highest,
-        preferred_element_type=jnp.float32,
-    )
-    downward = tree_field(root_coefficients, tree_up, tree_down, tree_coupling, me)
+    downward = tree_field(p, partner_p, weights, me)
     from_root = jnp.einsum(
         "rk,lkq->lrq",
         downward,

time: 124 us -> 127 us (1.024)
  the two profiles are of different devices: /device:TPU:394 before, /device:TPU:392 now
where the time goes in v6:
time: 127 us; the launch traced here: 126 us
  local copies, waits for them, and re-layouts  52 us (41%)
  starting transfers between devices  37.6 us (30%)
  matrix products  18.8 us (15%)
  other arithmetic  8.37 us (7%)
  waiting for transfers between devices  7.94 us (6%)
    ppermute x4, starting transfers between devices, receive_from(): lax.ppermute(value, AXES, [(s, s - step) for s in range(n) if 0 <= s - st...  21.9 us
    ppermute x3, starting transfers between devices, swap_with(): return lax.ppermute(value, AXES, [(i, i ^ mask) for i in range(n)])  9.83 us
    ppermute x4, waiting for transfers between devices, receive_from(): lax.ppermute(value, AXES, [(s, s - step) for s in range(n) if 0 <= s - st...  7.93 us
    gather x6, local copies, waits for them, and re-layouts, near_field(): jnp.take(by_leaf, base + near_offsets[:, near_slot], axis=0, mode='clip')  7.21 us
    reshape x1, local copies, waits for them, and re-layouts, local(): leaf_coupling.reshape(leaf_count, FAR_BLOCKS, RANK, RANK)  6.79 us
    dot_general x1, matrix products, near_field(): jnp.einsum('rlm,lbm->rlb', values, kernel, preferred_element_type=jnp.flo...  6.53 us
    dot_general x1, matrix products, local(): jnp.einsum('lfrk,lfkq->lrq', partner_blocks, leaf_coupling.reshape(leaf_c...  6.16 us
    unnamed x60, local copies, waits for them, and re-layouts  5.29 us
  transfers between devices with their start and end apart: 9, of which 3 were waited for; matrix products, arithmetic and copies ran while one was open for 49% of the time, Pallas kernels for 0%

profile of v6, /device:TPU:392, one launch (start us, length us, event | category | flops | bytes accessed | tf_op | source)
XLA Modules:
  0.0 125.6 jit_solution(13959319469499349820)
XLA Ops:
  0.0 1.9 %reshape.208 = bf16[16,64,64]{2,1,0:T(8,128)(2,1)} reshape(bf16[16,4096]{1,0:T(8,128)(2,1)} %param.13) | data formatting | bytes 262144 | tf_op jit(solution)/shard_map/reshape | solution.py:139
  2.0 0.9 convert_element_type.28
  2.9 1.2 copy.21
  4.2 1.1 copy.23
  5.2 1.1 copy.24
  6.3 0.8 copy.37
  7.1 1.3 %fusion.13 = f32[64,16,32]{2,1,0:T(8,128)S(1)} fusion(bf16[64,64,32]{1,2,0:T(8,128)(2,1)S(1)} %copy.23, bf16[16,64,64]{2,1,0:T(8,128)(2,1)} %reshape.208), kind=kOutput, calls=%fused_computation.34 | convolution fusion | flops 4194304 | bytes 524288 | tf_op jit(solution)/shard_map/rla,lak->lrk/dot_general | solution.py:140
  8.5 0.8 fusion.44
  10.5 0.7 pad_maximum_fusion.3
  11.3 4.0 %collective-permute-start.1 = (f32[37888]{0:T(1024)}, f32[37888]{0:T(1024)}, u32[]{:S(2)}, u32[]{:S(2)}) collective-permute-start(f32[37888]{0:T(1024)} %get-tuple-element.45), channel_id=1, source_target_pairs={{1,0},{2,1},{3,2},{4,3},{5,4},{6,5},{7,6},{8,7},{9,8},{10,9},{11,1... | collective-permute-start | bytes 454664 | tf_op jit(solution)/shard_map/ppermute | solution.py:167
  15.2 1.9 %collective-permute-start = (f32[37888]{0:T(1024)}, f32[37888]{0:T(1024)}, u32[]{:S(2)}, u32[]{:S(2)}) collective-permute-start(f32[37888]{0:T(1024)} %get-tuple-element.44), channel_id=1, source_target_pairs={{0,1},{1,2},{2,3},{3,4},{4,5},{5,6},{6,7},{7,8},{8,9},{9,10},{10,1... | collective-permute-start | bytes 454664 | tf_op jit(solution)/shard_map/ppermute | solution.py:166
  17.4 0.6 compare_and_fusion
  18.2 0.9 reshape.220
  19.4 0.6 pad_clamp_fusion.3
  20.0 0.6 pad_clamp_fusion.9
  20.6 0.6 pad_clamp_fusion.7
  21.2 0.6 pad_clamp_fusion.5
  22.1 0.6 broadcast_add_fusion.2
  22.7 2.2 %fusion.22 = f32[4,32,4,32]{3,1,2,0:T(8,128)} fusion(bf16[4,4,32,32]{3,2,1,0:T(8,128)(2,1)S(1)} %reshape.220, f32[1,32,32]{2,1,0:T(8,128)} %copy-done.15, f32[1,32,32]{2,1,0:T(8,128)S(1)} %convolution_bitcast_fusion.3, f32[1,32,32]{2,1,0:T(8,128)S(1)} %bitcast.145, f32[1,32,32]{2,1,0:T(8,128)S(1)} %reshape.225), kind=kOutput, calls=%fused_computation.59 | convolution fusion | flops 6303744 | bytes 114688 | tf_op jit(solution)/shard_map/sqkp,spm->sqkm/dot_general | solution.py:84
  24.8 1.0 copy.27
  25.8 0.7 sub.63
  26.5 0.7 sub.58
  27.2 0.7 sub.53
  27.9 1.4 %copy.30 = bf16[64,8,1024]{0,2,1:T(8,128)(2,1)S(1)} copy(bf16[64,8,1024]{2,1,0:T(8,128)(2,1)S(1)} %copy-done.5) | data formatting | bytes 2097152 | tf_op args[6]
  29.3 6.8 %copy.38 = bf16[64,8,32,32]{3,2,1,0:T(8,128)(2,1)} copy(bf16[64,8,32,32]{0,3,2,1:T(8,128)(2,1)S(1)} %bitcast.135) | data formatting | bytes 2097152 | tf_op jit(solution)/shard_map/reshape | solution.py:197
  36.1 0.8 copy.28
  37.0 0.9 copy.66
  38.0 1.5 %copy.46 = bf16[64,32,32]{2,1,0:T(8,128)(2,1)} copy(bf16[64,32,32]{0,2,1:T(8,128)(2,1)S(1)} %bitcast.141) | data formatting | bytes 262144 | tf_op jit(solution)/shard_map/reshape | solution.py:205
  39.6 1.3 %reshape.222 = bf16[64,32,64]{2,1,0:T(8,128)(2,1)} reshape(bf16[64,2048]{1,0:T(8,128)(2,1)S(1)} %copy-done.12) | data formatting | bytes 524288 | tf_op jit(solution)/shard_map/reshape | solution.py:213
  40.9 0.6 pad_clamp_fusion.1
  41.5 0.7 slice_select_fusion
  42.4 0.7 fusion.37
  43.0 3.7 %collective-permute-start.4 = (f32[5,16,32]{2,1,0:T(8,128)}, f32[5,16,32]{2,1,0:T(8,128)}, u32[]{:S(2)}, u32[]{:S(2)}) collective-permute-start(f32[5,16,32]{2,1,0:T(8,128)} %get-tuple-element.34), channel_id=1, source_target_pairs={{0,6},{1,7},{2,4},{3,5},{4,2},{5,3},{6,0},{7,1},{8,14},{9,15},{10,... | collective-permute-start | bytes 30728 | tf_op jit(solution)/shard_map/ppermute | solution.py:30
  46.8 3.1 %collective-permute-start.3 = (f32[5,16,32]{2,1,0:T(8,128)}, f32[5,16,32]{2,1,0:T(8,128)}, u32[]{:S(2)}, u32[]{:S(2)}) collective-permute-start(f32[5,16,32]{2,1,0:T(8,128)} %get-tuple-element.34), channel_id=1, source_target_pairs={{0,4},{1,5},{2,6},{3,7},{4,0},{5,1},{6,2},{7,3},{8,12},{9,13},{10,... | collective-permute-start | bytes 30728 | tf_op jit(solution)/shard_map/ppermute | solution.py:30
  49.9 3.0 %collective-permute-start.2 = (f32[5,16,32]{2,1,0:T(8,128)}, f32[5,16,32]{2,1,0:T(8,128)}, u32[]{:S(2)}, u32[]{:S(2)}) collective-permute-start(f32[5,16,32]{2,1,0:T(8,128)} %get-tuple-element.34), channel_id=1, source_target_pairs={{0,2},{1,3},{2,0},{3,1},{4,6},{5,7},{6,4},{7,5},{8,10},{9,11},{10,... | collective-permute-start | bytes 30728 | tf_op jit(solution)/shard_map/ppermute | solution.py:30
  52.9 0.9 slice.381
  53.8 0.9 slice.379
  55.7 0.8 gather_fusion
  56.5 0.8 gather_fusion.1
  57.2 0.8 gather_fusion.2
  58.0 1.6 %gather_fusion.3 = f32[64,19,64]{2,1,0:T(8,128)} fusion(f32[96,19,64]{2,1,0:T(8,128)S(1)} %bitcast.132, s32[1024]{0:T(1024)} %get-tuple-element.59), kind=kCustom, calls=%fused_computation.3 | custom fusion | bytes 622848 | tf_op jit(solution)/shard_map/jit(_take)/gather | solution.py:45
  59.6 1.7 %gather_fusion.4 = f32[64,19,64]{2,1,0:T(8,128)} fusion(f32[96,19,64]{2,1,0:T(8,128)S(1)} %bitcast.133, s32[1024]{0:T(1024)} %get-tuple-element.58), kind=kCustom, calls=%fused_computation.4 | custom fusion | bytes 622848 | tf_op jit(solution)/shard_map/jit(_take)/gather | solution.py:45
  61.3 1.6 %gather_fusion.5 = f32[64,19,64]{2,1,0:T(8,128)} fusion(f32[96,19,64]{2,1,0:T(8,128)S(1)} %bitcast.134, s32[1024]{0:T(1024)} %get-tuple-element.57), kind=kCustom, calls=%fused_computation.5 | custom fusion | bytes 622848 | tf_op jit(solution)/shard_map/jit(_take)/gather | solution.py:45
  62.9 4.4 %concatenate.56 = f32[64,19,384]{2,1,0:T(8,128)} concatenate(f32[64,19,64]{2,1,0:T(8,128)S(1)} %gather_fusion, f32[64,19,64]{2,1,0:T(8,128)S(1)} %gather_fusion.1, f32[64,19,64]{2,1,0:T(8,128)S(1)} %gather_fusion.2, f32[64,19,64]{2,1,0:T(8,128)} %gather_fusion.3, f32[64,19,64]{2,1,0:T(8,128)} %gather_fusion.4, f32[64,19,64]{2,1,0:T(8,128)} %gather_fusion.5), dimensions={2} | concatenate | bytes 3735552 | tf_op jit(solution)/shard_map/concatenate | solution.py:43
  67.4 2.2 %fusion.38 = (f32[1,64,384]{2,0,1:T(1,128)S(1)}, f32[1,64,384]{2,0,1:T(1,128)S(1)}, f32[1,64,384]{2,0,1:T(1,128)S(1)}) fusion(f32[19,64,384]{2,0,1:T(8,128)} %bitcast.136), kind=kLoop, calls=%fused_computation.130 | loop fusion | bytes 589824 | tf_op jit(solution)/shard_map/slice | solution.py:54
  69.5 0.7 copy.68
  70.2 0.6 copy.69
  70.8 0.8 slice.387
  71.7 0.8 slice.386
  72.6 1.6 %gather_fusion.6 = f32[512,512]{1,0:T(8,128)S(1)} fusion(f32[128,512]{1,0:T(8,128)S(1)} %pad_maximum_fusion.1, s32[1024]{0:T(1024)S(1)} %pad_clamp_fusion.4), kind=kCustom, calls=%fused_computation.6 | custom fusion | bytes 2099200 | tf_op jit(solution)/shard_map/jit(_take)/gather | solution.py:193
  74.2 2.6 %gather.48 = f32[64,8,16,32]{3,2,1,0:T(8,128)} reshape(f32[512,512]{1,0:T(8,128)S(1)} %gather_fusion.6) | data formatting | bytes 2097152 | tf_op jit(solution)/shard_map/jit(_take)/gather | solution.py:193
  76.8 6.5 %fusion.11 = f32[16,64,64]{2,0,1:T(8,128)} fusion(f32[64,64]{1,0:T(8,128)S(1)} %copy-done.16, f32[64,384]{1,0:T(8,128)S(1)} %bitcast.149, f32[64,64]{1,0:T(8,128)} %sub.58, f32[64,384]{1,0:T(8,128)} %bitcast.150, f32[64,64]{1,0:T(8,128)} %sub.53, f32[64,384]{1,0:T(8,128)} %bitcast.151, f32[19,64,384]{2,0,1:T(8,128)S(1)} %bitcast.137, ...), kind=kOutput, calls=%fused_computation.24 | convolution fusion | flops 67829760 | bytes 1540096 | tf_op jit(solution)/shard_map/rlm,lbm->rlb/dot_general | solution.py:59
  83.4 6.2 %fusion.6 = f32[64,16,32]{2,1,0:T(8,128)S(1)} fusion(bf16[64,8,32,32]{3,2,1,0:T(8,128)(2,1)S(1)} %copy-done, f32[64,8,16,32]{3,2,1,0:T(8,128)S(1)} %copy-done.1, pred[64,8]{1,0:T(8,128)(4,1)S(1)} %copy.26), kind=kOutput, calls=%fused_computation.19 | convolution fusion | flops 100925440 | bytes 2228736 | tf_op jit(solution)/shard_map/lfrk,lfkq->lrq/dot_general | solution.py:194
  89.6 0.9 pad_maximum_fusion.4
  90.5 0.7 gather_fusion.7
  91.3 3.5 %collective-permute-start.5 = (f32[9,16,32]{2,1,0:T(8,128)S(1)}, f32[9,16,32]{2,1,0:T(8,128)S(1)}, u32[]{:S(2)}, u32[]{:S(2)}) collective-permute-start(f32[9,16,32]{2,1,0:T(8,128)S(1)} %get-tuple-element.38), channel_id=1, source_target_pairs={{0,8},{1,9},{2,10},{3,11},{4,12},{5,13},{6,14},{7,15},{8,16},{9,17... | collective-permute-start | bytes 55304 | tf_op jit(solution)/shard_map/ppermute | solution.py:35
  94.8 4.7 %collective-permute-start.6 = (f32[9,16,32]{2,1,0:T(8,128)S(1)}, f32[9,16,32]{2,1,0:T(8,128)S(1)}, u32[]{:S(2)}, u32[]{:S(2)}) collective-permute-start(f32[9,16,32]{2,1,0:T(8,128)S(1)} %get-tuple-element.39), channel_id=1, source_target_pairs={{8,0},{9,1},{10,2},{11,3},{12,4},{13,5},{14,6},{15,7},{16,8},{17,9... | collective-permute-start | bytes 55304 | tf_op jit(solution)/shard_map/ppermute | solution.py:35
  99.9 1.6 %collective-permute-done.6 = f32[9,16,32]{2,1,0:T(8,128)S(1)} collective-permute-done((f32[9,16,32]{2,1,0:T(8,128)S(1)}, f32[9,16,32]{2,1,0:T(8,128)S(1)}, u32[]{:S(2)}, u32[]{:S(2)}) %collective-permute-start.6) | collective-permute-done | bytes 18464 | tf_op jit(solution)/shard_map/ppermute | solution.py:35
  101.5 11.8 %collective-permute-start.8 = (f32[3,16,32]{2,1,0:T(8,128)S(1)}, f32[3,16,32]{2,1,0:T(8,128)S(1)}, u32[]{:S(2)}, u32[]{:S(2)}) collective-permute-start(f32[3,16,32]{2,1,0:T(8,128)S(1)} %get-tuple-element.43), channel_id=1, source_target_pairs={{16,0},{17,1},{18,2},{19,3},{20,4},{21,5},{22,6},{23,7},{24,8},{25... | collective-permute-start | bytes 18440 | tf_op jit(solution)/shard_map/ppermute | solution.py:35
  113.3 1.9 %collective-permute-start.7 = (f32[3,16,32]{2,1,0:T(8,128)S(1)}, f32[3,16,32]{2,1,0:T(8,128)S(1)}, u32[]{:S(2)}, u32[]{:S(2)}) collective-permute-start(f32[3,16,32]{2,1,0:T(8,128)S(1)} %get-tuple-element.42), channel_id=1, source_target_pairs={{0,16},{1,17},{2,18},{3,19},{4,20},{5,21},{6,22},{7,23},{8,24},{9,... | collective-permute-start | bytes 18440 | tf_op jit(solution)/shard_map/ppermute | solution.py:35
  115.3 0.7 gather_fusion.9
  116.0 0.7 gather_fusion.8
  116.6 6.0 %collective-permute-done.7 = f32[3,16,32]{2,1,0:T(8,128)S(1)} collective-permute-done((f32[3,16,32]{2,1,0:T(8,128)S(1)}, f32[3,16,32]{2,1,0:T(8,128)S(1)}, u32[]{:S(2)}, u32[]{:S(2)}) %collective-permute-start.7) | collective-permute-done | bytes 6176 | tf_op jit(solution)/shard_map/ppermute | solution.py:35
  124.7 0.9 reshape.223
  (134 shorter events, 6.2 us)
Async XLA Ops:
  0.0 9.3 %copy-start.17 = (bf16[1,3,1024]{2,1,0:T(4,128)(2,1)S(1)}, bf16[1,3,1024]{2,1,0:T(4,128)(2,1)}, u32[]{:S(2)}) copy-start(bf16[1,3,1024]{2,1,0:T(4,128)(2,1)} %param.22) | copy-start | bytes 18436
  0.0 9.6 %copy-start.18 = (bf16[1,3,1024]{2,1,0:T(4,128)(2,1)S(1)}, bf16[1,3,1024]{2,1,0:T(4,128)(2,1)}, u32[]{:S(2)}) copy-start(bf16[1,3,1024]{2,1,0:T(4,128)(2,1)} %param.23) | copy-start | bytes 18436
  0.0 10.3 %copy-start.11 = (f32[3,4096]{1,0:T(4,128)S(1)}, f32[3,4096]{1,0:T(4,128)}, u32[]{:S(2)}) copy-start(f32[3,4096]{1,0:T(4,128)} %param.14) | copy-start | bytes 147460
  0.0 10.3 %copy-start.15 = (f32[1,32,32]{2,1,0:T(8,128)}, f32[1,32,32]{2,1,0:T(8,128)S(1)}, u32[]{:S(2)}) copy-start(f32[1,32,32]{2,1,0:T(8,128)S(1)} %fusion.32) | copy-start | bytes 12292
  4.1 13.3 %copy-start.21 = (s32[64,6]{0,1:T(8,128)S(1)}, s32[64,6]{0,1:T(8,128)}, u32[]{:S(2)}) copy-start(s32[64,6]{0,1:T(8,128)} %param.15) | copy-start | bytes 4612
  4.1 13.3 %copy-start.20 = (s32[64,8]{0,1:T(8,128)S(1)}, s32[64,8]{0,1:T(8,128)}, u32[]{:S(2)}) copy-start(s32[64,8]{0,1:T(8,128)} %param.16) | copy-start | bytes 6148
  4.1 17.9 %copy-start.24 = (s32[4]{0:T(128)S(1)}, s32[4]{0:T(128)}, u32[]{:S(2)}) copy-start(s32[4]{0:T(128)} %constant.61) | copy-start | bytes 52
  6.3 21.5 %copy-start.5 = (bf16[64,8,1024]{2,1,0:T(8,128)(2,1)S(1)}, bf16[64,8,1024]{2,1,0:T(8,128)(2,1)}, u32[]{:S(2)}) copy-start(bf16[64,8,1024]{2,1,0:T(8,128)(2,1)} %param.19) | copy-start | bytes 3145732
  11.3 30.2 %collective-permute-start.1 = (f32[37888]{0:T(1024)}, f32[37888]{0:T(1024)}, u32[]{:S(2)}, u32[]{:S(2)}) collective-permute-start(f32[37888]{0:T(1024)} %get-tuple-element.45), channel_id=1, source_target_pairs={{1,0},{2,1},{3,2},{4,3},{5,4},{6,5},{7,6},{8,7},{9,8},{10,9},{11,1... | collective-permute-start | bytes 454664 | tf_op jit(solution)/shard_map/ppermute | solution.py:167
  15.2 26.2 %collective-permute-start = (f32[37888]{0:T(1024)}, f32[37888]{0:T(1024)}, u32[]{:S(2)}, u32[]{:S(2)}) collective-permute-start(f32[37888]{0:T(1024)} %get-tuple-element.44), channel_id=1, source_target_pairs={{0,1},{1,2},{2,3},{3,4},{4,5},{5,6},{6,7},{7,8},{8,9},{9,10},{10,1... | collective-permute-start | bytes 454664 | tf_op jit(solution)/shard_map/ppermute | solution.py:166
  27.9 9.0 %copy-start.19 = (pred[64,8]{0,1:T(8,128)(4,1)S(1)}, pred[64,8]{0,1:T(8,128)(4,1)}, u32[]{:S(2)}) copy-start(pred[64,8]{0,1:T(8,128)(4,1)} %get-tuple-element.14) | copy-start | bytes 1540
  29.3 6.9 %copy-start.6 = (f32[64,16,32]{0,2,1:T(8,128)S(1)}, f32[64,16,32]{0,2,1:T(8,128)}, u32[]{:S(2)}) copy-start(f32[64,16,32]{0,2,1:T(8,128)} %copy.27) | copy-start | bytes 393220
  29.3 7.7 %copy-start.7 = (f32[4,32,4,32]{3,1,2,0:T(8,128)S(1)}, f32[4,32,4,32]{3,1,2,0:T(8,128)}, u32[]{:S(2)}) copy-start(f32[4,32,4,32]{3,1,2,0:T(8,128)} %fusion.22) | copy-start | bytes 196612
  29.3 8.6 %copy-start.14 = (bf16[64,1024]{1,0:T(8,128)(2,1)S(1)}, bf16[64,1024]{1,0:T(8,128)(2,1)}, u32[]{:S(2)}) copy-start(bf16[64,1024]{1,0:T(8,128)(2,1)} %param.21) | copy-start | bytes 393220
  29.3 10.3 %copy-start.12 = (bf16[64,2048]{1,0:T(8,128)(2,1)S(1)}, bf16[64,2048]{1,0:T(8,128)(2,1)}, u32[]{:S(2)}) copy-start(bf16[64,2048]{1,0:T(8,128)(2,1)} %param.18) | copy-start | bytes 786436
  29.3 11.6 %copy-start.22 = (s32[4]{0:T(128)S(1)}, s32[4]{0:T(128)}, u32[]{:S(2)}) copy-start(s32[4]{0:T(128)} %get-tuple-element.52) | copy-start | bytes 52
  29.3 11.6 %copy-start.23 = (s32[4]{0:T(128)S(1)}, s32[4]{0:T(128)}, u32[]{:S(2)}) copy-start(s32[4]{0:T(128)} %get-tuple-element.54) | copy-start | bytes 52
  43.0 46.5 %collective-permute-start.4 = (f32[5,16,32]{2,1,0:T(8,128)}, f32[5,16,32]{2,1,0:T(8,128)}, u32[]{:S(2)}, u32[]{:S(2)}) collective-permute-start(f32[5,16,32]{2,1,0:T(8,128)} %get-tuple-element.34), channel_id=1, source_target_pairs={{0,6},{1,7},{2,4},{3,5},{4,2},{5,3},{6,0},{7,1},{8,14},{9,15},{10,... | collective-permute-start | bytes 30728 | tf_op jit(solution)/shard_map/ppermute | solution.py:30
  46.8 42.8 %collective-permute-start.3 = (f32[5,16,32]{2,1,0:T(8,128)}, f32[5,16,32]{2,1,0:T(8,128)}, u32[]{:S(2)}, u32[]{:S(2)}) collective-permute-start(f32[5,16,32]{2,1,0:T(8,128)} %get-tuple-element.34), channel_id=1, source_target_pairs={{0,4},{1,5},{2,6},{3,7},{4,0},{5,1},{6,2},{7,3},{8,12},{9,13},{10,... | collective-permute-start | bytes 30728 | tf_op jit(solution)/shard_map/ppermute | solution.py:30
  49.9 39.7 %collective-permute-start.2 = (f32[5,16,32]{2,1,0:T(8,128)}, f32[5,16,32]{2,1,0:T(8,128)}, u32[]{:S(2)}, u32[]{:S(2)}) collective-permute-start(f32[5,16,32]{2,1,0:T(8,128)} %get-tuple-element.34), channel_id=1, source_target_pairs={{0,2},{1,3},{2,0},{3,1},{4,6},{5,7},{6,4},{7,5},{8,10},{9,11},{10,... | collective-permute-start | bytes 30728 | tf_op jit(solution)/shard_map/ppermute | solution.py:30
  62.9 9.6 %copy-start.9 = (f32[64,512]{1,0:T(8,128)S(1)}, f32[64,512]{1,0:T(8,128)}, u32[]{:S(2)}) copy-start(f32[64,512]{1,0:T(8,128)} %copy.28) | copy-start | bytes 393220
  74.2 2.6 %copy-start.2 = (f32[64,19,384]{2,1,0:T(8,128)S(1)}, f32[64,19,384]{2,1,0:T(8,128)}, u32[]{:S(2)}) copy-start(f32[64,19,384]{2,1,0:T(8,128)} %concatenate.56) | copy-start | bytes 5603332
  74.2 2.6 %copy-start.16 = (f32[64,64]{1,0:T(8,128)S(1)}, f32[64,64]{1,0:T(8,128)}, u32[]{:S(2)}) copy-start(f32[64,64]{1,0:T(8,128)} %sub.63) | copy-start | bytes 49156
  76.8 6.5 %copy-start = (bf16[64,8,32,32]{3,2,1,0:T(8,128)(2,1)S(1)}, bf16[64,8,32,32]{3,2,1,0:T(8,128)(2,1)}, u32[]{:S(2)}) copy-start(bf16[64,8,32,32]{3,2,1,0:T(8,128)(2,1)} %copy.38) | copy-start | bytes 3145732
  76.8 6.5 %copy-start.1 = (f32[64,8,16,32]{3,2,1,0:T(8,128)S(1)}, f32[64,8,16,32]{3,2,1,0:T(8,128)}, u32[]{:S(2)}) copy-start(f32[64,8,16,32]{3,2,1,0:T(8,128)} %gather.48) | copy-start | bytes 3145732
  83.4 6.2 %copy-start.13 = (f32[1,5,16,32]{3,2,1,0:T(8,128)S(1)}, f32[1,5,16,32]{3,2,1,0:T(8,128)}, u32[]{:S(2)}) copy-start(f32[1,5,16,32]{3,2,1,0:T(8,128)} %get-tuple-element.33) | copy-start | bytes 30724
  83.4 39.9 %copy-start.8 = (f32[4,32,4,32]{3,2,1,0:T(4,128)S(1)}, f32[4,32,4,32]{3,2,1,0:T(4,128)}, u32[]{:S(2)}) copy-start(f32[4,32,4,32]{3,2,1,0:T(4,128)} %copy.66) | copy-start | bytes 196612
  83.4 40.2 %copy-start.3 = (bf16[64,32,32]{2,1,0:T(8,128)(2,1)S(1)}, bf16[64,32,32]{2,1,0:T(8,128)(2,1)}, u32[]{:S(2)}) copy-start(bf16[64,32,32]{2,1,0:T(8,128)(2,1)} %copy.46) | copy-start | bytes 393220
  89.6 34.4 %copy-start.4 = (bf16[64,32,64]{2,1,0:T(8,128)(2,1)S(1)}, bf16[64,32,64]{2,1,0:T(8,128)(2,1)}, u32[]{:S(2)}) copy-start(bf16[64,32,64]{2,1,0:T(8,128)(2,1)} %reshape.222) | copy-start | bytes 786436
  89.6 34.4 %copy-start.10 = (f32[16,64,64]{2,0,1:T(8,128)S(1)}, f32[16,64,64]{2,0,1:T(8,128)}, u32[]{:S(2)}) copy-start(f32[16,64,64]{2,0,1:T(8,128)} %fusion.11) | copy-start | bytes 786436
  91.3 8.6 %collective-permute-start.5 = (f32[9,16,32]{2,1,0:T(8,128)S(1)}, f32[9,16,32]{2,1,0:T(8,128)S(1)}, u32[]{:S(2)}, u32[]{:S(2)}) collective-permute-start(f32[9,16,32]{2,1,0:T(8,128)S(1)} %get-tuple-element.38), channel_id=1, source_target_pairs={{0,8},{1,9},{2,10},{3,11},{4,12},{5,13},{6,14},{7,15},{8,16},{9,17... | collective-permute-start | bytes 55304 | tf_op jit(solution)/shard_map/ppermute | solution.py:35
  94.8 6.7 %collective-permute-start.6 = (f32[9,16,32]{2,1,0:T(8,128)S(1)}, f32[9,16,32]{2,1,0:T(8,128)S(1)}, u32[]{:S(2)}, u32[]{:S(2)}) collective-permute-start(f32[9,16,32]{2,1,0:T(8,128)S(1)} %get-tuple-element.39), channel_id=1, source_target_pairs={{8,0},{9,1},{10,2},{11,3},{12,4},{13,5},{14,6},{15,7},{16,8},{17,9... | collective-permute-start | bytes 55304 | tf_op jit(solution)/shard_map/ppermute | solution.py:35
  101.5 21.1 %collective-permute-start.8 = (f32[3,16,32]{2,1,0:T(8,128)S(1)}, f32[3,16,32]{2,1,0:T(8,128)S(1)}, u32[]{:S(2)}, u32[]{:S(2)}) collective-permute-start(f32[3,16,32]{2,1,0:T(8,128)S(1)} %get-tuple-element.43), channel_id=1, source_target_pairs={{16,0},{17,1},{18,2},{19,3},{20,4},{21,5},{22,6},{23,7},{24,8},{25... | collective-permute-start | bytes 18440 | tf_op jit(solution)/shard_map/ppermute | solution.py:35
  113.3 9.3 %collective-permute-start.7 = (f32[3,16,32]{2,1,0:T(8,128)S(1)}, f32[3,16,32]{2,1,0:T(8,128)S(1)}, u32[]{:S(2)}, u32[]{:S(2)}) collective-permute-start(f32[3,16,32]{2,1,0:T(8,128)S(1)} %get-tuple-element.42), channel_id=1, source_target_pairs={{0,16},{1,17},{2,18},{3,19},{4,20},{5,21},{6,22},{7,23},{8,24},{9,... | collective-permute-start | bytes 18440 | tf_op jit(solution)/shard_map/ppermute | solution.py:35

commit v7 on v3

--- a/solution.py
+++ b/solution.py
@@ -1,6 +1,8 @@
 import jax
 import jax.numpy as jnp
 from jax import lax
+from jax.experimental import pallas as pl
+from jax.experimental.pallas import tpu as pltpu
 from jax.sharding import PartitionSpec as P
 
 CLUSTER = 64
@@ -35,23 +37,51 @@
     return lax.ppermute(value, AXES, [(s, s - step) for s in range(n) if 0 <= s - step < n])
 
 
-def near_field(extended, target_points, near_offsets, leaf_values):
+def near_body(offsets_ref, table_ref, columns_ref, out_ref):
+    leaf_count = out_ref.shape[0]
+    rows = RHS + 3
+    lane = lax.broadcasted_iota(jnp.int32, (rows, 2 * CLUSTER), 1)
+    low_half = lane < CLUSTER
+
+    def one_leaf(i, carry):
+        own = table_ref[i + NEAR_REACH]
+        total = nugget * own[:RHS, :CLUSTER]
+        columns = columns_ref[i]
+        for pair in range(NEAR_BLOCKS // 2):
+            first = table_ref[i + NEAR_REACH + offsets_ref[i, 2 * pair]]
+            second = table_ref[i + NEAR_REACH + offsets_ref[i, 2 * pair + 1]]
+            joined = jnp.where(low_half, first, second)
+            squared = None
+            for component in range(3):
+                separation = joined[RHS + component : RHS + component + 1, :] - columns[:, component : component + 1]
+                term = separation * separation
+                squared = term if squared is None else squared + term
+            kernel = (amplitude * jnp.exp(-jnp.sqrt(squared) / length_scale)).astype(jnp.bfloat16)
+            values = joined[:RHS].astype(jnp.bfloat16)
+            total = total + lax.dot_general(
+                values, kernel, (((1,), (1,)), ((), ())), preferred_element_type=jnp.float32
+            )
+        out_ref[i] = total
+        return carry
+
+    lax.fori_loop(0, leaf_count, one_leaf, 0)
+
+
+def near_field_kernel(extended, target_points, near_offsets):
     leaf_count = target_points.shape[1]
-    column_count = extended.shape[0] - 3
     by_leaf = jnp.transpose(extended, (1, 0, 2))
-    source_leaf = jnp.arange(leaf_count, dtype=jnp.int32)[:, None] + NEAR_REACH + near_offsets
-    chosen = jnp.take(by_leaf, source_leaf, axis=0, mode="clip")
-    squared = jnp.zeros((leaf_count, NEAR_BLOCKS, CLUSTER, CLUSTER), jnp.float32)
-    for component in range(3):
-        separation = (
-            chosen[:, :, column_count + component, :, None]
-            - target_points[component][:, None, None, :]
-        )
-        squared = squared + separation * separation
-    kernel = (amplitude * jnp.exp(-jnp.sqrt(squared) / length_scale)).astype(jnp.bfloat16)
-    values = chosen[:, :, :column_count].astype(jnp.bfloat16)
-    near = jnp.einsum("lnra,lnab->rlb", values, kernel, preferred_element_type=jnp.float32)
-    return nugget * leaf_values.astype(jnp.float32) + near
+    table = jnp.concatenate([by_leaf, by_leaf], axis=2)
+    columns = jnp.pad(jnp.transpose(target_points, (1, 2, 0)), ((0, 0), (0, 0), (0, 125)))
+    return pl.pallas_call(
+        near_body,
+        out_shape=jax.ShapeDtypeStruct((leaf_count, RHS, CLUSTER), jnp.float32),
+        in_specs=[
+            pl.BlockSpec(memory_space=pltpu.SMEM),
+            pl.BlockSpec(memory_space=pltpu.VMEM),
+            pl.BlockSpec(memory_space=pltpu.VMEM),
+        ],
+        out_specs=pl.BlockSpec(memory_space=pltpu.VMEM),
+    )(near_offsets, table, columns)
 
 
 def mm(a, b):
@@ -170,7 +200,7 @@
     )
 
     target_points = points.reshape(3, leaf_count, CLUSTER)
-    near_sum = near_field(extended, target_points, near_offsets, leaf_values)
+    near_sum = near_field_kernel(extended, target_points, near_offsets)
 
     far_index = jnp.arange(leaf_count, dtype=jnp.int32)[:, None] + FAR_REACH + far_offsets
     partner_blocks = jnp.take(rimmed, far_index, axis=0).reshape(leaf_count, FAR_BLOCKS, RHS, RANK)
@@ -198,13 +228,14 @@
     )
     leaf_field = leaf_far + from_root
     far_out = jnp.einsum(
-        "lrk,lka->rla",
+        "lrk,lka->lra",
         leaf_field,
         target_basis.reshape(leaf_count, RANK, CLUSTER),
         precision=highest,
         preferred_element_type=jnp.float32,
     )
-    return (near_sum + far_out).reshape(RHS, leaf_count * CLUSTER)
+    product = jnp.transpose(near_sum + far_out, (1, 0, 2))
+    return product.reshape(RHS, leaf_count * CLUSTER)
 
 
 def solution(mesh):

time: 134 us -> 126 us (0.940)
  matrix products: 35.8 us -> 13.8 us
  Pallas kernels: 0 us -> 19.8 us
  local copies, waits for them, and re-layouts: 42.1 us -> 36.7 us
    dot_general x2 -> x1, matrix products: 23.5 us -> 0.53 us  [local(): jnp.einsum('lrk,lka->lra', leaf_field, target_basis.reshape(leaf_count, R...]
    pallas_call x0 -> x1, Pallas kernels: none -> 19.8 us  [near_field_kernel(): pl.pallas_call(near_body, out_shape=jax.ShapeDtypeStruct((leaf_count, RHS...]
    sub x6 -> x0, local copies, waits for them, and re-layouts: 3.46 us -> none  [near_field(): chosen[:, :, column_count + component, :, None]]
    gather x1 -> x0, local copies, waits for them, and re-layouts: 3.3 us -> none  [near_field(): chosen = jnp.take(by_leaf, source_leaf, axis=0, mode='clip')]
    slice x2 -> x0, local copies, waits for them, and re-layouts: 3.28 us -> none  [the longest x1 3.15 us: near_field(): chosen[:, :, column_count + component, :, None]]
    unnamed x61 -> x41, local copies, waits for them, and re-layouts: 3.09 us -> 5.77 us
    select_n x6, other arithmetic: 1.67 us -> 0.05 us  [ordered(): jnp.where(bit == 0, jnp.concatenate([own, other]), jnp.concatenate([other...]
    pad x0 -> x1, local copies, waits for them, and re-layouts: none -> 1.56 us  [near_field_kernel(): jnp.pad(jnp.transpose(target_points, (1, 2, 0)), ((0, 0), (0, 0), (0, 125)))]
  transfers between devices with their start and end apart: 9 -> 9, of which waited for: 4 -> 5; matrix products, arithmetic and copies ran while one was open for 23% -> 25% of each run, Pallas kernels for 0% -> 0%
where the time goes in v7:
time: 126 us; the launch traced here: 125 us
  starting transfers between devices  37.1 us (29%)
  local copies, waits for them, and re-layouts  36.7 us (29%)
  Pallas kernels  19.8 us (16%)
  matrix products  13.8 us (11%)
  waiting for transfers between devices  10.7 us (8%)
  other arithmetic  6.47 us (5%)
    ppermute x4, starting transfers between devices, receive_from(): lax.ppermute(value, AXES, [(s, s - step) for s in range(n) if 0 <= s - st...  22.2 us
    pallas_call x1, Pallas kernels, near_field_kernel(): pl.pallas_call(near_body, out_shape=jax.ShapeDtypeStruct((leaf_count, RHS...  19.8 us
    ppermute x3, starting transfers between devices, swap_with(): return lax.ppermute(value, AXES, [(i, i ^ mask) for i in range(n)])  9.13 us
    dot_general x1, matrix products, local(): jnp.einsum('lfrk,lfkq->lrq', partner_blocks, leaf_coupling.reshape(leaf_c...  8.32 us
    ppermute x4, waiting for transfers between devices, receive_from(): lax.ppermute(value, AXES, [(s, s - step) for s in range(n) if 0 <= s - st...  7.96 us
    reshape x1, local copies, waits for them, and re-layouts, local(): leaf_coupling.reshape(leaf_count, FAR_BLOCKS, RANK, RANK)  6.85 us
    unnamed x41, local copies, waits for them, and re-layouts  5.77 us
    gather x2, local copies, waits for them, and re-layouts, local(): jnp.take(rimmed, far_index, axis=0)  4.17 us
  transfers between devices with their start and end apart: 9, of which 5 were waited for; matrix products, arithmetic and copies ran while one was open for 25% of the time, Pallas kernels for 0%

profile of v7, /device:TPU:394, one launch (start us, length us, event | category | flops | bytes accessed | tf_op | source)
XLA Modules:
  0.0 125.2 jit_solution(12503771288474904208)
XLA Ops:
  0.0 1.2 reshape.139
  1.3 0.9 convert_element_type.22
  2.2 1.2 copy.20
  3.5 1.1 copy.22
  4.5 0.4 fusion.10
  5.2 0.7 pad_maximum_fusion.4
  5.9 2.4 %collective-permute-start.1 = (f32[35840]{0:T(1024)}, f32[35840]{0:T(1024)}, u32[]{:S(2)}, u32[]{:S(2)}) collective-permute-start(f32[35840]{0:T(1024)} %pad_maximum_fusion.4), channel_id=1, source_target_pairs={{1,0},{2,1},{3,2},{4,3},{5,4},{6,5},{7,6},{8,7},{9,8},{10,9},{11,1... | collective-permute-start | bytes 430088 | tf_op jit(solution)/shard_map/ppermute | solution.py:184
  8.4 0.7 pad_maximum_fusion.3
  9.1 3.4 %collective-permute-start = (f32[35840]{0:T(1024)}, f32[35840]{0:T(1024)}, u32[]{:S(2)}, u32[]{:S(2)}) collective-permute-start(f32[35840]{0:T(1024)} %pad_maximum_fusion.3), channel_id=1, source_target_pairs={{0,1},{1,2},{2,3},{3,4},{4,5},{5,6},{6,7},{7,8},{8,9},{9,10},{10,1... | collective-permute-start | bytes 430088 | tf_op jit(solution)/shard_map/ppermute | solution.py:183
  12.6 0.2 copy.31
  12.8 0.8 copy.37
  13.6 0.8 fusion.45
  14.8 0.1 convolution_bitcast_fusion.3
  14.9 0.2 convolution_bitcast_fusion.1
  15.1 2.5 %collective-permute-start.2 = (f32[4,16,32]{2,1,0:T(8,128)S(1)}, f32[4,16,32]{2,1,0:T(8,128)S(1)}, u32[]{:S(2)}, u32[]{:S(2)}) collective-permute-start(f32[4,16,32]{2,1,0:T(8,128)S(1)} %convolution_bitcast_fusion.1), channel_id=1, source_target_pairs={{0,1},{1,0},{2,3},{3,2},{4,5},{5,4},{6,7},{7,6},{8,9},{9,8},{10,11... | collective-permute-start | bytes 24584 | tf_op jit(solution)/shard_map/ppermute | solution.py:32
  17.7 0.1 reshape.149
  18.2 0.6 compare_and_fusion
  18.9 0.1 convolution_bitcast_fusion.2
  19.0 1.5 %fusion.22 = f32[4,32,4,32]{3,1,2,0:T(8,128)} fusion(bf16[4,4,32,32]{3,2,1,0:T(8,128)(2,1)S(1)} %reshape.149, f32[1,32,32]{2,1,0:T(8,128)S(1)} %fusion.32, f32[1,32,32]{2,1,0:T(8,128)S(1)} %convolution_bitcast_fusion.2, f32[1,32,32]{2,1,0:T(8,128)S(1)} %bitcast.76, f32[1,32,32]{2,1,0:T(8,128)S(1)} %reshape.154), kind=kOutput, calls=%fused_computation.49 | convolution fusion | flops 6303744 | bytes 114688 | tf_op jit(solution)/shard_map/sqkp,spm->sqkm/dot_general | solution.py:108
  20.5 0.6 pad_clamp_fusion.1
  21.3 4.7 %collective-permute-start.3 = (f32[5,16,32]{2,1,0:T(8,128)S(1)}, f32[5,16,32]{2,1,0:T(8,128)S(1)}, u32[]{:S(2)}, u32[]{:S(2)}) collective-permute-start(f32[5,16,32]{2,1,0:T(8,128)S(1)} %pad_maximum_fusion.18), channel_id=1, source_target_pairs={{0,2},{1,3},{2,0},{3,1},{4,6},{5,7},{6,4},{7,5},{8,10},{9,11},{10,... | collective-permute-start | bytes 30728 | tf_op jit(solution)/shard_map/ppermute | solution.py:32
  26.1 2.7 %collective-permute-done.3 = f32[5,16,32]{2,1,0:T(8,128)S(1)} collective-permute-done((f32[5,16,32]{2,1,0:T(8,128)S(1)}, f32[5,16,32]{2,1,0:T(8,128)S(1)}, u32[]{:S(2)}, u32[]{:S(2)}) %collective-permute-start.3) | collective-permute-done | bytes 10272 | tf_op jit(solution)/shard_map/ppermute | solution.py:32
  28.8 0.6 fusion.15
  29.4 1.9 %collective-permute-start.4 = (f32[8,16,32]{2,1,0:T(8,128)}, f32[8,16,32]{2,1,0:T(8,128)}, u32[]{:S(2)}, u32[]{:S(2)}) collective-permute-start(f32[8,16,32]{2,1,0:T(8,128)} %fusion.15), channel_id=1, source_target_pairs={{0,4},{1,5},{2,6},{3,7},{4,0},{5,1},{6,2},{7,3},{8,12},{9,13},{10,... | collective-permute-start | bytes 49160 | tf_op jit(solution)/shard_map/ppermute | solution.py:32
  31.3 2.0 %copy.24 = f32[3,4096]{0,1:T(8,128)} copy(f32[3,4096]{1,0:T(4,128)S(1)} %copy-done.5) | data formatting | bytes 98304 | tf_op args[1]
  33.3 0.9 copy.27
  34.3 0.7 copy.25.offsets_ref
  35.0 1.4 %copy.30 = bf16[64,8,1024]{0,2,1:T(8,128)(2,1)S(1)} copy(bf16[64,8,1024]{2,1,0:T(8,128)(2,1)S(1)} %copy-done.2) | data formatting | bytes 2097152 | tf_op args[6]
  36.5 6.9 %copy.35 = bf16[64,8,32,32]{3,2,1,0:T(8,128)(2,1)} copy(bf16[64,8,32,32]{0,3,2,1:T(8,128)(2,1)S(1)} %bitcast.68) | data formatting | bytes 2097152 | tf_op jit(solution)/shard_map/reshape | solution.py:210
  43.3 0.8 copy.28
  44.2 0.9 copy.54
  45.1 0.2 copy.33
  45.3 0.8 copy.44
  46.0 1.5 %reshape.151 = bf16[64,32,64]{2,1,0:T(8,128)(2,1)S(1)} reshape(bf16[64,2048]{1,0:T(8,128)(2,1)} %param.18) | data formatting | bytes 524288 | tf_op jit(solution)/shard_map/reshape | solution.py:233
  47.5 1.6 %pad.4.columns_ref = f32[64,64,128]{2,1,0:T(8,128)} pad(f32[64,64,3]{2,1,0:T(8,128)S(1)} %bitcast.69, f32[]{:T(128)} %constant.15.clone.1), padding=0_0x0_0x0_125 | pad | bytes 2146308 | tf_op jit(solution)/shard_map/jit(_pad)/pad | solution.py:74
  49.1 0.7 fusion.40
  49.8 0.7 slice.298
  50.5 0.8 slice.296
  51.4 3.5 %collective-permute-start.5 = (f32[9,16,32]{2,1,0:T(8,128)S(1)}, f32[9,16,32]{2,1,0:T(8,128)S(1)}, u32[]{:S(2)}, u32[]{:S(2)}) collective-permute-start(f32[9,16,32]{2,1,0:T(8,128)S(1)} %get-tuple-element.38), channel_id=1, source_target_pairs={{0,8},{1,9},{2,10},{3,11},{4,12},{5,13},{6,14},{7,15},{8,16},{9,17... | collective-permute-start | bytes 55304 | tf_op jit(solution)/shard_map/ppermute | solution.py:37
  54.8 5.0 %collective-permute-start.6 = (f32[9,16,32]{2,1,0:T(8,128)S(1)}, f32[9,16,32]{2,1,0:T(8,128)S(1)}, u32[]{:S(2)}, u32[]{:S(2)}) collective-permute-start(f32[9,16,32]{2,1,0:T(8,128)S(1)} %get-tuple-element.39), channel_id=1, source_target_pairs={{8,0},{9,1},{10,2},{11,3},{12,4},{13,5},{14,6},{15,7},{16,8},{17,9... | collective-permute-start | bytes 55304 | tf_op jit(solution)/shard_map/ppermute | solution.py:37
  59.9 1.0 collective-permute-done.5
  60.9 1.2 collective-permute-done.6
  62.0 11.6 %collective-permute-start.8 = (f32[3,16,32]{2,1,0:T(8,128)S(1)}, f32[3,16,32]{2,1,0:T(8,128)S(1)}, u32[]{:S(2)}, u32[]{:S(2)}) collective-permute-start(f32[3,16,32]{2,1,0:T(8,128)S(1)} %get-tuple-element.43), channel_id=1, source_target_pairs={{16,0},{17,1},{18,2},{19,3},{20,4},{21,5},{22,6},{23,7},{24,8},{25... | collective-permute-start | bytes 18440 | tf_op jit(solution)/shard_map/ppermute | solution.py:37
  73.6 2.1 %collective-permute-start.7 = (f32[3,16,32]{2,1,0:T(8,128)S(1)}, f32[3,16,32]{2,1,0:T(8,128)S(1)}, u32[]{:S(2)}, u32[]{:S(2)}) collective-permute-start(f32[3,16,32]{2,1,0:T(8,128)S(1)} %get-tuple-element.42), channel_id=1, source_target_pairs={{0,16},{1,17},{2,18},{3,19},{4,20},{5,21},{6,22},{7,23},{8,24},{9,... | collective-permute-start | bytes 18440 | tf_op jit(solution)/shard_map/ppermute | solution.py:37
  75.8 0.7 gather_fusion.2
  76.5 0.7 gather_fusion.1
  77.2 5.8 %collective-permute-done.7 = f32[3,16,32]{2,1,0:T(8,128)S(1)} collective-permute-done((f32[3,16,32]{2,1,0:T(8,128)S(1)}, f32[3,16,32]{2,1,0:T(8,128)S(1)}, u32[]{:S(2)}, u32[]{:S(2)}) %collective-permute-start.7) | collective-permute-done | bytes 6176 | tf_op jit(solution)/shard_map/ppermute | solution.py:37
  83.1 0.6 gather_fusion.3
  83.6 1.2 convolution_bitcast_fusion.4
  84.9 0.9 slice.281
  85.9 0.9 slice.279
  86.8 0.4 reshape.144
  87.2 0.6 copy.53
  87.8 1.4 %pad_maximum_fusion.table_ref = f32[96,19,128]{2,1,0:T(8,128)} fusion(f32[96,19,64]{2,1,0:T(8,128)S(1)} %bitcast.70), kind=kLoop, calls=%fused_computation.13 | loop fusion | flops 233472 | bytes 1400832 | tf_op jit(solution)/shard_map/concatenate | solution.py:73
  89.2 0.8 slice.283
  90.0 0.8 slice.282
  90.9 1.6 %gather_fusion = f32[512,512]{1,0:T(8,128)S(1)} fusion(f32[128,512]{1,0:T(8,128)S(1)} %pad_maximum_fusion.2, s32[1024]{0:T(1024)S(1)} %pad_clamp_fusion.3), kind=kCustom, calls=%fused_computation | custom fusion | bytes 2099200 | tf_op jit(solution)/shard_map/jit(_take)/gather | solution.py:206
  92.5 2.6 %gather.19 = f32[64,8,16,32]{3,2,1,0:T(8,128)} reshape(f32[512,512]{1,0:T(8,128)S(1)} %gather_fusion) | data formatting | bytes 2097152 | tf_op jit(solution)/shard_map/jit(_take)/gather | solution.py:206
  95.1 19.8 %shard_map.127 = f32[64,16,64]{2,1,0:T(8,128)} custom-call(s32[64,6]{1,0:T(8,128)} %copy.25.offsets_ref, f32[96,19,128]{2,1,0:T(8,128)} %pad_maximum_fusion.table_ref, f32[64,64,128]{2,1,0:T(8,128)} %pad.4.columns_ref), custom_call_target="tpu_custom_call" | custom-call | tf_op jit(solution)/shard_map/pallas_call | solution.py:75
  114.9 8.3 %fusion.4 = f32[64,16,32]{2,1,0:T(8,128)S(1)} fusion(bf16[64,8,32,32]{3,2,1,0:T(8,128)(2,1)} %copy.35, f32[64,8,16,32]{3,2,1,0:T(8,128)} %gather.19, pred[64,8]{1,0:T(8,128)(4,1)S(1)} %copy.26), kind=kOutput, calls=%fused_computation.8 | convolution fusion | flops 100925440 | bytes 2228736 | tf_op jit(solution)/shard_map/lfrk,lfkq->lrq/dot_general | solution.py:207
  123.2 0.4 fusion.8
  123.6 0.5 fusion.7
  124.1 0.2 copy.34
  124.3 0.9 reshape.152
  (98 shorter events, 2.0 us)
Async XLA Ops:
  0.0 5.1 %copy-start.5 = (f32[3,4096]{1,0:T(4,128)S(1)}, f32[3,4096]{1,0:T(4,128)}, u32[]{:S(2)}) copy-start(f32[3,4096]{1,0:T(4,128)} %param.14) | copy-start | bytes 147460
  0.0 12.5 %copy-start.10 = (bf16[1,3,1024]{2,1,0:T(4,128)(2,1)S(1)}, bf16[1,3,1024]{2,1,0:T(4,128)(2,1)}, u32[]{:S(2)}) copy-start(bf16[1,3,1024]{2,1,0:T(4,128)(2,1)} %param.22) | copy-start | bytes 18436
  0.0 12.6 %copy-start.11 = (bf16[1,3,1024]{2,1,0:T(4,128)(2,1)S(1)}, bf16[1,3,1024]{2,1,0:T(4,128)(2,1)}, u32[]{:S(2)}) copy-start(bf16[1,3,1024]{2,1,0:T(4,128)(2,1)} %param.23) | copy-start | bytes 18436
  0.0 12.6 %copy-start.7 = (bf16[64,1024]{1,0:T(8,128)(2,1)S(1)}, bf16[64,1024]{1,0:T(8,128)(2,1)}, u32[]{:S(2)}) copy-start(bf16[64,1024]{1,0:T(8,128)(2,1)} %param.20) | copy-start | bytes 393220
  3.4 14.3 %copy-start.9 = (bf16[1,4,4,1024]{3,2,1,0:T(4,128)(2,1)S(1)}, bf16[1,4,4,1024]{3,2,1,0:T(4,128)(2,1)}, u32[]{:S(2)}) copy-start(bf16[1,4,4,1024]{3,2,1,0:T(4,128)(2,1)} %param.24) | copy-start | bytes 98308
  3.4 14.7 %copy-start.14 = (s32[64,8]{0,1:T(8,128)S(1)}, s32[64,8]{0,1:T(8,128)}, u32[]{:S(2)}) copy-start(s32[64,8]{0,1:T(8,128)} %param.16) | copy-start | bytes 6148
  3.4 17.0 %copy-start.15 = (s32[4]{0:T(128)S(1)}, s32[4]{0:T(128)}, u32[]{:S(2)}) copy-start(s32[4]{0:T(128)} %constant.56) | copy-start | bytes 52
  5.1 29.2 %copy-start.12 = (s32[64,6]{0,1:T(8,128)S(1)}, s32[64,6]{0,1:T(8,128)}, u32[]{:S(2)}) copy-start(s32[64,6]{0,1:T(8,128)} %param.15) | copy-start | bytes 4612
  5.1 29.9 %copy-start.2 = (bf16[64,8,1024]{2,1,0:T(8,128)(2,1)S(1)}, bf16[64,8,1024]{2,1,0:T(8,128)(2,1)}, u32[]{:S(2)}) copy-start(bf16[64,8,1024]{2,1,0:T(8,128)(2,1)} %param.19) | copy-start | bytes 3145732
  5.9 79.0 %collective-permute-start.1 = (f32[35840]{0:T(1024)}, f32[35840]{0:T(1024)}, u32[]{:S(2)}, u32[]{:S(2)}) collective-permute-start(f32[35840]{0:T(1024)} %pad_maximum_fusion.4), channel_id=1, source_target_pairs={{1,0},{2,1},{3,2},{4,3},{5,4},{6,5},{7,6},{8,7},{9,8},{10,9},{11,1... | collective-permute-start | bytes 430088 | tf_op jit(solution)/shard_map/ppermute | solution.py:184
  9.1 76.8 %collective-permute-start = (f32[35840]{0:T(1024)}, f32[35840]{0:T(1024)}, u32[]{:S(2)}, u32[]{:S(2)}) collective-permute-start(f32[35840]{0:T(1024)} %pad_maximum_fusion.3), channel_id=1, source_target_pairs={{0,1},{1,2},{2,3},{3,4},{4,5},{5,6},{6,7},{7,8},{8,9},{9,10},{10,1... | collective-permute-start | bytes 430088 | tf_op jit(solution)/shard_map/ppermute | solution.py:183
  15.1 6.2 %collective-permute-start.2 = (f32[4,16,32]{2,1,0:T(8,128)S(1)}, f32[4,16,32]{2,1,0:T(8,128)S(1)}, u32[]{:S(2)}, u32[]{:S(2)}) collective-permute-start(f32[4,16,32]{2,1,0:T(8,128)S(1)} %convolution_bitcast_fusion.1), channel_id=1, source_target_pairs={{0,1},{1,0},{2,3},{3,2},{4,5},{5,4},{6,7},{7,6},{8,9},{9,8},{10,11... | collective-permute-start | bytes 24584 | tf_op jit(solution)/shard_map/ppermute | solution.py:32
  21.3 7.4 %collective-permute-start.3 = (f32[5,16,32]{2,1,0:T(8,128)S(1)}, f32[5,16,32]{2,1,0:T(8,128)S(1)}, u32[]{:S(2)}, u32[]{:S(2)}) collective-permute-start(f32[5,16,32]{2,1,0:T(8,128)S(1)} %pad_maximum_fusion.18), channel_id=1, source_target_pairs={{0,2},{1,3},{2,0},{3,1},{4,6},{5,7},{6,4},{7,5},{8,10},{9,11},{10,... | collective-permute-start | bytes 30728 | tf_op jit(solution)/shard_map/ppermute | solution.py:32
  29.4 19.7 %collective-permute-start.4 = (f32[8,16,32]{2,1,0:T(8,128)}, f32[8,16,32]{2,1,0:T(8,128)}, u32[]{:S(2)}, u32[]{:S(2)}) collective-permute-start(f32[8,16,32]{2,1,0:T(8,128)} %fusion.15), channel_id=1, source_target_pairs={{0,4},{1,5},{2,6},{3,7},{4,0},{5,1},{6,2},{7,3},{8,12},{9,13},{10,... | collective-permute-start | bytes 49160 | tf_op jit(solution)/shard_map/ppermute | solution.py:32
  36.4 6.9 %copy-start.3 = (f32[64,16,32]{0,2,1:T(8,128)S(1)}, f32[64,16,32]{0,2,1:T(8,128)}, u32[]{:S(2)}) copy-start(f32[64,16,32]{0,2,1:T(8,128)} %copy.27) | copy-start | bytes 393220
  36.4 7.7 %copy-start.13 = (pred[64,8]{0,1:T(8,128)(4,1)S(1)}, pred[64,8]{0,1:T(8,128)(4,1)}, u32[]{:S(2)}) copy-start(pred[64,8]{0,1:T(8,128)(4,1)} %get-tuple-element.11) | copy-start | bytes 1540
  36.4 7.8 %copy-start.4 = (f32[4,32,4,32]{3,1,2,0:T(8,128)S(1)}, f32[4,32,4,32]{3,1,2,0:T(8,128)}, u32[]{:S(2)}) copy-start(f32[4,32,4,32]{3,1,2,0:T(8,128)} %fusion.22) | copy-start | bytes 196612
  36.5 8.6 %copy-start.8 = (bf16[64,1024]{1,0:T(8,128)(2,1)S(1)}, bf16[64,1024]{1,0:T(8,128)(2,1)}, u32[]{:S(2)}) copy-start(bf16[64,1024]{1,0:T(8,128)(2,1)} %param.21) | copy-start | bytes 393220
  43.3 4.2 %copy-start = (f32[3,4096]{0,1:T(8,128)S(1)}, f32[3,4096]{0,1:T(8,128)}, u32[]{:S(2)}) copy-start(f32[3,4096]{0,1:T(8,128)} %copy.24) | copy-start | bytes 147460
  51.4 9.5 %collective-permute-start.5 = (f32[9,16,32]{2,1,0:T(8,128)S(1)}, f32[9,16,32]{2,1,0:T(8,128)S(1)}, u32[]{:S(2)}, u32[]{:S(2)}) collective-permute-start(f32[9,16,32]{2,1,0:T(8,128)S(1)} %get-tuple-element.38), channel_id=1, source_target_pairs={{0,8},{1,9},{2,10},{3,11},{4,12},{5,13},{6,14},{7,15},{8,16},{9,17... | collective-permute-start | bytes 55304 | tf_op jit(solution)/shard_map/ppermute | solution.py:37
  54.8 7.2 %collective-permute-start.6 = (f32[9,16,32]{2,1,0:T(8,128)S(1)}, f32[9,16,32]{2,1,0:T(8,128)S(1)}, u32[]{:S(2)}, u32[]{:S(2)}) collective-permute-start(f32[9,16,32]{2,1,0:T(8,128)S(1)} %get-tuple-element.39), channel_id=1, source_target_pairs={{8,0},{9,1},{10,2},{11,3},{12,4},{13,5},{14,6},{15,7},{16,8},{17,9... | collective-permute-start | bytes 55304 | tf_op jit(solution)/shard_map/ppermute | solution.py:37
  62.0 21.0 %collective-permute-start.8 = (f32[3,16,32]{2,1,0:T(8,128)S(1)}, f32[3,16,32]{2,1,0:T(8,128)S(1)}, u32[]{:S(2)}, u32[]{:S(2)}) collective-permute-start(f32[3,16,32]{2,1,0:T(8,128)S(1)} %get-tuple-element.43), channel_id=1, source_target_pairs={{16,0},{17,1},{18,2},{19,3},{20,4},{21,5},{22,6},{23,7},{24,8},{25... | collective-permute-start | bytes 18440 | tf_op jit(solution)/shard_map/ppermute | solution.py:37
  73.6 9.3 %collective-permute-start.7 = (f32[3,16,32]{2,1,0:T(8,128)S(1)}, f32[3,16,32]{2,1,0:T(8,128)S(1)}, u32[]{:S(2)}, u32[]{:S(2)}) collective-permute-start(f32[3,16,32]{2,1,0:T(8,128)S(1)} %get-tuple-element.42), channel_id=1, source_target_pairs={{0,16},{1,17},{2,18},{3,19},{4,20},{5,21},{6,22},{7,23},{8,24},{9,... | collective-permute-start | bytes 18440 | tf_op jit(solution)/shard_map/ppermute | solution.py:37
  84.8 6.0 %copy-start.6 = (f32[64,512]{1,0:T(8,128)S(1)}, f32[64,512]{1,0:T(8,128)}, u32[]{:S(2)}) copy-start(f32[64,512]{1,0:T(8,128)} %copy.28) | copy-start | bytes 393220
  114.9 8.7 %copy-start.1 = (f32[64,16,64]{2,1,0:T(8,128)S(1)}, f32[64,16,64]{2,1,0:T(8,128)}, u32[]{:S(2)}) copy-start(f32[64,16,64]{2,1,0:T(8,128)} %shard_map.127) | copy-start | bytes 786436

commit v8 on v7

--- a/solution.py
+++ b/solution.py
@@ -45,7 +45,7 @@
 
     def one_leaf(i, carry):
         own = table_ref[i + NEAR_REACH]
-        total = nugget * own[:RHS, :CLUSTER]
+        parts = []
         columns = columns_ref[i]
         for pair in range(NEAR_BLOCKS // 2):
             first = table_ref[i + NEAR_REACH + offsets_ref[i, 2 * pair]]
@@ -58,13 +58,15 @@
                 squared = term if squared is None else squared + term
             kernel = (amplitude * jnp.exp(-jnp.sqrt(squared) / length_scale)).astype(jnp.bfloat16)
             values = joined[:RHS].astype(jnp.bfloat16)
-            total = total + lax.dot_general(
-                values, kernel, (((1,), (1,)), ((), ())), preferred_element_type=jnp.float32
+            parts.append(
+                lax.dot_general(
+                    values, kernel, (((1,), (1,)), ((), ())), preferred_element_type=jnp.float32
+                )
             )
-        out_ref[i] = total
+        out_ref[i] = nugget * own[:RHS, :CLUSTER] + (parts[0] + parts[1] + parts[2])
         return carry
 
-    lax.fori_loop(0, leaf_count, one_leaf, 0)
+    lax.fori_loop(0, leaf_count, one_leaf, 0, unroll=8)
 
 
 def near_field_kernel(extended, target_points, near_offsets):

time: 126 us -> 115 us (0.913)
  Pallas kernels: 19.8 us -> 8.56 us
    pallas_call x1, Pallas kernels: 19.8 us -> 8.56 us  [near_field_kernel(): pl.pallas_call(near_body, out_shape=jax.ShapeDtypeStruct((leaf_count, RHS...]
  transfers between devices with their start and end apart: 9 -> 9, of which waited for: 5 -> 5; matrix products, arithmetic and copies ran while one was open for 25% -> 28% of each run, Pallas kernels for 0% -> 0%
where the time goes in v8:
time: 115 us; the launch traced here: 114 us
  starting transfers between devices  37.1 us (32%)
  local copies, waits for them, and re-layouts  36.7 us (32%)
  matrix products  13.8 us (12%)
  waiting for transfers between devices  10.7 us (9%)
  Pallas kernels  8.56 us (7%)
  other arithmetic  6.47 us (6%)
    ppermute x4, starting transfers between devices, receive_from(): lax.ppermute(value, AXES, [(s, s - step) for s in range(n) if 0 <= s - st...  22.2 us
    ppermute x3, starting transfers between devices, swap_with(): return lax.ppermute(value, AXES, [(i, i ^ mask) for i in range(n)])  9.13 us
    pallas_call x1, Pallas kernels, near_field_kernel(): pl.pallas_call(near_body, out_shape=jax.ShapeDtypeStruct((leaf_count, RHS...  8.56 us
    dot_general x1, matrix products, local(): jnp.einsum('lfrk,lfkq->lrq', partner_blocks, leaf_coupling.reshape(leaf_c...  8.32 us
    ppermute x4, waiting for transfers between devices, receive_from(): lax.ppermute(value, AXES, [(s, s - step) for s in range(n) if 0 <= s - st...  7.96 us
    reshape x1, local copies, waits for them, and re-layouts, local(): leaf_coupling.reshape(leaf_count, FAR_BLOCKS, RANK, RANK)  6.85 us
    unnamed x41, local copies, waits for them, and re-layouts  5.77 us
    gather x2, local copies, waits for them, and re-layouts, local(): jnp.take(rimmed, far_index, axis=0)  4.17 us
  transfers between devices with their start and end apart: 9, of which 5 were waited for; matrix products, arithmetic and copies ran while one was open for 28% of the time, Pallas kernels for 0%

profile of v8, /device:TPU:394, one launch (start us, length us, event | category | flops | bytes accessed | tf_op | source)
XLA Modules:
  0.0 114.0 jit_solution(2110252796429831887)
XLA Ops:
  0.0 1.2 %reshape.139 = bf16[16,64,64]{2,1,0:T(8,128)(2,1)S(1)} reshape(bf16[16,4096]{1,0:T(8,128)(2,1)} %param.13) | data formatting | bytes 262144 | tf_op jit(solution)/shard_map/reshape | solution.py:170
  1.3 0.9 convert_element_type.22
  2.2 1.2 %copy.20 = bf16[64,2048]{0,1:T(8,128)(2,1)S(1)} copy(bf16[64,2048]{1,0:T(8,128)(2,1)} %param.17) | data formatting | bytes 524288 | tf_op args[4]
  3.5 1.1 copy.22
  4.5 0.4 fusion.10
  5.2 0.7 pad_maximum_fusion.4
  5.9 2.4 %collective-permute-start.1 = (f32[35840]{0:T(1024)}, f32[35840]{0:T(1024)}, u32[]{:S(2)}, u32[]{:S(2)}) collective-permute-start(f32[35840]{0:T(1024)} %pad_maximum_fusion.4), channel_id=1, source_target_pairs={{1,0},{2,1},{3,2},{4,3},{5,4},{6,5},{7,6},{8,7},{9,8},{10,9},{11,1... | collective-permute-start | bytes 430088 | tf_op jit(solution)/shard_map/ppermute | solution.py:186
  8.4 0.7 pad_maximum_fusion.3
  9.1 3.4 %collective-permute-start = (f32[35840]{0:T(1024)}, f32[35840]{0:T(1024)}, u32[]{:S(2)}, u32[]{:S(2)}) collective-permute-start(f32[35840]{0:T(1024)} %pad_maximum_fusion.3), channel_id=1, source_target_pairs={{0,1},{1,2},{2,3},{3,4},{4,5},{5,6},{6,7},{7,8},{8,9},{9,10},{10,1... | collective-permute-start | bytes 430088 | tf_op jit(solution)/shard_map/ppermute | solution.py:185
  12.6 0.2 copy.31
  12.8 0.8 copy.37
  13.6 0.8 fusion.45
  14.8 0.1 convolution_bitcast_fusion.3
  14.9 0.2 convolution_bitcast_fusion.1
  15.1 2.5 %collective-permute-start.2 = (f32[4,16,32]{2,1,0:T(8,128)S(1)}, f32[4,16,32]{2,1,0:T(8,128)S(1)}, u32[]{:S(2)}, u32[]{:S(2)}) collective-permute-start(f32[4,16,32]{2,1,0:T(8,128)S(1)} %convolution_bitcast_fusion.1), channel_id=1, source_target_pairs={{0,1},{1,0},{2,3},{3,2},{4,5},{5,4},{6,7},{7,6},{8,9},{9,8},{10,11... | collective-permute-start | bytes 24584 | tf_op jit(solution)/shard_map/ppermute | solution.py:32
  17.7 0.1 reshape.149
  18.2 0.6 compare_and_fusion
  18.9 0.1 convolution_bitcast_fusion.2
  19.0 1.5 %fusion.22 = f32[4,32,4,32]{3,1,2,0:T(8,128)} fusion(bf16[4,4,32,32]{3,2,1,0:T(8,128)(2,1)S(1)} %reshape.149, f32[1,32,32]{2,1,0:T(8,128)S(1)} %fusion.32, f32[1,32,32]{2,1,0:T(8,128)S(1)} %convolution_bitcast_fusion.2, f32[1,32,32]{2,1,0:T(8,128)S(1)} %bitcast.76, f32[1,32,32]{2,1,0:T(8,128)S(1)} %reshape.154), kind=kOutput, calls=%fused_computation.49 | convolution fusion | flops 6303744 | bytes 114688 | tf_op jit(solution)/shard_map/sqkp,spm->sqkm/dot_general | solution.py:110
  20.5 0.6 pad_clamp_fusion.1
  21.3 4.7 %collective-permute-start.3 = (f32[5,16,32]{2,1,0:T(8,128)S(1)}, f32[5,16,32]{2,1,0:T(8,128)S(1)}, u32[]{:S(2)}, u32[]{:S(2)}) collective-permute-start(f32[5,16,32]{2,1,0:T(8,128)S(1)} %pad_maximum_fusion.18), channel_id=1, source_target_pairs={{0,2},{1,3},{2,0},{3,1},{4,6},{5,7},{6,4},{7,5},{8,10},{9,11},{10,... | collective-permute-start | bytes 30728 | tf_op jit(solution)/shard_map/ppermute | solution.py:32
  26.1 2.7 %collective-permute-done.3 = f32[5,16,32]{2,1,0:T(8,128)S(1)} collective-permute-done((f32[5,16,32]{2,1,0:T(8,128)S(1)}, f32[5,16,32]{2,1,0:T(8,128)S(1)}, u32[]{:S(2)}, u32[]{:S(2)}) %collective-permute-start.3) | collective-permute-done | bytes 10272 | tf_op jit(solution)/shard_map/ppermute | solution.py:32
  28.8 0.6 fusion.15
  29.4 1.9 %collective-permute-start.4 = (f32[8,16,32]{2,1,0:T(8,128)}, f32[8,16,32]{2,1,0:T(8,128)}, u32[]{:S(2)}, u32[]{:S(2)}) collective-permute-start(f32[8,16,32]{2,1,0:T(8,128)} %fusion.15), channel_id=1, source_target_pairs={{0,4},{1,5},{2,6},{3,7},{4,0},{5,1},{6,2},{7,3},{8,12},{9,13},{10,... | collective-permute-start | bytes 49160 | tf_op jit(solution)/shard_map/ppermute | solution.py:32
  31.3 2.0 %copy.24 = f32[3,4096]{0,1:T(8,128)} copy(f32[3,4096]{1,0:T(4,128)S(1)} %copy-done.5) | data formatting | bytes 98304 | tf_op args[1]
  33.3 0.9 copy.27
  34.3 0.7 copy.25.offsets_ref
  35.0 1.4 %copy.30 = bf16[64,8,1024]{0,2,1:T(8,128)(2,1)S(1)} copy(bf16[64,8,1024]{2,1,0:T(8,128)(2,1)S(1)} %copy-done.2) | data formatting | bytes 2097152 | tf_op args[6]
  36.5 6.9 %copy.35 = bf16[64,8,32,32]{3,2,1,0:T(8,128)(2,1)} copy(bf16[64,8,32,32]{0,3,2,1:T(8,128)(2,1)S(1)} %bitcast.68) | data formatting | bytes 2097152 | tf_op jit(solution)/shard_map/reshape | solution.py:212
  43.3 0.8 copy.28
  44.2 0.9 copy.54
  45.1 0.2 copy.33
  45.3 0.8 copy.44
  46.0 1.5 %reshape.151 = bf16[64,32,64]{2,1,0:T(8,128)(2,1)S(1)} reshape(bf16[64,2048]{1,0:T(8,128)(2,1)} %param.18) | data formatting | bytes 524288 | tf_op jit(solution)/shard_map/reshape | solution.py:235
  47.5 1.6 %pad.4.columns_ref = f32[64,64,128]{2,1,0:T(8,128)} pad(f32[64,64,3]{2,1,0:T(8,128)S(1)} %bitcast.69, f32[]{:T(128)} %constant.15.clone.1), padding=0_0x0_0x0_125 | pad | bytes 2146308 | tf_op jit(solution)/shard_map/jit(_pad)/pad | solution.py:76
  49.1 0.7 fusion.40
  49.8 0.7 slice.298
  50.5 0.8 slice.296
  51.4 3.5 %collective-permute-start.5 = (f32[9,16,32]{2,1,0:T(8,128)S(1)}, f32[9,16,32]{2,1,0:T(8,128)S(1)}, u32[]{:S(2)}, u32[]{:S(2)}) collective-permute-start(f32[9,16,32]{2,1,0:T(8,128)S(1)} %get-tuple-element.38), channel_id=1, source_target_pairs={{0,8},{1,9},{2,10},{3,11},{4,12},{5,13},{6,14},{7,15},{8,16},{9,17... | collective-permute-start | bytes 55304 | tf_op jit(solution)/shard_map/ppermute | solution.py:37
  54.8 5.0 %collective-permute-start.6 = (f32[9,16,32]{2,1,0:T(8,128)S(1)}, f32[9,16,32]{2,1,0:T(8,128)S(1)}, u32[]{:S(2)}, u32[]{:S(2)}) collective-permute-start(f32[9,16,32]{2,1,0:T(8,128)S(1)} %get-tuple-element.39), channel_id=1, source_target_pairs={{8,0},{9,1},{10,2},{11,3},{12,4},{13,5},{14,6},{15,7},{16,8},{17,9... | collective-permute-start | bytes 55304 | tf_op jit(solution)/shard_map/ppermute | solution.py:37
  59.9 1.0 collective-permute-done.5
  60.9 1.2 %collective-permute-done.6 = f32[9,16,32]{2,1,0:T(8,128)S(1)} collective-permute-done((f32[9,16,32]{2,1,0:T(8,128)S(1)}, f32[9,16,32]{2,1,0:T(8,128)S(1)}, u32[]{:S(2)}, u32[]{:S(2)}) %collective-permute-start.6) | collective-permute-done | bytes 18464 | tf_op jit(solution)/shard_map/ppermute | solution.py:37
  62.0 11.6 %collective-permute-start.8 = (f32[3,16,32]{2,1,0:T(8,128)S(1)}, f32[3,16,32]{2,1,0:T(8,128)S(1)}, u32[]{:S(2)}, u32[]{:S(2)}) collective-permute-start(f32[3,16,32]{2,1,0:T(8,128)S(1)} %get-tuple-element.43), channel_id=1, source_target_pairs={{16,0},{17,1},{18,2},{19,3},{20,4},{21,5},{22,6},{23,7},{24,8},{25... | collective-permute-start | bytes 18440 | tf_op jit(solution)/shard_map/ppermute | solution.py:37
  73.6 2.1 %collective-permute-start.7 = (f32[3,16,32]{2,1,0:T(8,128)S(1)}, f32[3,16,32]{2,1,0:T(8,128)S(1)}, u32[]{:S(2)}, u32[]{:S(2)}) collective-permute-start(f32[3,16,32]{2,1,0:T(8,128)S(1)} %get-tuple-element.42), channel_id=1, source_target_pairs={{0,16},{1,17},{2,18},{3,19},{4,20},{5,21},{6,22},{7,23},{8,24},{9,... | collective-permute-start | bytes 18440 | tf_op jit(solution)/shard_map/ppermute | solution.py:37
  75.8 0.7 gather_fusion.2
  76.5 0.7 gather_fusion.1
  77.2 5.8 %collective-permute-done.7 = f32[3,16,32]{2,1,0:T(8,128)S(1)} collective-permute-done((f32[3,16,32]{2,1,0:T(8,128)S(1)}, f32[3,16,32]{2,1,0:T(8,128)S(1)}, u32[]{:S(2)}, u32[]{:S(2)}) %collective-permute-start.7) | collective-permute-done | bytes 6176 | tf_op jit(solution)/shard_map/ppermute | solution.py:37
  83.1 0.6 gather_fusion.3
  83.6 1.2 %convolution_bitcast_fusion.4 = f32[16,32,1]{1,0,2:T(8,128)S(1)} fusion(f32[4,4,32,32]{2,1,3,0:T(4,128)} %bitcast.75, f32[1,4,16,32]{3,2,1,0:T(8,128)S(1)} %maximum_bitcast_fusion, f32[1,4,16,32]{3,2,1,0:T(8,128)S(1)} %bitcast.79, f32[1,4,16,32]{3,2,1,0:T(8,128)S(1)} %bitcast.77, f32[1,4,16,32]{3,2,1,0:T(8,128)S(1)} %bitcast.78), kind=kOutput, calls=%fused_computation.18 | convolution fusion | flops 3170304 | bytes 100352 | tf_op jit(solution)/shard_map/sqrk,sqkm->rm/dot_general | solution.py:150
  84.9 0.9 slice.281
  85.9 0.9 slice.279
  86.8 0.4 reshape.144
  87.2 0.6 copy.53
  87.8 1.4 %pad_maximum_fusion.table_ref = f32[96,19,128]{2,1,0:T(8,128)} fusion(f32[96,19,64]{2,1,0:T(8,128)S(1)} %bitcast.70), kind=kLoop, calls=%fused_computation.13 | loop fusion | flops 233472 | bytes 1400832 | tf_op jit(solution)/shard_map/concatenate | solution.py:75
  89.2 0.8 slice.283
  90.0 0.8 slice.282
  90.9 1.6 %gather_fusion = f32[512,512]{1,0:T(8,128)S(1)} fusion(f32[128,512]{1,0:T(8,128)S(1)} %pad_maximum_fusion.2, s32[1024]{0:T(1024)S(1)} %pad_clamp_fusion.3), kind=kCustom, calls=%fused_computation | custom fusion | bytes 2099200 | tf_op jit(solution)/shard_map/jit(_take)/gather | solution.py:208
  92.5 2.6 %gather.19 = f32[64,8,16,32]{3,2,1,0:T(8,128)} reshape(f32[512,512]{1,0:T(8,128)S(1)} %gather_fusion) | data formatting | bytes 2097152 | tf_op jit(solution)/shard_map/jit(_take)/gather | solution.py:208
  95.1 8.6 %shard_map.127 = f32[64,16,64]{2,1,0:T(8,128)} custom-call(s32[64,6]{1,0:T(8,128)} %copy.25.offsets_ref, f32[96,19,128]{2,1,0:T(8,128)} %pad_maximum_fusion.table_ref, f32[64,64,128]{2,1,0:T(8,128)} %pad.4.columns_ref), custom_call_target="tpu_custom_call" | custom-call | tf_op jit(solution)/shard_map/pallas_call | solution.py:77
  103.6 8.3 %fusion.4 = f32[64,16,32]{2,1,0:T(8,128)S(1)} fusion(bf16[64,8,32,32]{3,2,1,0:T(8,128)(2,1)} %copy.35, f32[64,8,16,32]{3,2,1,0:T(8,128)} %gather.19, pred[64,8]{1,0:T(8,128)(4,1)S(1)} %copy.26), kind=kOutput, calls=%fused_computation.8 | convolution fusion | flops 100925440 | bytes 2228736 | tf_op jit(solution)/shard_map/lfrk,lfkq->lrq/dot_general | solution.py:209
  112.0 0.4 fusion.8
  112.4 0.5 fusion.7
  112.9 0.2 copy.34
  113.1 0.9 reshape.152
  (98 shorter events, 2.0 us)
Async XLA Ops:
  0.0 5.1 %copy-start.5 = (f32[3,4096]{1,0:T(4,128)S(1)}, f32[3,4096]{1,0:T(4,128)}, u32[]{:S(2)}) copy-start(f32[3,4096]{1,0:T(4,128)} %param.14) | copy-start | bytes 147460
  0.0 12.5 %copy-start.10 = (bf16[1,3,1024]{2,1,0:T(4,128)(2,1)S(1)}, bf16[1,3,1024]{2,1,0:T(4,128)(2,1)}, u32[]{:S(2)}) copy-start(bf16[1,3,1024]{2,1,0:T(4,128)(2,1)} %param.22) | copy-start | bytes 18436
  0.0 12.6 %copy-start.11 = (bf16[1,3,1024]{2,1,0:T(4,128)(2,1)S(1)}, bf16[1,3,1024]{2,1,0:T(4,128)(2,1)}, u32[]{:S(2)}) copy-start(bf16[1,3,1024]{2,1,0:T(4,128)(2,1)} %param.23) | copy-start | bytes 18436
  0.0 12.6 %copy-start.7 = (bf16[64,1024]{1,0:T(8,128)(2,1)S(1)}, bf16[64,1024]{1,0:T(8,128)(2,1)}, u32[]{:S(2)}) copy-start(bf16[64,1024]{1,0:T(8,128)(2,1)} %param.20) | copy-start | bytes 393220
  3.4 14.3 %copy-start.9 = (bf16[1,4,4,1024]{3,2,1,0:T(4,128)(2,1)S(1)}, bf16[1,4,4,1024]{3,2,1,0:T(4,128)(2,1)}, u32[]{:S(2)}) copy-start(bf16[1,4,4,1024]{3,2,1,0:T(4,128)(2,1)} %param.24) | copy-start | bytes 98308
  3.4 14.7 %copy-start.14 = (s32[64,8]{0,1:T(8,128)S(1)}, s32[64,8]{0,1:T(8,128)}, u32[]{:S(2)}) copy-start(s32[64,8]{0,1:T(8,128)} %param.16) | copy-start | bytes 6148
  3.4 17.0 %copy-start.15 = (s32[4]{0:T(128)S(1)}, s32[4]{0:T(128)}, u32[]{:S(2)}) copy-start(s32[4]{0:T(128)} %constant.56) | copy-start | bytes 52
  5.1 29.2 %copy-start.12 = (s32[64,6]{0,1:T(8,128)S(1)}, s32[64,6]{0,1:T(8,128)}, u32[]{:S(2)}) copy-start(s32[64,6]{0,1:T(8,128)} %param.15) | copy-start | bytes 4612
  5.1 29.9 %copy-start.2 = (bf16[64,8,1024]{2,1,0:T(8,128)(2,1)S(1)}, bf16[64,8,1024]{2,1,0:T(8,128)(2,1)}, u32[]{:S(2)}) copy-start(bf16[64,8,1024]{2,1,0:T(8,128)(2,1)} %param.19) | copy-start | bytes 3145732
  5.9 79.0 %collective-permute-start.1 = (f32[35840]{0:T(1024)}, f32[35840]{0:T(1024)}, u32[]{:S(2)}, u32[]{:S(2)}) collective-permute-start(f32[35840]{0:T(1024)} %pad_maximum_fusion.4), channel_id=1, source_target_pairs={{1,0},{2,1},{3,2},{4,3},{5,4},{6,5},{7,6},{8,7},{9,8},{10,9},{11,1... | collective-permute-start | bytes 430088 | tf_op jit(solution)/shard_map/ppermute | solution.py:186
  9.1 76.8 %collective-permute-start = (f32[35840]{0:T(1024)}, f32[35840]{0:T(1024)}, u32[]{:S(2)}, u32[]{:S(2)}) collective-permute-start(f32[35840]{0:T(1024)} %pad_maximum_fusion.3), channel_id=1, source_target_pairs={{0,1},{1,2},{2,3},{3,4},{4,5},{5,6},{6,7},{7,8},{8,9},{9,10},{10,1... | collective-permute-start | bytes 430088 | tf_op jit(solution)/shard_map/ppermute | solution.py:185
  15.1 6.2 %collective-permute-start.2 = (f32[4,16,32]{2,1,0:T(8,128)S(1)}, f32[4,16,32]{2,1,0:T(8,128)S(1)}, u32[]{:S(2)}, u32[]{:S(2)}) collective-permute-start(f32[4,16,32]{2,1,0:T(8,128)S(1)} %convolution_bitcast_fusion.1), channel_id=1, source_target_pairs={{0,1},{1,0},{2,3},{3,2},{4,5},{5,4},{6,7},{7,6},{8,9},{9,8},{10,11... | collective-permute-start | bytes 24584 | tf_op jit(solution)/shard_map/ppermute | solution.py:32
  21.3 7.4 %collective-permute-start.3 = (f32[5,16,32]{2,1,0:T(8,128)S(1)}, f32[5,16,32]{2,1,0:T(8,128)S(1)}, u32[]{:S(2)}, u32[]{:S(2)}) collective-permute-start(f32[5,16,32]{2,1,0:T(8,128)S(1)} %pad_maximum_fusion.18), channel_id=1, source_target_pairs={{0,2},{1,3},{2,0},{3,1},{4,6},{5,7},{6,4},{7,5},{8,10},{9,11},{10,... | collective-permute-start | bytes 30728 | tf_op jit(solution)/shard_map/ppermute | solution.py:32
  29.4 19.7 %collective-permute-start.4 = (f32[8,16,32]{2,1,0:T(8,128)}, f32[8,16,32]{2,1,0:T(8,128)}, u32[]{:S(2)}, u32[]{:S(2)}) collective-permute-start(f32[8,16,32]{2,1,0:T(8,128)} %fusion.15), channel_id=1, source_target_pairs={{0,4},{1,5},{2,6},{3,7},{4,0},{5,1},{6,2},{7,3},{8,12},{9,13},{10,... | collective-permute-start | bytes 49160 | tf_op jit(solution)/shard_map/ppermute | solution.py:32
  36.4 6.9 %copy-start.3 = (f32[64,16,32]{0,2,1:T(8,128)S(1)}, f32[64,16,32]{0,2,1:T(8,128)}, u32[]{:S(2)}) copy-start(f32[64,16,32]{0,2,1:T(8,128)} %copy.27) | copy-start | bytes 393220
  36.4 7.7 %copy-start.13 = (pred[64,8]{0,1:T(8,128)(4,1)S(1)}, pred[64,8]{0,1:T(8,128)(4,1)}, u32[]{:S(2)}) copy-start(pred[64,8]{0,1:T(8,128)(4,1)} %get-tuple-element.11) | copy-start | bytes 1540
  36.4 7.8 %copy-start.4 = (f32[4,32,4,32]{3,1,2,0:T(8,128)S(1)}, f32[4,32,4,32]{3,1,2,0:T(8,128)}, u32[]{:S(2)}) copy-start(f32[4,32,4,32]{3,1,2,0:T(8,128)} %fusion.22) | copy-start | bytes 196612
  36.5 8.6 %copy-start.8 = (bf16[64,1024]{1,0:T(8,128)(2,1)S(1)}, bf16[64,1024]{1,0:T(8,128)(2,1)}, u32[]{:S(2)}) copy-start(bf16[64,1024]{1,0:T(8,128)(2,1)} %param.21) | copy-start | bytes 393220
  43.3 4.2 %copy-start = (f32[3,4096]{0,1:T(8,128)S(1)}, f32[3,4096]{0,1:T(8,128)}, u32[]{:S(2)}) copy-start(f32[3,4096]{0,1:T(8,128)} %copy.24) | copy-start | bytes 147460
  51.4 9.5 %collective-permute-start.5 = (f32[9,16,32]{2,1,0:T(8,128)S(1)}, f32[9,16,32]{2,1,0:T(8,128)S(1)}, u32[]{:S(2)}, u32[]{:S(2)}) collective-permute-start(f32[9,16,32]{2,1,0:T(8,128)S(1)} %get-tuple-element.38), channel_id=1, source_target_pairs={{0,8},{1,9},{2,10},{3,11},{4,12},{5,13},{6,14},{7,15},{8,16},{9,17... | collective-permute-start | bytes 55304 | tf_op jit(solution)/shard_map/ppermute | solution.py:37
  54.8 7.2 %collective-permute-start.6 = (f32[9,16,32]{2,1,0:T(8,128)S(1)}, f32[9,16,32]{2,1,0:T(8,128)S(1)}, u32[]{:S(2)}, u32[]{:S(2)}) collective-permute-start(f32[9,16,32]{2,1,0:T(8,128)S(1)} %get-tuple-element.39), channel_id=1, source_target_pairs={{8,0},{9,1},{10,2},{11,3},{12,4},{13,5},{14,6},{15,7},{16,8},{17,9... | collective-permute-start | bytes 55304 | tf_op jit(solution)/shard_map/ppermute | solution.py:37
  62.0 21.0 %collective-permute-start.8 = (f32[3,16,32]{2,1,0:T(8,128)S(1)}, f32[3,16,32]{2,1,0:T(8,128)S(1)}, u32[]{:S(2)}, u32[]{:S(2)}) collective-permute-start(f32[3,16,32]{2,1,0:T(8,128)S(1)} %get-tuple-element.43), channel_id=1, source_target_pairs={{16,0},{17,1},{18,2},{19,3},{20,4},{21,5},{22,6},{23,7},{24,8},{25... | collective-permute-start | bytes 18440 | tf_op jit(solution)/shard_map/ppermute | solution.py:37
  73.6 9.3 %collective-permute-start.7 = (f32[3,16,32]{2,1,0:T(8,128)S(1)}, f32[3,16,32]{2,1,0:T(8,128)S(1)}, u32[]{:S(2)}, u32[]{:S(2)}) collective-permute-start(f32[3,16,32]{2,1,0:T(8,128)S(1)} %get-tuple-element.42), channel_id=1, source_target_pairs={{0,16},{1,17},{2,18},{3,19},{4,20},{5,21},{6,22},{7,23},{8,24},{9,... | collective-permute-start | bytes 18440 | tf_op jit(solution)/shard_map/ppermute | solution.py:37
  84.8 6.0 %copy-start.6 = (f32[64,512]{1,0:T(8,128)S(1)}, f32[64,512]{1,0:T(8,128)}, u32[]{:S(2)}) copy-start(f32[64,512]{1,0:T(8,128)} %copy.28) | copy-start | bytes 393220
  103.6 8.7 %copy-start.1 = (f32[64,16,64]{2,1,0:T(8,128)S(1)}, f32[64,16,64]{2,1,0:T(8,128)}, u32[]{:S(2)}) copy-start(f32[64,16,64]{2,1,0:T(8,128)} %shard_map.127) | copy-start | bytes 786436

commit v9 on v8

--- a/solution.py
+++ b/solution.py
@@ -20,6 +20,7 @@
 nugget = 0.5
 partner_steps = (-3, -2, 2, 3)
 highest = lax.Precision.HIGHEST
+bf16_weights = lax.Precision.HIGH
 AXES = ("leaf", "grp")
 
 
@@ -66,7 +67,7 @@
         out_ref[i] = nugget * own[:RHS, :CLUSTER] + (parts[0] + parts[1] + parts[2])
         return carry
 
-    lax.fori_loop(0, leaf_count, one_leaf, 0, unroll=8)
+    lax.fori_loop(0, leaf_count, one_leaf, 0, unroll=16)
 
 
 def near_field_kernel(extended, target_points, near_offsets):
@@ -210,14 +211,14 @@
         "lfrk,lfkq->lrq",
         partner_blocks,
         leaf_coupling.reshape(leaf_count, FAR_BLOCKS, RANK, RANK),
-        precision=highest,
+        precision=bf16_weights,
         preferred_element_type=jnp.float32,
     )
     root_coefficients = jnp.einsum(
         "lrk,lkq->rq",
         leaf_coefficients,
         leaf_up.reshape(leaf_count, RANK, RANK),
-        precision=highest,
+        precision=bf16_weights,
         preferred_element_type=jnp.float32,
     )
     downward = tree_field(root_coefficients, tree_up, tree_down, tree_coupling, me)
@@ -225,7 +226,7 @@
         "rk,lkq->lrq",
         downward,
         leaf_down.reshape(leaf_count, RANK, RANK),
-        precision=highest,
+        precision=bf16_weights,
         preferred_element_type=jnp.float32,
     )
     leaf_field = leaf_far + from_root
@@ -233,7 +234,7 @@
         "lrk,lka->lra",
         leaf_field,
         target_basis.reshape(leaf_count, RANK, CLUSTER),
-        precision=highest,
+        precision=bf16_weights,
         preferred_element_type=jnp.float32,
     )
     product = jnp.transpose(near_sum + far_out, (1, 0, 2))

time: 115 us -> 112 us (0.974)
  matrix products: 13.8 us -> 11.7 us
    dot_general x1, matrix products: 8.32 us -> 6.69 us  [local(): jnp.einsum('lfrk,lfkq->lrq', partner_blocks, leaf_coupling.reshape(leaf_c...]
where the time goes in v9:
time: 112 us; the launch traced here: 111 us
  starting transfers between devices  37.1 us (33%)
  local copies, waits for them, and re-layouts  36.7 us (33%)
  matrix products  11.7 us (10%)
  waiting for transfers between devices  10.7 us (10%)
  Pallas kernels  7.78 us (7%)
  other arithmetic  6.47 us (6%)
    ppermute x4, starting transfers between devices, receive_from(): lax.ppermute(value, AXES, [(s, s - step) for s in range(n) if 0 <= s - st...  22.2 us
    ppermute x3, starting transfers between devices, swap_with(): return lax.ppermute(value, AXES, [(i, i ^ mask) for i in range(n)])  9.13 us
    ppermute x4, waiting for transfers between devices, receive_from(): lax.ppermute(value, AXES, [(s, s - step) for s in range(n) if 0 <= s - st...  7.96 us
    pallas_call x1, Pallas kernels, near_field_kernel(): pl.pallas_call(near_body, out_shape=jax.ShapeDtypeStruct((leaf_count, RHS...  7.78 us
    reshape x1, local copies, waits for them, and re-layouts, local(): leaf_coupling.reshape(leaf_count, FAR_BLOCKS, RANK, RANK)  6.85 us
    dot_general x1, matrix products, local(): jnp.einsum('lfrk,lfkq->lrq', partner_blocks, leaf_coupling.reshape(leaf_c...  6.69 us
    unnamed x41, local copies, waits for them, and re-layouts  5.77 us
    gather x2, local copies, waits for them, and re-layouts, local(): jnp.take(rimmed, far_index, axis=0)  4.17 us
  transfers between devices with their start and end apart: 9, of which 5 were waited for; matrix products, arithmetic and copies ran while one was open for 28% of the time, Pallas kernels for 0%

profile of v9, /device:TPU:394, one launch (start us, length us, event | category | flops | bytes accessed | tf_op | source)
XLA Modules:
  0.0 111.1 jit_solution(4277594654124951869)
XLA Ops:
  0.0 1.2 %reshape.139 = bf16[16,64,64]{2,1,0:T(8,128)(2,1)S(1)} reshape(bf16[16,4096]{1,0:T(8,128)(2,1)} %param.13) | data formatting | bytes 262144 | tf_op jit(solution)/shard_map/reshape | solution.py:171
  1.3 0.9 convert_element_type.22
  2.2 1.2 %copy.20 = bf16[64,2048]{0,1:T(8,128)(2,1)S(1)} copy(bf16[64,2048]{1,0:T(8,128)(2,1)} %param.17) | data formatting | bytes 524288 | tf_op args[4]
  3.5 1.1 copy.22
  4.5 0.4 fusion.10
  5.2 0.7 pad_maximum_fusion.4
  5.9 2.4 %collective-permute-start.1 = (f32[35840]{0:T(1024)}, f32[35840]{0:T(1024)}, u32[]{:S(2)}, u32[]{:S(2)}) collective-permute-start(f32[35840]{0:T(1024)} %pad_maximum_fusion.4), channel_id=1, source_target_pairs={{1,0},{2,1},{3,2},{4,3},{5,4},{6,5},{7,6},{8,7},{9,8},{10,9},{11,1... | collective-permute-start | bytes 430088 | tf_op jit(solution)/shard_map/ppermute | solution.py:187
  8.4 0.7 pad_maximum_fusion.3
  9.1 3.4 %collective-permute-start = (f32[35840]{0:T(1024)}, f32[35840]{0:T(1024)}, u32[]{:S(2)}, u32[]{:S(2)}) collective-permute-start(f32[35840]{0:T(1024)} %pad_maximum_fusion.3), channel_id=1, source_target_pairs={{0,1},{1,2},{2,3},{3,4},{4,5},{5,6},{6,7},{7,8},{8,9},{9,10},{10,1... | collective-permute-start | bytes 430088 | tf_op jit(solution)/shard_map/ppermute | solution.py:186
  12.6 0.2 copy.31
  12.8 0.8 copy.37
  13.6 0.6 fusion.45
  14.6 0.1 convolution_bitcast_fusion.3
  14.7 0.2 convolution_bitcast_fusion.1
  14.9 2.5 %collective-permute-start.2 = (f32[4,16,32]{2,1,0:T(8,128)S(1)}, f32[4,16,32]{2,1,0:T(8,128)S(1)}, u32[]{:S(2)}, u32[]{:S(2)}) collective-permute-start(f32[4,16,32]{2,1,0:T(8,128)S(1)} %convolution_bitcast_fusion.1), channel_id=1, source_target_pairs={{0,1},{1,0},{2,3},{3,2},{4,5},{5,4},{6,7},{7,6},{8,9},{9,8},{10,11... | collective-permute-start | bytes 24584 | tf_op jit(solution)/shard_map/ppermute | solution.py:33
  17.5 0.1 reshape.149
  18.0 0.6 compare_and_fusion
  18.7 0.1 convolution_bitcast_fusion.2
  18.8 1.5 %fusion.22 = f32[4,32,4,32]{3,1,2,0:T(8,128)} fusion(bf16[4,4,32,32]{3,2,1,0:T(8,128)(2,1)S(1)} %reshape.149, f32[1,32,32]{2,1,0:T(8,128)S(1)} %fusion.32, f32[1,32,32]{2,1,0:T(8,128)S(1)} %convolution_bitcast_fusion.2, f32[1,32,32]{2,1,0:T(8,128)S(1)} %bitcast.76, f32[1,32,32]{2,1,0:T(8,128)S(1)} %reshape.154), kind=kOutput, calls=%fused_computation.49 | convolution fusion | flops 6303744 | bytes 114688 | tf_op jit(solution)/shard_map/sqkp,spm->sqkm/dot_general | solution.py:111
  20.3 0.6 pad_clamp_fusion.1
  21.1 4.7 %collective-permute-start.3 = (f32[5,16,32]{2,1,0:T(8,128)S(1)}, f32[5,16,32]{2,1,0:T(8,128)S(1)}, u32[]{:S(2)}, u32[]{:S(2)}) collective-permute-start(f32[5,16,32]{2,1,0:T(8,128)S(1)} %pad_maximum_fusion.18), channel_id=1, source_target_pairs={{0,2},{1,3},{2,0},{3,1},{4,6},{5,7},{6,4},{7,5},{8,10},{9,11},{10,... | collective-permute-start | bytes 30728 | tf_op jit(solution)/shard_map/ppermute | solution.py:33
  25.9 2.7 %collective-permute-done.3 = f32[5,16,32]{2,1,0:T(8,128)S(1)} collective-permute-done((f32[5,16,32]{2,1,0:T(8,128)S(1)}, f32[5,16,32]{2,1,0:T(8,128)S(1)}, u32[]{:S(2)}, u32[]{:S(2)}) %collective-permute-start.3) | collective-permute-done | bytes 10272 | tf_op jit(solution)/shard_map/ppermute | solution.py:33
  28.6 0.6 fusion.15
  29.2 1.9 %collective-permute-start.4 = (f32[8,16,32]{2,1,0:T(8,128)}, f32[8,16,32]{2,1,0:T(8,128)}, u32[]{:S(2)}, u32[]{:S(2)}) collective-permute-start(f32[8,16,32]{2,1,0:T(8,128)} %fusion.15), channel_id=1, source_target_pairs={{0,4},{1,5},{2,6},{3,7},{4,0},{5,1},{6,2},{7,3},{8,12},{9,13},{10,... | collective-permute-start | bytes 49160 | tf_op jit(solution)/shard_map/ppermute | solution.py:33
  31.1 2.0 %copy.24 = f32[3,4096]{0,1:T(8,128)} copy(f32[3,4096]{1,0:T(4,128)S(1)} %copy-done.5) | data formatting | bytes 98304 | tf_op args[1]
  33.1 0.9 copy.27
  34.1 0.7 copy.25.offsets_ref
  34.8 1.4 %copy.30 = bf16[64,8,1024]{0,2,1:T(8,128)(2,1)S(1)} copy(bf16[64,8,1024]{2,1,0:T(8,128)(2,1)S(1)} %copy-done.2) | data formatting | bytes 2097152 | tf_op args[6]
  36.3 6.9 %copy.35 = bf16[64,8,32,32]{3,2,1,0:T(8,128)(2,1)} copy(bf16[64,8,32,32]{0,3,2,1:T(8,128)(2,1)S(1)} %bitcast.68) | data formatting | bytes 2097152 | tf_op jit(solution)/shard_map/reshape | solution.py:213
  43.1 0.8 copy.28
  44.0 0.9 copy.54
  44.9 0.2 copy.33
  45.0 0.8 copy.44
  45.8 1.5 %reshape.151 = bf16[64,32,64]{2,1,0:T(8,128)(2,1)S(1)} reshape(bf16[64,2048]{1,0:T(8,128)(2,1)} %param.18) | data formatting | bytes 524288 | tf_op jit(solution)/shard_map/reshape | solution.py:236
  47.3 1.6 %pad.4.columns_ref = f32[64,64,128]{2,1,0:T(8,128)} pad(f32[64,64,3]{2,1,0:T(8,128)S(1)} %bitcast.69, f32[]{:T(128)} %constant.15.clone.1), padding=0_0x0_0x0_125 | pad | bytes 2146308 | tf_op jit(solution)/shard_map/jit(_pad)/pad | solution.py:77
  48.9 0.7 fusion.40
  49.6 0.7 slice.298
  50.3 0.8 slice.296
  51.1 3.5 %collective-permute-start.5 = (f32[9,16,32]{2,1,0:T(8,128)S(1)}, f32[9,16,32]{2,1,0:T(8,128)S(1)}, u32[]{:S(2)}, u32[]{:S(2)}) collective-permute-start(f32[9,16,32]{2,1,0:T(8,128)S(1)} %get-tuple-element.38), channel_id=1, source_target_pairs={{0,8},{1,9},{2,10},{3,11},{4,12},{5,13},{6,14},{7,15},{8,16},{9,17... | collective-permute-start | bytes 55304 | tf_op jit(solution)/shard_map/ppermute | solution.py:38
  54.6 5.0 %collective-permute-start.6 = (f32[9,16,32]{2,1,0:T(8,128)S(1)}, f32[9,16,32]{2,1,0:T(8,128)S(1)}, u32[]{:S(2)}, u32[]{:S(2)}) collective-permute-start(f32[9,16,32]{2,1,0:T(8,128)S(1)} %get-tuple-element.39), channel_id=1, source_target_pairs={{8,0},{9,1},{10,2},{11,3},{12,4},{13,5},{14,6},{15,7},{16,8},{17,9... | collective-permute-start | bytes 55304 | tf_op jit(solution)/shard_map/ppermute | solution.py:38
  59.7 1.0 collective-permute-done.5
  60.6 1.2 %collective-permute-done.6 = f32[9,16,32]{2,1,0:T(8,128)S(1)} collective-permute-done((f32[9,16,32]{2,1,0:T(8,128)S(1)}, f32[9,16,32]{2,1,0:T(8,128)S(1)}, u32[]{:S(2)}, u32[]{:S(2)}) %collective-permute-start.6) | collective-permute-done | bytes 18464 | tf_op jit(solution)/shard_map/ppermute | solution.py:38
  61.8 11.6 %collective-permute-start.8 = (f32[3,16,32]{2,1,0:T(8,128)S(1)}, f32[3,16,32]{2,1,0:T(8,128)S(1)}, u32[]{:S(2)}, u32[]{:S(2)}) collective-permute-start(f32[3,16,32]{2,1,0:T(8,128)S(1)} %get-tuple-element.43), channel_id=1, source_target_pairs={{16,0},{17,1},{18,2},{19,3},{20,4},{21,5},{22,6},{23,7},{24,8},{25... | collective-permute-start | bytes 18440 | tf_op jit(solution)/shard_map/ppermute | solution.py:38
  73.4 2.1 %collective-permute-start.7 = (f32[3,16,32]{2,1,0:T(8,128)S(1)}, f32[3,16,32]{2,1,0:T(8,128)S(1)}, u32[]{:S(2)}, u32[]{:S(2)}) collective-permute-start(f32[3,16,32]{2,1,0:T(8,128)S(1)} %get-tuple-element.42), channel_id=1, source_target_pairs={{0,16},{1,17},{2,18},{3,19},{4,20},{5,21},{6,22},{7,23},{8,24},{9,... | collective-permute-start | bytes 18440 | tf_op jit(solution)/shard_map/ppermute | solution.py:38
  75.6 0.7 gather_fusion.2
  76.3 0.7 gather_fusion.1
  77.0 5.8 %collective-permute-done.7 = f32[3,16,32]{2,1,0:T(8,128)S(1)} collective-permute-done((f32[3,16,32]{2,1,0:T(8,128)S(1)}, f32[3,16,32]{2,1,0:T(8,128)S(1)}, u32[]{:S(2)}, u32[]{:S(2)}) %collective-permute-start.7) | collective-permute-done | bytes 6176 | tf_op jit(solution)/shard_map/ppermute | solution.py:38
  82.8 0.6 gather_fusion.3
  83.4 1.2 %convolution_bitcast_fusion.4 = f32[16,32,1]{1,0,2:T(8,128)S(1)} fusion(f32[4,4,32,32]{2,1,3,0:T(4,128)} %bitcast.75, f32[1,4,16,32]{3,2,1,0:T(8,128)S(1)} %maximum_bitcast_fusion, f32[1,4,16,32]{3,2,1,0:T(8,128)S(1)} %bitcast.79, f32[1,4,16,32]{3,2,1,0:T(8,128)S(1)} %bitcast.77, f32[1,4,16,32]{3,2,1,0:T(8,128)S(1)} %bitcast.78), kind=kOutput, calls=%fused_computation.18 | convolution fusion | flops 3170304 | bytes 100352 | tf_op jit(solution)/shard_map/sqrk,sqkm->rm/dot_general | solution.py:151
  84.7 0.9 slice.281
  85.7 0.9 slice.279
  86.6 0.4 reshape.144
  87.0 0.6 copy.53
  87.6 1.4 %pad_maximum_fusion.table_ref = f32[96,19,128]{2,1,0:T(8,128)} fusion(f32[96,19,64]{2,1,0:T(8,128)S(1)} %bitcast.70), kind=kLoop, calls=%fused_computation.13 | loop fusion | flops 233472 | bytes 1400832 | tf_op jit(solution)/shard_map/concatenate | solution.py:76
  88.9 0.8 slice.283
  89.8 0.8 slice.282
  90.7 1.6 %gather_fusion = f32[512,512]{1,0:T(8,128)S(1)} fusion(f32[128,512]{1,0:T(8,128)S(1)} %pad_maximum_fusion.2, s32[1024]{0:T(1024)S(1)} %pad_clamp_fusion.3), kind=kCustom, calls=%fused_computation | custom fusion | bytes 2099200 | tf_op jit(solution)/shard_map/jit(_take)/gather | solution.py:209
  92.3 2.6 %gather.19 = f32[64,8,16,32]{3,2,1,0:T(8,128)} reshape(f32[512,512]{1,0:T(8,128)S(1)} %gather_fusion) | data formatting | bytes 2097152 | tf_op jit(solution)/shard_map/jit(_take)/gather | solution.py:209
  94.9 7.8 %shard_map.127 = f32[64,16,64]{2,1,0:T(8,128)} custom-call(s32[64,6]{1,0:T(8,128)} %copy.25.offsets_ref, f32[96,19,128]{2,1,0:T(8,128)} %pad_maximum_fusion.table_ref, f32[64,64,128]{2,1,0:T(8,128)} %pad.4.columns_ref), custom_call_target="tpu_custom_call" | custom-call | tf_op jit(solution)/shard_map/pallas_call | solution.py:78
  102.7 6.7 %fusion.4 = f32[64,16,32]{2,1,0:T(8,128)S(1)} fusion(bf16[64,8,32,32]{3,2,1,0:T(8,128)(2,1)} %copy.35, f32[64,8,16,32]{3,2,1,0:T(8,128)} %gather.19, pred[64,8]{1,0:T(8,128)(4,1)S(1)} %copy.26), kind=kOutput, calls=%fused_computation.8 | convolution fusion | flops 50593792 | bytes 2228736 | tf_op jit(solution)/shard_map/lfrk,lfkq->lrq/dot_general | solution.py:210
  109.4 0.3 fusion.8
  109.7 0.4 fusion.7
  110.1 0.2 copy.34
  110.3 0.9 reshape.152
  (98 shorter events, 2.0 us)
Async XLA Ops:
  0.0 5.1 %copy-start.5 = (f32[3,4096]{1,0:T(4,128)S(1)}, f32[3,4096]{1,0:T(4,128)}, u32[]{:S(2)}) copy-start(f32[3,4096]{1,0:T(4,128)} %param.14) | copy-start | bytes 147460
  0.0 12.5 %copy-start.10 = (bf16[1,3,1024]{2,1,0:T(4,128)(2,1)S(1)}, bf16[1,3,1024]{2,1,0:T(4,128)(2,1)}, u32[]{:S(2)}) copy-start(bf16[1,3,1024]{2,1,0:T(4,128)(2,1)} %param.22) | copy-start | bytes 18436
  0.0 12.6 %copy-start.11 = (bf16[1,3,1024]{2,1,0:T(4,128)(2,1)S(1)}, bf16[1,3,1024]{2,1,0:T(4,128)(2,1)}, u32[]{:S(2)}) copy-start(bf16[1,3,1024]{2,1,0:T(4,128)(2,1)} %param.23) | copy-start | bytes 18436
  0.0 12.6 %copy-start.7 = (bf16[64,1024]{1,0:T(8,128)(2,1)S(1)}, bf16[64,1024]{1,0:T(8,128)(2,1)}, u32[]{:S(2)}) copy-start(bf16[64,1024]{1,0:T(8,128)(2,1)} %param.20) | copy-start | bytes 393220
  3.4 14.1 %copy-start.9 = (bf16[1,4,4,1024]{3,2,1,0:T(4,128)(2,1)S(1)}, bf16[1,4,4,1024]{3,2,1,0:T(4,128)(2,1)}, u32[]{:S(2)}) copy-start(bf16[1,4,4,1024]{3,2,1,0:T(4,128)(2,1)} %param.24) | copy-start | bytes 98308
  3.4 14.5 %copy-start.14 = (s32[64,8]{0,1:T(8,128)S(1)}, s32[64,8]{0,1:T(8,128)}, u32[]{:S(2)}) copy-start(s32[64,8]{0,1:T(8,128)} %param.16) | copy-start | bytes 6148
  3.4 16.8 %copy-start.15 = (s32[4]{0:T(128)S(1)}, s32[4]{0:T(128)}, u32[]{:S(2)}) copy-start(s32[4]{0:T(128)} %constant.56) | copy-start | bytes 52
  5.1 29.0 %copy-start.12 = (s32[64,6]{0,1:T(8,128)S(1)}, s32[64,6]{0,1:T(8,128)}, u32[]{:S(2)}) copy-start(s32[64,6]{0,1:T(8,128)} %param.15) | copy-start | bytes 4612
  5.1 29.7 %copy-start.2 = (bf16[64,8,1024]{2,1,0:T(8,128)(2,1)S(1)}, bf16[64,8,1024]{2,1,0:T(8,128)(2,1)}, u32[]{:S(2)}) copy-start(bf16[64,8,1024]{2,1,0:T(8,128)(2,1)} %param.19) | copy-start | bytes 3145732
  5.9 78.8 %collective-permute-start.1 = (f32[35840]{0:T(1024)}, f32[35840]{0:T(1024)}, u32[]{:S(2)}, u32[]{:S(2)}) collective-permute-start(f32[35840]{0:T(1024)} %pad_maximum_fusion.4), channel_id=1, source_target_pairs={{1,0},{2,1},{3,2},{4,3},{5,4},{6,5},{7,6},{8,7},{9,8},{10,9},{11,1... | collective-permute-start | bytes 430088 | tf_op jit(solution)/shard_map/ppermute | solution.py:187
  9.1 76.5 %collective-permute-start = (f32[35840]{0:T(1024)}, f32[35840]{0:T(1024)}, u32[]{:S(2)}, u32[]{:S(2)}) collective-permute-start(f32[35840]{0:T(1024)} %pad_maximum_fusion.3), channel_id=1, source_target_pairs={{0,1},{1,2},{2,3},{3,4},{4,5},{5,6},{6,7},{7,8},{8,9},{9,10},{10,1... | collective-permute-start | bytes 430088 | tf_op jit(solution)/shard_map/ppermute | solution.py:186
  14.9 6.2 %collective-permute-start.2 = (f32[4,16,32]{2,1,0:T(8,128)S(1)}, f32[4,16,32]{2,1,0:T(8,128)S(1)}, u32[]{:S(2)}, u32[]{:S(2)}) collective-permute-start(f32[4,16,32]{2,1,0:T(8,128)S(1)} %convolution_bitcast_fusion.1), channel_id=1, source_target_pairs={{0,1},{1,0},{2,3},{3,2},{4,5},{5,4},{6,7},{7,6},{8,9},{9,8},{10,11... | collective-permute-start | bytes 24584 | tf_op jit(solution)/shard_map/ppermute | solution.py:33
  21.1 7.4 %collective-permute-start.3 = (f32[5,16,32]{2,1,0:T(8,128)S(1)}, f32[5,16,32]{2,1,0:T(8,128)S(1)}, u32[]{:S(2)}, u32[]{:S(2)}) collective-permute-start(f32[5,16,32]{2,1,0:T(8,128)S(1)} %pad_maximum_fusion.18), channel_id=1, source_target_pairs={{0,2},{1,3},{2,0},{3,1},{4,6},{5,7},{6,4},{7,5},{8,10},{9,11},{10,... | collective-permute-start | bytes 30728 | tf_op jit(solution)/shard_map/ppermute | solution.py:33
  29.2 19.7 %collective-permute-start.4 = (f32[8,16,32]{2,1,0:T(8,128)}, f32[8,16,32]{2,1,0:T(8,128)}, u32[]{:S(2)}, u32[]{:S(2)}) collective-permute-start(f32[8,16,32]{2,1,0:T(8,128)} %fusion.15), channel_id=1, source_target_pairs={{0,4},{1,5},{2,6},{3,7},{4,0},{5,1},{6,2},{7,3},{8,12},{9,13},{10,... | collective-permute-start | bytes 49160 | tf_op jit(solution)/shard_map/ppermute | solution.py:33
  36.2 6.9 %copy-start.3 = (f32[64,16,32]{0,2,1:T(8,128)S(1)}, f32[64,16,32]{0,2,1:T(8,128)}, u32[]{:S(2)}) copy-start(f32[64,16,32]{0,2,1:T(8,128)} %copy.27) | copy-start | bytes 393220
  36.2 7.7 %copy-start.13 = (pred[64,8]{0,1:T(8,128)(4,1)S(1)}, pred[64,8]{0,1:T(8,128)(4,1)}, u32[]{:S(2)}) copy-start(pred[64,8]{0,1:T(8,128)(4,1)} %get-tuple-element.11) | copy-start | bytes 1540
  36.2 7.8 %copy-start.4 = (f32[4,32,4,32]{3,1,2,0:T(8,128)S(1)}, f32[4,32,4,32]{3,1,2,0:T(8,128)}, u32[]{:S(2)}) copy-start(f32[4,32,4,32]{3,1,2,0:T(8,128)} %fusion.22) | copy-start | bytes 196612
  36.2 8.6 %copy-start.8 = (bf16[64,1024]{1,0:T(8,128)(2,1)S(1)}, bf16[64,1024]{1,0:T(8,128)(2,1)}, u32[]{:S(2)}) copy-start(bf16[64,1024]{1,0:T(8,128)(2,1)} %param.21) | copy-start | bytes 393220
  43.1 4.2 %copy-start = (f32[3,4096]{0,1:T(8,128)S(1)}, f32[3,4096]{0,1:T(8,128)}, u32[]{:S(2)}) copy-start(f32[3,4096]{0,1:T(8,128)} %copy.24) | copy-start | bytes 147460
  51.1 9.5 %collective-permute-start.5 = (f32[9,16,32]{2,1,0:T(8,128)S(1)}, f32[9,16,32]{2,1,0:T(8,128)S(1)}, u32[]{:S(2)}, u32[]{:S(2)}) collective-permute-start(f32[9,16,32]{2,1,0:T(8,128)S(1)} %get-tuple-element.38), channel_id=1, source_target_pairs={{0,8},{1,9},{2,10},{3,11},{4,12},{5,13},{6,14},{7,15},{8,16},{9,17... | collective-permute-start | bytes 55304 | tf_op jit(solution)/shard_map/ppermute | solution.py:38
  54.6 7.2 %collective-permute-start.6 = (f32[9,16,32]{2,1,0:T(8,128)S(1)}, f32[9,16,32]{2,1,0:T(8,128)S(1)}, u32[]{:S(2)}, u32[]{:S(2)}) collective-permute-start(f32[9,16,32]{2,1,0:T(8,128)S(1)} %get-tuple-element.39), channel_id=1, source_target_pairs={{8,0},{9,1},{10,2},{11,3},{12,4},{13,5},{14,6},{15,7},{16,8},{17,9... | collective-permute-start | bytes 55304 | tf_op jit(solution)/shard_map/ppermute | solution.py:38
  61.8 21.0 %collective-permute-start.8 = (f32[3,16,32]{2,1,0:T(8,128)S(1)}, f32[3,16,32]{2,1,0:T(8,128)S(1)}, u32[]{:S(2)}, u32[]{:S(2)}) collective-permute-start(f32[3,16,32]{2,1,0:T(8,128)S(1)} %get-tuple-element.43), channel_id=1, source_target_pairs={{16,0},{17,1},{18,2},{19,3},{20,4},{21,5},{22,6},{23,7},{24,8},{25... | collective-permute-start | bytes 18440 | tf_op jit(solution)/shard_map/ppermute | solution.py:38
  73.4 9.3 %collective-permute-start.7 = (f32[3,16,32]{2,1,0:T(8,128)S(1)}, f32[3,16,32]{2,1,0:T(8,128)S(1)}, u32[]{:S(2)}, u32[]{:S(2)}) collective-permute-start(f32[3,16,32]{2,1,0:T(8,128)S(1)} %get-tuple-element.42), channel_id=1, source_target_pairs={{0,16},{1,17},{2,18},{3,19},{4,20},{5,21},{6,22},{7,23},{8,24},{9,... | collective-permute-start | bytes 18440 | tf_op jit(solution)/shard_map/ppermute | solution.py:38
  84.6 6.0 %copy-start.6 = (f32[64,512]{1,0:T(8,128)S(1)}, f32[64,512]{1,0:T(8,128)}, u32[]{:S(2)}) copy-start(f32[64,512]{1,0:T(8,128)} %copy.28) | copy-start | bytes 393220
  102.7 7.0 %copy-start.1 = (f32[64,16,64]{2,1,0:T(8,128)S(1)}, f32[64,16,64]{2,1,0:T(8,128)}, u32[]{:S(2)}) copy-start(f32[64,16,64]{2,1,0:T(8,128)} %shard_map.127) | copy-start | bytes 786436

commit v10 on v9

--- a/solution.py
+++ b/solution.py
@@ -95,7 +95,7 @@
     return jnp.where(bit == 0, jnp.concatenate([own, other]), jnp.concatenate([other, own]))
 
 
-def tree_field(root_coefficients, tree_up, tree_down, tree_coupling, me):
+def tree_field(root_coefficients, tree_up, tree_down, tree_coupling, me, first, second):
     up = tree_up[0].astype(jnp.float32).reshape(TOP_LEVELS, RANK, RANK)
     down = tree_down[0].astype(jnp.float32).reshape(TOP_LEVELS, RANK, RANK)
     cross = tree_coupling[0].astype(jnp.float32).reshape(TOP_LEVELS + 1, 4, RANK, RANK)
@@ -132,10 +132,16 @@
     coef3 = (part3 + got3[7])[None]
 
     node = 8
-    ahead1 = receive_from(jnp.concatenate([octs0[0:3], quads1[0:3], pairs2, coef3]), node)
-    behind1 = receive_from(jnp.concatenate([octs0[5:8], quads1[1:4], pairs2, coef3]), -node)
-    ahead2 = receive_from(jnp.concatenate([pairs2[0:1], coef3, ahead1[8:9]]), 2 * node)
-    behind2 = receive_from(jnp.concatenate([pairs2[1:2], coef3, behind1[8:9]]), -2 * node)
+    to_ahead = jnp.concatenate([octs0[5:8], quads1[1:4], pairs2, coef3])
+    to_behind = jnp.concatenate([octs0[0:3], quads1[0:3], pairs2, coef3])
+    to_ahead, to_behind, first = lax.optimization_barrier((to_ahead, to_behind, first))
+    ahead1 = receive_from(to_behind, node)
+    behind1 = receive_from(to_ahead, -node)
+    to_behind = jnp.concatenate([pairs2[0:1], coef3, ahead1[8:9]])
+    to_ahead = jnp.concatenate([pairs2[1:2], coef3, behind1[8:9]])
+    to_ahead, to_behind, second = lax.optimization_barrier((to_ahead, to_behind, second))
+    ahead2 = receive_from(to_behind, 2 * node)
+    behind2 = receive_from(to_ahead, -2 * node)
     ahead3 = ahead2[2:3]
     behind3 = behind2[2:3]
 
@@ -148,7 +154,7 @@
     chosen2 = jnp.take(window2, bit2 + steps, axis=0, mode="clip")
     chosen3 = jnp.concatenate([behind3, behind2[1:2], ahead2[1:2], ahead3])
     chosen = jnp.stack([chosen0, chosen1, chosen2, chosen3])
-    return jnp.einsum("sqrk,sqkm->rm", chosen, weights, precision=highest)
+    return jnp.einsum("sqrk,sqkm->rm", chosen, weights, precision=highest), first, second
 
 
 def local(
@@ -221,7 +227,9 @@
         precision=bf16_weights,
         preferred_element_type=jnp.float32,
     )
-    downward = tree_field(root_coefficients, tree_up, tree_down, tree_coupling, me)
+    downward, near_sum, leaf_far = tree_field(
+        root_coefficients, tree_up, tree_down, tree_coupling, me, near_sum, leaf_far
+    )
     from_root = jnp.einsum(
         "rk,lkq->lrq",
         downward,

time: 112 us -> 111 us (level)
  the two profiles are of different devices: /device:TPU:394 before, /device:TPU:398 now
where the time goes in v10:
time: 111 us; the launch traced here: 110 us
  local copies, waits for them, and re-layouts  39.6 us (36%)
  starting transfers between devices  33.3 us (30%)
  waiting for transfers between devices  11.1 us (10%)
  matrix products  10.8 us (10%)
  Pallas kernels  7.85 us (7%)
  other arithmetic  6.9 us (6%)
    ppermute x4, starting transfers between devices, receive_from(): lax.ppermute(value, AXES, [(s, s - step) for s in range(n) if 0 <= s - st...  19.7 us
    pallas_call x1, Pallas kernels, near_field_kernel(): pl.pallas_call(near_body, out_shape=jax.ShapeDtypeStruct((leaf_count, RHS...  7.85 us
    reshape x1, local copies, waits for them, and re-layouts, local(): leaf_coupling.reshape(leaf_count, FAR_BLOCKS, RANK, RANK)  6.89 us
    ppermute x3, starting transfers between devices, swap_with(): return lax.ppermute(value, AXES, [(i, i ^ mask) for i in range(n)])  6.87 us
    unnamed x59, local copies, waits for them, and re-layouts  6.74 us
    dot_general x1, matrix products, local(): jnp.einsum('lfrk,lfkq->lrq', partner_blocks, leaf_coupling.reshape(leaf_c...  6.71 us
    ppermute x4, waiting for transfers between devices, receive_from(): lax.ppermute(value, AXES, [(s, s - step) for s in range(n) if 0 <= s - st...  5.99 us
    ppermute x3, waiting for transfers between devices, swap_with(): return lax.ppermute(value, AXES, [(i, i ^ mask) for i in range(n)])  5.15 us
  transfers between devices with their start and end apart: 9, of which 2 were waited for; matrix products, arithmetic and copies ran while one was open for 39% of the time, Pallas kernels for 0%

profile of v10, /device:TPU:398, one launch (start us, length us, event | category | flops | bytes accessed | tf_op | source)
XLA Modules:
  0.0 110.5 jit_solution(7669938471119909605)
XLA Ops:
  0.0 1.3 %copy.20 = bf16[64,2048]{0,1:T(8,128)(2,1)S(1)} copy(bf16[64,2048]{1,0:T(8,128)(2,1)} %param.17) | data formatting | bytes 524288 | tf_op args[4]
  1.3 1.1 copy.22
  2.4 1.2 %reshape.138 = bf16[16,64,64]{2,1,0:T(8,128)(2,1)S(1)} reshape(bf16[16,4096]{1,0:T(8,128)(2,1)} %param.13) | data formatting | bytes 262144 | tf_op jit(solution)/shard_map/reshape | solution.py:177
  3.6 1.1 copy.23
  4.7 0.8 copy.36
  5.5 0.9 slice_reduce_fusion.2
  6.6 0.7 convert_reduce_fusion
  7.4 0.4 fusion.10
  7.8 0.6 fusion.45
  8.6 0.2 convolution_bitcast_fusion.1
  8.8 2.7 %collective-permute-start = (f32[4,16,32]{2,1,0:T(8,128)S(1)}, f32[4,16,32]{2,1,0:T(8,128)S(1)}, u32[]{:S(2)}, u32[]{:S(2)}) collective-permute-start(f32[4,16,32]{2,1,0:T(8,128)S(1)} %convolution_bitcast_fusion.1), channel_id=1, source_target_pairs={{0,1},{1,0},{2,3},{3,2},{4,5},{5,4},{6,7},{7,6},{8,9},{9,8},{10,11... | collective-permute-start | bytes 24584 | tf_op jit(solution)/shard_map/ppermute | solution.py:33
  11.8 0.7 pad_maximum_fusion.4
  12.5 3.1 %collective-permute-start.4 = (f32[35840]{0:T(1024)}, f32[35840]{0:T(1024)}, u32[]{:S(2)}, u32[]{:S(2)}) collective-permute-start(f32[35840]{0:T(1024)} %pad_maximum_fusion.4), channel_id=1, source_target_pairs={{1,0},{2,1},{3,2},{4,3},{5,4},{6,5},{7,6},{8,7},{9,8},{10,9},{11,1... | collective-permute-start | bytes 430088 | tf_op jit(solution)/shard_map/ppermute | solution.py:193
  15.7 0.7 pad_maximum_fusion.3
  16.4 3.7 %collective-permute-start.3 = (f32[35840]{0:T(1024)}, f32[35840]{0:T(1024)}, u32[]{:S(2)}, u32[]{:S(2)}) collective-permute-start(f32[35840]{0:T(1024)} %pad_maximum_fusion.3), channel_id=1, source_target_pairs={{0,1},{1,2},{2,3},{3,4},{4,5},{5,6},{6,7},{7,8},{8,9},{9,10},{10,1... | collective-permute-start | bytes 430088 | tf_op jit(solution)/shard_map/ppermute | solution.py:192
  20.1 0.1 reshape.149
  20.6 0.6 compare_and_fusion
  21.4 1.5 %fusion.22 = f32[4,32,4,32]{3,1,2,0:T(8,128)} fusion(bf16[4,4,32,32]{3,2,1,0:T(8,128)(2,1)S(1)} %reshape.149, f32[1,32,32]{2,1,0:T(8,128)S(1)} %fusion.32, f32[1,32,32]{2,1,0:T(8,128)S(1)} %convolution_bitcast_fusion.2, f32[1,32,32]{2,1,0:T(8,128)S(1)} %bitcast.76, f32[1,32,32]{2,1,0:T(8,128)S(1)} %reshape.154), kind=kOutput, calls=%fused_computation.49 | convolution fusion | flops 6303744 | bytes 114688 | tf_op jit(solution)/shard_map/sqkp,spm->sqkm/dot_general | solution.py:111
  22.9 0.6 pad_clamp_fusion.1
  23.7 2.2 %collective-permute-start.1 = (f32[5,16,32]{2,1,0:T(8,128)S(1)}, f32[5,16,32]{2,1,0:T(8,128)S(1)}, u32[]{:S(2)}, u32[]{:S(2)}) collective-permute-start(f32[5,16,32]{2,1,0:T(8,128)S(1)} %pad_maximum_fusion.18), channel_id=1, source_target_pairs={{0,2},{1,3},{2,0},{3,1},{4,6},{5,7},{6,4},{7,5},{8,10},{9,11},{10,... | collective-permute-start | bytes 30728 | tf_op jit(solution)/shard_map/ppermute | solution.py:33
  26.0 5.1 %collective-permute-done.1 = f32[5,16,32]{2,1,0:T(8,128)S(1)} collective-permute-done((f32[5,16,32]{2,1,0:T(8,128)S(1)}, f32[5,16,32]{2,1,0:T(8,128)S(1)}, u32[]{:S(2)}, u32[]{:S(2)}) %collective-permute-start.1) | collective-permute-done | bytes 10272 | tf_op jit(solution)/shard_map/ppermute | solution.py:33
  31.2 0.6 fusion.15
  31.8 1.9 %collective-permute-start.2 = (f32[8,16,32]{2,1,0:T(8,128)}, f32[8,16,32]{2,1,0:T(8,128)}, u32[]{:S(2)}, u32[]{:S(2)}) collective-permute-start(f32[8,16,32]{2,1,0:T(8,128)} %fusion.15), channel_id=1, source_target_pairs={{0,4},{1,5},{2,6},{3,7},{4,0},{5,1},{6,2},{7,3},{8,12},{9,13},{10,... | collective-permute-start | bytes 49160 | tf_op jit(solution)/shard_map/ppermute | solution.py:33
  33.8 2.0 %copy.25 = f32[3,4096]{0,1:T(8,128)} copy(f32[3,4096]{1,0:T(4,128)S(1)} %copy-done.6) | data formatting | bytes 98304 | tf_op args[1]
  35.8 0.9 copy.28
  36.7 0.7 copy.26.offsets_ref
  37.4 1.4 %copy.31 = bf16[64,8,1024]{0,2,1:T(8,128)(2,1)S(1)} copy(bf16[64,8,1024]{2,1,0:T(8,128)(2,1)S(1)} %copy-done.2) | data formatting | bytes 2097152 | tf_op args[6]
  38.9 6.9 %copy.32 = bf16[64,8,32,32]{3,2,1,0:T(8,128)(2,1)} copy(bf16[64,8,32,32]{0,3,2,1:T(8,128)(2,1)S(1)} %bitcast.68) | data formatting | bytes 2097152 | tf_op jit(solution)/shard_map/reshape | solution.py:219
  45.8 0.8 copy.29
  46.5 0.7 copy.27
  47.2 0.9 copy.54
  48.1 0.2 copy.34
  48.3 0.8 copy.44
  49.1 1.5 %reshape.151 = bf16[64,32,64]{2,1,0:T(8,128)(2,1)S(1)} reshape(bf16[64,2048]{1,0:T(8,128)(2,1)} %param.18) | data formatting | bytes 524288 | tf_op jit(solution)/shard_map/reshape | solution.py:244
  50.6 1.5 %pad.4.columns_ref = f32[64,64,128]{2,1,0:T(8,128)} pad(f32[64,64,3]{2,1,0:T(8,128)S(1)} %bitcast.69, f32[]{:T(128)} %constant.36.clone.1), padding=0_0x0_0x0_125 | pad | bytes 2146308 | tf_op jit(solution)/shard_map/jit(_pad)/pad | solution.py:77
  52.1 0.7 fusion.40
  52.8 0.7 slice.292
  53.6 0.8 slice.290
  54.4 0.6 fusion.43
  55.0 0.7 pad_maximum_fusion.7
  55.7 0.9 slice.301
  56.6 0.9 slice.299
  57.6 0.4 reshape.145
  57.9 0.6 copy.53
  58.5 1.4 %pad_maximum_fusion.table_ref = f32[96,19,128]{2,1,0:T(8,128)} fusion(f32[96,19,64]{2,1,0:T(8,128)S(1)} %bitcast.70), kind=kLoop, calls=%fused_computation.13 | loop fusion | flops 233472 | bytes 1400832 | tf_op jit(solution)/shard_map/concatenate | solution.py:76
  59.9 7.9 %shard_map.127 = f32[64,16,64]{2,1,0:T(8,128)} custom-call(s32[64,6]{1,0:T(8,128)} %copy.26.offsets_ref, f32[96,19,128]{2,1,0:T(8,128)} %pad_maximum_fusion.table_ref, f32[64,64,128]{2,1,0:T(8,128)} %pad.4.columns_ref), custom_call_target="tpu_custom_call" | custom-call | tf_op jit(solution)/shard_map/pallas_call | solution.py:78
  67.7 2.5 %collective-permute-start.6 = (f32[9,16,32]{2,1,0:T(8,128)}, f32[9,16,32]{2,1,0:T(8,128)S(1)}, u32[]{:S(2)}, u32[]{:S(2)}) collective-permute-start(f32[9,16,32]{2,1,0:T(8,128)} %get-tuple-element.13), channel_id=1, source_target_pairs={{8,0},{9,1},{10,2},{11,3},{12,4},{13,5},{14,6},{15,7},{16,8},{17,9... | collective-permute-start | bytes 55304 | tf_op jit(solution)/shard_map/ppermute | solution.py:38
  70.3 3.5 %collective-permute-start.5 = (f32[9,16,32]{2,1,0:T(8,128)}, f32[9,16,32]{2,1,0:T(8,128)S(1)}, u32[]{:S(2)}, u32[]{:S(2)}) collective-permute-start(f32[9,16,32]{2,1,0:T(8,128)} %get-tuple-element.12), channel_id=1, source_target_pairs={{0,8},{1,9},{2,10},{3,11},{4,12},{5,13},{6,14},{7,15},{8,16},{9,17... | collective-permute-start | bytes 55304 | tf_op jit(solution)/shard_map/ppermute | solution.py:38
  73.7 0.8 slice.307
  74.6 0.8 slice.306
  75.5 1.6 %gather_fusion = f32[512,512]{1,0:T(8,128)S(1)} fusion(f32[128,512]{1,0:T(8,128)S(1)} %pad_maximum_fusion.2, s32[1024]{0:T(1024)S(1)} %pad_clamp_fusion.3), kind=kCustom, calls=%fused_computation | custom fusion | bytes 2099200 | tf_op jit(solution)/shard_map/jit(_take)/gather | solution.py:215
  77.1 2.6 %gather.19 = f32[64,8,16,32]{3,2,1,0:T(8,128)} reshape(f32[512,512]{1,0:T(8,128)S(1)} %gather_fusion) | data formatting | bytes 2097152 | tf_op jit(solution)/shard_map/jit(_take)/gather | solution.py:215
  79.8 6.7 %fusion.4 = f32[64,16,32]{2,1,0:T(8,128)S(1)} fusion(bf16[64,8,32,32]{3,2,1,0:T(8,128)(2,1)} %copy.32, f32[64,8,16,32]{3,2,1,0:T(8,128)} %gather.19, pred[64,8]{1,0:T(8,128)(4,1)S(1)} %copy-done.16), kind=kOutput, calls=%fused_computation.8 | convolution fusion | flops 50593792 | bytes 2228736 | tf_op jit(solution)/shard_map/lfrk,lfkq->lrq/dot_general | solution.py:216
  86.6 11.8 %collective-permute-start.8 = (f32[3,16,32]{2,1,0:T(8,128)S(1)}, f32[3,16,32]{2,1,0:T(8,128)S(1)}, u32[]{:S(2)}, u32[]{:S(2)}) collective-permute-start(f32[3,16,32]{2,1,0:T(8,128)S(1)} %get-tuple-element.16), channel_id=1, source_target_pairs={{16,0},{17,1},{18,2},{19,3},{20,4},{21,5},{22,6},{23,7},{24,8},{25... | collective-permute-start | bytes 18440 | tf_op jit(solution)/shard_map/ppermute | solution.py:38
  98.4 1.9 %collective-permute-start.7 = (f32[3,16,32]{2,1,0:T(8,128)S(1)}, f32[3,16,32]{2,1,0:T(8,128)S(1)}, u32[]{:S(2)}, u32[]{:S(2)}) collective-permute-start(f32[3,16,32]{2,1,0:T(8,128)S(1)} %get-tuple-element.15), channel_id=1, source_target_pairs={{0,16},{1,17},{2,18},{3,19},{4,20},{5,21},{6,22},{7,23},{8,24},{9,... | collective-permute-start | bytes 18440 | tf_op jit(solution)/shard_map/ppermute | solution.py:38
  100.4 0.7 gather_fusion.2
  101.1 0.7 gather_fusion.1
  101.7 6.0 %collective-permute-done.7 = f32[3,16,32]{2,1,0:T(8,128)S(1)} collective-permute-done((f32[3,16,32]{2,1,0:T(8,128)S(1)}, f32[3,16,32]{2,1,0:T(8,128)S(1)}, u32[]{:S(2)}, u32[]{:S(2)}) %collective-permute-start.7) | collective-permute-done | bytes 6176 | tf_op jit(solution)/shard_map/ppermute | solution.py:38
  107.8 0.6 gather_fusion.3
  108.4 0.3 convolution_bitcast_fusion.4
  108.7 0.3 fusion.8
  109.0 0.4 fusion.7
  109.4 0.2 copy.35
  109.6 0.9 reshape.152
  (116 shorter events, 2.1 us)
Async XLA Ops:
  0.0 11.6 %copy-start.7 = (bf16[16,4096]{1,0:T(8,128)(2,1)S(1)}, bf16[16,4096]{1,0:T(8,128)(2,1)}, u32[]{:S(2)}) copy-start(bf16[16,4096]{1,0:T(8,128)(2,1)} %param.13) | copy-start | bytes 393220
  0.0 11.7 %copy-start.6 = (f32[3,4096]{1,0:T(4,128)S(1)}, f32[3,4096]{1,0:T(4,128)}, u32[]{:S(2)}) copy-start(f32[3,4096]{1,0:T(4,128)} %param.14) | copy-start | bytes 147460
  1.3 18.8 %copy-start.18 = (bf16[1,3,1024]{2,1,0:T(4,128)(2,1)S(1)}, bf16[1,3,1024]{2,1,0:T(4,128)(2,1)}, u32[]{:S(2)}) copy-start(bf16[1,3,1024]{2,1,0:T(4,128)(2,1)} %param.23) | copy-start | bytes 18436
  1.3 18.8 %copy-start.17 = (bf16[1,4,4,1024]{3,2,1,0:T(4,128)(2,1)S(1)}, bf16[1,4,4,1024]{3,2,1,0:T(4,128)(2,1)}, u32[]{:S(2)}) copy-start(bf16[1,4,4,1024]{3,2,1,0:T(4,128)(2,1)} %param.24) | copy-start | bytes 98308
  2.4 18.2 %copy-start.23 = (s32[64,8]{0,1:T(8,128)S(1)}, s32[64,8]{0,1:T(8,128)}, u32[]{:S(2)}) copy-start(s32[64,8]{0,1:T(8,128)} %param.16) | copy-start | bytes 6148
  3.6 19.3 %copy-start.24 = (s32[4]{0:T(128)S(1)}, s32[4]{0:T(128)}, u32[]{:S(2)}) copy-start(s32[4]{0:T(128)} %constant.56) | copy-start | bytes 52
  8.3 28.4 %copy-start.21 = (s32[64,6]{0,1:T(8,128)S(1)}, s32[64,6]{0,1:T(8,128)}, u32[]{:S(2)}) copy-start(s32[64,6]{0,1:T(8,128)} %param.15) | copy-start | bytes 4612
  8.3 29.1 %copy-start.2 = (bf16[64,8,1024]{2,1,0:T(8,128)(2,1)S(1)}, bf16[64,8,1024]{2,1,0:T(8,128)(2,1)}, u32[]{:S(2)}) copy-start(bf16[64,8,1024]{2,1,0:T(8,128)(2,1)} %param.19) | copy-start | bytes 3145732
  8.8 14.9 %collective-permute-start = (f32[4,16,32]{2,1,0:T(8,128)S(1)}, f32[4,16,32]{2,1,0:T(8,128)S(1)}, u32[]{:S(2)}, u32[]{:S(2)}) collective-permute-start(f32[4,16,32]{2,1,0:T(8,128)S(1)} %convolution_bitcast_fusion.1), channel_id=1, source_target_pairs={{0,1},{1,0},{2,3},{3,2},{4,5},{5,4},{6,7},{7,6},{8,9},{9,8},{10,11... | collective-permute-start | bytes 24584 | tf_op jit(solution)/shard_map/ppermute | solution.py:33
  12.5 43.2 %collective-permute-start.4 = (f32[35840]{0:T(1024)}, f32[35840]{0:T(1024)}, u32[]{:S(2)}, u32[]{:S(2)}) collective-permute-start(f32[35840]{0:T(1024)} %pad_maximum_fusion.4), channel_id=1, source_target_pairs={{1,0},{2,1},{3,2},{4,3},{5,4},{6,5},{7,6},{8,7},{9,8},{10,9},{11,1... | collective-permute-start | bytes 430088 | tf_op jit(solution)/shard_map/ppermute | solution.py:193
  16.4 40.2 %collective-permute-start.3 = (f32[35840]{0:T(1024)}, f32[35840]{0:T(1024)}, u32[]{:S(2)}, u32[]{:S(2)}) collective-permute-start(f32[35840]{0:T(1024)} %pad_maximum_fusion.3), channel_id=1, source_target_pairs={{0,1},{1,2},{2,3},{3,4},{4,5},{5,6},{6,7},{7,8},{8,9},{9,10},{10,1... | collective-permute-start | bytes 430088 | tf_op jit(solution)/shard_map/ppermute | solution.py:192
  23.7 7.4 %collective-permute-start.1 = (f32[5,16,32]{2,1,0:T(8,128)S(1)}, f32[5,16,32]{2,1,0:T(8,128)S(1)}, u32[]{:S(2)}, u32[]{:S(2)}) collective-permute-start(f32[5,16,32]{2,1,0:T(8,128)S(1)} %pad_maximum_fusion.18), channel_id=1, source_target_pairs={{0,2},{1,3},{2,0},{3,1},{4,6},{5,7},{6,4},{7,5},{8,10},{9,11},{10,... | collective-permute-start | bytes 30728 | tf_op jit(solution)/shard_map/ppermute | solution.py:33
  31.2 14.6 %copy-start.9 = (f32[4,16,32]{2,1,0:T(8,128)}, f32[4,16,32]{2,1,0:T(8,128)S(1)}, u32[]{:S(2)}) copy-start(f32[4,16,32]{2,1,0:T(8,128)S(1)} %maximum_select_fusion) | copy-start | bytes 24580
  31.8 20.3 %collective-permute-start.2 = (f32[8,16,32]{2,1,0:T(8,128)}, f32[8,16,32]{2,1,0:T(8,128)}, u32[]{:S(2)}, u32[]{:S(2)}) collective-permute-start(f32[8,16,32]{2,1,0:T(8,128)} %fusion.15), channel_id=1, source_target_pairs={{0,4},{1,5},{2,6},{3,7},{4,0},{5,1},{6,2},{7,3},{8,12},{9,13},{10,... | collective-permute-start | bytes 49160 | tf_op jit(solution)/shard_map/ppermute | solution.py:33
  37.4 9.1 %copy-start.22 = (pred[64,8]{0,1:T(8,128)(4,1)S(1)}, pred[64,8]{0,1:T(8,128)(4,1)}, u32[]{:S(2)}) copy-start(pred[64,8]{0,1:T(8,128)(4,1)} %get-tuple-element.23) | copy-start | bytes 1540
  38.8 6.9 %copy-start.3 = (f32[64,16,32]{0,2,1:T(8,128)S(1)}, f32[64,16,32]{0,2,1:T(8,128)}, u32[]{:S(2)}) copy-start(f32[64,16,32]{0,2,1:T(8,128)} %copy.28) | copy-start | bytes 393220
  38.8 8.4 %copy-start.4 = (f32[4,32,4,32]{3,1,2,0:T(8,128)S(1)}, f32[4,32,4,32]{3,1,2,0:T(8,128)}, u32[]{:S(2)}) copy-start(f32[4,32,4,32]{3,1,2,0:T(8,128)} %fusion.22) | copy-start | bytes 196612
  38.8 9.3 %copy-start.11 = (bf16[64,1024]{1,0:T(8,128)(2,1)S(1)}, bf16[64,1024]{1,0:T(8,128)(2,1)}, u32[]{:S(2)}) copy-start(bf16[64,1024]{1,0:T(8,128)(2,1)} %param.21) | copy-start | bytes 393220
  45.7 4.8 %copy-start = (f32[3,4096]{0,1:T(8,128)S(1)}, f32[3,4096]{0,1:T(8,128)}, u32[]{:S(2)}) copy-start(f32[3,4096]{0,1:T(8,128)} %copy.25) | copy-start | bytes 147460
  50.5 3.8 %copy-start.10 = (f32[4,16,32]{2,1,0:T(8,128)S(1)}, f32[4,16,32]{2,1,0:T(8,128)}, u32[]{:S(2)}) copy-start(f32[4,16,32]{2,1,0:T(8,128)} %copy-done.9) | copy-start | bytes 24580
  52.8 0.8 copy-start.12
  52.8 2.8 %copy-start.14 = (f32[1,16,32]{2,1,0:T(8,128)}, f32[1,16,32]{2,1,0:T(8,128)S(1)}, u32[]{:S(2)}) copy-start(f32[1,16,32]{2,1,0:T(8,128)S(1)} %get-tuple-element.36) | copy-start | bytes 6148
  57.9 17.5 %copy-start.8 = (f32[64,512]{1,0:T(8,128)S(1)}, f32[64,512]{1,0:T(8,128)}, u32[]{:S(2)}) copy-start(f32[64,512]{1,0:T(8,128)} %copy.29) | copy-start | bytes 393220
  67.7 18.8 %collective-permute-start.6 = (f32[9,16,32]{2,1,0:T(8,128)}, f32[9,16,32]{2,1,0:T(8,128)S(1)}, u32[]{:S(2)}, u32[]{:S(2)}) collective-permute-start(f32[9,16,32]{2,1,0:T(8,128)} %get-tuple-element.13), channel_id=1, source_target_pairs={{8,0},{9,1},{10,2},{11,3},{12,4},{13,5},{14,6},{15,7},{16,8},{17,9... | collective-permute-start | bytes 55304 | tf_op jit(solution)/shard_map/ppermute | solution.py:38
  70.3 16.3 %collective-permute-start.5 = (f32[9,16,32]{2,1,0:T(8,128)}, f32[9,16,32]{2,1,0:T(8,128)S(1)}, u32[]{:S(2)}, u32[]{:S(2)}) collective-permute-start(f32[9,16,32]{2,1,0:T(8,128)} %get-tuple-element.12), channel_id=1, source_target_pairs={{0,8},{1,9},{2,10},{3,11},{4,12},{5,13},{6,14},{7,15},{8,16},{9,17... | collective-permute-start | bytes 55304 | tf_op jit(solution)/shard_map/ppermute | solution.py:38
  77.1 2.6 %copy-start.16 = (pred[64,8]{1,0:T(8,128)(4,1)S(1)}, pred[64,8]{1,0:T(8,128)(4,1)}, u32[]{:S(2)}) copy-start(pred[64,8]{1,0:T(8,128)(4,1)} %copy.27) | copy-start | bytes 1540
  79.7 6.8 %copy-start.15 = (f32[1,16,32]{2,1,0:T(8,128)S(1)}, f32[1,16,32]{2,1,0:T(8,128)}, u32[]{:S(2)}) copy-start(f32[1,16,32]{2,1,0:T(8,128)} %copy-done.14) | copy-start | bytes 6148
  79.7 6.8 %copy-start.19 = (f32[1,16,32]{2,1,0:T(8,128)S(1)}, f32[1,16,32]{2,1,0:T(8,128)}, u32[]{:S(2)}) copy-start(f32[1,16,32]{2,1,0:T(8,128)} %get-tuple-element.52) | copy-start | bytes 6148
  79.7 6.8 %copy-start.20 = (f32[1,16,32]{2,1,0:T(8,128)S(1)}, f32[1,16,32]{2,1,0:T(8,128)}, u32[]{:S(2)}) copy-start(f32[1,16,32]{2,1,0:T(8,128)} %get-tuple-element.53) | copy-start | bytes 6148
  79.8 28.0 %copy-start.13 = (f32[1,16,32]{2,1,0:T(8,128)S(1)}, f32[1,16,32]{2,1,0:T(8,128)}, u32[]{:S(2)}) copy-start(f32[1,16,32]{2,1,0:T(8,128)} %copy-done.12) | copy-start | bytes 6148
  79.8 28.6 %copy-start.5 = (f32[4,32,4,32]{3,2,1,0:T(4,128)S(1)}, f32[4,32,4,32]{3,2,1,0:T(4,128)}, u32[]{:S(2)}) copy-start(f32[4,32,4,32]{3,2,1,0:T(4,128)} %copy.54) | copy-start | bytes 196612
  79.8 29.2 %copy-start.1 = (f32[64,16,64]{2,1,0:T(8,128)S(1)}, f32[64,16,64]{2,1,0:T(8,128)}, u32[]{:S(2)}) copy-start(f32[64,16,64]{2,1,0:T(8,128)} %shard_map.127) | copy-start | bytes 786436
  86.6 21.2 %collective-permute-start.8 = (f32[3,16,32]{2,1,0:T(8,128)S(1)}, f32[3,16,32]{2,1,0:T(8,128)S(1)}, u32[]{:S(2)}, u32[]{:S(2)}) collective-permute-start(f32[3,16,32]{2,1,0:T(8,128)S(1)} %get-tuple-element.16), channel_id=1, source_target_pairs={{16,0},{17,1},{18,2},{19,3},{20,4},{21,5},{22,6},{23,7},{24,8},{25... | collective-permute-start | bytes 18440 | tf_op jit(solution)/shard_map/ppermute | solution.py:38
  98.4 9.3 %collective-permute-start.7 = (f32[3,16,32]{2,1,0:T(8,128)S(1)}, f32[3,16,32]{2,1,0:T(8,128)S(1)}, u32[]{:S(2)}, u32[]{:S(2)}) collective-permute-start(f32[3,16,32]{2,1,0:T(8,128)S(1)} %get-tuple-element.15), channel_id=1, source_target_pairs={{0,16},{1,17},{2,18},{3,19},{4,20},{5,21},{6,22},{7,23},{8,24},{9,... | collective-permute-start | bytes 18440 | tf_op jit(solution)/shard_map/ppermute | solution.py:38

commit v11 on v10

--- a/solution.py
+++ b/solution.py
@@ -95,7 +95,7 @@
     return jnp.where(bit == 0, jnp.concatenate([own, other]), jnp.concatenate([other, own]))
 
 
-def tree_field(root_coefficients, tree_up, tree_down, tree_coupling, me, first, second):
+def tree_weights(tree_up, tree_down, tree_coupling):
     up = tree_up[0].astype(jnp.float32).reshape(TOP_LEVELS, RANK, RANK)
     down = tree_down[0].astype(jnp.float32).reshape(TOP_LEVELS, RANK, RANK)
     cross = tree_coupling[0].astype(jnp.float32).reshape(TOP_LEVELS + 1, 4, RANK, RANK)
@@ -109,27 +109,22 @@
     push3 = mm(down[2], push2)
     pushes = jnp.stack([eye, push1, push2, push3])
     weights = jnp.einsum("sqkp,spm->sqkm", cross, pushes, precision=highest)
-
-    p = jnp.einsum("rk,skq->srq", root_coefficients, lifts, precision=highest)
-
+    return lifts, weights
+
+
+def tree_field(p, partner_p, weights, me, first, second):
     bit0 = me & 1
-    bit1 = (me >> 1) & 1
+    pair = (me >> 1) & 3
     bit2 = (me >> 2) & 1
-    got1 = swap_with(p, 1)
-    pairs0 = ordered(bit0, p[0:1], got1[0:1])
-    coef1 = p[1] + got1[1]
-    part2 = p[2] + got1[2]
-    part3 = p[3] + got1[3]
-    got2 = swap_with(jnp.concatenate([pairs0, coef1[None], part2[None], part3[None]]), 2)
-    quads0 = ordered(bit1, pairs0, got2[0:2])
-    pairs1 = ordered(bit1, coef1[None], got2[2:3])
-    coef2 = part2 + got2[3]
-    part3 = part3 + got2[4]
-    got3 = swap_with(jnp.concatenate([quads0, pairs1, coef2[None], part3[None]]), 4)
-    octs0 = ordered(bit2, quads0, got3[0:4])
-    quads1 = ordered(bit2, pairs1, got3[4:6])
-    pairs2 = ordered(bit2, coef2[None], got3[6:7])
-    coef3 = (part3 + got3[7])[None]
+    pairs0 = ordered(bit0, p[0:1], partner_p[0:1])
+    summed = p[1:4] + partner_p[1:4]
+    mine = jnp.concatenate([pairs0, summed])
+    held = jnp.stack([mine, swap_with(mine, 2), swap_with(mine, 4), swap_with(mine, 6)])
+    node_pairs = jnp.take(held, pair ^ jnp.arange(4, dtype=jnp.int32), axis=0, mode="clip")
+    octs0 = node_pairs[:, 0:2].reshape(8, RHS, RANK)
+    quads1 = node_pairs[:, 2]
+    pairs2 = node_pairs[0::2, 3] + node_pairs[1::2, 3]
+    coef3 = jnp.sum(node_pairs[:, 4], axis=0)[None]
 
     node = 8
     to_ahead = jnp.concatenate([octs0[5:8], quads1[1:4], pairs2, coef3])
@@ -150,7 +145,7 @@
     window2 = jnp.concatenate([behind2[0:1], behind1[6:8], pairs2, ahead1[6:8], ahead2[0:1]])
     steps = jnp.array(partner_steps, dtype=jnp.int32) + 3
     chosen0 = jnp.take(window0, (me & 7) + steps, axis=0, mode="clip")
-    chosen1 = jnp.take(window1, ((me >> 1) & 3) + steps, axis=0, mode="clip")
+    chosen1 = jnp.take(window1, pair + steps, axis=0, mode="clip")
     chosen2 = jnp.take(window2, bit2 + steps, axis=0, mode="clip")
     chosen3 = jnp.concatenate([behind3, behind2[1:2], ahead2[1:2], ahead3])
     chosen = jnp.stack([chosen0, chosen1, chosen2, chosen3])
@@ -183,15 +178,31 @@
     )
     coef_rows = leaf_coefficients.reshape(leaf_count, RHS * RANK)
 
+    root_coefficients = jnp.einsum(
+        "lrk,lkq->rq",
+        leaf_coefficients,
+        leaf_up.reshape(leaf_count, RANK, RANK),
+        precision=bf16_weights,
+        preferred_element_type=jnp.float32,
+    )
+    lifts, weights = tree_weights(tree_up, tree_down, tree_coupling)
+    p = jnp.einsum("rk,skq->srq", root_coefficients, lifts, precision=highest)
+
     packed = jnp.concatenate([sources.astype(jnp.float32), points], axis=0)
     width = NEAR_REACH * CLUSTER
     to_right = jnp.concatenate(
-        [packed[:, -width:].reshape(-1), coef_rows[-FAR_REACH:].reshape(-1)]
-    )
-    to_left = jnp.concatenate([packed[:, :width].reshape(-1), coef_rows[:FAR_REACH].reshape(-1)])
+        [packed[:, -width:].reshape(-1), coef_rows[-FAR_REACH:].reshape(-1), p.reshape(-1)]
+    )
+    to_left = jnp.concatenate(
+        [packed[:, :width].reshape(-1), coef_rows[:FAR_REACH].reshape(-1), p.reshape(-1)]
+    )
     from_left = lax.ppermute(to_right, AXES, [(i, i + 1) for i in range(n - 1)])
     from_right = lax.ppermute(to_left, AXES, [(i + 1, i) for i in range(n - 1)])
     split = (RHS + 3) * width
+    split2 = split + FAR_REACH * RHS * RANK
+    partner_p = jnp.where(
+        (me & 1) == 0, from_right[split2:], from_left[split2:]
+    ).reshape(TOP_LEVELS + 1, RHS, RANK)
     extended = jnp.concatenate(
         [
             from_left[:split].reshape(RHS + 3, width),
@@ -202,9 +213,9 @@
     ).reshape(RHS + 3, leaf_count + 2 * NEAR_REACH, CLUSTER)
     rimmed = jnp.concatenate(
         [
-            from_left[split:].reshape(FAR_REACH, RHS * RANK),
+            from_left[split:split2].reshape(FAR_REACH, RHS * RANK),
             coef_rows,
-            from_right[split:].reshape(FAR_REACH, RHS * RANK),
+            from_right[split:split2].reshape(FAR_REACH, RHS * RANK),
         ]
     )
 
@@ -220,16 +231,7 @@
         precision=bf16_weights,
         preferred_element_type=jnp.float32,
     )
-    root_coefficients = jnp.einsum(
-        "lrk,lkq->rq",
-        leaf_coefficients,
-        leaf_up.reshape(leaf_count, RANK, RANK),
-        precision=bf16_weights,
-        preferred_element_type=jnp.float32,
-    )
-    downward, near_sum, leaf_far = tree_field(
-        root_coefficients, tree_up, tree_down, tree_coupling, me, near_sum, leaf_far
-    )
+    downward, near_sum, leaf_far = tree_field(p, partner_p, weights, me, near_sum, leaf_far)
     from_root = jnp.einsum(
         "rk,lkq->lrq",
         downward,

time: 111 us -> 113 us (1.018)
  the two profiles are of different devices: /device:TPU:398 before, /device:TPU:384 now
where the time goes in v11:
time: 113 us; the launch traced here: 112 us
  local copies, waits for them, and re-layouts  38.4 us (34%)
  starting transfers between devices  33.7 us (30%)
  matrix products  11.4 us (10%)
  other arithmetic  11 us (10%)
  waiting for transfers between devices  9.44 us (8%)
  Pallas kernels  7.79 us (7%)
    ppermute x4, starting transfers between devices, receive_from(): lax.ppermute(value, AXES, [(s, s - step) for s in range(n) if 0 <= s - st...  13.2 us
    ppermute x3, starting transfers between devices, swap_with(): return lax.ppermute(value, AXES, [(i, i ^ mask) for i in range(n)])  9.54 us
    ppermute x4, waiting for transfers between devices, receive_from(): lax.ppermute(value, AXES, [(s, s - step) for s in range(n) if 0 <= s - st...  9.43 us
    pallas_call x1, Pallas kernels, near_field_kernel(): pl.pallas_call(near_body, out_shape=jax.ShapeDtypeStruct((leaf_count, RHS...  7.79 us
    ppermute x1, starting transfers between devices, local(): from_right = lax.ppermute(to_left, AXES, [(i + 1, i) for i in range(n - 1)])  7.59 us
    reshape x1, local copies, waits for them, and re-layouts, local(): leaf_coupling.reshape(leaf_count, FAR_BLOCKS, RANK, RANK)  6.9 us
    unnamed x45, local copies, waits for them, and re-layouts  6.67 us
    dot_general x1, matrix products, local(): jnp.einsum('lfrk,lfkq->lrq', partner_blocks, leaf_coupling.reshape(leaf_c...  6.63 us
  transfers between devices with their start and end apart: 9, of which 3 were waited for; matrix products, arithmetic and copies ran while one was open for 40% of the time, Pallas kernels for 7%

profile of v11, /device:TPU:384, one launch (start us, length us, event | category | flops | bytes accessed | tf_op | source)
XLA Modules:
  0.0 112.4 jit_solution(10123068444811003684)
XLA Ops:
  0.0 1.2 %reshape.186 = bf16[16,64,64]{2,1,0:T(8,128)(2,1)S(1)} reshape(bf16[16,4096]{1,0:T(8,128)(2,1)} %param.13) | data formatting | bytes 262144 | tf_op jit(solution)/shard_map/reshape | solution.py:172
  1.3 0.9 convert_element_type.23
  2.2 1.2 %copy.23 = bf16[64,2048]{0,1:T(8,128)(2,1)S(1)} copy(bf16[64,2048]{1,0:T(8,128)(2,1)} %param.17) | data formatting | bytes 524288 | tf_op args[4]
  3.4 1.1 copy.25
  4.5 1.1 copy.26
  5.6 0.8 copy.42
  6.4 0.4 fusion.10
  6.8 0.6 fusion.39
  8.0 0.2 convolution_bitcast_fusion.1
  8.6 0.7 pad_maximum_fusion.4
  9.4 3.4 %collective-permute-start.1 = (f32[37888]{0:T(1024)}, f32[37888]{0:T(1024)}, u32[]{:S(2)}, u32[]{:S(2)}) collective-permute-start(f32[37888]{0:T(1024)} %get-tuple-element.51), channel_id=1, source_target_pairs={{0,1},{1,2},{2,3},{3,4},{4,5},{5,6},{6,7},{7,8},{8,9},{9,10},{10,1... | collective-permute-start | bytes 454664 | tf_op jit(solution)/shard_map/ppermute | solution.py:199
  12.8 7.6 %collective-permute-start = (f32[37888]{0:T(1024)}, f32[37888]{0:T(1024)}, u32[]{:S(2)}, u32[]{:S(2)}) collective-permute-start(f32[37888]{0:T(1024)} %get-tuple-element.50), channel_id=1, source_target_pairs={{1,0},{2,1},{3,2},{4,3},{5,4},{6,5},{7,6},{8,7},{9,8},{10,9},{11,1... | collective-permute-start | bytes 454664 | tf_op jit(solution)/shard_map/ppermute | solution.py:200
  20.5 0.6 pad_clamp_fusion.4
  21.1 0.6 compare_and_fusion
  21.8 0.9 reshape.199
  23.3 0.5 broadcast_add_fusion.2
  23.9 2.2 %fusion.19 = f32[4,32,4,32]{3,1,2,0:T(8,128)} fusion(bf16[4,4,32,32]{3,2,1,0:T(8,128)(2,1)S(1)} %reshape.199, f32[1,32,32]{2,1,0:T(8,128)} %copy-done.10, f32[1,32,32]{2,1,0:T(8,128)S(1)} %convolution_bitcast_fusion.2, f32[1,32,32]{2,1,0:T(8,128)S(1)} %bitcast.114, f32[1,32,32]{2,1,0:T(8,128)S(1)} %reshape.204), kind=kOutput, calls=%fused_computation.46 | convolution fusion | flops 6303744 | bytes 114688 | tf_op jit(solution)/shard_map/sqkp,spm->sqkm/dot_general | solution.py:111
  26.0 2.0 %copy.31 = f32[3,4096]{0,1:T(8,128)} copy(f32[3,4096]{1,0:T(4,128)S(1)} %copy-done.6) | data formatting | bytes 98304 | tf_op args[1]
  28.0 0.9 copy.34
  29.0 0.7 copy.32.offsets_ref
  29.7 1.4 %copy.37 = bf16[64,8,1024]{0,2,1:T(8,128)(2,1)S(1)} copy(bf16[64,8,1024]{2,1,0:T(8,128)(2,1)S(1)} %copy-done.2) | data formatting | bytes 2097152 | tf_op args[6]
  31.1 6.9 %copy.38 = bf16[64,8,32,32]{3,2,1,0:T(8,128)(2,1)} copy(bf16[64,8,32,32]{0,3,2,1:T(8,128)(2,1)S(1)} %bitcast.104) | data formatting | bytes 2097152 | tf_op jit(solution)/shard_map/reshape | solution.py:230
  38.1 0.8 copy.35
  38.8 0.7 copy.33
  39.5 0.9 copy.63
  40.6 0.8 copy.50
  41.4 1.5 %reshape.201 = bf16[64,32,64]{2,1,0:T(8,128)(2,1)S(1)} reshape(bf16[64,2048]{1,0:T(8,128)(2,1)} %param.18) | data formatting | bytes 524288 | tf_op jit(solution)/shard_map/reshape | solution.py:246
  42.8 1.6 %pad.4.columns_ref = f32[64,64,128]{2,1,0:T(8,128)} pad(f32[64,64,3]{2,1,0:T(8,128)S(1)} %bitcast.105, f32[]{:T(128)} %constant.14.clone.1), padding=0_0x0_0x0_125 | pad | bytes 2146308 | tf_op jit(solution)/shard_map/jit(_pad)/pad | solution.py:77
  44.4 1.2 %pad_clamp_fusion.1 = (s32[1024]{0:T(1024)}, s32[1024]{0:T(1024)}) fusion(s32[4]{0:T(128)} %get-tuple-element.54, s32[4]{0:T(128)} %get-tuple-element.52), kind=kLoop, calls=%fused_computation.78 | loop fusion | flops 2048 | bytes 8224 | tf_op jit(solution)/shard_map/jit(_take)/gather | solution.py:148
  45.6 0.7 slice_select_fusion
  46.4 0.7 slice_add_fusion
  47.3 0.6 fusion.33
  47.9 1.9 %collective-permute-start.4 = (f32[5,16,32]{2,1,0:T(8,128)}, f32[5,16,32]{2,1,0:T(8,128)}, u32[]{:S(2)}, u32[]{:S(2)}) collective-permute-start(f32[5,16,32]{2,1,0:T(8,128)} %get-tuple-element.40), channel_id=1, source_target_pairs={{0,6},{1,7},{2,4},{3,5},{4,2},{5,3},{6,0},{7,1},{8,14},{9,15},{10,... | collective-permute-start | bytes 30728 | tf_op jit(solution)/shard_map/ppermute | solution.py:33
  49.8 1.9 %collective-permute-start.3 = (f32[5,16,32]{2,1,0:T(8,128)}, f32[5,16,32]{2,1,0:T(8,128)}, u32[]{:S(2)}, u32[]{:S(2)}) collective-permute-start(f32[5,16,32]{2,1,0:T(8,128)} %get-tuple-element.40), channel_id=1, source_target_pairs={{0,4},{1,5},{2,6},{3,7},{4,0},{5,1},{6,2},{7,3},{8,12},{9,13},{10,... | collective-permute-start | bytes 30728 | tf_op jit(solution)/shard_map/ppermute | solution.py:33
  51.8 5.7 %collective-permute-start.2 = (f32[5,16,32]{2,1,0:T(8,128)}, f32[5,16,32]{2,1,0:T(8,128)}, u32[]{:S(2)}, u32[]{:S(2)}) collective-permute-start(f32[5,16,32]{2,1,0:T(8,128)} %get-tuple-element.40), channel_id=1, source_target_pairs={{0,2},{1,3},{2,0},{3,1},{4,6},{5,7},{6,4},{7,5},{8,10},{9,11},{10,... | collective-permute-start | bytes 30728 | tf_op jit(solution)/shard_map/ppermute | solution.py:33
  57.5 0.9 slice.325
  58.4 0.9 slice.324
  59.3 0.9 pad_maximum_fusion.1
  60.2 0.4 reshape.195
  60.6 0.6 copy.62
  61.1 0.8 slice.331
  62.0 0.8 slice.330
  62.8 0.9 pad_maximum_fusion.2
  63.8 1.6 %gather_fusion.1 = f32[512,512]{1,0:T(8,128)S(1)} fusion(f32[128,512]{1,0:T(8,128)S(1)} %pad_maximum_fusion.2, s32[1024]{0:T(1024)S(1)} %pad_clamp_fusion.3), kind=kCustom, calls=%fused_computation.1 | custom fusion | bytes 2099200 | tf_op jit(solution)/shard_map/jit(_take)/gather | solution.py:226
  65.4 2.6 %gather.24 = f32[64,8,16,32]{3,2,1,0:T(8,128)} reshape(f32[512,512]{1,0:T(8,128)S(1)} %gather_fusion.1) | data formatting | bytes 2097152 | tf_op jit(solution)/shard_map/jit(_take)/gather | solution.py:226
  68.0 6.6 %fusion.4 = f32[64,16,32]{2,1,0:T(8,128)S(1)} fusion(bf16[64,8,32,32]{3,2,1,0:T(8,128)(2,1)} %copy.38, f32[64,8,16,32]{3,2,1,0:T(8,128)} %gather.24, pred[64,8]{1,0:T(8,128)(4,1)S(1)} %copy-done.11), kind=kOutput, calls=%fused_computation.9 | convolution fusion | flops 50593792 | bytes 2228736 | tf_op jit(solution)/shard_map/lfrk,lfkq->lrq/dot_general | solution.py:227
  74.6 1.4 %pad_maximum_fusion.table_ref = f32[96,19,128]{2,1,0:T(8,128)} fusion(f32[96,19,64]{2,1,0:T(8,128)S(1)} %bitcast.106), kind=kLoop, calls=%fused_computation.14 | loop fusion | flops 233472 | bytes 1400832 | tf_op jit(solution)/shard_map/concatenate | solution.py:76
  76.0 7.8 %shard_map.127 = f32[64,16,64]{2,1,0:T(8,128)} custom-call(s32[64,6]{1,0:T(8,128)} %copy.32.offsets_ref, f32[96,19,128]{2,1,0:T(8,128)} %pad_maximum_fusion.table_ref, f32[64,64,128]{2,1,0:T(8,128)} %pad.4.columns_ref), custom_call_target="tpu_custom_call" | custom-call | tf_op jit(solution)/shard_map/pallas_call | solution.py:78
  83.9 0.9 pad_maximum_fusion.5
  84.8 0.7 gather_fusion
  85.5 3.3 %collective-permute-start.6 = (f32[9,16,32]{2,1,0:T(8,128)S(1)}, f32[9,16,32]{2,1,0:T(8,128)S(1)}, u32[]{:S(2)}, u32[]{:S(2)}) collective-permute-start(f32[9,16,32]{2,1,0:T(8,128)S(1)} %get-tuple-element.13), channel_id=1, source_target_pairs={{8,0},{9,1},{10,2},{11,3},{12,4},{13,5},{14,6},{15,7},{16,8},{17,9... | collective-permute-start | bytes 55304 | tf_op jit(solution)/shard_map/ppermute | solution.py:38
  88.8 2.6 %collective-permute-start.5 = (f32[9,16,32]{2,1,0:T(8,128)S(1)}, f32[9,16,32]{2,1,0:T(8,128)S(1)}, u32[]{:S(2)}, u32[]{:S(2)}) collective-permute-start(f32[9,16,32]{2,1,0:T(8,128)S(1)} %get-tuple-element.12), channel_id=1, source_target_pairs={{0,8},{1,9},{2,10},{3,11},{4,12},{5,13},{6,14},{7,15},{8,16},{9,17... | collective-permute-start | bytes 55304 | tf_op jit(solution)/shard_map/ppermute | solution.py:38
  91.4 0.4 collective-permute-done.6
  91.8 6.6 %collective-permute-done.5 = f32[9,16,32]{2,1,0:T(8,128)S(1)} collective-permute-done((f32[9,16,32]{2,1,0:T(8,128)S(1)}, f32[9,16,32]{2,1,0:T(8,128)S(1)}, u32[]{:S(2)}, u32[]{:S(2)}) %collective-permute-start.5) | collective-permute-done | bytes 18464 | tf_op jit(solution)/shard_map/ppermute | solution.py:38
  98.4 1.9 %collective-permute-start.8 = (f32[3,16,32]{2,1,0:T(8,128)S(1)}, f32[3,16,32]{2,1,0:T(8,128)S(1)}, u32[]{:S(2)}, u32[]{:S(2)}) collective-permute-start(f32[3,16,32]{2,1,0:T(8,128)S(1)} %get-tuple-element.16), channel_id=1, source_target_pairs={{16,0},{17,1},{18,2},{19,3},{20,4},{21,5},{22,6},{23,7},{24,8},{25... | collective-permute-start | bytes 18440 | tf_op jit(solution)/shard_map/ppermute | solution.py:38
  100.3 5.4 %collective-permute-start.7 = (f32[3,16,32]{2,1,0:T(8,128)S(1)}, f32[3,16,32]{2,1,0:T(8,128)S(1)}, u32[]{:S(2)}, u32[]{:S(2)}) collective-permute-start(f32[3,16,32]{2,1,0:T(8,128)S(1)} %get-tuple-element.15), channel_id=1, source_target_pairs={{0,16},{1,17},{2,18},{3,19},{4,20},{5,21},{6,22},{7,23},{8,24},{9,... | collective-permute-start | bytes 18440 | tf_op jit(solution)/shard_map/ppermute | solution.py:38
  105.8 0.7 gather_fusion.3
  106.5 0.7 gather_fusion.2
  107.2 2.5 %collective-permute-done.7 = f32[3,16,32]{2,1,0:T(8,128)S(1)} collective-permute-done((f32[3,16,32]{2,1,0:T(8,128)S(1)}, f32[3,16,32]{2,1,0:T(8,128)S(1)}, u32[]{:S(2)}, u32[]{:S(2)}) %collective-permute-start.7) | collective-permute-done | bytes 6176 | tf_op jit(solution)/shard_map/ppermute | solution.py:38
  109.7 0.6 gather_fusion.4
  110.3 0.3 convolution_bitcast_fusion.4
  110.6 0.3 fusion.8
  110.9 0.4 fusion.7
  111.5 0.9 reshape.202
  (106 shorter events, 2.6 us)
Async XLA Ops:
  0.0 7.4 %copy-start.12 = (bf16[1,3,1024]{2,1,0:T(4,128)(2,1)S(1)}, bf16[1,3,1024]{2,1,0:T(4,128)(2,1)}, u32[]{:S(2)}) copy-start(bf16[1,3,1024]{2,1,0:T(4,128)(2,1)} %param.22) | copy-start | bytes 18436
  0.0 7.7 %copy-start.13 = (bf16[1,3,1024]{2,1,0:T(4,128)(2,1)S(1)}, bf16[1,3,1024]{2,1,0:T(4,128)(2,1)}, u32[]{:S(2)}) copy-start(bf16[1,3,1024]{2,1,0:T(4,128)(2,1)} %param.23) | copy-start | bytes 18436
  0.0 8.4 %copy-start.6 = (f32[3,4096]{1,0:T(4,128)S(1)}, f32[3,4096]{1,0:T(4,128)}, u32[]{:S(2)}) copy-start(f32[3,4096]{1,0:T(4,128)} %param.14) | copy-start | bytes 147460
  0.0 8.4 %copy-start.10 = (f32[1,32,32]{2,1,0:T(8,128)}, f32[1,32,32]{2,1,0:T(8,128)S(1)}, u32[]{:S(2)}) copy-start(f32[1,32,32]{2,1,0:T(8,128)S(1)} %fusion.29) | copy-start | bytes 12292
  3.4 17.6 %copy-start.16 = (s32[64,8]{0,1:T(8,128)S(1)}, s32[64,8]{0,1:T(8,128)}, u32[]{:S(2)}) copy-start(s32[64,8]{0,1:T(8,128)} %param.16) | copy-start | bytes 6148
  3.4 19.9 %copy-start.17 = (s32[4]{0:T(128)S(1)}, s32[4]{0:T(128)}, u32[]{:S(2)}) copy-start(s32[4]{0:T(128)} %constant.57) | copy-start | bytes 52
  6.8 22.2 %copy-start.14 = (s32[64,6]{0,1:T(8,128)S(1)}, s32[64,6]{0,1:T(8,128)}, u32[]{:S(2)}) copy-start(s32[64,6]{0,1:T(8,128)} %param.15) | copy-start | bytes 4612
  6.8 22.9 %copy-start.2 = (bf16[64,8,1024]{2,1,0:T(8,128)(2,1)S(1)}, bf16[64,8,1024]{2,1,0:T(8,128)(2,1)}, u32[]{:S(2)}) copy-start(bf16[64,8,1024]{2,1,0:T(8,128)(2,1)} %param.19) | copy-start | bytes 3145732
  8.2 22.9 %copy-start.9 = (f32[4,16,32]{2,1,0:T(8,128)}, f32[4,16,32]{2,1,0:T(8,128)S(1)}, u32[]{:S(2)}) copy-start(f32[4,16,32]{2,1,0:T(8,128)S(1)} %convolution_bitcast_fusion.1) | copy-start | bytes 24580
  9.4 36.2 %collective-permute-start.1 = (f32[37888]{0:T(1024)}, f32[37888]{0:T(1024)}, u32[]{:S(2)}, u32[]{:S(2)}) collective-permute-start(f32[37888]{0:T(1024)} %get-tuple-element.51), channel_id=1, source_target_pairs={{0,1},{1,2},{2,3},{3,4},{4,5},{5,6},{6,7},{7,8},{8,9},{9,10},{10,1... | collective-permute-start | bytes 454664 | tf_op jit(solution)/shard_map/ppermute | solution.py:199
  12.8 32.8 %collective-permute-start = (f32[37888]{0:T(1024)}, f32[37888]{0:T(1024)}, u32[]{:S(2)}, u32[]{:S(2)}) collective-permute-start(f32[37888]{0:T(1024)} %get-tuple-element.50), channel_id=1, source_target_pairs={{1,0},{2,1},{3,2},{4,3},{5,4},{6,5},{7,6},{8,7},{9,8},{10,9},{11,1... | collective-permute-start | bytes 454664 | tf_op jit(solution)/shard_map/ppermute | solution.py:200
  29.7 9.1 %copy-start.15 = (pred[64,8]{0,1:T(8,128)(4,1)S(1)}, pred[64,8]{0,1:T(8,128)(4,1)}, u32[]{:S(2)}) copy-start(pred[64,8]{0,1:T(8,128)(4,1)} %get-tuple-element.23) | copy-start | bytes 1540
  31.1 6.9 %copy-start.3 = (f32[64,16,32]{0,2,1:T(8,128)S(1)}, f32[64,16,32]{0,2,1:T(8,128)}, u32[]{:S(2)}) copy-start(f32[64,16,32]{0,2,1:T(8,128)} %copy.34) | copy-start | bytes 393220
  31.1 8.4 %copy-start.4 = (f32[4,32,4,32]{3,1,2,0:T(8,128)S(1)}, f32[4,32,4,32]{3,1,2,0:T(8,128)}, u32[]{:S(2)}) copy-start(f32[4,32,4,32]{3,1,2,0:T(8,128)} %fusion.19) | copy-start | bytes 196612
  31.1 9.3 %copy-start.8 = (bf16[64,1024]{1,0:T(8,128)(2,1)S(1)}, bf16[64,1024]{1,0:T(8,128)(2,1)}, u32[]{:S(2)}) copy-start(bf16[64,1024]{1,0:T(8,128)(2,1)} %param.21) | copy-start | bytes 393220
  38.0 4.8 %copy-start = (f32[3,4096]{0,1:T(8,128)S(1)}, f32[3,4096]{0,1:T(8,128)}, u32[]{:S(2)}) copy-start(f32[3,4096]{0,1:T(8,128)} %copy.31) | copy-start | bytes 147460
  38.0 9.2 %slice-start = ((f32[4,16,32]{2,1,0:T(8,128)}), f32[1,16,32]{2,1,0:T(8,128)S(1)}, s32[]{:S(2)}) async-start(f32[4,16,32]{2,1,0:T(8,128)} %copy-done.9), calls=%async_computation | async-start | bytes 16384 | tf_op jit(solution)/shard_map/slice | solution.py:119
  47.9 35.9 %collective-permute-start.4 = (f32[5,16,32]{2,1,0:T(8,128)}, f32[5,16,32]{2,1,0:T(8,128)}, u32[]{:S(2)}, u32[]{:S(2)}) collective-permute-start(f32[5,16,32]{2,1,0:T(8,128)} %get-tuple-element.40), channel_id=1, source_target_pairs={{0,6},{1,7},{2,4},{3,5},{4,2},{5,3},{6,0},{7,1},{8,14},{9,15},{10,... | collective-permute-start | bytes 30728 | tf_op jit(solution)/shard_map/ppermute | solution.py:33
  49.8 34.0 %collective-permute-start.3 = (f32[5,16,32]{2,1,0:T(8,128)}, f32[5,16,32]{2,1,0:T(8,128)}, u32[]{:S(2)}, u32[]{:S(2)}) collective-permute-start(f32[5,16,32]{2,1,0:T(8,128)} %get-tuple-element.40), channel_id=1, source_target_pairs={{0,4},{1,5},{2,6},{3,7},{4,0},{5,1},{6,2},{7,3},{8,12},{9,13},{10,... | collective-permute-start | bytes 30728 | tf_op jit(solution)/shard_map/ppermute | solution.py:33
  51.8 32.1 %collective-permute-start.2 = (f32[5,16,32]{2,1,0:T(8,128)}, f32[5,16,32]{2,1,0:T(8,128)}, u32[]{:S(2)}, u32[]{:S(2)}) collective-permute-start(f32[5,16,32]{2,1,0:T(8,128)} %get-tuple-element.40), channel_id=1, source_target_pairs={{0,2},{1,3},{2,0},{3,1},{4,6},{5,7},{6,4},{7,5},{8,10},{9,11},{10,... | collective-permute-start | bytes 30728 | tf_op jit(solution)/shard_map/ppermute | solution.py:33
  65.4 2.6 %copy-start.11 = (pred[64,8]{1,0:T(8,128)(4,1)S(1)}, pred[64,8]{1,0:T(8,128)(4,1)}, u32[]{:S(2)}) copy-start(pred[64,8]{1,0:T(8,128)(4,1)} %copy.33) | copy-start | bytes 1540
  74.6 9.3 %copy-start.7 = (f32[1,5,16,32]{3,2,1,0:T(8,128)S(1)}, f32[1,5,16,32]{3,2,1,0:T(8,128)}, u32[]{:S(2)}) copy-start(f32[1,5,16,32]{3,2,1,0:T(8,128)} %get-tuple-element.39) | copy-start | bytes 30724
  74.6 35.7 %copy-start.5 = (f32[4,32,4,32]{3,2,1,0:T(4,128)S(1)}, f32[4,32,4,32]{3,2,1,0:T(4,128)}, u32[]{:S(2)}) copy-start(f32[4,32,4,32]{3,2,1,0:T(4,128)} %copy.63) | copy-start | bytes 196612
  83.8 27.1 %copy-start.1 = (f32[64,16,64]{2,1,0:T(8,128)S(1)}, f32[64,16,64]{2,1,0:T(8,128)}, u32[]{:S(2)}) copy-start(f32[64,16,64]{2,1,0:T(8,128)} %shard_map.127) | copy-start | bytes 786436
  85.5 6.2 %collective-permute-start.6 = (f32[9,16,32]{2,1,0:T(8,128)S(1)}, f32[9,16,32]{2,1,0:T(8,128)S(1)}, u32[]{:S(2)}, u32[]{:S(2)}) collective-permute-start(f32[9,16,32]{2,1,0:T(8,128)S(1)} %get-tuple-element.13), channel_id=1, source_target_pairs={{8,0},{9,1},{10,2},{11,3},{12,4},{13,5},{14,6},{15,7},{16,8},{17,9... | collective-permute-start | bytes 55304 | tf_op jit(solution)/shard_map/ppermute | solution.py:38
  88.8 9.6 %collective-permute-start.5 = (f32[9,16,32]{2,1,0:T(8,128)S(1)}, f32[9,16,32]{2,1,0:T(8,128)S(1)}, u32[]{:S(2)}, u32[]{:S(2)}) collective-permute-start(f32[9,16,32]{2,1,0:T(8,128)S(1)} %get-tuple-element.12), channel_id=1, source_target_pairs={{0,8},{1,9},{2,10},{3,11},{4,12},{5,13},{6,14},{7,15},{8,16},{9,17... | collective-permute-start | bytes 55304 | tf_op jit(solution)/shard_map/ppermute | solution.py:38
  98.4 11.3 %collective-permute-start.8 = (f32[3,16,32]{2,1,0:T(8,128)S(1)}, f32[3,16,32]{2,1,0:T(8,128)S(1)}, u32[]{:S(2)}, u32[]{:S(2)}) collective-permute-start(f32[3,16,32]{2,1,0:T(8,128)S(1)} %get-tuple-element.16), channel_id=1, source_target_pairs={{16,0},{17,1},{18,2},{19,3},{20,4},{21,5},{22,6},{23,7},{24,8},{25... | collective-permute-start | bytes 18440 | tf_op jit(solution)/shard_map/ppermute | solution.py:38
  100.3 9.3 %collective-permute-start.7 = (f32[3,16,32]{2,1,0:T(8,128)S(1)}, f32[3,16,32]{2,1,0:T(8,128)S(1)}, u32[]{:S(2)}, u32[]{:S(2)}) collective-permute-start(f32[3,16,32]{2,1,0:T(8,128)S(1)} %get-tuple-element.15), channel_id=1, source_target_pairs={{0,16},{1,17},{2,18},{3,19},{4,20},{5,21},{6,22},{7,23},{8,24},{9,... | collective-permute-start | bytes 18440 | tf_op jit(solution)/shard_map/ppermute | solution.py:38

commit v12 on v10

--- a/solution.py
+++ b/solution.py
@@ -132,18 +132,19 @@
     coef3 = (part3 + got3[7])[None]
 
     node = 8
-    to_ahead = jnp.concatenate([octs0[5:8], quads1[1:4], pairs2, coef3])
-    to_behind = jnp.concatenate([octs0[0:3], quads1[0:3], pairs2, coef3])
-    to_ahead, to_behind, first = lax.optimization_barrier((to_ahead, to_behind, first))
+    to_ahead = jnp.concatenate([octs0[5:8], quads1[1:4], pairs2])
+    to_behind = jnp.concatenate([octs0[0:3], quads1[0:3], pairs2])
+    far_ahead = jnp.concatenate([pairs2[1:2], coef3])
+    far_behind = jnp.concatenate([pairs2[0:1], coef3])
+    to_ahead, to_behind, far_ahead, far_behind, first = lax.optimization_barrier(
+        (to_ahead, to_behind, far_ahead, far_behind, first)
+    )
     ahead1 = receive_from(to_behind, node)
     behind1 = receive_from(to_ahead, -node)
-    to_behind = jnp.concatenate([pairs2[0:1], coef3, ahead1[8:9]])
-    to_ahead = jnp.concatenate([pairs2[1:2], coef3, behind1[8:9]])
-    to_ahead, to_behind, second = lax.optimization_barrier((to_ahead, to_behind, second))
-    ahead2 = receive_from(to_behind, 2 * node)
-    behind2 = receive_from(to_ahead, -2 * node)
-    ahead3 = ahead2[2:3]
-    behind3 = behind2[2:3]
+    ahead2 = receive_from(far_behind, 2 * node)
+    behind2 = receive_from(far_ahead, -2 * node)
+    ahead3 = receive_from(far_behind[1:2], 3 * node)
+    behind3 = receive_from(far_ahead[1:2], -3 * node)
 
     window0 = jnp.concatenate([behind1[0:3], octs0, ahead1[0:3]])
     window1 = jnp.concatenate([behind1[3:6], quads1, ahead1[3:6]])

time: 111 us -> 116 us (1.045)
  the two profiles are of different devices: /device:TPU:398 before, /device:TPU:390 now
where the time goes in v12:
time: 116 us; the launch traced here: 115 us
  local copies, waits for them, and re-layouts  39.6 us (34%)
  starting transfers between devices  39.5 us (34%)
  matrix products  10.7 us (9%)
  waiting for transfers between devices  8.79 us (8%)
  Pallas kernels  7.86 us (7%)
  other arithmetic  7.5 us (6%)
    ppermute x6, starting transfers between devices, receive_from(): lax.ppermute(value, AXES, [(s, s - step) for s in range(n) if 0 <= s - st...  25.9 us
    pallas_call x1, Pallas kernels, near_field_kernel(): pl.pallas_call(near_body, out_shape=jax.ShapeDtypeStruct((leaf_count, RHS...  7.86 us
    ppermute x3, starting transfers between devices, swap_with(): return lax.ppermute(value, AXES, [(i, i ^ mask) for i in range(n)])  6.88 us
    reshape x1, local copies, waits for them, and re-layouts, local(): leaf_coupling.reshape(leaf_count, FAR_BLOCKS, RANK, RANK)  6.8 us
    unnamed x57, local copies, waits for them, and re-layouts  6.76 us
    dot_general x1, matrix products, local(): jnp.einsum('lfrk,lfkq->lrq', partner_blocks, leaf_coupling.reshape(leaf_c...  6.64 us
    ppermute x3, waiting for transfers between devices, swap_with(): return lax.ppermute(value, AXES, [(i, i ^ mask) for i in range(n)])  5.15 us
    gather x2, local copies, waits for them, and re-layouts, local(): jnp.take(rimmed, far_index, axis=0)  4.21 us
  transfers between devices with their start and end apart: 11, of which 2 were waited for; matrix products, arithmetic and copies ran while one was open for 38% of the time, Pallas kernels for 0%

profile of v12, /device:TPU:390, one launch (start us, length us, event | category | flops | bytes accessed | tf_op | source)
XLA Modules:
  0.0 114.8 jit_solution(585996431782441534)
XLA Ops:
  0.0 1.3 %copy.20 = bf16[64,2048]{0,1:T(8,128)(2,1)S(1)} copy(bf16[64,2048]{1,0:T(8,128)(2,1)} %param.17) | data formatting | bytes 524288 | tf_op args[4]
  1.3 1.1 copy.22
  2.4 1.2 %reshape.138 = bf16[16,64,64]{2,1,0:T(8,128)(2,1)S(1)} reshape(bf16[16,4096]{1,0:T(8,128)(2,1)} %param.13) | data formatting | bytes 262144 | tf_op jit(solution)/shard_map/reshape | solution.py:178
  3.6 1.1 copy.23
  4.7 0.8 copy.35
  5.5 0.9 slice_reduce_fusion.2
  6.6 0.7 convert_reduce_fusion
  7.4 0.4 fusion.10
  7.8 0.6 fusion.42
  8.6 0.2 convolution_bitcast_fusion.1
  8.8 2.7 %collective-permute-start = (f32[4,16,32]{2,1,0:T(8,128)S(1)}, f32[4,16,32]{2,1,0:T(8,128)S(1)}, u32[]{:S(2)}, u32[]{:S(2)}) collective-permute-start(f32[4,16,32]{2,1,0:T(8,128)S(1)} %convolution_bitcast_fusion.1), channel_id=1, source_target_pairs={{0,1},{1,0},{2,3},{3,2},{4,5},{5,4},{6,7},{7,6},{8,9},{9,8},{10,11... | collective-permute-start | bytes 24584 | tf_op jit(solution)/shard_map/ppermute | solution.py:33
  11.8 0.7 pad_maximum_fusion.4
  12.5 3.1 %collective-permute-start.4 = (f32[35840]{0:T(1024)}, f32[35840]{0:T(1024)}, u32[]{:S(2)}, u32[]{:S(2)}) collective-permute-start(f32[35840]{0:T(1024)} %pad_maximum_fusion.4), channel_id=1, source_target_pairs={{1,0},{2,1},{3,2},{4,3},{5,4},{6,5},{7,6},{8,7},{9,8},{10,9},{11,1... | collective-permute-start | bytes 430088 | tf_op jit(solution)/shard_map/ppermute | solution.py:194
  15.7 0.7 pad_maximum_fusion.3
  16.4 3.7 %collective-permute-start.3 = (f32[35840]{0:T(1024)}, f32[35840]{0:T(1024)}, u32[]{:S(2)}, u32[]{:S(2)}) collective-permute-start(f32[35840]{0:T(1024)} %pad_maximum_fusion.3), channel_id=1, source_target_pairs={{0,1},{1,2},{2,3},{3,4},{4,5},{5,6},{6,7},{7,8},{8,9},{9,10},{10,1... | collective-permute-start | bytes 430088 | tf_op jit(solution)/shard_map/ppermute | solution.py:193
  20.6 0.6 compare_and_fusion
  21.4 1.5 %fusion.22 = f32[4,32,4,32]{3,1,2,0:T(8,128)} fusion(bf16[4,4,32,32]{3,2,1,0:T(8,128)(2,1)S(1)} %reshape.149, f32[1,32,32]{2,1,0:T(8,128)S(1)} %fusion.30, f32[1,32,32]{2,1,0:T(8,128)S(1)} %convolution_bitcast_fusion.2, f32[1,32,32]{2,1,0:T(8,128)S(1)} %bitcast.76, f32[1,32,32]{2,1,0:T(8,128)S(1)} %reshape.154), kind=kOutput, calls=%fused_computation.47 | convolution fusion | flops 6303744 | bytes 114688 | tf_op jit(solution)/shard_map/sqkp,spm->sqkm/dot_general | solution.py:111
  22.9 0.6 pad_clamp_fusion.1
  23.8 2.2 %collective-permute-start.1 = (f32[5,16,32]{2,1,0:T(8,128)S(1)}, f32[5,16,32]{2,1,0:T(8,128)S(1)}, u32[]{:S(2)}, u32[]{:S(2)}) collective-permute-start(f32[5,16,32]{2,1,0:T(8,128)S(1)} %pad_maximum_fusion.16), channel_id=1, source_target_pairs={{0,2},{1,3},{2,0},{3,1},{4,6},{5,7},{6,4},{7,5},{8,10},{9,11},{10,... | collective-permute-start | bytes 30728 | tf_op jit(solution)/shard_map/ppermute | solution.py:33
  26.0 5.1 %collective-permute-done.1 = f32[5,16,32]{2,1,0:T(8,128)S(1)} collective-permute-done((f32[5,16,32]{2,1,0:T(8,128)S(1)}, f32[5,16,32]{2,1,0:T(8,128)S(1)}, u32[]{:S(2)}, u32[]{:S(2)}) %collective-permute-start.1) | collective-permute-done | bytes 10272 | tf_op jit(solution)/shard_map/ppermute | solution.py:33
  31.2 0.6 fusion.15
  31.8 1.9 %collective-permute-start.2 = (f32[8,16,32]{2,1,0:T(8,128)}, f32[8,16,32]{2,1,0:T(8,128)}, u32[]{:S(2)}, u32[]{:S(2)}) collective-permute-start(f32[8,16,32]{2,1,0:T(8,128)} %fusion.15), channel_id=1, source_target_pairs={{0,4},{1,5},{2,6},{3,7},{4,0},{5,1},{6,2},{7,3},{8,12},{9,13},{10,... | collective-permute-start | bytes 49160 | tf_op jit(solution)/shard_map/ppermute | solution.py:33
  33.8 2.0 %copy.25 = f32[3,4096]{0,1:T(8,128)} copy(f32[3,4096]{1,0:T(4,128)S(1)} %copy-done.6) | data formatting | bytes 98304 | tf_op args[1]
  35.8 0.9 copy.28
  36.7 0.7 copy.26.offsets_ref
  37.5 1.4 %copy.31 = bf16[64,8,1024]{0,2,1:T(8,128)(2,1)S(1)} copy(bf16[64,8,1024]{2,1,0:T(8,128)(2,1)S(1)} %copy-done.2) | data formatting | bytes 2097152 | tf_op args[6]
  38.9 6.8 %copy.36 = bf16[64,8,32,32]{3,2,1,0:T(8,128)(2,1)} copy(bf16[64,8,32,32]{0,3,2,1:T(8,128)(2,1)S(1)} %bitcast.68) | data formatting | bytes 2097152 | tf_op jit(solution)/shard_map/reshape | solution.py:220
  45.7 0.8 copy.29
  46.5 0.7 copy.27
  47.2 0.9 copy.54
  48.2 0.8 copy.44
  49.0 1.5 %reshape.151 = bf16[64,32,64]{2,1,0:T(8,128)(2,1)S(1)} reshape(bf16[64,2048]{1,0:T(8,128)(2,1)} %param.18) | data formatting | bytes 524288 | tf_op jit(solution)/shard_map/reshape | solution.py:245
  50.5 1.5 %pad.4.columns_ref = f32[64,64,128]{2,1,0:T(8,128)} pad(f32[64,64,3]{2,1,0:T(8,128)S(1)} %bitcast.69, f32[]{:T(128)} %constant.36.clone.1), padding=0_0x0_0x0_125 | pad | bytes 2146308 | tf_op jit(solution)/shard_map/jit(_pad)/pad | solution.py:77
  52.1 0.7 slice_add_fusion
  52.8 0.7 slice.286
  53.5 0.8 slice.284
  54.3 0.6 pad_maximum_fusion.17
  54.9 0.7 pad_maximum_fusion.11
  55.6 0.9 slice.297
  56.5 0.9 slice.295
  57.5 0.4 reshape.145
  57.9 0.6 copy.53
  58.4 1.4 %pad_maximum_fusion.table_ref = f32[96,19,128]{2,1,0:T(8,128)} fusion(f32[96,19,64]{2,1,0:T(8,128)S(1)} %bitcast.70), kind=kLoop, calls=%fused_computation.13 | loop fusion | flops 233472 | bytes 1400832 | tf_op jit(solution)/shard_map/concatenate | solution.py:76
  59.8 7.9 %shard_map.127 = f32[64,16,64]{2,1,0:T(8,128)} custom-call(s32[64,6]{1,0:T(8,128)} %copy.26.offsets_ref, f32[96,19,128]{2,1,0:T(8,128)} %pad_maximum_fusion.table_ref, f32[64,64,128]{2,1,0:T(8,128)} %pad.4.columns_ref), custom_call_target="tpu_custom_call" | custom-call | tf_op jit(solution)/shard_map/pallas_call | solution.py:78
  67.7 0.7 slice.256
  68.4 6.9 %collective-permute-start.8 = (f32[2,16,32]{2,1,0:T(8,128)}, f32[2,16,32]{2,1,0:T(8,128)S(1)}, u32[]{:S(2)}, u32[]{:S(2)}) collective-permute-start(f32[2,16,32]{2,1,0:T(8,128)} %get-tuple-element.14), channel_id=1, source_target_pairs={{16,0},{17,1},{18,2},{19,3},{20,4},{21,5},{22,6},{23,7},{24,8},{25... | collective-permute-start | bytes 12296 | tf_op jit(solution)/shard_map/ppermute | solution.py:38
  75.3 0.8 slice.299
  76.2 0.8 slice.298
  77.1 1.6 %gather_fusion = f32[512,512]{1,0:T(8,128)S(1)} fusion(f32[128,512]{1,0:T(8,128)S(1)} %pad_maximum_fusion.2, s32[1024]{0:T(1024)S(1)} %pad_clamp_fusion.3), kind=kCustom, calls=%fused_computation | custom fusion | bytes 2099200 | tf_op jit(solution)/shard_map/jit(_take)/gather | solution.py:216
  78.7 2.6 %gather.19 = f32[64,8,16,32]{3,2,1,0:T(8,128)} reshape(f32[512,512]{1,0:T(8,128)S(1)} %gather_fusion) | data formatting | bytes 2097152 | tf_op jit(solution)/shard_map/jit(_take)/gather | solution.py:216
  81.3 4.6 %collective-permute-start.10 = (f32[1,16,32]{2,1,0:T(8,128)S(1)}, f32[1,16,32]{2,1,0:T(8,128)S(1)}, u32[]{:S(2)}, u32[]{:S(2)}) collective-permute-start(f32[1,16,32]{2,1,0:T(8,128)S(1)} %slice.256), channel_id=1, source_target_pairs={{24,0},{25,1},{26,2},{27,3},{28,4},{29,5},{30,6},{31,7},{32,8},{33... | collective-permute-start | bytes 6152 | tf_op jit(solution)/shard_map/ppermute | solution.py:38
  85.9 3.3 %collective-permute-start.7 = (f32[2,16,32]{2,1,0:T(8,128)S(1)}, f32[2,16,32]{2,1,0:T(8,128)S(1)}, u32[]{:S(2)}, u32[]{:S(2)}) collective-permute-start(f32[2,16,32]{2,1,0:T(8,128)S(1)} %copy-done.16), channel_id=1, source_target_pairs={{0,16},{1,17},{2,18},{3,19},{4,20},{5,21},{6,22},{7,23},{8,24},{9,... | collective-permute-start | bytes 12296 | tf_op jit(solution)/shard_map/ppermute | solution.py:38
  89.2 6.6 %fusion.4 = f32[64,16,32]{2,1,0:T(8,128)S(1)} fusion(bf16[64,8,32,32]{3,2,1,0:T(8,128)(2,1)} %copy.36, f32[64,8,16,32]{3,2,1,0:T(8,128)} %gather.19, pred[64,8]{1,0:T(8,128)(4,1)S(1)} %copy-done.17), kind=kOutput, calls=%fused_computation.8 | convolution fusion | flops 50593792 | bytes 2228736 | tf_op jit(solution)/shard_map/lfrk,lfkq->lrq/dot_general | solution.py:217
  95.9 2.1 %collective-permute-start.5 = (f32[8,16,32]{2,1,0:T(8,128)S(1)}, f32[8,16,32]{2,1,0:T(8,128)S(1)}, u32[]{:S(2)}, u32[]{:S(2)}) collective-permute-start(f32[8,16,32]{2,1,0:T(8,128)S(1)} %copy-done.15), channel_id=1, source_target_pairs={{0,8},{1,9},{2,10},{3,11},{4,12},{5,13},{6,14},{7,15},{8,16},{9,17... | collective-permute-start | bytes 49160 | tf_op jit(solution)/shard_map/ppermute | solution.py:38
  98.0 7.1 %collective-permute-start.6 = (f32[8,16,32]{2,1,0:T(8,128)S(1)}, f32[8,16,32]{2,1,0:T(8,128)S(1)}, u32[]{:S(2)}, u32[]{:S(2)}) collective-permute-start(f32[8,16,32]{2,1,0:T(8,128)S(1)} %copy-done.14), channel_id=1, source_target_pairs={{8,0},{9,1},{10,2},{11,3},{12,4},{13,5},{14,6},{15,7},{16,8},{17,9... | collective-permute-start | bytes 49160 | tf_op jit(solution)/shard_map/ppermute | solution.py:38
  105.1 1.9 %collective-permute-start.9 = (f32[1,16,32]{2,1,0:T(8,128)S(1)}, f32[1,16,32]{2,1,0:T(8,128)S(1)}, u32[]{:S(2)}, u32[]{:S(2)}) collective-permute-start(f32[1,16,32]{2,1,0:T(8,128)S(1)} %slice.253), channel_id=1, source_target_pairs={{0,24},{1,25},{2,26},{3,27},{4,28},{5,29},{6,30},{7,31},{8,32},{9,... | collective-permute-start | bytes 6152 | tf_op jit(solution)/shard_map/ppermute | solution.py:38
  107.2 0.6 gather_fusion.3
  107.7 0.7 gather_fusion.2
  108.4 0.7 gather_fusion.1
  109.1 3.6 %collective-permute-done.9 = f32[1,16,32]{2,1,0:T(8,128)S(1)} collective-permute-done((f32[1,16,32]{2,1,0:T(8,128)S(1)}, f32[1,16,32]{2,1,0:T(8,128)S(1)}, u32[]{:S(2)}, u32[]{:S(2)}) %collective-permute-start.9) | collective-permute-done | bytes 2080 | tf_op jit(solution)/shard_map/ppermute | solution.py:38
  112.7 0.3 convolution_bitcast_fusion.4
  113.0 0.3 fusion.8
  113.4 0.4 fusion.7
  113.9 0.9 reshape.152
  (117 shorter events, 2.6 us)
Async XLA Ops:
  0.0 11.6 %copy-start.7 = (bf16[16,4096]{1,0:T(8,128)(2,1)S(1)}, bf16[16,4096]{1,0:T(8,128)(2,1)}, u32[]{:S(2)}) copy-start(bf16[16,4096]{1,0:T(8,128)(2,1)} %param.13) | copy-start | bytes 393220
  0.0 11.7 %copy-start.6 = (f32[3,4096]{1,0:T(4,128)S(1)}, f32[3,4096]{1,0:T(4,128)}, u32[]{:S(2)}) copy-start(f32[3,4096]{1,0:T(4,128)} %param.14) | copy-start | bytes 147460
  1.3 18.8 %copy-start.19 = (bf16[1,3,1024]{2,1,0:T(4,128)(2,1)S(1)}, bf16[1,3,1024]{2,1,0:T(4,128)(2,1)}, u32[]{:S(2)}) copy-start(bf16[1,3,1024]{2,1,0:T(4,128)(2,1)} %param.23) | copy-start | bytes 18436
  1.3 18.8 %copy-start.18 = (bf16[1,4,4,1024]{3,2,1,0:T(4,128)(2,1)S(1)}, bf16[1,4,4,1024]{3,2,1,0:T(4,128)(2,1)}, u32[]{:S(2)}) copy-start(bf16[1,4,4,1024]{3,2,1,0:T(4,128)(2,1)} %param.24) | copy-start | bytes 98308
  2.4 18.2 %copy-start.22 = (s32[64,8]{0,1:T(8,128)S(1)}, s32[64,8]{0,1:T(8,128)}, u32[]{:S(2)}) copy-start(s32[64,8]{0,1:T(8,128)} %param.16) | copy-start | bytes 6148
  3.6 19.3 %copy-start.23 = (s32[4]{0:T(128)S(1)}, s32[4]{0:T(128)}, u32[]{:S(2)}) copy-start(s32[4]{0:T(128)} %constant.56) | copy-start | bytes 52
  8.3 28.4 %copy-start.20 = (s32[64,6]{0,1:T(8,128)S(1)}, s32[64,6]{0,1:T(8,128)}, u32[]{:S(2)}) copy-start(s32[64,6]{0,1:T(8,128)} %param.15) | copy-start | bytes 4612
  8.3 29.1 %copy-start.2 = (bf16[64,8,1024]{2,1,0:T(8,128)(2,1)S(1)}, bf16[64,8,1024]{2,1,0:T(8,128)(2,1)}, u32[]{:S(2)}) copy-start(bf16[64,8,1024]{2,1,0:T(8,128)(2,1)} %param.19) | copy-start | bytes 3145732
  8.8 14.9 %collective-permute-start = (f32[4,16,32]{2,1,0:T(8,128)S(1)}, f32[4,16,32]{2,1,0:T(8,128)S(1)}, u32[]{:S(2)}, u32[]{:S(2)}) collective-permute-start(f32[4,16,32]{2,1,0:T(8,128)S(1)} %convolution_bitcast_fusion.1), channel_id=1, source_target_pairs={{0,1},{1,0},{2,3},{3,2},{4,5},{5,4},{6,7},{7,6},{8,9},{9,8},{10,11... | collective-permute-start | bytes 24584 | tf_op jit(solution)/shard_map/ppermute | solution.py:33
  12.5 43.1 %collective-permute-start.4 = (f32[35840]{0:T(1024)}, f32[35840]{0:T(1024)}, u32[]{:S(2)}, u32[]{:S(2)}) collective-permute-start(f32[35840]{0:T(1024)} %pad_maximum_fusion.4), channel_id=1, source_target_pairs={{1,0},{2,1},{3,2},{4,3},{5,4},{6,5},{7,6},{8,7},{9,8},{10,9},{11,1... | collective-permute-start | bytes 430088 | tf_op jit(solution)/shard_map/ppermute | solution.py:194
  16.4 40.1 %collective-permute-start.3 = (f32[35840]{0:T(1024)}, f32[35840]{0:T(1024)}, u32[]{:S(2)}, u32[]{:S(2)}) collective-permute-start(f32[35840]{0:T(1024)} %pad_maximum_fusion.3), channel_id=1, source_target_pairs={{0,1},{1,2},{2,3},{3,4},{4,5},{5,6},{6,7},{7,8},{8,9},{9,10},{10,1... | collective-permute-start | bytes 430088 | tf_op jit(solution)/shard_map/ppermute | solution.py:193
  23.8 7.4 %collective-permute-start.1 = (f32[5,16,32]{2,1,0:T(8,128)S(1)}, f32[5,16,32]{2,1,0:T(8,128)S(1)}, u32[]{:S(2)}, u32[]{:S(2)}) collective-permute-start(f32[5,16,32]{2,1,0:T(8,128)S(1)} %pad_maximum_fusion.16), channel_id=1, source_target_pairs={{0,2},{1,3},{2,0},{3,1},{4,6},{5,7},{6,4},{7,5},{8,10},{9,11},{10,... | collective-permute-start | bytes 30728 | tf_op jit(solution)/shard_map/ppermute | solution.py:33
  31.2 14.5 %copy-start.9 = (f32[4,16,32]{2,1,0:T(8,128)}, f32[4,16,32]{2,1,0:T(8,128)S(1)}, u32[]{:S(2)}) copy-start(f32[4,16,32]{2,1,0:T(8,128)S(1)} %maximum_select_fusion) | copy-start | bytes 24580
  31.8 20.2 %collective-permute-start.2 = (f32[8,16,32]{2,1,0:T(8,128)}, f32[8,16,32]{2,1,0:T(8,128)}, u32[]{:S(2)}, u32[]{:S(2)}) collective-permute-start(f32[8,16,32]{2,1,0:T(8,128)} %fusion.15), channel_id=1, source_target_pairs={{0,4},{1,5},{2,6},{3,7},{4,0},{5,1},{6,2},{7,3},{8,12},{9,13},{10,... | collective-permute-start | bytes 49160 | tf_op jit(solution)/shard_map/ppermute | solution.py:33
  37.5 9.0 %copy-start.21 = (pred[64,8]{0,1:T(8,128)(4,1)S(1)}, pred[64,8]{0,1:T(8,128)(4,1)}, u32[]{:S(2)}) copy-start(pred[64,8]{0,1:T(8,128)(4,1)} %get-tuple-element.21) | copy-start | bytes 1540
  38.9 6.8 %copy-start.3 = (f32[64,16,32]{0,2,1:T(8,128)S(1)}, f32[64,16,32]{0,2,1:T(8,128)}, u32[]{:S(2)}) copy-start(f32[64,16,32]{0,2,1:T(8,128)} %copy.28) | copy-start | bytes 393220
  38.9 8.3 %copy-start.4 = (f32[4,32,4,32]{3,1,2,0:T(8,128)S(1)}, f32[4,32,4,32]{3,1,2,0:T(8,128)}, u32[]{:S(2)}) copy-start(f32[4,32,4,32]{3,1,2,0:T(8,128)} %fusion.22) | copy-start | bytes 196612
  38.9 9.2 %copy-start.11 = (bf16[64,1024]{1,0:T(8,128)(2,1)S(1)}, bf16[64,1024]{1,0:T(8,128)(2,1)}, u32[]{:S(2)}) copy-start(bf16[64,1024]{1,0:T(8,128)(2,1)} %param.21) | copy-start | bytes 393220
  45.7 4.8 %copy-start = (f32[3,4096]{0,1:T(8,128)S(1)}, f32[3,4096]{0,1:T(8,128)}, u32[]{:S(2)}) copy-start(f32[3,4096]{0,1:T(8,128)} %copy.25) | copy-start | bytes 147460
  50.5 3.8 %copy-start.10 = (f32[4,16,32]{2,1,0:T(8,128)S(1)}, f32[4,16,32]{2,1,0:T(8,128)}, u32[]{:S(2)}) copy-start(f32[4,16,32]{2,1,0:T(8,128)} %copy-done.9) | copy-start | bytes 24580
  52.8 0.8 copy-start.12
  57.9 19.2 %copy-start.8 = (f32[64,512]{1,0:T(8,128)S(1)}, f32[64,512]{1,0:T(8,128)}, u32[]{:S(2)}) copy-start(f32[64,512]{1,0:T(8,128)} %copy.29) | copy-start | bytes 393220
  68.4 38.7 %collective-permute-start.8 = (f32[2,16,32]{2,1,0:T(8,128)}, f32[2,16,32]{2,1,0:T(8,128)S(1)}, u32[]{:S(2)}, u32[]{:S(2)}) collective-permute-start(f32[2,16,32]{2,1,0:T(8,128)} %get-tuple-element.14), channel_id=1, source_target_pairs={{16,0},{17,1},{18,2},{19,3},{20,4},{21,5},{22,6},{23,7},{24,8},{25... | collective-permute-start | bytes 12296 | tf_op jit(solution)/shard_map/ppermute | solution.py:38
  78.7 7.2 %copy-start.16 = (f32[2,16,32]{2,1,0:T(8,128)S(1)}, f32[2,16,32]{2,1,0:T(8,128)}, u32[]{:S(2)}) copy-start(f32[2,16,32]{2,1,0:T(8,128)} %get-tuple-element.13) | copy-start | bytes 12292
  78.7 10.5 %copy-start.17 = (pred[64,8]{1,0:T(8,128)(4,1)S(1)}, pred[64,8]{1,0:T(8,128)(4,1)}, u32[]{:S(2)}) copy-start(pred[64,8]{1,0:T(8,128)(4,1)} %copy.27) | copy-start | bytes 1540
  81.3 14.6 %copy-start.15 = (f32[8,16,32]{2,1,0:T(8,128)S(1)}, f32[8,16,32]{2,1,0:T(8,128)}, u32[]{:S(2)}) copy-start(f32[8,16,32]{2,1,0:T(8,128)} %get-tuple-element.11) | copy-start | bytes 49156
  81.3 16.7 %copy-start.14 = (f32[8,16,32]{2,1,0:T(8,128)S(1)}, f32[8,16,32]{2,1,0:T(8,128)}, u32[]{:S(2)}) copy-start(f32[8,16,32]{2,1,0:T(8,128)} %get-tuple-element.12) | copy-start | bytes 49156
  81.3 25.7 %copy-start.13 = (f32[1,16,32]{2,1,0:T(8,128)S(1)}, f32[1,16,32]{2,1,0:T(8,128)}, u32[]{:S(2)}) copy-start(f32[1,16,32]{2,1,0:T(8,128)} %copy-done.12) | copy-start | bytes 6148
  81.3 31.4 %copy-start.5 = (f32[4,32,4,32]{3,2,1,0:T(4,128)S(1)}, f32[4,32,4,32]{3,2,1,0:T(4,128)}, u32[]{:S(2)}) copy-start(f32[4,32,4,32]{3,2,1,0:T(4,128)} %copy.54) | copy-start | bytes 196612
  81.3 32.0 %copy-start.1 = (f32[64,16,64]{2,1,0:T(8,128)S(1)}, f32[64,16,64]{2,1,0:T(8,128)}, u32[]{:S(2)}) copy-start(f32[64,16,64]{2,1,0:T(8,128)} %shard_map.127) | copy-start | bytes 786436
  81.3 27.8 %collective-permute-start.10 = (f32[1,16,32]{2,1,0:T(8,128)S(1)}, f32[1,16,32]{2,1,0:T(8,128)S(1)}, u32[]{:S(2)}, u32[]{:S(2)}) collective-permute-start(f32[1,16,32]{2,1,0:T(8,128)S(1)} %slice.256), channel_id=1, source_target_pairs={{24,0},{25,1},{26,2},{27,3},{28,4},{29,5},{30,6},{31,7},{32,8},{33... | collective-permute-start | bytes 6152 | tf_op jit(solution)/shard_map/ppermute | solution.py:38
  85.9 19.1 %collective-permute-start.7 = (f32[2,16,32]{2,1,0:T(8,128)S(1)}, f32[2,16,32]{2,1,0:T(8,128)S(1)}, u32[]{:S(2)}, u32[]{:S(2)}) collective-permute-start(f32[2,16,32]{2,1,0:T(8,128)S(1)} %copy-done.16), channel_id=1, source_target_pairs={{0,16},{1,17},{2,18},{3,19},{4,20},{5,21},{6,22},{7,23},{8,24},{9,... | collective-permute-start | bytes 12296 | tf_op jit(solution)/shard_map/ppermute | solution.py:38
  95.9 11.1 %collective-permute-start.5 = (f32[8,16,32]{2,1,0:T(8,128)S(1)}, f32[8,16,32]{2,1,0:T(8,128)S(1)}, u32[]{:S(2)}, u32[]{:S(2)}) collective-permute-start(f32[8,16,32]{2,1,0:T(8,128)S(1)} %copy-done.15), channel_id=1, source_target_pairs={{0,8},{1,9},{2,10},{3,11},{4,12},{5,13},{6,14},{7,15},{8,16},{9,17... | collective-permute-start | bytes 49160 | tf_op jit(solution)/shard_map/ppermute | solution.py:38
  98.0 9.1 %collective-permute-start.6 = (f32[8,16,32]{2,1,0:T(8,128)S(1)}, f32[8,16,32]{2,1,0:T(8,128)S(1)}, u32[]{:S(2)}, u32[]{:S(2)}) collective-permute-start(f32[8,16,32]{2,1,0:T(8,128)S(1)} %copy-done.14), channel_id=1, source_target_pairs={{8,0},{9,1},{10,2},{11,3},{12,4},{13,5},{14,6},{15,7},{16,8},{17,9... | collective-permute-start | bytes 49160 | tf_op jit(solution)/shard_map/ppermute | solution.py:38
  105.1 7.7 %collective-permute-start.9 = (f32[1,16,32]{2,1,0:T(8,128)S(1)}, f32[1,16,32]{2,1,0:T(8,128)S(1)}, u32[]{:S(2)}, u32[]{:S(2)}) collective-permute-start(f32[1,16,32]{2,1,0:T(8,128)S(1)} %slice.253), channel_id=1, source_target_pairs={{0,24},{1,25},{2,26},{3,27},{4,28},{5,29},{6,30},{7,31},{8,32},{9,... | collective-permute-start | bytes 6152 | tf_op jit(solution)/shard_map/ppermute | solution.py:38

commit v13 on v10

--- a/solution.py
+++ b/solution.py
@@ -47,7 +47,7 @@
     def one_leaf(i, carry):
         own = table_ref[i + NEAR_REACH]
         parts = []
-        columns = columns_ref[i]
+        columns = jnp.transpose(columns_ref[i])[:CLUSTER]
         for pair in range(NEAR_BLOCKS // 2):
             first = table_ref[i + NEAR_REACH + offsets_ref[i, 2 * pair]]
             second = table_ref[i + NEAR_REACH + offsets_ref[i, 2 * pair + 1]]
@@ -74,7 +74,7 @@
     leaf_count = target_points.shape[1]
     by_leaf = jnp.transpose(extended, (1, 0, 2))
     table = jnp.concatenate([by_leaf, by_leaf], axis=2)
-    columns = jnp.pad(jnp.transpose(target_points, (1, 2, 0)), ((0, 0), (0, 0), (0, 125)))
+    columns = jnp.pad(jnp.transpose(target_points, (1, 0, 2)), ((0, 0), (0, 5), (0, CLUSTER)))
     return pl.pallas_call(
         near_body,
         out_shape=jax.ShapeDtypeStruct((leaf_count, RHS, CLUSTER), jnp.float32),

time: 111 us -> 110 us (level)
  local copies, waits for them, and re-layouts: 39.6 us -> 36.9 us
    unnamed x59 -> x58, local copies, waits for them, and re-layouts: 6.74 us -> 5.62 us
  transfers between devices with their start and end apart: 9 -> 9, of which waited for: 2 -> 2; matrix products, arithmetic and copies ran while one was open for 39% -> 37% of each run, Pallas kernels for 0% -> 0%
where the time goes in v13:
time: 110 us; the launch traced here: 109 us
  local copies, waits for them, and re-layouts  36.9 us (34%)
  starting transfers between devices  33.3 us (30%)
  waiting for transfers between devices  11.1 us (10%)
  matrix products  10.8 us (10%)
  Pallas kernels  7.89 us (7%)
  other arithmetic  7.8 us (7%)
    ppermute x4, starting transfers between devices, receive_from(): lax.ppermute(value, AXES, [(s, s - step) for s in range(n) if 0 <= s - st...  19.7 us
    pallas_call x1, Pallas kernels, near_field_kernel(): pl.pallas_call(near_body, out_shape=jax.ShapeDtypeStruct((leaf_count, RHS...  7.89 us
    reshape x1, local copies, waits for them, and re-layouts, local(): leaf_coupling.reshape(leaf_count, FAR_BLOCKS, RANK, RANK)  6.89 us
    ppermute x3, starting transfers between devices, swap_with(): return lax.ppermute(value, AXES, [(i, i ^ mask) for i in range(n)])  6.88 us
    dot_general x1, matrix products, local(): jnp.einsum('lfrk,lfkq->lrq', partner_blocks, leaf_coupling.reshape(leaf_c...  6.71 us
    ppermute x4, waiting for transfers between devices, receive_from(): lax.ppermute(value, AXES, [(s, s - step) for s in range(n) if 0 <= s - st...  5.98 us
    unnamed x58, local copies, waits for them, and re-layouts  5.62 us
    ppermute x3, waiting for transfers between devices, swap_with(): return lax.ppermute(value, AXES, [(i, i ^ mask) for i in range(n)])  5.15 us
  transfers between devices with their start and end apart: 9, of which 2 were waited for; matrix products, arithmetic and copies ran while one was open for 37% of the time, Pallas kernels for 0%

profile of v13, /device:TPU:398, one launch (start us, length us, event | category | flops | bytes accessed | tf_op | source)
XLA Modules:
  0.0 108.7 jit_solution(9298853927665697381)
XLA Ops:
  0.0 1.3 %copy.19 = bf16[64,2048]{0,1:T(8,128)(2,1)S(1)} copy(bf16[64,2048]{1,0:T(8,128)(2,1)} %param.17) | data formatting | bytes 524288 | tf_op args[4]
  1.3 1.1 copy.21
  2.4 1.2 %reshape.138 = bf16[16,64,64]{2,1,0:T(8,128)(2,1)S(1)} reshape(bf16[16,4096]{1,0:T(8,128)(2,1)} %param.13) | data formatting | bytes 262144 | tf_op jit(solution)/shard_map/reshape | solution.py:177
  3.6 1.1 copy.22
  4.7 0.8 copy.35
  5.5 0.9 slice_reduce_fusion.2
  6.6 0.7 convert_reduce_fusion
  7.4 0.4 fusion.10
  7.8 0.6 fusion.45
  8.6 0.2 convolution_bitcast_fusion.1
  8.8 2.7 %collective-permute-start = (f32[4,16,32]{2,1,0:T(8,128)S(1)}, f32[4,16,32]{2,1,0:T(8,128)S(1)}, u32[]{:S(2)}, u32[]{:S(2)}) collective-permute-start(f32[4,16,32]{2,1,0:T(8,128)S(1)} %convolution_bitcast_fusion.1), channel_id=1, source_target_pairs={{0,1},{1,0},{2,3},{3,2},{4,5},{5,4},{6,7},{7,6},{8,9},{9,8},{10,11... | collective-permute-start | bytes 24584 | tf_op jit(solution)/shard_map/ppermute | solution.py:33
  11.8 0.7 pad_maximum_fusion.4
  12.5 3.1 %collective-permute-start.4 = (f32[35840]{0:T(1024)}, f32[35840]{0:T(1024)}, u32[]{:S(2)}, u32[]{:S(2)}) collective-permute-start(f32[35840]{0:T(1024)} %pad_maximum_fusion.4), channel_id=1, source_target_pairs={{1,0},{2,1},{3,2},{4,3},{5,4},{6,5},{7,6},{8,7},{9,8},{10,9},{11,1... | collective-permute-start | bytes 430088 | tf_op jit(solution)/shard_map/ppermute | solution.py:193
  15.7 0.7 pad_maximum_fusion.3
  16.4 3.7 %collective-permute-start.3 = (f32[35840]{0:T(1024)}, f32[35840]{0:T(1024)}, u32[]{:S(2)}, u32[]{:S(2)}) collective-permute-start(f32[35840]{0:T(1024)} %pad_maximum_fusion.3), channel_id=1, source_target_pairs={{0,1},{1,2},{2,3},{3,4},{4,5},{5,6},{6,7},{7,8},{8,9},{9,10},{10,1... | collective-permute-start | bytes 430088 | tf_op jit(solution)/shard_map/ppermute | solution.py:192
  20.1 0.1 reshape.149
  20.6 0.6 compare_and_fusion
  21.4 1.5 %fusion.22 = f32[4,32,4,32]{3,1,2,0:T(8,128)} fusion(bf16[4,4,32,32]{3,2,1,0:T(8,128)(2,1)S(1)} %reshape.149, f32[1,32,32]{2,1,0:T(8,128)S(1)} %fusion.32, f32[1,32,32]{2,1,0:T(8,128)S(1)} %convolution_bitcast_fusion.2, f32[1,32,32]{2,1,0:T(8,128)S(1)} %bitcast.76, f32[1,32,32]{2,1,0:T(8,128)S(1)} %reshape.154), kind=kOutput, calls=%fused_computation.50 | convolution fusion | flops 6303744 | bytes 114688 | tf_op jit(solution)/shard_map/sqkp,spm->sqkm/dot_general | solution.py:111
  22.9 0.6 pad_clamp_fusion.1
  23.7 2.2 %collective-permute-start.1 = (f32[5,16,32]{2,1,0:T(8,128)S(1)}, f32[5,16,32]{2,1,0:T(8,128)S(1)}, u32[]{:S(2)}, u32[]{:S(2)}) collective-permute-start(f32[5,16,32]{2,1,0:T(8,128)S(1)} %pad_maximum_fusion.18), channel_id=1, source_target_pairs={{0,2},{1,3},{2,0},{3,1},{4,6},{5,7},{6,4},{7,5},{8,10},{9,11},{10,... | collective-permute-start | bytes 30728 | tf_op jit(solution)/shard_map/ppermute | solution.py:33
  26.0 5.1 %collective-permute-done.1 = f32[5,16,32]{2,1,0:T(8,128)S(1)} collective-permute-done((f32[5,16,32]{2,1,0:T(8,128)S(1)}, f32[5,16,32]{2,1,0:T(8,128)S(1)}, u32[]{:S(2)}, u32[]{:S(2)}) %collective-permute-start.1) | collective-permute-done | bytes 10272 | tf_op jit(solution)/shard_map/ppermute | solution.py:33
  31.2 0.6 fusion.15
  31.8 1.9 %collective-permute-start.2 = (f32[8,16,32]{2,1,0:T(8,128)}, f32[8,16,32]{2,1,0:T(8,128)}, u32[]{:S(2)}, u32[]{:S(2)}) collective-permute-start(f32[8,16,32]{2,1,0:T(8,128)} %fusion.15), channel_id=1, source_target_pairs={{0,4},{1,5},{2,6},{3,7},{4,0},{5,1},{6,2},{7,3},{8,12},{9,13},{10,... | collective-permute-start | bytes 49160 | tf_op jit(solution)/shard_map/ppermute | solution.py:33
  33.9 0.9 copy.27
  34.8 0.7 copy.25.offsets_ref
  35.5 0.7 copy.55
  36.2 1.4 %copy.30 = bf16[64,8,1024]{0,2,1:T(8,128)(2,1)S(1)} copy(bf16[64,8,1024]{2,1,0:T(8,128)(2,1)S(1)} %copy-done.1) | data formatting | bytes 2097152 | tf_op args[6]
  37.7 6.9 %copy.31 = bf16[64,8,32,32]{3,2,1,0:T(8,128)(2,1)} copy(bf16[64,8,32,32]{0,3,2,1:T(8,128)(2,1)S(1)} %bitcast.68) | data formatting | bytes 2097152 | tf_op jit(solution)/shard_map/reshape | solution.py:219
  44.7 0.7 copy.26
  45.4 0.9 copy.54
  46.3 1.1 copy.33
  47.4 0.8 copy.43
  48.2 0.5 reshape.151
  48.7 0.7 pad.4.columns_ref
  49.4 0.7 fusion.40
  50.1 0.7 slice.292
  50.9 0.8 slice.290
  51.7 0.8 fusion.13
  52.5 0.6 fusion.43
  53.1 0.7 pad_maximum_fusion.7
  53.8 0.9 slice.301
  54.7 0.9 slice.299
  55.7 0.4 reshape.145
  56.1 0.6 copy.53
  56.6 1.4 %pad_maximum_fusion.table_ref = f32[96,19,128]{2,1,0:T(8,128)} fusion(f32[96,19,64]{2,1,0:T(8,128)S(1)} %bitcast.69), kind=kLoop, calls=%fused_computation.13 | loop fusion | flops 233472 | bytes 1400832 | tf_op jit(solution)/shard_map/concatenate | solution.py:76
  58.1 7.9 %shard_map.127 = f32[64,16,64]{2,1,0:T(8,128)} custom-call(s32[64,6]{1,0:T(8,128)} %copy.25.offsets_ref, f32[96,19,128]{2,1,0:T(8,128)} %pad_maximum_fusion.table_ref, f32[64,8,128]{2,1,0:T(8,128)} %pad.4.columns_ref), custom_call_target="tpu_custom_call" | custom-call | tf_op jit(solution)/shard_map/pallas_call | solution.py:78
  65.9 2.3 %collective-permute-start.6 = (f32[9,16,32]{2,1,0:T(8,128)}, f32[9,16,32]{2,1,0:T(8,128)S(1)}, u32[]{:S(2)}, u32[]{:S(2)}) collective-permute-start(f32[9,16,32]{2,1,0:T(8,128)} %get-tuple-element.13), channel_id=1, source_target_pairs={{8,0},{9,1},{10,2},{11,3},{12,4},{13,5},{14,6},{15,7},{16,8},{17,9... | collective-permute-start | bytes 55304 | tf_op jit(solution)/shard_map/ppermute | solution.py:38
  68.3 3.7 %collective-permute-start.5 = (f32[9,16,32]{2,1,0:T(8,128)}, f32[9,16,32]{2,1,0:T(8,128)S(1)}, u32[]{:S(2)}, u32[]{:S(2)}) collective-permute-start(f32[9,16,32]{2,1,0:T(8,128)} %get-tuple-element.12), channel_id=1, source_target_pairs={{0,8},{1,9},{2,10},{3,11},{4,12},{5,13},{6,14},{7,15},{8,16},{9,17... | collective-permute-start | bytes 55304 | tf_op jit(solution)/shard_map/ppermute | solution.py:38
  72.0 0.8 slice.307
  72.8 0.8 slice.306
  73.7 1.6 %gather_fusion = f32[512,512]{1,0:T(8,128)S(1)} fusion(f32[128,512]{1,0:T(8,128)S(1)} %pad_maximum_fusion.2, s32[1024]{0:T(1024)S(1)} %pad_clamp_fusion.3), kind=kCustom, calls=%fused_computation | custom fusion | bytes 2099200 | tf_op jit(solution)/shard_map/jit(_take)/gather | solution.py:215
  75.4 2.6 %gather.19 = f32[64,8,16,32]{3,2,1,0:T(8,128)} reshape(f32[512,512]{1,0:T(8,128)S(1)} %gather_fusion) | data formatting | bytes 2097152 | tf_op jit(solution)/shard_map/jit(_take)/gather | solution.py:215
  78.0 6.7 %fusion.4 = f32[64,16,32]{2,1,0:T(8,128)S(1)} fusion(bf16[64,8,32,32]{3,2,1,0:T(8,128)(2,1)} %copy.31, f32[64,8,16,32]{3,2,1,0:T(8,128)} %gather.19, pred[64,8]{1,0:T(8,128)(4,1)S(1)} %copy-done.16), kind=kOutput, calls=%fused_computation.8 | convolution fusion | flops 50593792 | bytes 2228736 | tf_op jit(solution)/shard_map/lfrk,lfkq->lrq/dot_general | solution.py:216
  84.8 11.8 %collective-permute-start.8 = (f32[3,16,32]{2,1,0:T(8,128)S(1)}, f32[3,16,32]{2,1,0:T(8,128)S(1)}, u32[]{:S(2)}, u32[]{:S(2)}) collective-permute-start(f32[3,16,32]{2,1,0:T(8,128)S(1)} %get-tuple-element.16), channel_id=1, source_target_pairs={{16,0},{17,1},{18,2},{19,3},{20,4},{21,5},{22,6},{23,7},{24,8},{25... | collective-permute-start | bytes 18440 | tf_op jit(solution)/shard_map/ppermute | solution.py:38
  96.6 1.9 %collective-permute-start.7 = (f32[3,16,32]{2,1,0:T(8,128)S(1)}, f32[3,16,32]{2,1,0:T(8,128)S(1)}, u32[]{:S(2)}, u32[]{:S(2)}) collective-permute-start(f32[3,16,32]{2,1,0:T(8,128)S(1)} %get-tuple-element.15), channel_id=1, source_target_pairs={{0,16},{1,17},{2,18},{3,19},{4,20},{5,21},{6,22},{7,23},{8,24},{9,... | collective-permute-start | bytes 18440 | tf_op jit(solution)/shard_map/ppermute | solution.py:38
  98.6 0.7 gather_fusion.2
  99.3 0.7 gather_fusion.1
  100.0 6.0 %collective-permute-done.7 = f32[3,16,32]{2,1,0:T(8,128)S(1)} collective-permute-done((f32[3,16,32]{2,1,0:T(8,128)S(1)}, f32[3,16,32]{2,1,0:T(8,128)S(1)}, u32[]{:S(2)}, u32[]{:S(2)}) %collective-permute-start.7) | collective-permute-done | bytes 6176 | tf_op jit(solution)/shard_map/ppermute | solution.py:38
  106.0 0.6 gather_fusion.3
  106.6 0.3 convolution_bitcast_fusion.4
  106.9 0.3 fusion.8
  107.2 0.4 fusion.7
  107.6 0.2 copy.34
  107.8 0.9 reshape.152
  (117 shorter events, 2.3 us)
Async XLA Ops:
  0.0 11.6 %copy-start.6 = (bf16[16,4096]{1,0:T(8,128)(2,1)S(1)}, bf16[16,4096]{1,0:T(8,128)(2,1)}, u32[]{:S(2)}) copy-start(bf16[16,4096]{1,0:T(8,128)(2,1)} %param.13) | copy-start | bytes 393220
  0.0 11.7 %copy-start.5 = (f32[3,4096]{1,0:T(4,128)S(1)}, f32[3,4096]{1,0:T(4,128)}, u32[]{:S(2)}) copy-start(f32[3,4096]{1,0:T(4,128)} %param.14) | copy-start | bytes 147460
  1.3 18.8 %copy-start.18 = (bf16[1,3,1024]{2,1,0:T(4,128)(2,1)S(1)}, bf16[1,3,1024]{2,1,0:T(4,128)(2,1)}, u32[]{:S(2)}) copy-start(bf16[1,3,1024]{2,1,0:T(4,128)(2,1)} %param.23) | copy-start | bytes 18436
  1.3 18.8 %copy-start.17 = (bf16[1,4,4,1024]{3,2,1,0:T(4,128)(2,1)S(1)}, bf16[1,4,4,1024]{3,2,1,0:T(4,128)(2,1)}, u32[]{:S(2)}) copy-start(bf16[1,4,4,1024]{3,2,1,0:T(4,128)(2,1)} %param.24) | copy-start | bytes 98308
  2.4 18.2 %copy-start.23 = (s32[64,8]{0,1:T(8,128)S(1)}, s32[64,8]{0,1:T(8,128)}, u32[]{:S(2)}) copy-start(s32[64,8]{0,1:T(8,128)} %param.16) | copy-start | bytes 6148
  3.6 19.3 %copy-start.24 = (s32[4]{0:T(128)S(1)}, s32[4]{0:T(128)}, u32[]{:S(2)}) copy-start(s32[4]{0:T(128)} %constant.56) | copy-start | bytes 52
  7.4 28.8 %copy-start.1 = (bf16[64,8,1024]{2,1,0:T(8,128)(2,1)S(1)}, bf16[64,8,1024]{2,1,0:T(8,128)(2,1)}, u32[]{:S(2)}) copy-start(bf16[64,8,1024]{2,1,0:T(8,128)(2,1)} %param.19) | copy-start | bytes 3145732
  7.8 27.1 %copy-start.21 = (s32[64,6]{0,1:T(8,128)S(1)}, s32[64,6]{0,1:T(8,128)}, u32[]{:S(2)}) copy-start(s32[64,6]{0,1:T(8,128)} %param.15) | copy-start | bytes 4612
  8.8 14.9 %collective-permute-start = (f32[4,16,32]{2,1,0:T(8,128)S(1)}, f32[4,16,32]{2,1,0:T(8,128)S(1)}, u32[]{:S(2)}, u32[]{:S(2)}) collective-permute-start(f32[4,16,32]{2,1,0:T(8,128)S(1)} %convolution_bitcast_fusion.1), channel_id=1, source_target_pairs={{0,1},{1,0},{2,3},{3,2},{4,5},{5,4},{6,7},{7,6},{8,9},{9,8},{10,11... | collective-permute-start | bytes 24584 | tf_op jit(solution)/shard_map/ppermute | solution.py:33
  12.5 41.3 %collective-permute-start.4 = (f32[35840]{0:T(1024)}, f32[35840]{0:T(1024)}, u32[]{:S(2)}, u32[]{:S(2)}) collective-permute-start(f32[35840]{0:T(1024)} %pad_maximum_fusion.4), channel_id=1, source_target_pairs={{1,0},{2,1},{3,2},{4,3},{5,4},{6,5},{7,6},{8,7},{9,8},{10,9},{11,1... | collective-permute-start | bytes 430088 | tf_op jit(solution)/shard_map/ppermute | solution.py:193
  16.4 38.3 %collective-permute-start.3 = (f32[35840]{0:T(1024)}, f32[35840]{0:T(1024)}, u32[]{:S(2)}, u32[]{:S(2)}) collective-permute-start(f32[35840]{0:T(1024)} %pad_maximum_fusion.3), channel_id=1, source_target_pairs={{0,1},{1,2},{2,3},{3,4},{4,5},{5,6},{6,7},{7,8},{8,9},{9,10},{10,1... | collective-permute-start | bytes 430088 | tf_op jit(solution)/shard_map/ppermute | solution.py:192
  23.7 7.4 %collective-permute-start.1 = (f32[5,16,32]{2,1,0:T(8,128)S(1)}, f32[5,16,32]{2,1,0:T(8,128)S(1)}, u32[]{:S(2)}, u32[]{:S(2)}) collective-permute-start(f32[5,16,32]{2,1,0:T(8,128)S(1)} %pad_maximum_fusion.18), channel_id=1, source_target_pairs={{0,2},{1,3},{2,0},{3,1},{4,6},{5,7},{6,4},{7,5},{8,10},{9,11},{10,... | collective-permute-start | bytes 30728 | tf_op jit(solution)/shard_map/ppermute | solution.py:33
  31.2 19.7 %copy-start.10 = (f32[4,16,32]{2,1,0:T(8,128)}, f32[4,16,32]{2,1,0:T(8,128)S(1)}, u32[]{:S(2)}) copy-start(f32[4,16,32]{2,1,0:T(8,128)S(1)} %maximum_select_fusion) | copy-start | bytes 24580
  31.8 17.6 %collective-permute-start.2 = (f32[8,16,32]{2,1,0:T(8,128)}, f32[8,16,32]{2,1,0:T(8,128)}, u32[]{:S(2)}, u32[]{:S(2)}) collective-permute-start(f32[8,16,32]{2,1,0:T(8,128)} %fusion.15), channel_id=1, source_target_pairs={{0,4},{1,5},{2,6},{3,7},{4,0},{5,1},{6,2},{7,3},{8,12},{9,13},{10,... | collective-permute-start | bytes 49160 | tf_op jit(solution)/shard_map/ppermute | solution.py:33
  36.2 8.5 %copy-start.22 = (pred[64,8]{0,1:T(8,128)(4,1)S(1)}, pred[64,8]{0,1:T(8,128)(4,1)}, u32[]{:S(2)}) copy-start(pred[64,8]{0,1:T(8,128)(4,1)} %get-tuple-element.23) | copy-start | bytes 1540
  37.6 6.9 %copy-start.2 = (f32[64,16,32]{0,2,1:T(8,128)S(1)}, f32[64,16,32]{0,2,1:T(8,128)}, u32[]{:S(2)}) copy-start(f32[64,16,32]{0,2,1:T(8,128)} %copy.27) | copy-start | bytes 393220
  37.6 7.7 %copy-start.3 = (f32[4,32,4,32]{3,1,2,0:T(8,128)S(1)}, f32[4,32,4,32]{3,1,2,0:T(8,128)}, u32[]{:S(2)}) copy-start(f32[4,32,4,32]{3,1,2,0:T(8,128)} %fusion.22) | copy-start | bytes 196612
  37.7 10.5 %copy-start.11 = (bf16[64,2048]{1,0:T(8,128)(2,1)S(1)}, bf16[64,2048]{1,0:T(8,128)(2,1)}, u32[]{:S(2)}) copy-start(bf16[64,2048]{1,0:T(8,128)(2,1)} %param.18) | copy-start | bytes 786436
  37.7 11.0 %copy-start.7 = (f32[3,64,64]{2,0,1:T(4,128)S(1)}, f32[3,64,64]{2,0,1:T(4,128)}, u32[]{:S(2)}) copy-start(f32[3,64,64]{2,0,1:T(4,128)} %copy.55) | copy-start | bytes 147460
  50.1 0.8 copy-start.12
  50.1 7.9 %copy-start.14 = (f32[1,16,32]{2,1,0:T(8,128)}, f32[1,16,32]{2,1,0:T(8,128)S(1)}, u32[]{:S(2)}) copy-start(f32[1,16,32]{2,1,0:T(8,128)S(1)} %get-tuple-element.36) | copy-start | bytes 6148
  50.9 7.2 %copy-start.8 = (f32[4,16,32]{2,1,0:T(8,128)}, f32[4,16,32]{2,1,0:T(8,128)S(1)}, u32[]{:S(2)}) copy-start(f32[4,16,32]{2,1,0:T(8,128)S(1)} %maximum_select_fusion.1) | copy-start | bytes 24580
  65.9 18.8 %collective-permute-start.6 = (f32[9,16,32]{2,1,0:T(8,128)}, f32[9,16,32]{2,1,0:T(8,128)S(1)}, u32[]{:S(2)}, u32[]{:S(2)}) collective-permute-start(f32[9,16,32]{2,1,0:T(8,128)} %get-tuple-element.13), channel_id=1, source_target_pairs={{8,0},{9,1},{10,2},{11,3},{12,4},{13,5},{14,6},{15,7},{16,8},{17,9... | collective-permute-start | bytes 55304 | tf_op jit(solution)/shard_map/ppermute | solution.py:38
  68.3 16.4 %collective-permute-start.5 = (f32[9,16,32]{2,1,0:T(8,128)}, f32[9,16,32]{2,1,0:T(8,128)S(1)}, u32[]{:S(2)}, u32[]{:S(2)}) collective-permute-start(f32[9,16,32]{2,1,0:T(8,128)} %get-tuple-element.12), channel_id=1, source_target_pairs={{0,8},{1,9},{2,10},{3,11},{4,12},{5,13},{6,14},{7,15},{8,16},{9,17... | collective-permute-start | bytes 55304 | tf_op jit(solution)/shard_map/ppermute | solution.py:38
  75.3 2.6 %copy-start.16 = (pred[64,8]{1,0:T(8,128)(4,1)S(1)}, pred[64,8]{1,0:T(8,128)(4,1)}, u32[]{:S(2)}) copy-start(pred[64,8]{1,0:T(8,128)(4,1)} %copy.26) | copy-start | bytes 1540
  78.0 6.8 %copy-start.15 = (f32[1,16,32]{2,1,0:T(8,128)S(1)}, f32[1,16,32]{2,1,0:T(8,128)}, u32[]{:S(2)}) copy-start(f32[1,16,32]{2,1,0:T(8,128)} %copy-done.14) | copy-start | bytes 6148
  78.0 6.8 %copy-start.19 = (f32[1,16,32]{2,1,0:T(8,128)S(1)}, f32[1,16,32]{2,1,0:T(8,128)}, u32[]{:S(2)}) copy-start(f32[1,16,32]{2,1,0:T(8,128)} %get-tuple-element.52) | copy-start | bytes 6148
  78.0 6.8 %copy-start.20 = (f32[1,16,32]{2,1,0:T(8,128)S(1)}, f32[1,16,32]{2,1,0:T(8,128)}, u32[]{:S(2)}) copy-start(f32[1,16,32]{2,1,0:T(8,128)} %get-tuple-element.53) | copy-start | bytes 6148
  78.0 20.6 %copy-start.9 = (f32[4,16,32]{2,1,0:T(8,128)S(1)}, f32[4,16,32]{2,1,0:T(8,128)}, u32[]{:S(2)}) copy-start(f32[4,16,32]{2,1,0:T(8,128)} %copy-done.8) | copy-start | bytes 24580
  78.0 28.0 %copy-start.13 = (f32[1,16,32]{2,1,0:T(8,128)S(1)}, f32[1,16,32]{2,1,0:T(8,128)}, u32[]{:S(2)}) copy-start(f32[1,16,32]{2,1,0:T(8,128)} %copy-done.12) | copy-start | bytes 6148
  78.0 28.6 %copy-start.4 = (f32[4,32,4,32]{3,2,1,0:T(4,128)S(1)}, f32[4,32,4,32]{3,2,1,0:T(4,128)}, u32[]{:S(2)}) copy-start(f32[4,32,4,32]{3,2,1,0:T(4,128)} %copy.54) | copy-start | bytes 196612
  78.0 29.2 %copy-start = (f32[64,16,64]{2,1,0:T(8,128)S(1)}, f32[64,16,64]{2,1,0:T(8,128)}, u32[]{:S(2)}) copy-start(f32[64,16,64]{2,1,0:T(8,128)} %shard_map.127) | copy-start | bytes 786436
  84.8 21.2 %collective-permute-start.8 = (f32[3,16,32]{2,1,0:T(8,128)S(1)}, f32[3,16,32]{2,1,0:T(8,128)S(1)}, u32[]{:S(2)}, u32[]{:S(2)}) collective-permute-start(f32[3,16,32]{2,1,0:T(8,128)S(1)} %get-tuple-element.16), channel_id=1, source_target_pairs={{16,0},{17,1},{18,2},{19,3},{20,4},{21,5},{22,6},{23,7},{24,8},{25... | collective-permute-start | bytes 18440 | tf_op jit(solution)/shard_map/ppermute | solution.py:38
  96.6 9.3 %collective-permute-start.7 = (f32[3,16,32]{2,1,0:T(8,128)S(1)}, f32[3,16,32]{2,1,0:T(8,128)S(1)}, u32[]{:S(2)}, u32[]{:S(2)}) collective-permute-start(f32[3,16,32]{2,1,0:T(8,128)S(1)} %get-tuple-element.15), channel_id=1, source_target_pairs={{0,16},{1,17},{2,18},{3,19},{4,20},{5,21},{6,22},{7,23},{8,24},{9,... | collective-permute-start | bytes 18440 | tf_op jit(solution)/shard_map/ppermute | solution.py:38

commit v14 on v13

--- a/solution.py
+++ b/solution.py
@@ -41,8 +41,6 @@
 def near_body(offsets_ref, table_ref, columns_ref, out_ref):
     leaf_count = out_ref.shape[0]
     rows = RHS + 3
-    lane = lax.broadcasted_iota(jnp.int32, (rows, 2 * CLUSTER), 1)
-    low_half = lane < CLUSTER
 
     def one_leaf(i, carry):
         own = table_ref[i + NEAR_REACH]
@@ -51,7 +49,7 @@
         for pair in range(NEAR_BLOCKS // 2):
             first = table_ref[i + NEAR_REACH + offsets_ref[i, 2 * pair]]
             second = table_ref[i + NEAR_REACH + offsets_ref[i, 2 * pair + 1]]
-            joined = jnp.where(low_half, first, second)
+            joined = jnp.concatenate([first, second], axis=1)
             squared = None
             for component in range(3):
                 separation = joined[RHS + component : RHS + component + 1, :] - columns[:, component : component + 1]
@@ -64,7 +62,7 @@
                     values, kernel, (((1,), (1,)), ((), ())), preferred_element_type=jnp.float32
                 )
             )
-        out_ref[i] = nugget * own[:RHS, :CLUSTER] + (parts[0] + parts[1] + parts[2])
+        out_ref[i] = nugget * own[:RHS] + (parts[0] + parts[1] + parts[2])
         return carry
 
     lax.fori_loop(0, leaf_count, one_leaf, 0, unroll=16)
@@ -73,7 +71,7 @@
 def near_field_kernel(extended, target_points, near_offsets):
     leaf_count = target_points.shape[1]
     by_leaf = jnp.transpose(extended, (1, 0, 2))
-    table = jnp.concatenate([by_leaf, by_leaf], axis=2)
+    table = by_leaf
     columns = jnp.pad(jnp.transpose(target_points, (1, 0, 2)), ((0, 0), (0, 5), (0, CLUSTER)))
     return pl.pallas_call(
         near_body,

time: 110 us -> 109 us (level)
  other arithmetic: 7.8 us -> 6.36 us
  local copies, waits for them, and re-layouts: 36.9 us -> 38 us
    concatenate x1 -> x0, other arithmetic: 1.44 us -> none  [near_field_kernel(): table = jnp.concatenate([by_leaf, by_leaf], axis=2)]
  transfers between devices with their start and end apart: 9 -> 9, of which waited for: 2 -> 2; matrix products, arithmetic and copies ran while one was open for 37% -> 38% of each run, Pallas kernels for 0% -> 0%
where the time goes in v14:
time: 109 us; the launch traced here: 108 us
  local copies, waits for them, and re-layouts  38 us (35%)
  starting transfers between devices  33.3 us (31%)
  waiting for transfers between devices  11.1 us (10%)
  matrix products  10.8 us (10%)
  Pallas kernels  7.9 us (7%)
  other arithmetic  6.36 us (6%)
    ppermute x4, starting transfers between devices, receive_from(): lax.ppermute(value, AXES, [(s, s - step) for s in range(n) if 0 <= s - st...  19.7 us
    pallas_call x1, Pallas kernels, near_field_kernel(): pl.pallas_call(near_body, out_shape=jax.ShapeDtypeStruct((leaf_count, RHS...  7.9 us
    reshape x1, local copies, waits for them, and re-layouts, local(): leaf_coupling.reshape(leaf_count, FAR_BLOCKS, RANK, RANK)  6.89 us
    ppermute x3, starting transfers between devices, swap_with(): return lax.ppermute(value, AXES, [(i, i ^ mask) for i in range(n)])  6.88 us
    dot_general x1, matrix products, local(): jnp.einsum('lfrk,lfkq->lrq', partner_blocks, leaf_coupling.reshape(leaf_c...  6.71 us
    ppermute x4, waiting for transfers between devices, receive_from(): lax.ppermute(value, AXES, [(s, s - step) for s in range(n) if 0 <= s - st...  5.98 us
    unnamed x58, local copies, waits for them, and re-layouts  5.62 us
    ppermute x3, waiting for transfers between devices, swap_with(): return lax.ppermute(value, AXES, [(i, i ^ mask) for i in range(n)])  5.15 us
  transfers between devices with their start and end apart: 9, of which 2 were waited for; matrix products, arithmetic and copies ran while one was open for 38% of the time, Pallas kernels for 0%

profile of v14, /device:TPU:398, one launch (start us, length us, event | category | flops | bytes accessed | tf_op | source)
XLA Modules:
  0.0 108.3 jit_solution(3120420270192932931)
XLA Ops:
  0.0 1.3 %copy.19 = bf16[64,2048]{0,1:T(8,128)(2,1)S(1)} copy(bf16[64,2048]{1,0:T(8,128)(2,1)} %param.17) | data formatting | bytes 524288 | tf_op args[4]
  1.3 1.1 copy.21
  2.4 1.2 %reshape.138 = bf16[16,64,64]{2,1,0:T(8,128)(2,1)S(1)} reshape(bf16[16,4096]{1,0:T(8,128)(2,1)} %param.13) | data formatting | bytes 262144 | tf_op jit(solution)/shard_map/reshape | solution.py:175
  3.6 1.1 copy.22
  4.7 0.8 copy.35
  5.5 0.9 slice_reduce_fusion.2
  6.6 0.7 convert_reduce_fusion
  7.4 0.4 fusion.10
  7.8 0.6 fusion.45
  8.3 0.1 fusion.44
  8.6 0.2 convolution_bitcast_fusion.1
  8.8 2.7 %collective-permute-start = (f32[4,16,32]{2,1,0:T(8,128)S(1)}, f32[4,16,32]{2,1,0:T(8,128)S(1)}, u32[]{:S(2)}, u32[]{:S(2)}) collective-permute-start(f32[4,16,32]{2,1,0:T(8,128)S(1)} %convolution_bitcast_fusion.1), channel_id=1, source_target_pairs={{0,1},{1,0},{2,3},{3,2},{4,5},{5,4},{6,7},{7,6},{8,9},{9,8},{10,11... | collective-permute-start | bytes 24584 | tf_op jit(solution)/shard_map/ppermute | solution.py:33
  11.8 0.7 pad_maximum_fusion.3
  12.5 3.1 %collective-permute-start.4 = (f32[35840]{0:T(1024)}, f32[35840]{0:T(1024)}, u32[]{:S(2)}, u32[]{:S(2)}) collective-permute-start(f32[35840]{0:T(1024)} %pad_maximum_fusion.3), channel_id=1, source_target_pairs={{1,0},{2,1},{3,2},{4,3},{5,4},{6,5},{7,6},{8,7},{9,8},{10,9},{11,1... | collective-permute-start | bytes 430088 | tf_op jit(solution)/shard_map/ppermute | solution.py:191
  15.7 0.7 pad_maximum_fusion.2
  16.4 3.7 %collective-permute-start.3 = (f32[35840]{0:T(1024)}, f32[35840]{0:T(1024)}, u32[]{:S(2)}, u32[]{:S(2)}) collective-permute-start(f32[35840]{0:T(1024)} %pad_maximum_fusion.2), channel_id=1, source_target_pairs={{0,1},{1,2},{2,3},{3,4},{4,5},{5,6},{6,7},{7,8},{8,9},{9,10},{10,1... | collective-permute-start | bytes 430088 | tf_op jit(solution)/shard_map/ppermute | solution.py:190
  20.1 0.1 reshape.149
  20.6 0.6 compare_and_fusion
  21.4 1.5 %fusion.22 = f32[4,32,4,32]{3,1,2,0:T(8,128)} fusion(bf16[4,4,32,32]{3,2,1,0:T(8,128)(2,1)S(1)} %reshape.149, f32[1,32,32]{2,1,0:T(8,128)S(1)} %fusion.32, f32[1,32,32]{2,1,0:T(8,128)S(1)} %convolution_bitcast_fusion.2, f32[1,32,32]{2,1,0:T(8,128)S(1)} %bitcast.76, f32[1,32,32]{2,1,0:T(8,128)S(1)} %reshape.154), kind=kOutput, calls=%fused_computation.49 | convolution fusion | flops 6303744 | bytes 114688 | tf_op jit(solution)/shard_map/sqkp,spm->sqkm/dot_general | solution.py:109
  22.9 0.6 pad_clamp_fusion.1
  23.7 2.2 %collective-permute-start.1 = (f32[5,16,32]{2,1,0:T(8,128)S(1)}, f32[5,16,32]{2,1,0:T(8,128)S(1)}, u32[]{:S(2)}, u32[]{:S(2)}) collective-permute-start(f32[5,16,32]{2,1,0:T(8,128)S(1)} %pad_maximum_fusion.17), channel_id=1, source_target_pairs={{0,2},{1,3},{2,0},{3,1},{4,6},{5,7},{6,4},{7,5},{8,10},{9,11},{10,... | collective-permute-start | bytes 30728 | tf_op jit(solution)/shard_map/ppermute | solution.py:33
  26.0 5.1 %collective-permute-done.1 = f32[5,16,32]{2,1,0:T(8,128)S(1)} collective-permute-done((f32[5,16,32]{2,1,0:T(8,128)S(1)}, f32[5,16,32]{2,1,0:T(8,128)S(1)}, u32[]{:S(2)}, u32[]{:S(2)}) %collective-permute-start.1) | collective-permute-done | bytes 10272 | tf_op jit(solution)/shard_map/ppermute | solution.py:33
  31.2 0.6 fusion.15
  31.8 1.9 %collective-permute-start.2 = (f32[8,16,32]{2,1,0:T(8,128)}, f32[8,16,32]{2,1,0:T(8,128)}, u32[]{:S(2)}, u32[]{:S(2)}) collective-permute-start(f32[8,16,32]{2,1,0:T(8,128)} %fusion.15), channel_id=1, source_target_pairs={{0,4},{1,5},{2,6},{3,7},{4,0},{5,1},{6,2},{7,3},{8,12},{9,13},{10,... | collective-permute-start | bytes 49160 | tf_op jit(solution)/shard_map/ppermute | solution.py:33
  33.9 0.9 copy.27
  34.8 0.7 copy.25.offsets_ref
  35.5 0.7 copy.55
  36.2 1.4 %copy.30 = bf16[64,8,1024]{0,2,1:T(8,128)(2,1)S(1)} copy(bf16[64,8,1024]{2,1,0:T(8,128)(2,1)S(1)} %copy-done.1) | data formatting | bytes 2097152 | tf_op args[6]
  37.7 6.9 %copy.31 = bf16[64,8,32,32]{3,2,1,0:T(8,128)(2,1)} copy(bf16[64,8,32,32]{0,3,2,1:T(8,128)(2,1)S(1)} %bitcast.68) | data formatting | bytes 2097152 | tf_op jit(solution)/shard_map/reshape | solution.py:217
  44.7 0.7 copy.26
  45.4 0.9 copy.54
  46.3 1.1 copy.33
  47.4 0.8 copy.43
  48.2 0.5 reshape.151
  48.7 0.7 pad.4.columns_ref
  49.4 0.7 fusion.40
  50.1 0.7 slice.292
  50.9 0.8 slice.290
  51.7 0.8 fusion.13
  52.5 0.6 fusion.43
  53.1 0.7 pad_maximum_fusion.6
  53.8 0.9 slice.301
  54.7 0.9 slice.299
  55.7 0.4 reshape.145
  56.1 1.6 %copy.53 = f32[19,96,64]{2,0,1:T(8,128)} copy(f32[19,96,64]{2,1,0:T(8,128)S(1)} %reshape.145) | data formatting | bytes 933888 | tf_op jit(solution)/shard_map/reshape | solution.py:200
  57.7 7.9 %shard_map.127 = f32[64,16,64]{2,1,0:T(8,128)} custom-call(s32[64,6]{1,0:T(8,128)} %copy.25.offsets_ref, f32[96,19,64]{2,1,0:T(8,128)} %bitcast.69, f32[64,8,128]{2,1,0:T(8,128)} %pad.4.columns_ref), custom_call_target="tpu_custom_call" | custom-call | tf_op jit(solution)/shard_map/pallas_call | solution.py:76
  65.6 2.3 %collective-permute-start.6 = (f32[9,16,32]{2,1,0:T(8,128)}, f32[9,16,32]{2,1,0:T(8,128)S(1)}, u32[]{:S(2)}, u32[]{:S(2)}) collective-permute-start(f32[9,16,32]{2,1,0:T(8,128)} %get-tuple-element.13), channel_id=1, source_target_pairs={{8,0},{9,1},{10,2},{11,3},{12,4},{13,5},{14,6},{15,7},{16,8},{17,9... | collective-permute-start | bytes 55304 | tf_op jit(solution)/shard_map/ppermute | solution.py:38
  67.9 3.7 %collective-permute-start.5 = (f32[9,16,32]{2,1,0:T(8,128)}, f32[9,16,32]{2,1,0:T(8,128)S(1)}, u32[]{:S(2)}, u32[]{:S(2)}) collective-permute-start(f32[9,16,32]{2,1,0:T(8,128)} %get-tuple-element.12), channel_id=1, source_target_pairs={{0,8},{1,9},{2,10},{3,11},{4,12},{5,13},{6,14},{7,15},{8,16},{9,17... | collective-permute-start | bytes 55304 | tf_op jit(solution)/shard_map/ppermute | solution.py:38
  71.6 0.8 slice.307
  72.5 0.8 slice.306
  73.4 1.6 %gather_fusion = f32[512,512]{1,0:T(8,128)S(1)} fusion(f32[128,512]{1,0:T(8,128)S(1)} %pad_maximum_fusion.1, s32[1024]{0:T(1024)S(1)} %pad_clamp_fusion.3), kind=kCustom, calls=%fused_computation | custom fusion | bytes 2099200 | tf_op jit(solution)/shard_map/jit(_take)/gather | solution.py:213
  75.0 2.6 %gather.19 = f32[64,8,16,32]{3,2,1,0:T(8,128)} reshape(f32[512,512]{1,0:T(8,128)S(1)} %gather_fusion) | data formatting | bytes 2097152 | tf_op jit(solution)/shard_map/jit(_take)/gather | solution.py:213
  77.6 6.7 %fusion.4 = f32[64,16,32]{2,1,0:T(8,128)S(1)} fusion(bf16[64,8,32,32]{3,2,1,0:T(8,128)(2,1)} %copy.31, f32[64,8,16,32]{3,2,1,0:T(8,128)} %gather.19, pred[64,8]{1,0:T(8,128)(4,1)S(1)} %copy-done.16), kind=kOutput, calls=%fused_computation.8 | convolution fusion | flops 50593792 | bytes 2228736 | tf_op jit(solution)/shard_map/lfrk,lfkq->lrq/dot_general | solution.py:214
  84.5 11.8 %collective-permute-start.8 = (f32[3,16,32]{2,1,0:T(8,128)S(1)}, f32[3,16,32]{2,1,0:T(8,128)S(1)}, u32[]{:S(2)}, u32[]{:S(2)}) collective-permute-start(f32[3,16,32]{2,1,0:T(8,128)S(1)} %get-tuple-element.16), channel_id=1, source_target_pairs={{16,0},{17,1},{18,2},{19,3},{20,4},{21,5},{22,6},{23,7},{24,8},{25... | collective-permute-start | bytes 18440 | tf_op jit(solution)/shard_map/ppermute | solution.py:38
  96.2 1.9 %collective-permute-start.7 = (f32[3,16,32]{2,1,0:T(8,128)S(1)}, f32[3,16,32]{2,1,0:T(8,128)S(1)}, u32[]{:S(2)}, u32[]{:S(2)}) collective-permute-start(f32[3,16,32]{2,1,0:T(8,128)S(1)} %get-tuple-element.15), channel_id=1, source_target_pairs={{0,16},{1,17},{2,18},{3,19},{4,20},{5,21},{6,22},{7,23},{8,24},{9,... | collective-permute-start | bytes 18440 | tf_op jit(solution)/shard_map/ppermute | solution.py:38
  98.2 0.7 gather_fusion.2
  98.9 0.7 gather_fusion.1
  99.6 6.0 %collective-permute-done.7 = f32[3,16,32]{2,1,0:T(8,128)S(1)} collective-permute-done((f32[3,16,32]{2,1,0:T(8,128)S(1)}, f32[3,16,32]{2,1,0:T(8,128)S(1)}, u32[]{:S(2)}, u32[]{:S(2)}) %collective-permute-start.7) | collective-permute-done | bytes 6176 | tf_op jit(solution)/shard_map/ppermute | solution.py:38
  105.6 0.6 gather_fusion.3
  106.2 0.3 convolution_bitcast_fusion.4
  106.5 0.3 fusion.8
  106.9 0.4 fusion.7
  107.3 0.2 copy.34
  107.4 0.9 reshape.152
  (116 shorter events, 2.2 us)
Async XLA Ops:
  0.0 11.6 %copy-start.6 = (bf16[16,4096]{1,0:T(8,128)(2,1)S(1)}, bf16[16,4096]{1,0:T(8,128)(2,1)}, u32[]{:S(2)}) copy-start(bf16[16,4096]{1,0:T(8,128)(2,1)} %param.13) | copy-start | bytes 393220
  0.0 11.7 %copy-start.5 = (f32[3,4096]{1,0:T(4,128)S(1)}, f32[3,4096]{1,0:T(4,128)}, u32[]{:S(2)}) copy-start(f32[3,4096]{1,0:T(4,128)} %param.14) | copy-start | bytes 147460
  1.3 18.8 %copy-start.18 = (bf16[1,3,1024]{2,1,0:T(4,128)(2,1)S(1)}, bf16[1,3,1024]{2,1,0:T(4,128)(2,1)}, u32[]{:S(2)}) copy-start(bf16[1,3,1024]{2,1,0:T(4,128)(2,1)} %param.23) | copy-start | bytes 18436
  1.3 18.8 %copy-start.17 = (bf16[1,4,4,1024]{3,2,1,0:T(4,128)(2,1)S(1)}, bf16[1,4,4,1024]{3,2,1,0:T(4,128)(2,1)}, u32[]{:S(2)}) copy-start(bf16[1,4,4,1024]{3,2,1,0:T(4,128)(2,1)} %param.24) | copy-start | bytes 98308
  2.4 18.2 %copy-start.23 = (s32[64,8]{0,1:T(8,128)S(1)}, s32[64,8]{0,1:T(8,128)}, u32[]{:S(2)}) copy-start(s32[64,8]{0,1:T(8,128)} %param.16) | copy-start | bytes 6148
  3.6 19.3 %copy-start.24 = (s32[4]{0:T(128)S(1)}, s32[4]{0:T(128)}, u32[]{:S(2)}) copy-start(s32[4]{0:T(128)} %constant.56) | copy-start | bytes 52
  7.4 28.8 %copy-start.1 = (bf16[64,8,1024]{2,1,0:T(8,128)(2,1)S(1)}, bf16[64,8,1024]{2,1,0:T(8,128)(2,1)}, u32[]{:S(2)}) copy-start(bf16[64,8,1024]{2,1,0:T(8,128)(2,1)} %param.19) | copy-start | bytes 3145732
  7.8 27.1 %copy-start.21 = (s32[64,6]{0,1:T(8,128)S(1)}, s32[64,6]{0,1:T(8,128)}, u32[]{:S(2)}) copy-start(s32[64,6]{0,1:T(8,128)} %param.15) | copy-start | bytes 4612
  8.8 14.9 %collective-permute-start = (f32[4,16,32]{2,1,0:T(8,128)S(1)}, f32[4,16,32]{2,1,0:T(8,128)S(1)}, u32[]{:S(2)}, u32[]{:S(2)}) collective-permute-start(f32[4,16,32]{2,1,0:T(8,128)S(1)} %convolution_bitcast_fusion.1), channel_id=1, source_target_pairs={{0,1},{1,0},{2,3},{3,2},{4,5},{5,4},{6,7},{7,6},{8,9},{9,8},{10,11... | collective-permute-start | bytes 24584 | tf_op jit(solution)/shard_map/ppermute | solution.py:33
  12.5 41.3 %collective-permute-start.4 = (f32[35840]{0:T(1024)}, f32[35840]{0:T(1024)}, u32[]{:S(2)}, u32[]{:S(2)}) collective-permute-start(f32[35840]{0:T(1024)} %pad_maximum_fusion.3), channel_id=1, source_target_pairs={{1,0},{2,1},{3,2},{4,3},{5,4},{6,5},{7,6},{8,7},{9,8},{10,9},{11,1... | collective-permute-start | bytes 430088 | tf_op jit(solution)/shard_map/ppermute | solution.py:191
  16.4 38.3 %collective-permute-start.3 = (f32[35840]{0:T(1024)}, f32[35840]{0:T(1024)}, u32[]{:S(2)}, u32[]{:S(2)}) collective-permute-start(f32[35840]{0:T(1024)} %pad_maximum_fusion.2), channel_id=1, source_target_pairs={{0,1},{1,2},{2,3},{3,4},{4,5},{5,6},{6,7},{7,8},{8,9},{9,10},{10,1... | collective-permute-start | bytes 430088 | tf_op jit(solution)/shard_map/ppermute | solution.py:190
  23.7 7.4 %collective-permute-start.1 = (f32[5,16,32]{2,1,0:T(8,128)S(1)}, f32[5,16,32]{2,1,0:T(8,128)S(1)}, u32[]{:S(2)}, u32[]{:S(2)}) collective-permute-start(f32[5,16,32]{2,1,0:T(8,128)S(1)} %pad_maximum_fusion.17), channel_id=1, source_target_pairs={{0,2},{1,3},{2,0},{3,1},{4,6},{5,7},{6,4},{7,5},{8,10},{9,11},{10,... | collective-permute-start | bytes 30728 | tf_op jit(solution)/shard_map/ppermute | solution.py:33
  31.2 19.7 %copy-start.10 = (f32[4,16,32]{2,1,0:T(8,128)}, f32[4,16,32]{2,1,0:T(8,128)S(1)}, u32[]{:S(2)}) copy-start(f32[4,16,32]{2,1,0:T(8,128)S(1)} %maximum_select_fusion) | copy-start | bytes 24580
  31.8 17.6 %collective-permute-start.2 = (f32[8,16,32]{2,1,0:T(8,128)}, f32[8,16,32]{2,1,0:T(8,128)}, u32[]{:S(2)}, u32[]{:S(2)}) collective-permute-start(f32[8,16,32]{2,1,0:T(8,128)} %fusion.15), channel_id=1, source_target_pairs={{0,4},{1,5},{2,6},{3,7},{4,0},{5,1},{6,2},{7,3},{8,12},{9,13},{10,... | collective-permute-start | bytes 49160 | tf_op jit(solution)/shard_map/ppermute | solution.py:33
  36.2 8.5 %copy-start.22 = (pred[64,8]{0,1:T(8,128)(4,1)S(1)}, pred[64,8]{0,1:T(8,128)(4,1)}, u32[]{:S(2)}) copy-start(pred[64,8]{0,1:T(8,128)(4,1)} %get-tuple-element.23) | copy-start | bytes 1540
  37.6 6.9 %copy-start.2 = (f32[64,16,32]{0,2,1:T(8,128)S(1)}, f32[64,16,32]{0,2,1:T(8,128)}, u32[]{:S(2)}) copy-start(f32[64,16,32]{0,2,1:T(8,128)} %copy.27) | copy-start | bytes 393220
  37.6 7.7 %copy-start.3 = (f32[4,32,4,32]{3,1,2,0:T(8,128)S(1)}, f32[4,32,4,32]{3,1,2,0:T(8,128)}, u32[]{:S(2)}) copy-start(f32[4,32,4,32]{3,1,2,0:T(8,128)} %fusion.22) | copy-start | bytes 196612
  37.7 10.5 %copy-start.11 = (bf16[64,2048]{1,0:T(8,128)(2,1)S(1)}, bf16[64,2048]{1,0:T(8,128)(2,1)}, u32[]{:S(2)}) copy-start(bf16[64,2048]{1,0:T(8,128)(2,1)} %param.18) | copy-start | bytes 786436
  37.7 11.0 %copy-start.7 = (f32[3,64,64]{2,0,1:T(4,128)S(1)}, f32[3,64,64]{2,0,1:T(4,128)}, u32[]{:S(2)}) copy-start(f32[3,64,64]{2,0,1:T(4,128)} %copy.55) | copy-start | bytes 147460
  50.1 0.8 copy-start.12
  50.1 21.5 %copy-start.14 = (f32[1,16,32]{2,1,0:T(8,128)}, f32[1,16,32]{2,1,0:T(8,128)S(1)}, u32[]{:S(2)}) copy-start(f32[1,16,32]{2,1,0:T(8,128)S(1)} %get-tuple-element.36) | copy-start | bytes 6148
  50.9 22.4 %copy-start.8 = (f32[4,16,32]{2,1,0:T(8,128)}, f32[4,16,32]{2,1,0:T(8,128)S(1)}, u32[]{:S(2)}) copy-start(f32[4,16,32]{2,1,0:T(8,128)S(1)} %maximum_select_fusion.1) | copy-start | bytes 24580
  65.6 18.8 %collective-permute-start.6 = (f32[9,16,32]{2,1,0:T(8,128)}, f32[9,16,32]{2,1,0:T(8,128)S(1)}, u32[]{:S(2)}, u32[]{:S(2)}) collective-permute-start(f32[9,16,32]{2,1,0:T(8,128)} %get-tuple-element.13), channel_id=1, source_target_pairs={{8,0},{9,1},{10,2},{11,3},{12,4},{13,5},{14,6},{15,7},{16,8},{17,9... | collective-permute-start | bytes 55304 | tf_op jit(solution)/shard_map/ppermute | solution.py:38
  67.9 16.5 %collective-permute-start.5 = (f32[9,16,32]{2,1,0:T(8,128)}, f32[9,16,32]{2,1,0:T(8,128)S(1)}, u32[]{:S(2)}, u32[]{:S(2)}) collective-permute-start(f32[9,16,32]{2,1,0:T(8,128)} %get-tuple-element.12), channel_id=1, source_target_pairs={{0,8},{1,9},{2,10},{3,11},{4,12},{5,13},{6,14},{7,15},{8,16},{9,17... | collective-permute-start | bytes 55304 | tf_op jit(solution)/shard_map/ppermute | solution.py:38
  75.0 2.6 %copy-start.16 = (pred[64,8]{1,0:T(8,128)(4,1)S(1)}, pred[64,8]{1,0:T(8,128)(4,1)}, u32[]{:S(2)}) copy-start(pred[64,8]{1,0:T(8,128)(4,1)} %copy.26) | copy-start | bytes 1540
  77.6 6.8 %copy-start.15 = (f32[1,16,32]{2,1,0:T(8,128)S(1)}, f32[1,16,32]{2,1,0:T(8,128)}, u32[]{:S(2)}) copy-start(f32[1,16,32]{2,1,0:T(8,128)} %copy-done.14) | copy-start | bytes 6148
  77.6 6.8 %copy-start.19 = (f32[1,16,32]{2,1,0:T(8,128)S(1)}, f32[1,16,32]{2,1,0:T(8,128)}, u32[]{:S(2)}) copy-start(f32[1,16,32]{2,1,0:T(8,128)} %get-tuple-element.52) | copy-start | bytes 6148
  77.6 6.8 %copy-start.20 = (f32[1,16,32]{2,1,0:T(8,128)S(1)}, f32[1,16,32]{2,1,0:T(8,128)}, u32[]{:S(2)}) copy-start(f32[1,16,32]{2,1,0:T(8,128)} %get-tuple-element.53) | copy-start | bytes 6148
  77.6 20.6 %copy-start.9 = (f32[4,16,32]{2,1,0:T(8,128)S(1)}, f32[4,16,32]{2,1,0:T(8,128)}, u32[]{:S(2)}) copy-start(f32[4,16,32]{2,1,0:T(8,128)} %copy-done.8) | copy-start | bytes 24580
  77.6 28.0 %copy-start.13 = (f32[1,16,32]{2,1,0:T(8,128)S(1)}, f32[1,16,32]{2,1,0:T(8,128)}, u32[]{:S(2)}) copy-start(f32[1,16,32]{2,1,0:T(8,128)} %copy-done.12) | copy-start | bytes 6148
  77.6 28.6 %copy-start.4 = (f32[4,32,4,32]{3,2,1,0:T(4,128)S(1)}, f32[4,32,4,32]{3,2,1,0:T(4,128)}, u32[]{:S(2)}) copy-start(f32[4,32,4,32]{3,2,1,0:T(4,128)} %copy.54) | copy-start | bytes 196612
  77.6 29.2 %copy-start = (f32[64,16,64]{2,1,0:T(8,128)S(1)}, f32[64,16,64]{2,1,0:T(8,128)}, u32[]{:S(2)}) copy-start(f32[64,16,64]{2,1,0:T(8,128)} %shard_map.127) | copy-start | bytes 786436
  84.5 21.2 %collective-permute-start.8 = (f32[3,16,32]{2,1,0:T(8,128)S(1)}, f32[3,16,32]{2,1,0:T(8,128)S(1)}, u32[]{:S(2)}, u32[]{:S(2)}) collective-permute-start(f32[3,16,32]{2,1,0:T(8,128)S(1)} %get-tuple-element.16), channel_id=1, source_target_pairs={{16,0},{17,1},{18,2},{19,3},{20,4},{21,5},{22,6},{23,7},{24,8},{25... | collective-permute-start | bytes 18440 | tf_op jit(solution)/shard_map/ppermute | solution.py:38
  96.2 9.3 %collective-permute-start.7 = (f32[3,16,32]{2,1,0:T(8,128)S(1)}, f32[3,16,32]{2,1,0:T(8,128)S(1)}, u32[]{:S(2)}, u32[]{:S(2)}) collective-permute-start(f32[3,16,32]{2,1,0:T(8,128)S(1)} %get-tuple-element.15), channel_id=1, source_target_pairs={{0,16},{1,17},{2,18},{3,19},{4,20},{5,21},{6,22},{7,23},{8,24},{9,... | collective-permute-start | bytes 18440 | tf_op jit(solution)/shard_map/ppermute | solution.py:38

commit v15 on v14

--- a/solution.py
+++ b/solution.py
@@ -65,7 +65,7 @@
         out_ref[i] = nugget * own[:RHS] + (parts[0] + parts[1] + parts[2])
         return carry
 
-    lax.fori_loop(0, leaf_count, one_leaf, 0, unroll=16)
+    lax.fori_loop(0, leaf_count, one_leaf, 0, unroll=True)
 
 
 def near_field_kernel(extended, target_points, near_offsets):

time: 109 us -> 109 us (level)
  no operation moved by 1% of the time
where the time goes in v15:
time: 109 us; the launch traced here: 108 us
  local copies, waits for them, and re-layouts  38 us (35%)
  starting transfers between devices  33.6 us (31%)
  waiting for transfers between devices  11.1 us (10%)
  matrix products  10.8 us (10%)
  Pallas kernels  7.03 us (6%)
  other arithmetic  6.36 us (6%)
    ppermute x4, starting transfers between devices, receive_from(): lax.ppermute(value, AXES, [(s, s - step) for s in range(n) if 0 <= s - st...  19.8 us
    ppermute x3, starting transfers between devices, swap_with(): return lax.ppermute(value, AXES, [(i, i ^ mask) for i in range(n)])  7.06 us
    pallas_call x1, Pallas kernels, near_field_kernel(): pl.pallas_call(near_body, out_shape=jax.ShapeDtypeStruct((leaf_count, RHS...  7.03 us
    reshape x1, local copies, waits for them, and re-layouts, local(): leaf_coupling.reshape(leaf_count, FAR_BLOCKS, RANK, RANK)  6.89 us
    dot_general x1, matrix products, local(): jnp.einsum('lfrk,lfkq->lrq', partner_blocks, leaf_coupling.reshape(leaf_c...  6.71 us
    ppermute x4, waiting for transfers between devices, receive_from(): lax.ppermute(value, AXES, [(s, s - step) for s in range(n) if 0 <= s - st...  5.98 us
    unnamed x58, local copies, waits for them, and re-layouts  5.62 us
    ppermute x3, waiting for transfers between devices, swap_with(): return lax.ppermute(value, AXES, [(i, i ^ mask) for i in range(n)])  5.15 us
  transfers between devices with their start and end apart: 9, of which 2 were waited for; matrix products, arithmetic and copies ran while one was open for 38% of the time, Pallas kernels for 0%

profile of v15, /device:TPU:398, one launch (start us, length us, event | category | flops | bytes accessed | tf_op | source)
XLA Modules:
  0.0 107.7 jit_solution(15555584248835415954)
XLA Ops:
  0.0 1.3 %copy.19 = bf16[64,2048]{0,1:T(8,128)(2,1)S(1)} copy(bf16[64,2048]{1,0:T(8,128)(2,1)} %param.17) | data formatting | bytes 524288 | tf_op args[4]
  1.3 1.1 copy.21
  2.4 1.2 %reshape.138 = bf16[16,64,64]{2,1,0:T(8,128)(2,1)S(1)} reshape(bf16[16,4096]{1,0:T(8,128)(2,1)} %param.13) | data formatting | bytes 262144 | tf_op jit(solution)/shard_map/reshape | solution.py:175
  3.6 1.1 %copy.22 = bf16[64,1024]{0,1:T(8,128)(2,1)S(1)} copy(bf16[64,1024]{1,0:T(8,128)(2,1)} %param.20) | data formatting | bytes 262144 | tf_op args[7]
  4.7 0.8 copy.35
  5.5 0.9 slice_reduce_fusion.2
  6.6 0.7 convert_reduce_fusion
  7.4 0.4 fusion.10
  7.8 0.6 fusion.45
  8.3 0.1 fusion.44
  8.6 0.2 convolution_bitcast_fusion.1
  8.8 2.7 %collective-permute-start = (f32[4,16,32]{2,1,0:T(8,128)S(1)}, f32[4,16,32]{2,1,0:T(8,128)S(1)}, u32[]{:S(2)}, u32[]{:S(2)}) collective-permute-start(f32[4,16,32]{2,1,0:T(8,128)S(1)} %convolution_bitcast_fusion.1), channel_id=1, source_target_pairs={{0,1},{1,0},{2,3},{3,2},{4,5},{5,4},{6,7},{7,6},{8,9},{9,8},{10,11... | collective-permute-start | bytes 24584 | tf_op jit(solution)/shard_map/ppermute | solution.py:33
  11.8 0.7 pad_maximum_fusion.3
  12.5 3.1 %collective-permute-start.4 = (f32[35840]{0:T(1024)}, f32[35840]{0:T(1024)}, u32[]{:S(2)}, u32[]{:S(2)}) collective-permute-start(f32[35840]{0:T(1024)} %pad_maximum_fusion.3), channel_id=1, source_target_pairs={{1,0},{2,1},{3,2},{4,3},{5,4},{6,5},{7,6},{8,7},{9,8},{10,9},{11,1... | collective-permute-start | bytes 430088 | tf_op jit(solution)/shard_map/ppermute | solution.py:191
  15.7 0.7 pad_maximum_fusion.2
  16.4 3.7 %collective-permute-start.3 = (f32[35840]{0:T(1024)}, f32[35840]{0:T(1024)}, u32[]{:S(2)}, u32[]{:S(2)}) collective-permute-start(f32[35840]{0:T(1024)} %pad_maximum_fusion.2), channel_id=1, source_target_pairs={{0,1},{1,2},{2,3},{3,4},{4,5},{5,6},{6,7},{7,8},{8,9},{9,10},{10,1... | collective-permute-start | bytes 430088 | tf_op jit(solution)/shard_map/ppermute | solution.py:190
  20.1 0.1 reshape.149
  20.6 0.6 compare_and_fusion
  21.4 1.5 %fusion.22 = f32[4,32,4,32]{3,1,2,0:T(8,128)} fusion(bf16[4,4,32,32]{3,2,1,0:T(8,128)(2,1)S(1)} %reshape.149, f32[1,32,32]{2,1,0:T(8,128)S(1)} %fusion.32, f32[1,32,32]{2,1,0:T(8,128)S(1)} %convolution_bitcast_fusion.2, f32[1,32,32]{2,1,0:T(8,128)S(1)} %bitcast.76, f32[1,32,32]{2,1,0:T(8,128)S(1)} %reshape.154), kind=kOutput, calls=%fused_computation.49 | convolution fusion | flops 6303744 | bytes 114688 | tf_op jit(solution)/shard_map/sqkp,spm->sqkm/dot_general | solution.py:109
  22.9 0.6 pad_clamp_fusion.1
  23.7 2.2 %collective-permute-start.1 = (f32[5,16,32]{2,1,0:T(8,128)S(1)}, f32[5,16,32]{2,1,0:T(8,128)S(1)}, u32[]{:S(2)}, u32[]{:S(2)}) collective-permute-start(f32[5,16,32]{2,1,0:T(8,128)S(1)} %pad_maximum_fusion.17), channel_id=1, source_target_pairs={{0,2},{1,3},{2,0},{3,1},{4,6},{5,7},{6,4},{7,5},{8,10},{9,11},{10,... | collective-permute-start | bytes 30728 | tf_op jit(solution)/shard_map/ppermute | solution.py:33
  26.0 5.1 %collective-permute-done.1 = f32[5,16,32]{2,1,0:T(8,128)S(1)} collective-permute-done((f32[5,16,32]{2,1,0:T(8,128)S(1)}, f32[5,16,32]{2,1,0:T(8,128)S(1)}, u32[]{:S(2)}, u32[]{:S(2)}) %collective-permute-start.1) | collective-permute-done | bytes 10272 | tf_op jit(solution)/shard_map/ppermute | solution.py:33
  31.2 0.6 fusion.15
  31.8 2.1 %collective-permute-start.2 = (f32[8,16,32]{2,1,0:T(8,128)}, f32[8,16,32]{2,1,0:T(8,128)}, u32[]{:S(2)}, u32[]{:S(2)}) collective-permute-start(f32[8,16,32]{2,1,0:T(8,128)} %fusion.15), channel_id=1, source_target_pairs={{0,4},{1,5},{2,6},{3,7},{4,0},{5,1},{6,2},{7,3},{8,12},{9,13},{10,... | collective-permute-start | bytes 49160 | tf_op jit(solution)/shard_map/ppermute | solution.py:33
  34.1 0.9 copy.27
  35.0 0.7 copy.25.offsets_ref
  35.7 0.7 copy.55
  36.4 1.4 %copy.30 = bf16[64,8,1024]{0,2,1:T(8,128)(2,1)S(1)} copy(bf16[64,8,1024]{2,1,0:T(8,128)(2,1)S(1)} %copy-done.1) | data formatting | bytes 2097152 | tf_op args[6]
  37.9 6.9 %copy.31 = bf16[64,8,32,32]{3,2,1,0:T(8,128)(2,1)} copy(bf16[64,8,32,32]{0,3,2,1:T(8,128)(2,1)S(1)} %bitcast.68) | data formatting | bytes 2097152 | tf_op jit(solution)/shard_map/reshape | solution.py:217
  44.9 0.7 copy.26
  45.6 0.9 copy.54
  46.5 1.1 copy.33
  47.5 0.8 copy.43
  48.3 0.5 reshape.151
  48.9 0.7 pad.4.columns_ref
  49.6 0.7 fusion.40
  50.3 0.7 slice.292
  51.1 0.8 slice.290
  51.9 0.8 fusion.13
  52.7 0.6 fusion.43
  53.3 0.7 pad_maximum_fusion.6
  54.0 0.9 slice.301
  54.9 0.9 slice.299
  55.9 0.4 reshape.145
  56.2 1.6 %copy.53 = f32[19,96,64]{2,0,1:T(8,128)} copy(f32[19,96,64]{2,1,0:T(8,128)S(1)} %reshape.145) | data formatting | bytes 933888 | tf_op jit(solution)/shard_map/reshape | solution.py:200
  57.9 7.0 %shard_map.127 = f32[64,16,64]{2,1,0:T(8,128)} custom-call(s32[64,6]{1,0:T(8,128)} %copy.25.offsets_ref, f32[96,19,64]{2,1,0:T(8,128)} %bitcast.69, f32[64,8,128]{2,1,0:T(8,128)} %pad.4.columns_ref), custom_call_target="tpu_custom_call" | custom-call | tf_op jit(solution)/shard_map/pallas_call | solution.py:76
  64.9 2.3 %collective-permute-start.6 = (f32[9,16,32]{2,1,0:T(8,128)}, f32[9,16,32]{2,1,0:T(8,128)S(1)}, u32[]{:S(2)}, u32[]{:S(2)}) collective-permute-start(f32[9,16,32]{2,1,0:T(8,128)} %get-tuple-element.13), channel_id=1, source_target_pairs={{8,0},{9,1},{10,2},{11,3},{12,4},{13,5},{14,6},{15,7},{16,8},{17,9... | collective-permute-start | bytes 55304 | tf_op jit(solution)/shard_map/ppermute | solution.py:38
  67.2 3.7 %collective-permute-start.5 = (f32[9,16,32]{2,1,0:T(8,128)}, f32[9,16,32]{2,1,0:T(8,128)S(1)}, u32[]{:S(2)}, u32[]{:S(2)}) collective-permute-start(f32[9,16,32]{2,1,0:T(8,128)} %get-tuple-element.12), channel_id=1, source_target_pairs={{0,8},{1,9},{2,10},{3,11},{4,12},{5,13},{6,14},{7,15},{8,16},{9,17... | collective-permute-start | bytes 55304 | tf_op jit(solution)/shard_map/ppermute | solution.py:38
  71.0 0.8 slice.307
  71.8 0.8 slice.306
  72.7 1.6 %gather_fusion = f32[512,512]{1,0:T(8,128)S(1)} fusion(f32[128,512]{1,0:T(8,128)S(1)} %pad_maximum_fusion.1, s32[1024]{0:T(1024)S(1)} %pad_clamp_fusion.3), kind=kCustom, calls=%fused_computation | custom fusion | bytes 2099200 | tf_op jit(solution)/shard_map/jit(_take)/gather | solution.py:213
  74.4 2.6 %gather.19 = f32[64,8,16,32]{3,2,1,0:T(8,128)} reshape(f32[512,512]{1,0:T(8,128)S(1)} %gather_fusion) | data formatting | bytes 2097152 | tf_op jit(solution)/shard_map/jit(_take)/gather | solution.py:213
  77.0 6.7 %fusion.4 = f32[64,16,32]{2,1,0:T(8,128)S(1)} fusion(bf16[64,8,32,32]{3,2,1,0:T(8,128)(2,1)} %copy.31, f32[64,8,16,32]{3,2,1,0:T(8,128)} %gather.19, pred[64,8]{1,0:T(8,128)(4,1)S(1)} %copy-done.16), kind=kOutput, calls=%fused_computation.8 | convolution fusion | flops 50593792 | bytes 2228736 | tf_op jit(solution)/shard_map/lfrk,lfkq->lrq/dot_general | solution.py:214
  83.8 11.8 %collective-permute-start.8 = (f32[3,16,32]{2,1,0:T(8,128)S(1)}, f32[3,16,32]{2,1,0:T(8,128)S(1)}, u32[]{:S(2)}, u32[]{:S(2)}) collective-permute-start(f32[3,16,32]{2,1,0:T(8,128)S(1)} %get-tuple-element.16), channel_id=1, source_target_pairs={{16,0},{17,1},{18,2},{19,3},{20,4},{21,5},{22,6},{23,7},{24,8},{25... | collective-permute-start | bytes 18440 | tf_op jit(solution)/shard_map/ppermute | solution.py:38
  95.6 1.9 %collective-permute-start.7 = (f32[3,16,32]{2,1,0:T(8,128)S(1)}, f32[3,16,32]{2,1,0:T(8,128)S(1)}, u32[]{:S(2)}, u32[]{:S(2)}) collective-permute-start(f32[3,16,32]{2,1,0:T(8,128)S(1)} %get-tuple-element.15), channel_id=1, source_target_pairs={{0,16},{1,17},{2,18},{3,19},{4,20},{5,21},{6,22},{7,23},{8,24},{9,... | collective-permute-start | bytes 18440 | tf_op jit(solution)/shard_map/ppermute | solution.py:38
  97.6 0.7 gather_fusion.2
  98.3 0.7 gather_fusion.1
  99.0 6.0 %collective-permute-done.7 = f32[3,16,32]{2,1,0:T(8,128)S(1)} collective-permute-done((f32[3,16,32]{2,1,0:T(8,128)S(1)}, f32[3,16,32]{2,1,0:T(8,128)S(1)}, u32[]{:S(2)}, u32[]{:S(2)}) %collective-permute-start.7) | collective-permute-done | bytes 6176 | tf_op jit(solution)/shard_map/ppermute | solution.py:38
  105.0 0.6 gather_fusion.3
  105.6 0.3 convolution_bitcast_fusion.4
  105.9 0.3 fusion.8
  106.2 0.4 fusion.7
  106.6 0.2 copy.34
  106.8 0.9 reshape.152
  (116 shorter events, 2.2 us)
Async XLA Ops:
  0.0 11.6 %copy-start.6 = (bf16[16,4096]{1,0:T(8,128)(2,1)S(1)}, bf16[16,4096]{1,0:T(8,128)(2,1)}, u32[]{:S(2)}) copy-start(bf16[16,4096]{1,0:T(8,128)(2,1)} %param.13) | copy-start | bytes 393220
  0.0 11.7 %copy-start.5 = (f32[3,4096]{1,0:T(4,128)S(1)}, f32[3,4096]{1,0:T(4,128)}, u32[]{:S(2)}) copy-start(f32[3,4096]{1,0:T(4,128)} %param.14) | copy-start | bytes 147460
  1.3 18.8 %copy-start.18 = (bf16[1,3,1024]{2,1,0:T(4,128)(2,1)S(1)}, bf16[1,3,1024]{2,1,0:T(4,128)(2,1)}, u32[]{:S(2)}) copy-start(bf16[1,3,1024]{2,1,0:T(4,128)(2,1)} %param.23) | copy-start | bytes 18436
  1.3 18.8 %copy-start.17 = (bf16[1,4,4,1024]{3,2,1,0:T(4,128)(2,1)S(1)}, bf16[1,4,4,1024]{3,2,1,0:T(4,128)(2,1)}, u32[]{:S(2)}) copy-start(bf16[1,4,4,1024]{3,2,1,0:T(4,128)(2,1)} %param.24) | copy-start | bytes 98308
  2.4 18.2 %copy-start.23 = (s32[64,8]{0,1:T(8,128)S(1)}, s32[64,8]{0,1:T(8,128)}, u32[]{:S(2)}) copy-start(s32[64,8]{0,1:T(8,128)} %param.16) | copy-start | bytes 6148
  3.6 19.3 %copy-start.24 = (s32[4]{0:T(128)S(1)}, s32[4]{0:T(128)}, u32[]{:S(2)}) copy-start(s32[4]{0:T(128)} %constant.56) | copy-start | bytes 52
  7.4 29.0 %copy-start.1 = (bf16[64,8,1024]{2,1,0:T(8,128)(2,1)S(1)}, bf16[64,8,1024]{2,1,0:T(8,128)(2,1)}, u32[]{:S(2)}) copy-start(bf16[64,8,1024]{2,1,0:T(8,128)(2,1)} %param.19) | copy-start | bytes 3145732
  7.8 27.3 %copy-start.21 = (s32[64,6]{0,1:T(8,128)S(1)}, s32[64,6]{0,1:T(8,128)}, u32[]{:S(2)}) copy-start(s32[64,6]{0,1:T(8,128)} %param.15) | copy-start | bytes 4612
  8.8 14.9 %collective-permute-start = (f32[4,16,32]{2,1,0:T(8,128)S(1)}, f32[4,16,32]{2,1,0:T(8,128)S(1)}, u32[]{:S(2)}, u32[]{:S(2)}) collective-permute-start(f32[4,16,32]{2,1,0:T(8,128)S(1)} %convolution_bitcast_fusion.1), channel_id=1, source_target_pairs={{0,1},{1,0},{2,3},{3,2},{4,5},{5,4},{6,7},{7,6},{8,9},{9,8},{10,11... | collective-permute-start | bytes 24584 | tf_op jit(solution)/shard_map/ppermute | solution.py:33
  12.5 41.5 %collective-permute-start.4 = (f32[35840]{0:T(1024)}, f32[35840]{0:T(1024)}, u32[]{:S(2)}, u32[]{:S(2)}) collective-permute-start(f32[35840]{0:T(1024)} %pad_maximum_fusion.3), channel_id=1, source_target_pairs={{1,0},{2,1},{3,2},{4,3},{5,4},{6,5},{7,6},{8,7},{9,8},{10,9},{11,1... | collective-permute-start | bytes 430088 | tf_op jit(solution)/shard_map/ppermute | solution.py:191
  16.4 38.5 %collective-permute-start.3 = (f32[35840]{0:T(1024)}, f32[35840]{0:T(1024)}, u32[]{:S(2)}, u32[]{:S(2)}) collective-permute-start(f32[35840]{0:T(1024)} %pad_maximum_fusion.2), channel_id=1, source_target_pairs={{0,1},{1,2},{2,3},{3,4},{4,5},{5,6},{6,7},{7,8},{8,9},{9,10},{10,1... | collective-permute-start | bytes 430088 | tf_op jit(solution)/shard_map/ppermute | solution.py:190
  23.7 7.4 %collective-permute-start.1 = (f32[5,16,32]{2,1,0:T(8,128)S(1)}, f32[5,16,32]{2,1,0:T(8,128)S(1)}, u32[]{:S(2)}, u32[]{:S(2)}) collective-permute-start(f32[5,16,32]{2,1,0:T(8,128)S(1)} %pad_maximum_fusion.17), channel_id=1, source_target_pairs={{0,2},{1,3},{2,0},{3,1},{4,6},{5,7},{6,4},{7,5},{8,10},{9,11},{10,... | collective-permute-start | bytes 30728 | tf_op jit(solution)/shard_map/ppermute | solution.py:33
  31.2 19.9 %copy-start.10 = (f32[4,16,32]{2,1,0:T(8,128)}, f32[4,16,32]{2,1,0:T(8,128)S(1)}, u32[]{:S(2)}) copy-start(f32[4,16,32]{2,1,0:T(8,128)S(1)} %maximum_select_fusion) | copy-start | bytes 24580
  31.8 17.8 %collective-permute-start.2 = (f32[8,16,32]{2,1,0:T(8,128)}, f32[8,16,32]{2,1,0:T(8,128)}, u32[]{:S(2)}, u32[]{:S(2)}) collective-permute-start(f32[8,16,32]{2,1,0:T(8,128)} %fusion.15), channel_id=1, source_target_pairs={{0,4},{1,5},{2,6},{3,7},{4,0},{5,1},{6,2},{7,3},{8,12},{9,13},{10,... | collective-permute-start | bytes 49160 | tf_op jit(solution)/shard_map/ppermute | solution.py:33
  36.4 8.5 %copy-start.22 = (pred[64,8]{0,1:T(8,128)(4,1)S(1)}, pred[64,8]{0,1:T(8,128)(4,1)}, u32[]{:S(2)}) copy-start(pred[64,8]{0,1:T(8,128)(4,1)} %get-tuple-element.23) | copy-start | bytes 1540
  37.8 6.9 %copy-start.2 = (f32[64,16,32]{0,2,1:T(8,128)S(1)}, f32[64,16,32]{0,2,1:T(8,128)}, u32[]{:S(2)}) copy-start(f32[64,16,32]{0,2,1:T(8,128)} %copy.27) | copy-start | bytes 393220
  37.8 7.7 %copy-start.3 = (f32[4,32,4,32]{3,1,2,0:T(8,128)S(1)}, f32[4,32,4,32]{3,1,2,0:T(8,128)}, u32[]{:S(2)}) copy-start(f32[4,32,4,32]{3,1,2,0:T(8,128)} %fusion.22) | copy-start | bytes 196612
  37.8 10.5 %copy-start.11 = (bf16[64,2048]{1,0:T(8,128)(2,1)S(1)}, bf16[64,2048]{1,0:T(8,128)(2,1)}, u32[]{:S(2)}) copy-start(bf16[64,2048]{1,0:T(8,128)(2,1)} %param.18) | copy-start | bytes 786436
  37.9 11.0 %copy-start.7 = (f32[3,64,64]{2,0,1:T(4,128)S(1)}, f32[3,64,64]{2,0,1:T(4,128)}, u32[]{:S(2)}) copy-start(f32[3,64,64]{2,0,1:T(4,128)} %copy.55) | copy-start | bytes 147460
  50.3 0.8 copy-start.12
  50.3 20.6 %copy-start.14 = (f32[1,16,32]{2,1,0:T(8,128)}, f32[1,16,32]{2,1,0:T(8,128)S(1)}, u32[]{:S(2)}) copy-start(f32[1,16,32]{2,1,0:T(8,128)S(1)} %get-tuple-element.36) | copy-start | bytes 6148
  51.1 21.6 %copy-start.8 = (f32[4,16,32]{2,1,0:T(8,128)}, f32[4,16,32]{2,1,0:T(8,128)S(1)}, u32[]{:S(2)}) copy-start(f32[4,16,32]{2,1,0:T(8,128)S(1)} %maximum_select_fusion.1) | copy-start | bytes 24580
  64.9 18.8 %collective-permute-start.6 = (f32[9,16,32]{2,1,0:T(8,128)}, f32[9,16,32]{2,1,0:T(8,128)S(1)}, u32[]{:S(2)}, u32[]{:S(2)}) collective-permute-start(f32[9,16,32]{2,1,0:T(8,128)} %get-tuple-element.13), channel_id=1, source_target_pairs={{8,0},{9,1},{10,2},{11,3},{12,4},{13,5},{14,6},{15,7},{16,8},{17,9... | collective-permute-start | bytes 55304 | tf_op jit(solution)/shard_map/ppermute | solution.py:38
  67.2 16.5 %collective-permute-start.5 = (f32[9,16,32]{2,1,0:T(8,128)}, f32[9,16,32]{2,1,0:T(8,128)S(1)}, u32[]{:S(2)}, u32[]{:S(2)}) collective-permute-start(f32[9,16,32]{2,1,0:T(8,128)} %get-tuple-element.12), channel_id=1, source_target_pairs={{0,8},{1,9},{2,10},{3,11},{4,12},{5,13},{6,14},{7,15},{8,16},{9,17... | collective-permute-start | bytes 55304 | tf_op jit(solution)/shard_map/ppermute | solution.py:38
  74.3 2.6 %copy-start.16 = (pred[64,8]{1,0:T(8,128)(4,1)S(1)}, pred[64,8]{1,0:T(8,128)(4,1)}, u32[]{:S(2)}) copy-start(pred[64,8]{1,0:T(8,128)(4,1)} %copy.26) | copy-start | bytes 1540
  77.0 6.8 %copy-start.15 = (f32[1,16,32]{2,1,0:T(8,128)S(1)}, f32[1,16,32]{2,1,0:T(8,128)}, u32[]{:S(2)}) copy-start(f32[1,16,32]{2,1,0:T(8,128)} %copy-done.14) | copy-start | bytes 6148
  77.0 6.8 %copy-start.19 = (f32[1,16,32]{2,1,0:T(8,128)S(1)}, f32[1,16,32]{2,1,0:T(8,128)}, u32[]{:S(2)}) copy-start(f32[1,16,32]{2,1,0:T(8,128)} %get-tuple-element.52) | copy-start | bytes 6148
  77.0 6.8 %copy-start.20 = (f32[1,16,32]{2,1,0:T(8,128)S(1)}, f32[1,16,32]{2,1,0:T(8,128)}, u32[]{:S(2)}) copy-start(f32[1,16,32]{2,1,0:T(8,128)} %get-tuple-element.53) | copy-start | bytes 6148
  77.0 20.6 %copy-start.9 = (f32[4,16,32]{2,1,0:T(8,128)S(1)}, f32[4,16,32]{2,1,0:T(8,128)}, u32[]{:S(2)}) copy-start(f32[4,16,32]{2,1,0:T(8,128)} %copy-done.8) | copy-start | bytes 24580
  77.0 28.0 %copy-start.13 = (f32[1,16,32]{2,1,0:T(8,128)S(1)}, f32[1,16,32]{2,1,0:T(8,128)}, u32[]{:S(2)}) copy-start(f32[1,16,32]{2,1,0:T(8,128)} %copy-done.12) | copy-start | bytes 6148
  77.0 28.6 %copy-start.4 = (f32[4,32,4,32]{3,2,1,0:T(4,128)S(1)}, f32[4,32,4,32]{3,2,1,0:T(4,128)}, u32[]{:S(2)}) copy-start(f32[4,32,4,32]{3,2,1,0:T(4,128)} %copy.54) | copy-start | bytes 196612
  77.0 29.2 %copy-start = (f32[64,16,64]{2,1,0:T(8,128)S(1)}, f32[64,16,64]{2,1,0:T(8,128)}, u32[]{:S(2)}) copy-start(f32[64,16,64]{2,1,0:T(8,128)} %shard_map.127) | copy-start | bytes 786436
  83.8 21.2 %collective-permute-start.8 = (f32[3,16,32]{2,1,0:T(8,128)S(1)}, f32[3,16,32]{2,1,0:T(8,128)S(1)}, u32[]{:S(2)}, u32[]{:S(2)}) collective-permute-start(f32[3,16,32]{2,1,0:T(8,128)S(1)} %get-tuple-element.16), channel_id=1, source_target_pairs={{16,0},{17,1},{18,2},{19,3},{20,4},{21,5},{22,6},{23,7},{24,8},{25... | collective-permute-start | bytes 18440 | tf_op jit(solution)/shard_map/ppermute | solution.py:38
  95.6 9.3 %collective-permute-start.7 = (f32[3,16,32]{2,1,0:T(8,128)S(1)}, f32[3,16,32]{2,1,0:T(8,128)S(1)}, u32[]{:S(2)}, u32[]{:S(2)}) collective-permute-start(f32[3,16,32]{2,1,0:T(8,128)S(1)} %get-tuple-element.15), channel_id=1, source_target_pairs={{0,16},{1,17},{2,18},{3,19},{4,20},{5,21},{6,22},{7,23},{8,24},{9,... | collective-permute-start | bytes 18440 | tf_op jit(solution)/shard_map/ppermute | solution.py:38

commit v16 on v15

--- a/solution.py
+++ b/solution.py
@@ -210,7 +210,7 @@
     near_sum = near_field_kernel(extended, target_points, near_offsets)
 
     far_index = jnp.arange(leaf_count, dtype=jnp.int32)[:, None] + FAR_REACH + far_offsets
-    partner_blocks = jnp.take(rimmed, far_index, axis=0).reshape(leaf_count, FAR_BLOCKS, RHS, RANK)
+    partner_blocks = jnp.take(rimmed, far_index, axis=0, mode="clip").reshape(leaf_count, FAR_BLOCKS, RHS, RANK)
     leaf_far = jnp.einsum(
         "lfrk,lfkq->lrq",
         partner_blocks,

time: 109 us -> 107 us (0.982)
  local copies, waits for them, and re-layouts: 38 us -> 36.3 us
    gather x2 -> x1, local copies, waits for them, and re-layouts: 4.22 us -> 1.62 us  [local(): jnp.take(rimmed, far_index, axis=0, mode='clip')]
    reshape x0 -> x1, local copies, waits for them, and re-layouts: none -> 2.59 us  [local(): jnp.take(rimmed, far_index, axis=0, mode='clip')]
    unnamed x58 -> x56, local copies, waits for them, and re-layouts: 5.62 us -> 4.72 us
  transfers between devices with their start and end apart: 9 -> 9, of which waited for: 2 -> 2; matrix products, arithmetic and copies ran while one was open for 38% -> 37% of each run, Pallas kernels for 0% -> 0%
where the time goes in v16:
time: 107 us; the launch traced here: 106 us
  local copies, waits for them, and re-layouts  36.3 us (34%)
  starting transfers between devices  33.6 us (31%)
  waiting for transfers between devices  11.1 us (10%)
  matrix products  11 us (10%)
  Pallas kernels  7.04 us (7%)
  other arithmetic  5.77 us (5%)
    ppermute x4, starting transfers between devices, receive_from(): lax.ppermute(value, AXES, [(s, s - step) for s in range(n) if 0 <= s - st...  19.8 us
    ppermute x3, starting transfers between devices, swap_with(): return lax.ppermute(value, AXES, [(i, i ^ mask) for i in range(n)])  7.05 us
    pallas_call x1, Pallas kernels, near_field_kernel(): pl.pallas_call(near_body, out_shape=jax.ShapeDtypeStruct((leaf_count, RHS...  7.04 us
    dot_general x1, matrix products, local(): jnp.einsum('lfrk,lfkq->lrq', partner_blocks, leaf_coupling.reshape(leaf_c...  6.92 us
    reshape x1, local copies, waits for them, and re-layouts, local(): leaf_coupling.reshape(leaf_count, FAR_BLOCKS, RANK, RANK)  6.8 us
    ppermute x4, waiting for transfers between devices, receive_from(): lax.ppermute(value, AXES, [(s, s - step) for s in range(n) if 0 <= s - st...  5.98 us
    ppermute x3, waiting for transfers between devices, swap_with(): return lax.ppermute(value, AXES, [(i, i ^ mask) for i in range(n)])  5.15 us
    unnamed x56, local copies, waits for them, and re-layouts  4.72 us
  transfers between devices with their start and end apart: 9, of which 2 were waited for; matrix products, arithmetic and copies ran while one was open for 37% of the time, Pallas kernels for 0%

profile of v16, /device:TPU:398, one launch (start us, length us, event | category | flops | bytes accessed | tf_op | source)
XLA Modules:
  0.0 105.6 jit_solution(17241796586528076273)
XLA Ops:
  0.0 1.3 %copy.18 = bf16[64,2048]{0,1:T(8,128)(2,1)S(1)} copy(bf16[64,2048]{1,0:T(8,128)(2,1)} %param.17) | data formatting | bytes 524288 | tf_op args[4]
  1.3 1.1 %copy.20 = bf16[64,64,32]{1,2,0:T(8,128)(2,1)S(1)} copy(bf16[64,64,32]{0,2,1:T(8,128)(2,1)S(1)} %bitcast.71) | data formatting | bytes 524288 | tf_op jit(solution)/shard_map/reshape | solution.py:179
  2.4 1.2 %reshape.134 = bf16[16,64,64]{2,1,0:T(8,128)(2,1)S(1)} reshape(bf16[16,4096]{1,0:T(8,128)(2,1)} %param.13) | data formatting | bytes 262144 | tf_op jit(solution)/shard_map/reshape | solution.py:175
  3.6 1.1 %copy.21 = bf16[64,1024]{0,1:T(8,128)(2,1)S(1)} copy(bf16[64,1024]{1,0:T(8,128)(2,1)} %param.20) | data formatting | bytes 262144 | tf_op args[7]
  4.7 0.8 copy.33
  5.5 0.9 slice_reduce_fusion.2
  6.6 0.7 convert_reduce_fusion
  7.4 0.4 fusion.3
  7.8 0.6 fusion.37
  8.3 0.1 fusion.36
  8.6 0.2 convolution_bitcast_fusion.2
  8.8 2.7 %collective-permute-start = (f32[4,16,32]{2,1,0:T(8,128)S(1)}, f32[4,16,32]{2,1,0:T(8,128)S(1)}, u32[]{:S(2)}, u32[]{:S(2)}) collective-permute-start(f32[4,16,32]{2,1,0:T(8,128)S(1)} %convolution_bitcast_fusion.2), channel_id=1, source_target_pairs={{0,1},{1,0},{2,3},{3,2},{4,5},{5,4},{6,7},{7,6},{8,9},{9,8},{10,11... | collective-permute-start | bytes 24584 | tf_op jit(solution)/shard_map/ppermute | solution.py:33
  11.8 0.7 pad_maximum_fusion.3
  12.5 3.1 %collective-permute-start.4 = (f32[35840]{0:T(1024)}, f32[35840]{0:T(1024)}, u32[]{:S(2)}, u32[]{:S(2)}) collective-permute-start(f32[35840]{0:T(1024)} %pad_maximum_fusion.3), channel_id=1, source_target_pairs={{1,0},{2,1},{3,2},{4,3},{5,4},{6,5},{7,6},{8,7},{9,8},{10,9},{11,1... | collective-permute-start | bytes 430088 | tf_op jit(solution)/shard_map/ppermute | solution.py:191
  15.7 0.7 pad_maximum_fusion.2
  16.4 3.7 %collective-permute-start.3 = (f32[35840]{0:T(1024)}, f32[35840]{0:T(1024)}, u32[]{:S(2)}, u32[]{:S(2)}) collective-permute-start(f32[35840]{0:T(1024)} %pad_maximum_fusion.2), channel_id=1, source_target_pairs={{0,1},{1,2},{2,3},{3,4},{4,5},{5,6},{6,7},{7,8},{8,9},{9,10},{10,1... | collective-permute-start | bytes 430088 | tf_op jit(solution)/shard_map/ppermute | solution.py:190
  20.1 0.1 reshape.146
  20.7 0.1 convolution_bitcast_fusion.3
  20.8 1.5 %fusion.15 = f32[4,32,4,32]{3,1,2,0:T(8,128)} fusion(bf16[4,4,32,32]{3,2,1,0:T(8,128)(2,1)S(1)} %reshape.146, f32[1,32,32]{2,1,0:T(8,128)S(1)} %fusion.25, f32[1,32,32]{2,1,0:T(8,128)S(1)} %convolution_bitcast_fusion.3, f32[1,32,32]{2,1,0:T(8,128)S(1)} %bitcast.77, f32[1,32,32]{2,1,0:T(8,128)S(1)} %reshape.151), kind=kOutput, calls=%fused_computation.45 | convolution fusion | flops 6303744 | bytes 114688 | tf_op jit(solution)/shard_map/sqkp,spm->sqkm/dot_general | solution.py:109
  22.3 0.6 pad_clamp_fusion.1
  23.2 2.2 %collective-permute-start.1 = (f32[5,16,32]{2,1,0:T(8,128)S(1)}, f32[5,16,32]{2,1,0:T(8,128)S(1)}, u32[]{:S(2)}, u32[]{:S(2)}) collective-permute-start(f32[5,16,32]{2,1,0:T(8,128)S(1)} %pad_maximum_fusion.17), channel_id=1, source_target_pairs={{0,2},{1,3},{2,0},{3,1},{4,6},{5,7},{6,4},{7,5},{8,10},{9,11},{10,... | collective-permute-start | bytes 30728 | tf_op jit(solution)/shard_map/ppermute | solution.py:33
  25.4 5.1 %collective-permute-done.1 = f32[5,16,32]{2,1,0:T(8,128)S(1)} collective-permute-done((f32[5,16,32]{2,1,0:T(8,128)S(1)}, f32[5,16,32]{2,1,0:T(8,128)S(1)}, u32[]{:S(2)}, u32[]{:S(2)}) %collective-permute-start.1) | collective-permute-done | bytes 10272 | tf_op jit(solution)/shard_map/ppermute | solution.py:33
  30.6 0.6 fusion.8
  31.2 2.1 %collective-permute-start.2 = (f32[8,16,32]{2,1,0:T(8,128)}, f32[8,16,32]{2,1,0:T(8,128)}, u32[]{:S(2)}, u32[]{:S(2)}) collective-permute-start(f32[8,16,32]{2,1,0:T(8,128)} %fusion.8), channel_id=1, source_target_pairs={{0,4},{1,5},{2,6},{3,7},{4,0},{5,1},{6,2},{7,3},{8,12},{9,13},{10,... | collective-permute-start | bytes 49160 | tf_op jit(solution)/shard_map/ppermute | solution.py:33
  33.5 0.2 copy.25
  33.7 0.7 copy.24.offsets_ref
  34.4 0.7 copy.53
  35.1 0.8 copy.26
  35.9 1.4 %copy.28 = bf16[64,8,1024]{0,2,1:T(8,128)(2,1)S(1)} copy(bf16[64,8,1024]{2,1,0:T(8,128)(2,1)S(1)} %copy-done.1) | data formatting | bytes 2097152 | tf_op args[6]
  37.4 6.8 %copy.29 = bf16[64,8,32,32]{3,2,1,0:T(8,128)(2,1)} copy(bf16[64,8,32,32]{0,3,2,1:T(8,128)(2,1)S(1)} %bitcast.69) | data formatting | bytes 2097152 | tf_op jit(solution)/shard_map/reshape | solution.py:217
  44.2 0.9 copy.52
  45.0 0.2 copy.31
  45.2 0.8 copy.41
  46.0 0.5 reshape.148
  46.5 0.7 pad.4.columns_ref
  47.3 0.7 fusion.32
  48.0 0.7 slice.292
  48.8 0.8 slice.290
  49.5 0.8 fusion.6
  50.4 0.6 fusion.35
  51.0 0.7 pad_maximum_fusion.6
  51.7 0.9 slice.301
  52.6 0.9 slice.299
  53.6 0.4 reshape.141
  54.0 1.6 %copy.51 = f32[19,96,64]{2,0,1:T(8,128)} copy(f32[19,96,64]{2,1,0:T(8,128)S(1)} %reshape.141) | data formatting | bytes 933888 | tf_op jit(solution)/shard_map/reshape | solution.py:200
  55.6 7.0 %shard_map.127 = f32[64,16,64]{2,1,0:T(8,128)} custom-call(s32[64,6]{1,0:T(8,128)} %copy.24.offsets_ref, f32[96,19,64]{2,1,0:T(8,128)} %bitcast.70, f32[64,8,128]{2,1,0:T(8,128)} %pad.4.columns_ref), custom_call_target="tpu_custom_call" | custom-call | tf_op jit(solution)/shard_map/pallas_call | solution.py:76
  62.6 2.3 %collective-permute-start.6 = (f32[9,16,32]{2,1,0:T(8,128)}, f32[9,16,32]{2,1,0:T(8,128)S(1)}, u32[]{:S(2)}, u32[]{:S(2)}) collective-permute-start(f32[9,16,32]{2,1,0:T(8,128)} %get-tuple-element.13), channel_id=1, source_target_pairs={{8,0},{9,1},{10,2},{11,3},{12,4},{13,5},{14,6},{15,7},{16,8},{17,9... | collective-permute-start | bytes 55304 | tf_op jit(solution)/shard_map/ppermute | solution.py:38
  65.0 3.7 %collective-permute-start.5 = (f32[9,16,32]{2,1,0:T(8,128)}, f32[9,16,32]{2,1,0:T(8,128)S(1)}, u32[]{:S(2)}, u32[]{:S(2)}) collective-permute-start(f32[9,16,32]{2,1,0:T(8,128)} %get-tuple-element.12), channel_id=1, source_target_pairs={{0,8},{1,9},{2,10},{3,11},{4,12},{5,13},{6,14},{7,15},{8,16},{9,17... | collective-permute-start | bytes 55304 | tf_op jit(solution)/shard_map/ppermute | solution.py:38
  68.7 0.8 slice.307
  69.5 0.8 slice.306
  70.4 1.6 %gather_fusion = f32[512,512]{1,0:T(8,128)S(1)} fusion(f32[128,512]{1,0:T(8,128)S(1)} %pad_maximum_fusion.1, s32[1024]{0:T(1024)S(1)} %pad_clamp_fusion.3), kind=kCustom, calls=%fused_computation | custom fusion | bytes 2099200 | tf_op jit(solution)/shard_map/jit(_take)/gather | solution.py:213
  72.1 2.6 %reshape.144 = f32[64,8,16,32]{3,2,1,0:T(8,128)} reshape(f32[512,512]{1,0:T(8,128)S(1)} %gather_fusion) | data formatting | bytes 2097152 | tf_op jit(solution)/shard_map/reshape | solution.py:213
  74.7 6.9 %convolution_bitcast_fusion.1 = f32[64,16,32]{2,1,0:T(8,128)S(1)} fusion(f32[64,8,16,32]{3,2,1,0:T(8,128)} %reshape.144, bf16[64,8,32,32]{3,2,1,0:T(8,128)(2,1)} %copy.29), kind=kOutput, calls=%fused_computation.7 | convolution fusion | flops 50331648 | bytes 2228224 | tf_op jit(solution)/shard_map/lfrk,lfkq->lrq/dot_general | solution.py:214
  81.7 11.8 %collective-permute-start.8 = (f32[3,16,32]{2,1,0:T(8,128)S(1)}, f32[3,16,32]{2,1,0:T(8,128)S(1)}, u32[]{:S(2)}, u32[]{:S(2)}) collective-permute-start(f32[3,16,32]{2,1,0:T(8,128)S(1)} %get-tuple-element.16), channel_id=1, source_target_pairs={{16,0},{17,1},{18,2},{19,3},{20,4},{21,5},{22,6},{23,7},{24,8},{25... | collective-permute-start | bytes 18440 | tf_op jit(solution)/shard_map/ppermute | solution.py:38
  93.5 1.9 %collective-permute-start.7 = (f32[3,16,32]{2,1,0:T(8,128)S(1)}, f32[3,16,32]{2,1,0:T(8,128)S(1)}, u32[]{:S(2)}, u32[]{:S(2)}) collective-permute-start(f32[3,16,32]{2,1,0:T(8,128)S(1)} %get-tuple-element.15), channel_id=1, source_target_pairs={{0,16},{1,17},{2,18},{3,19},{4,20},{5,21},{6,22},{7,23},{8,24},{9,... | collective-permute-start | bytes 18440 | tf_op jit(solution)/shard_map/ppermute | solution.py:38
  95.5 0.7 gather_fusion.2
  96.2 0.7 gather_fusion.1
  96.9 6.0 %collective-permute-done.7 = f32[3,16,32]{2,1,0:T(8,128)S(1)} collective-permute-done((f32[3,16,32]{2,1,0:T(8,128)S(1)}, f32[3,16,32]{2,1,0:T(8,128)S(1)}, u32[]{:S(2)}, u32[]{:S(2)}) %collective-permute-start.7) | collective-permute-done | bytes 6176 | tf_op jit(solution)/shard_map/ppermute | solution.py:38
  102.9 0.6 gather_fusion.3
  103.5 0.3 convolution_bitcast_fusion.5
  103.8 0.3 fusion.1
  104.1 0.4 fusion
  104.5 0.2 copy.32
  104.7 0.9 reshape.149
  (113 shorter events, 2.0 us)
Async XLA Ops:
  0.0 11.6 %copy-start.5 = (bf16[16,4096]{1,0:T(8,128)(2,1)S(1)}, bf16[16,4096]{1,0:T(8,128)(2,1)}, u32[]{:S(2)}) copy-start(bf16[16,4096]{1,0:T(8,128)(2,1)} %param.13) | copy-start | bytes 393220
  0.0 11.7 %copy-start.4 = (f32[3,4096]{1,0:T(4,128)S(1)}, f32[3,4096]{1,0:T(4,128)}, u32[]{:S(2)}) copy-start(f32[3,4096]{1,0:T(4,128)} %param.14) | copy-start | bytes 147460
  1.3 18.8 %copy-start.18 = (bf16[1,3,1024]{2,1,0:T(4,128)(2,1)S(1)}, bf16[1,3,1024]{2,1,0:T(4,128)(2,1)}, u32[]{:S(2)}) copy-start(bf16[1,3,1024]{2,1,0:T(4,128)(2,1)} %param.23) | copy-start | bytes 18436
  1.3 18.8 %copy-start.17 = (bf16[1,4,4,1024]{3,2,1,0:T(4,128)(2,1)S(1)}, bf16[1,4,4,1024]{3,2,1,0:T(4,128)(2,1)}, u32[]{:S(2)}) copy-start(bf16[1,4,4,1024]{3,2,1,0:T(4,128)(2,1)} %param.24) | copy-start | bytes 98308
  2.4 18.2 %copy-start.22 = (s32[64,8]{0,1:T(8,128)S(1)}, s32[64,8]{0,1:T(8,128)}, u32[]{:S(2)}) copy-start(s32[64,8]{0,1:T(8,128)} %param.16) | copy-start | bytes 6148
  3.6 18.7 %copy-start.23 = (s32[4]{0:T(128)S(1)}, s32[4]{0:T(128)}, u32[]{:S(2)}) copy-start(s32[4]{0:T(128)} %constant.41) | copy-start | bytes 52
  7.8 26.0 %copy-start.21 = (s32[64,6]{0,1:T(8,128)S(1)}, s32[64,6]{0,1:T(8,128)}, u32[]{:S(2)}) copy-start(s32[64,6]{0,1:T(8,128)} %param.15) | copy-start | bytes 4612
  7.8 28.1 %copy-start.1 = (bf16[64,8,1024]{2,1,0:T(8,128)(2,1)S(1)}, bf16[64,8,1024]{2,1,0:T(8,128)(2,1)}, u32[]{:S(2)}) copy-start(bf16[64,8,1024]{2,1,0:T(8,128)(2,1)} %param.19) | copy-start | bytes 3145732
  8.8 14.3 %collective-permute-start = (f32[4,16,32]{2,1,0:T(8,128)S(1)}, f32[4,16,32]{2,1,0:T(8,128)S(1)}, u32[]{:S(2)}, u32[]{:S(2)}) collective-permute-start(f32[4,16,32]{2,1,0:T(8,128)S(1)} %convolution_bitcast_fusion.2), channel_id=1, source_target_pairs={{0,1},{1,0},{2,3},{3,2},{4,5},{5,4},{6,7},{7,6},{8,9},{9,8},{10,11... | collective-permute-start | bytes 24584 | tf_op jit(solution)/shard_map/ppermute | solution.py:33
  12.5 39.2 %collective-permute-start.4 = (f32[35840]{0:T(1024)}, f32[35840]{0:T(1024)}, u32[]{:S(2)}, u32[]{:S(2)}) collective-permute-start(f32[35840]{0:T(1024)} %pad_maximum_fusion.3), channel_id=1, source_target_pairs={{1,0},{2,1},{3,2},{4,3},{5,4},{6,5},{7,6},{8,7},{9,8},{10,9},{11,1... | collective-permute-start | bytes 430088 | tf_op jit(solution)/shard_map/ppermute | solution.py:191
  16.4 36.2 %collective-permute-start.3 = (f32[35840]{0:T(1024)}, f32[35840]{0:T(1024)}, u32[]{:S(2)}, u32[]{:S(2)}) collective-permute-start(f32[35840]{0:T(1024)} %pad_maximum_fusion.2), channel_id=1, source_target_pairs={{0,1},{1,2},{2,3},{3,4},{4,5},{5,6},{6,7},{7,8},{8,9},{9,10},{10,1... | collective-permute-start | bytes 430088 | tf_op jit(solution)/shard_map/ppermute | solution.py:190
  23.2 7.4 %collective-permute-start.1 = (f32[5,16,32]{2,1,0:T(8,128)S(1)}, f32[5,16,32]{2,1,0:T(8,128)S(1)}, u32[]{:S(2)}, u32[]{:S(2)}) collective-permute-start(f32[5,16,32]{2,1,0:T(8,128)S(1)} %pad_maximum_fusion.17), channel_id=1, source_target_pairs={{0,2},{1,3},{2,0},{3,1},{4,6},{5,7},{6,4},{7,5},{8,10},{9,11},{10,... | collective-permute-start | bytes 30728 | tf_op jit(solution)/shard_map/ppermute | solution.py:33
  30.6 18.2 %copy-start.10 = (f32[4,16,32]{2,1,0:T(8,128)}, f32[4,16,32]{2,1,0:T(8,128)S(1)}, u32[]{:S(2)}) copy-start(f32[4,16,32]{2,1,0:T(8,128)S(1)} %maximum_select_fusion) | copy-start | bytes 24580
  31.2 16.0 %collective-permute-start.2 = (f32[8,16,32]{2,1,0:T(8,128)}, f32[8,16,32]{2,1,0:T(8,128)}, u32[]{:S(2)}, u32[]{:S(2)}) collective-permute-start(f32[8,16,32]{2,1,0:T(8,128)} %fusion.8), channel_id=1, source_target_pairs={{0,4},{1,5},{2,6},{3,7},{4,0},{5,1},{6,2},{7,3},{8,12},{9,13},{10,... | collective-permute-start | bytes 49160 | tf_op jit(solution)/shard_map/ppermute | solution.py:33
  37.3 6.9 %copy-start.2 = (f32[4,32,4,32]{3,1,2,0:T(8,128)S(1)}, f32[4,32,4,32]{3,1,2,0:T(8,128)}, u32[]{:S(2)}) copy-start(f32[4,32,4,32]{3,1,2,0:T(8,128)} %fusion.15) | copy-start | bytes 196612
  37.3 7.7 %copy-start.12 = (bf16[64,1024]{1,0:T(8,128)(2,1)S(1)}, bf16[64,1024]{1,0:T(8,128)(2,1)}, u32[]{:S(2)}) copy-start(bf16[64,1024]{1,0:T(8,128)(2,1)} %param.21) | copy-start | bytes 393220
  37.3 8.7 %copy-start.11 = (bf16[64,2048]{1,0:T(8,128)(2,1)S(1)}, bf16[64,2048]{1,0:T(8,128)(2,1)}, u32[]{:S(2)}) copy-start(bf16[64,2048]{1,0:T(8,128)(2,1)} %param.18) | copy-start | bytes 786436
  37.3 9.2 %copy-start.6 = (f32[3,64,64]{2,0,1:T(4,128)S(1)}, f32[3,64,64]{2,0,1:T(4,128)}, u32[]{:S(2)}) copy-start(f32[3,64,64]{2,0,1:T(4,128)} %copy.53) | copy-start | bytes 147460
  48.0 0.8 copy-start.13
  48.0 3.7 %copy-start.15 = (f32[1,16,32]{2,1,0:T(8,128)}, f32[1,16,32]{2,1,0:T(8,128)S(1)}, u32[]{:S(2)}) copy-start(f32[1,16,32]{2,1,0:T(8,128)S(1)} %get-tuple-element.34) | copy-start | bytes 6148
  48.7 21.7 %copy-start.8 = (f32[4,16,32]{2,1,0:T(8,128)}, f32[4,16,32]{2,1,0:T(8,128)S(1)}, u32[]{:S(2)}) copy-start(f32[4,16,32]{2,1,0:T(8,128)S(1)} %maximum_select_fusion.1) | copy-start | bytes 24580
  50.4 20.0 %copy-start.7 = (f32[64,512]{1,0:T(8,128)S(1)}, f32[64,512]{1,0:T(8,128)}, u32[]{:S(2)}) copy-start(f32[64,512]{1,0:T(8,128)} %copy.26) | copy-start | bytes 393220
  62.6 19.0 %collective-permute-start.6 = (f32[9,16,32]{2,1,0:T(8,128)}, f32[9,16,32]{2,1,0:T(8,128)S(1)}, u32[]{:S(2)}, u32[]{:S(2)}) collective-permute-start(f32[9,16,32]{2,1,0:T(8,128)} %get-tuple-element.13), channel_id=1, source_target_pairs={{8,0},{9,1},{10,2},{11,3},{12,4},{13,5},{14,6},{15,7},{16,8},{17,9... | collective-permute-start | bytes 55304 | tf_op jit(solution)/shard_map/ppermute | solution.py:38
  65.0 16.7 %collective-permute-start.5 = (f32[9,16,32]{2,1,0:T(8,128)}, f32[9,16,32]{2,1,0:T(8,128)S(1)}, u32[]{:S(2)}, u32[]{:S(2)}) collective-permute-start(f32[9,16,32]{2,1,0:T(8,128)} %get-tuple-element.12), channel_id=1, source_target_pairs={{0,8},{1,9},{2,10},{3,11},{4,12},{5,13},{6,14},{7,15},{8,16},{9,17... | collective-permute-start | bytes 55304 | tf_op jit(solution)/shard_map/ppermute | solution.py:38
  74.7 7.0 %copy-start.16 = (f32[1,16,32]{2,1,0:T(8,128)S(1)}, f32[1,16,32]{2,1,0:T(8,128)}, u32[]{:S(2)}) copy-start(f32[1,16,32]{2,1,0:T(8,128)} %copy-done.15) | copy-start | bytes 6148
  74.7 7.0 %copy-start.19 = (f32[1,16,32]{2,1,0:T(8,128)S(1)}, f32[1,16,32]{2,1,0:T(8,128)}, u32[]{:S(2)}) copy-start(f32[1,16,32]{2,1,0:T(8,128)} %get-tuple-element.50) | copy-start | bytes 6148
  74.7 7.0 %copy-start.20 = (f32[1,16,32]{2,1,0:T(8,128)S(1)}, f32[1,16,32]{2,1,0:T(8,128)}, u32[]{:S(2)}) copy-start(f32[1,16,32]{2,1,0:T(8,128)} %get-tuple-element.51) | copy-start | bytes 6148
  74.7 20.8 %copy-start.9 = (f32[4,16,32]{2,1,0:T(8,128)S(1)}, f32[4,16,32]{2,1,0:T(8,128)}, u32[]{:S(2)}) copy-start(f32[4,16,32]{2,1,0:T(8,128)} %copy-done.8) | copy-start | bytes 24580
  74.7 28.2 %copy-start.14 = (f32[1,16,32]{2,1,0:T(8,128)S(1)}, f32[1,16,32]{2,1,0:T(8,128)}, u32[]{:S(2)}) copy-start(f32[1,16,32]{2,1,0:T(8,128)} %copy-done.13) | copy-start | bytes 6148
  74.7 28.8 %copy-start.3 = (f32[4,32,4,32]{3,2,1,0:T(4,128)S(1)}, f32[4,32,4,32]{3,2,1,0:T(4,128)}, u32[]{:S(2)}) copy-start(f32[4,32,4,32]{3,2,1,0:T(4,128)} %copy.52) | copy-start | bytes 196612
  74.7 29.4 %copy-start = (f32[64,16,64]{2,1,0:T(8,128)S(1)}, f32[64,16,64]{2,1,0:T(8,128)}, u32[]{:S(2)}) copy-start(f32[64,16,64]{2,1,0:T(8,128)} %shard_map.127) | copy-start | bytes 786436
  81.7 21.2 %collective-permute-start.8 = (f32[3,16,32]{2,1,0:T(8,128)S(1)}, f32[3,16,32]{2,1,0:T(8,128)S(1)}, u32[]{:S(2)}, u32[]{:S(2)}) collective-permute-start(f32[3,16,32]{2,1,0:T(8,128)S(1)} %get-tuple-element.16), channel_id=1, source_target_pairs={{16,0},{17,1},{18,2},{19,3},{20,4},{21,5},{22,6},{23,7},{24,8},{25... | collective-permute-start | bytes 18440 | tf_op jit(solution)/shard_map/ppermute | solution.py:38
  93.5 9.3 %collective-permute-start.7 = (f32[3,16,32]{2,1,0:T(8,128)S(1)}, f32[3,16,32]{2,1,0:T(8,128)S(1)}, u32[]{:S(2)}, u32[]{:S(2)}) collective-permute-start(f32[3,16,32]{2,1,0:T(8,128)S(1)} %get-tuple-element.15), channel_id=1, source_target_pairs={{0,16},{1,17},{2,18},{3,19},{4,20},{5,21},{6,22},{7,23},{8,24},{9,... | collective-permute-start | bytes 18440 | tf_op jit(solution)/shard_map/ppermute | solution.py:38
